TPU v7x, 32 devices: a whole 2x2x4 slice. The times are simulated.
32 devices in a mesh: dp: 2 (over y), expert: 16 (over z, x, core).
Axes of the slice: x: 2, y: 2, z: 4, core: 2. Of those that a mesh axis runs over, the one named last changes fastest.
Arguments:
- tokens: bfloat16 [2048, 1024], P(('dp', 'expert')), may hold values from -6 to 6
- cotangent: bfloat16 [2048, 1024], P(('dp', 'expert')), may hold values from -6 to 6
- expert_ids: int32 [2048, 6], P(('dp', 'expert')), may hold values from 0 to 15, all different within a row; in each aligned block of 64 rows (0 to 63, 64 to 127, ...) at most 32 rows name the same one
- gate_probs: float32 [2048, 6], P(('dp', 'expert')), may hold values from 0.1 to 1
- w_gate_up: bfloat16 [16, 1024, 1408], P('expert', 'dp'), may hold values from -0.1875 to 0.1875
- w_down: bfloat16 [16, 704, 1024], P('expert'), may hold values from -0.21875 to 0.21875
Outputs:
- layer_out: bfloat16 [2048, 1024], P(('dp', 'expert'))
- input_grad: bfloat16 [2048, 1024], P(('dp', 'expert'))
- prob_grad: float32 [2048, 6], P(('dp', 'expert'))
- gate_up_grad: bfloat16 [16, 1024, 1408], P('expert', 'dp')
Inputs may be any that keep to these rules, and one draw needn't show every extreme that they name: `expert_ids`: each row names 6 different experts. Within each aligned block of 64 rows no expert is named by more than 32 rows, and in some block an expert is named by exactly 32 rows.
All inputs are finite; a program needn't handle non-finite values.
Results may differ from a plain program's by a relative error of at most 0.013.
Values may be sent and summed in bfloat16 or wider, within the bound.
No kernel may reach another device: no remote copies, remote signals or barrier semaphores. Data moves between devices by JAX's collectives and lax.ppermute only.
A program may use at most 64 MiB of HBM per device.

v0:
```python
import jax
import jax.numpy as jnp
from jax import lax
from jax.sharding import PartitionSpec as P


def local(tokens, cotangent, expert_ids, gate_probs, w_gate_up, w_down):
    experts = lax.axis_size("expert")
    token_count = tokens.shape[0]
    model_width = tokens.shape[1]
    top_count = expert_ids.shape[1]
    hidden_units = w_down.shape[1]
    capacity = 4 * token_count * top_count // (3 * experts)
    flat_routes = expert_ids.reshape(token_count * top_count)
    onehot = (flat_routes[:, None] == jnp.arange(experts, dtype=jnp.int32)[None, :]).astype(
        jnp.int32
    )
    before = jnp.cumsum(onehot, axis=0) - onehot
    slot_rank = jnp.sum(before * onehot, axis=1)
    target_rows = flat_routes * capacity + slot_rank
    token_copies = jnp.broadcast_to(tokens[:, None, :], (token_count, top_count, model_width))
    token_copies = token_copies.reshape(token_count * top_count, model_width)
    cot_copies = (gate_probs[:, :, None] * cotangent[:, None, :].astype(jnp.float32)).astype(
        jnp.bfloat16
    )
    cot_copies = cot_copies.reshape(token_count * top_count, model_width)
    token_send = (
        jnp.zeros((experts * capacity, model_width), jnp.bfloat16).at[target_rows].set(token_copies)
    )
    cot_send = (
        jnp.zeros((experts * capacity, model_width), jnp.bfloat16).at[target_rows].set(cot_copies)
    )
    token_send = token_send.reshape(experts, capacity, model_width)
    cot_send = cot_send.reshape(experts, capacity, model_width)
    token_recv, cot_early = (
        lax.all_to_all(token_send, "expert", split_axis=0, concat_axis=0, tiled=True),
        lax.all_to_all(cot_send, "expert", split_axis=0, concat_axis=0, tiled=True),
    )
    input_rows = token_recv.reshape(experts * capacity, model_width)
    weight_down = w_down[0]
    weight_fwd = lax.all_gather(w_gate_up, "dp", axis=1, tiled=True)[0]
    gate_up = jnp.dot(input_rows, weight_fwd, preferred_element_type=jnp.float32)
    gate = gate_up[:, :hidden_units]
    upper = gate_up[:, hidden_units:]
    sigma = jax.nn.sigmoid(gate)
    active = gate * sigma
    hidden = (active * upper).astype(jnp.bfloat16)
    output_rows = jnp.dot(hidden, weight_down, preferred_element_type=jnp.float32).astype(
        jnp.bfloat16
    )
    cot_rows = cot_early.reshape(experts * capacity, model_width)
    hidden_grad = lax.dot_general(
        cot_rows, weight_down, (((1,), (1,)), ((), ())), preferred_element_type=jnp.float32
    )
    gate_cot = hidden_grad * upper * sigma * (1.0 + gate * (1.0 - sigma))
    upper_cot = hidden_grad * active
    pair_cot = jnp.concatenate([gate_cot, upper_cot], axis=1).astype(jnp.bfloat16)
    input_cot = lax.dot_general(
        pair_cot, weight_fwd, (((1,), (1,)), ((), ())), preferred_element_type=jnp.float32
    ).astype(jnp.bfloat16)
    weight_cot = lax.dot_general(
        input_rows, pair_cot, (((0,), (0,)), ((), ())), preferred_element_type=jnp.float32
    )
    output_back, input_back = (
        lax.all_to_all(
            output_rows.reshape(experts, capacity, model_width),
            "expert",
            split_axis=0,
            concat_axis=0,
            tiled=True,
        ),
        lax.all_to_all(
            input_cot.reshape(experts, capacity, model_width),
            "expert",
            split_axis=0,
            concat_axis=0,
            tiled=True,
        ),
    )
    slot_out = output_back.reshape(experts * capacity, model_width)[target_rows].reshape(
        token_count, top_count, model_width
    )
    slot_in = input_back.reshape(experts * capacity, model_width)[target_rows].reshape(
        token_count, top_count, model_width
    )
    layer_out = jnp.sum(gate_probs[:, :, None] * slot_out.astype(jnp.float32), axis=1).astype(
        jnp.bfloat16
    )
    input_grad = jnp.sum(slot_in.astype(jnp.float32), axis=1).astype(jnp.bfloat16)
    prob_grad = jnp.einsum("td,tkd->tk", cotangent, slot_out, preferred_element_type=jnp.float32)
    grad_rows = lax.psum_scatter(
        weight_cot.astype(jnp.bfloat16), "dp", scatter_dimension=0, tiled=True
    )
    return (layer_out, input_grad, prob_grad, grad_rows[None])


def solution(mesh):
    placed = (
        P(("dp", "expert"), None),
        P(("dp", "expert"), None),
        P(("dp", "expert"), None),
        P(("dp", "expert"), None),
        P("expert", "dp", None),
        P("expert", None, None),
    )
    return jax.shard_map(
        local,
        mesh=mesh,
        in_specs=placed,
        out_specs=(
            P(("dp", "expert"), None),
            P(("dp", "expert"), None),
            P(("dp", "expert"), None),
            P("expert", "dp", None),
        ),
        check_vma=False,
    )
```

profile of v0, /device:TPU:11, one launch (start us, length us, event | category | flops | bytes accessed | tf_op | source)
XLA Modules:
  0.0 166.2 jit_solution(6136234102006525579)
XLA Ops:
  7.2 0.0 copy-start
  7.2 0.8 broadcast_multiply_fusion
  8.0 0.8 copy.15
  8.8 0.1 eq.29
  8.9 0.1 eq.25
  9.0 0.1 copy.14
  9.1 0.1 mul.69
  9.3 0.9 reduce-window.6
  10.2 0.2 slice_reduce_fusion
  10.4 1.1 broadcast_in_dim.4
  11.5 0.3 reshape.126
  11.8 0.1 fusion.21
  11.9 3.1 %scatter_custom_fusion = bf16[512,1024]{1,0:T(8,128)(2,1)} fusion(s32[384]{0:T(512)S(1)} %fusion.23, bf16[384,1024]{1,0:T(8,128)(2,1)S(1)} %reshape.126, bf16[]{:T(256)} %constant.6.clone.1), kind=kCustom, calls=%fused_computation.25 | custom fusion | bytes 1048578 | tf_op jit(solution)/shard_map/scatter | solution.py:28
  15.0 0.0 copy-start.3
  15.0 6.7 %all-to-all-start = ((bf16[16,32,1024]{2,1,0:T(8,128)(2,1)}), bf16[16,32,1024]{2,1,0:T(8,128)(2,1)}, u32[]{:S(2)}, u32[]{:S(2)}) async-start(bf16[16,32,1024]{2,1,0:T(8,128)(2,1)} %bitcast.1), calls=%async_computation | async-start | bytes 2097152 | tf_op jit(solution)/shard_map/all_to_all | solution.py:36
  21.7 0.0 all-gather.2.cloned.1.call-start
  21.7 0.7 all-gather.2.cloned.1.call-update
  22.4 0.0 copy-done.3
  22.4 0.1 copy.13
  22.5 0.0 copy-start.1
  22.5 0.6 copy-done.1
  23.1 0.1 mul.74
  23.2 1.2 mul.76
  24.4 1.4 mul.77
  25.8 4.0 %scatter_custom_fusion.1 = bf16[512,1024]{1,0:T(8,128)(2,1)} fusion(s32[384]{0:T(512)S(1)} %fusion.23, f32[384,1024]{1,0:T(8,128)} %mul.77, f32[384]{0:T(512)S(1)} %mul.74, bf16[]{:T(256)} %constant.6.clone.1), kind=kCustom, calls=%fused_computation.22 | custom fusion | flops 786432 | bytes 2623490 | tf_op jit(solution)/shard_map/scatter | solution.py:31
  29.8 17.2 %all-to-all-done = bf16[16,32,1024]{2,1,0:T(8,128)(2,1)} async-done(((bf16[16,32,1024]{2,1,0:T(8,128)(2,1)}), bf16[16,32,1024]{2,1,0:T(8,128)(2,1)}, u32[]{:S(2)}, u32[]{:S(2)}) %all-to-all-start) | async-done | bytes 1048608 | tf_op jit(solution)/shard_map/all_to_all | solution.py:36
  46.9 4.6 %all-to-all-start.2 = ((bf16[16,32,1024]{2,1,0:T(8,128)(2,1)}), bf16[16,32,1024]{2,1,0:T(8,128)(2,1)S(1)}, u32[]{:S(2)}, u32[]{:S(2)}) async-start(bf16[16,32,1024]{2,1,0:T(8,128)(2,1)} %bitcast.7), calls=%async_computation.2 | async-start | bytes 2097152 | tf_op jit(solution)/shard_map/all_to_all | solution.py:37
  51.6 0.0 reduce-scatter.2.cloned.1.call-start
  51.6 15.0 %all-gather.2.cloned.1.call-done = bf16[1,1024,1408]{2,1,0:T(8,128)(2,1)} async-done(((bf16[1,512,1408]{2,1,0:T(8,128)(2,1)}), bf16[1,1024,1408]{2,1,0:T(8,128)(2,1)}) %all-gather.2.cloned.1.call-update) | async-done | bytes 2883600 | tf_op jit(solution)/shard_map/all_gather | solution.py:41
  66.6 5.5 %fusion.2 = f32[512,1408]{1,0:T(8,128)} fusion(bf16[512,1024]{1,0:T(8,128)(2,1)} %bitcast.2, bf16[1,1024,1408]{2,1,0:T(8,128)(2,1)} %all-gather.2.cloned.1.call-done), kind=kOutput, calls=%fused_computation.7 | convolution fusion | flops 1476395008 | bytes 6815744 | tf_op jit(solution)/shard_map/dot_general | solution.py:42
  72.2 4.3 %all-to-all-done.2 = bf16[16,32,1024]{2,1,0:T(8,128)(2,1)S(1)} async-done(((bf16[16,32,1024]{2,1,0:T(8,128)(2,1)}), bf16[16,32,1024]{2,1,0:T(8,128)(2,1)S(1)}, u32[]{:S(2)}, u32[]{:S(2)}) %all-to-all-start.2) | async-done | bytes 1048608 | tf_op jit(solution)/shard_map/all_to_all | solution.py:37
  76.5 0.0 copy-done
  76.5 3.3 %multiply_convert_fusion.1 = (bf16[512,704]{1,0:T(8,128)(2,1)S(1)}, bf16[512,704]{1,0:T(8,128)(2,1)S(1)}) fusion(f32[512,1408]{1,0:T(8,128)} %fusion.2, bf16[512,1024]{1,0:T(8,128)(2,1)S(1)} %bitcast.53, bf16[1,704,1024]{2,1,0:T(8,128)(2,1)S(1)} %copy-done), kind=kOutput, calls=%fused_computation.11 | convolution fusion | flops 742883328 | bytes 6815744 | tf_op jit(solution)/shard_map/dot_general | solution.py:52
  79.8 0.0 copy-start.4
  79.8 0.9 copy-done.4
  80.7 4.7 %convolution_convert_fusion = bf16[1024,1408]{1,0:T(8,128)(2,1)} fusion(bf16[512,1024]{1,0:T(8,128)(2,1)} %bitcast.2, bf16[512,704]{1,0:T(8,128)(2,1)S(1)} %get-tuple-element.5, bf16[512,704]{1,0:T(8,128)(2,1)S(1)} %get-tuple-element.4), kind=kOutput, calls=%fused_computation.4 | convolution fusion | flops 1480720384 | bytes 5373952 | tf_op jit(solution)/shard_map/dot_general | solution.py:61
  85.3 0.0 reduce-scatter.2.cloned.1.call-update
  85.4 4.0 %convolution_convert_fusion.1 = bf16[512,1024]{1,0:T(8,128)(2,1)} fusion(bf16[1,704,1024]{2,1,0:T(8,128)(2,1)S(1)} %copy-done, f32[512,1408]{1,0:T(8,128)} %fusion.2), kind=kOutput, calls=%fused_computation.17 | convolution fusion | flops 740884480 | bytes 5636096 | tf_op jit(solution)/shard_map/dot_general | solution.py:48
  89.3 4.9 %all-to-all-start.1 = ((bf16[16,32,1024]{2,1,0:T(8,128)(2,1)}), bf16[16,32,1024]{2,1,0:T(8,128)(2,1)S(1)}, u32[]{:S(2)}, u32[]{:S(2)}) async-start(bf16[16,32,1024]{2,1,0:T(8,128)(2,1)} %bitcast.5), calls=%async_computation.1 | async-start | bytes 2097152 | tf_op jit(solution)/shard_map/all_to_all | solution.py:65
  94.3 4.9 %fusion.5 = bf16[512,1024]{1,0:T(8,128)(2,1)} fusion(bf16[1,1024,1408]{2,1,0:T(8,128)(2,1)} %all-gather.2.cloned.1.call-done, bf16[512,704]{1,0:T(8,128)(2,1)} %copy-done.4, bf16[512,704]{1,0:T(8,128)(2,1)S(1)} %get-tuple-element.4), kind=kOutput, calls=%fused_computation.16 | convolution fusion | flops 1479802880 | bytes 5373952 | tf_op jit(solution)/shard_map/dot_general | solution.py:58
  99.2 20.4 %all-to-all-done.1 = bf16[16,32,1024]{2,1,0:T(8,128)(2,1)S(1)} async-done(((bf16[16,32,1024]{2,1,0:T(8,128)(2,1)}), bf16[16,32,1024]{2,1,0:T(8,128)(2,1)S(1)}, u32[]{:S(2)}, u32[]{:S(2)}) %all-to-all-start.1) | async-done | bytes 1048608 | tf_op jit(solution)/shard_map/all_to_all | solution.py:65
  119.6 4.5 %all-to-all-start.3 = ((bf16[16,32,1024]{2,1,0:T(8,128)(2,1)}), bf16[16,32,1024]{2,1,0:T(8,128)(2,1)S(1)}, u32[]{:S(2)}, u32[]{:S(2)}) async-start(bf16[16,32,1024]{2,1,0:T(8,128)(2,1)} %bitcast.54), calls=%async_computation.3 | async-start | bytes 2097152 | tf_op jit(solution)/shard_map/all_to_all | solution.py:72
  124.1 2.7 %gather_fusion = bf16[384,1024]{1,0:T(8,128)(2,1)} fusion(bf16[512,1024]{1,0:T(8,128)(2,1)S(1)} %bitcast.51, s32[1024]{0:T(1024)S(1)} %pad_clamp_fusion), kind=kCustom, calls=%fused_computation | custom fusion | bytes 1574400 | tf_op jit(solution)/shard_map/gather | solution.py:80
  126.8 22.2 %all-to-all-done.3 = bf16[16,32,1024]{2,1,0:T(8,128)(2,1)S(1)} async-done(((bf16[16,32,1024]{2,1,0:T(8,128)(2,1)}), bf16[16,32,1024]{2,1,0:T(8,128)(2,1)S(1)}, u32[]{:S(2)}, u32[]{:S(2)}) %all-to-all-start.3) | async-done | bytes 1048608 | tf_op jit(solution)/shard_map/all_to_all | solution.py:72
  149.0 2.7 %gather_fusion.1 = bf16[384,1024]{1,0:T(8,128)(2,1)} fusion(bf16[512,1024]{1,0:T(8,128)(2,1)S(1)} %bitcast.52, s32[1024]{0:T(1024)S(1)} %pad_clamp_fusion), kind=kCustom, calls=%fused_computation.1 | custom fusion | bytes 1574400 | tf_op jit(solution)/shard_map/gather | solution.py:83
  151.6 0.0 copy-start.2
  151.6 1.4 reshape.100
  153.0 0.0 copy-done.2
  153.0 0.7 fusion.16
  153.8 0.7 copy.23
  154.4 1.3 reshape.105
  155.8 1.4 reduce_sum.35
  157.1 2.2 %multiply_reduce_fusion = bf16[64,1024]{1,0:T(8,128)(2,1)} fusion(bf16[64,6,1024]{2,1,0:T(8,128)(2,1)S(1)} %reshape.100, f32[64,6]{1,0:T(8,128)} %copy-done.1), kind=kLoop, calls=%fused_computation.9 | loop fusion | flops 1114112 | bytes 919040 | tf_op jit(solution)/shard_map/reduce_sum | solution.py:86
  159.3 0.0 reduce-scatter.2.cloned.1.call-done
  (4 shorter events, 0.1 us)
Async XLA Ops:
  7.2 69.3 %copy-start = (bf16[1,704,1024]{2,1,0:T(8,128)(2,1)S(1)}, bf16[1,704,1024]{2,1,0:T(8,128)(2,1)}, u32[]{:S(2)}) copy-start(bf16[1,704,1024]{2,1,0:T(8,128)(2,1)} %param.11) | copy-start | bytes 4325380
  15.0 7.4 %copy-start.3 = (f32[64,6]{0,1:T(8,128)S(1)}, f32[64,6]{0,1:T(8,128)}, u32[]{:S(2)}) copy-start(f32[64,6]{0,1:T(8,128)} %param.9) | copy-start | bytes 4612
  15.0 32.0 %all-to-all-start = ((bf16[16,32,1024]{2,1,0:T(8,128)(2,1)}), bf16[16,32,1024]{2,1,0:T(8,128)(2,1)}, u32[]{:S(2)}, u32[]{:S(2)}) async-start(bf16[16,32,1024]{2,1,0:T(8,128)(2,1)} %bitcast.1), calls=%async_computation | async-start | bytes 2097152 | tf_op jit(solution)/shard_map/all_to_all | solution.py:36
  21.7 45.0 %all-gather.2.cloned.1.call-start = ((), (), s32[]{:S(2)}) async-start(), calls=%async_computation.5 | async-start | bytes 4325376 | tf_op jit(solution)/shard_map/all_gather | solution.py:41
  22.5 0.6 copy-start.1
  46.9 29.5 %all-to-all-start.2 = ((bf16[16,32,1024]{2,1,0:T(8,128)(2,1)}), bf16[16,32,1024]{2,1,0:T(8,128)(2,1)S(1)}, u32[]{:S(2)}, u32[]{:S(2)}) async-start(bf16[16,32,1024]{2,1,0:T(8,128)(2,1)} %bitcast.7), calls=%async_computation.2 | async-start | bytes 2097152 | tf_op jit(solution)/shard_map/all_to_all | solution.py:37
  51.6 107.8 %reduce-scatter.2.cloned.1.call-start = ((), (), s32[]{:S(2)}) async-start(), calls=%async_computation.6 | async-start | bytes 4325376 | tf_op jit(solution)/shard_map/reduce_scatter | solution.py:91
  79.8 0.9 copy-start.4
  89.3 30.2 %all-to-all-start.1 = ((bf16[16,32,1024]{2,1,0:T(8,128)(2,1)}), bf16[16,32,1024]{2,1,0:T(8,128)(2,1)S(1)}, u32[]{:S(2)}, u32[]{:S(2)}) async-start(bf16[16,32,1024]{2,1,0:T(8,128)(2,1)} %bitcast.5), calls=%async_computation.1 | async-start | bytes 2097152 | tf_op jit(solution)/shard_map/all_to_all | solution.py:65
  119.6 29.4 %all-to-all-start.3 = ((bf16[16,32,1024]{2,1,0:T(8,128)(2,1)}), bf16[16,32,1024]{2,1,0:T(8,128)(2,1)S(1)}, u32[]{:S(2)}, u32[]{:S(2)}) async-start(bf16[16,32,1024]{2,1,0:T(8,128)(2,1)} %bitcast.54), calls=%async_computation.3 | async-start | bytes 2097152 | tf_op jit(solution)/shard_map/all_to_all | solution.py:72
  151.6 1.4 copy-start.2
Sparse Core Ops, SparseCore 0:
  24.0 42.5 all-gather.1
  85.5 39.9 reduce-scatter.1
where the time goes:
time: 167 us; the launch traced here: 166 us
  waiting for transfers between devices  79.7 us (48%)
  matrix products  23.1 us (14%)
  starting transfers between devices  20.9 us (13%)
  local copies, waits for them, and re-layouts  18.9 us (11%)
  between operations  14.2 us (9%)
  other arithmetic  9.39 us (6%)
    all_to_all x1, waiting for transfers between devices, local(): lax.all_to_all(input_cot.reshape(experts, capacity, model_width), 'expert...  22.2 us
    all_to_all x1, waiting for transfers between devices, local(): lax.all_to_all(output_rows.reshape(experts, capacity, model_width), 'expe...  20.4 us
    all_to_all x1, waiting for transfers between devices, local(): lax.all_to_all(token_send, 'expert', split_axis=0, concat_axis=0, tiled=T...  17.2 us
    all_gather x1, waiting for transfers between devices, local(): weight_fwd = lax.all_gather(w_gate_up, 'dp', axis=1, tiled=True)[0]  15 us
    all_to_all x1, starting transfers between devices, local(): lax.all_to_all(token_send, 'expert', split_axis=0, concat_axis=0, tiled=T...  6.69 us
    dot_general x1, matrix products, local(): jnp.dot(input_rows, weight_fwd, preferred_element_type=jnp.float32)  5.5 us
    all_to_all x1, starting transfers between devices, local(): lax.all_to_all(output_rows.reshape(experts, capacity, model_width), 'expe...  4.94 us
    dot_general x1, matrix products, local(): lax.dot_general(pair_cot, weight_fwd, (((1,), (1,)), ((), ())), preferred...  4.88 us
  transfers between devices with their start and end apart: 6, of which 5 were waited for; matrix products, arithmetic and copies ran while one was open for 21% of the time, Pallas kernels for 0%

commit v1 on v0

v1 whole, which is shorter than its diff:
```python
import jax
import jax.numpy as jnp
from jax import lax
from jax.sharding import PartitionSpec as P


def gather_rows(own, axis_name, width):
    count = lax.axis_size(axis_name)
    me = lax.axis_index(axis_name)
    pieces = [(me, own)]
    for shift in range(1, count):
        moved = lax.ppermute(own, axis_name, [(i, (i + shift) % count) for i in range(count)])
        pieces.append(((me - shift) % count, moved))
    return pieces


def local(tokens, cotangent, expert_ids, gate_probs, w_gate_up, w_down):
    experts = lax.axis_size("expert")
    replicas = lax.axis_size("dp")
    me_dp = lax.axis_index("dp")
    token_count = tokens.shape[0]
    model_width = tokens.shape[1]
    top_count = expert_ids.shape[1]
    hidden_units = w_down.shape[1]
    block_rows = w_gate_up.shape[1]
    capacity = 4 * token_count * top_count // (3 * experts)
    weight_blocks = gather_rows(w_gate_up[0], "dp", block_rows)
    flat_routes = expert_ids.reshape(token_count * top_count)
    onehot = (flat_routes[:, None] == jnp.arange(experts, dtype=jnp.int32)[None, :]).astype(
        jnp.int32
    )
    before = jnp.cumsum(onehot, axis=0) - onehot
    slot_rank = jnp.sum(before * onehot, axis=1)
    target_rows = flat_routes * capacity + slot_rank
    token_copies = jnp.broadcast_to(tokens[:, None, :], (token_count, top_count, model_width))
    token_copies = token_copies.reshape(token_count * top_count, model_width)
    cot_copies = (gate_probs[:, :, None] * cotangent[:, None, :].astype(jnp.float32)).astype(
        jnp.bfloat16
    )
    cot_copies = cot_copies.reshape(token_count * top_count, model_width)
    both_copies = jnp.concatenate([token_copies, cot_copies], axis=1)
    both_send = (
        jnp.zeros((experts * capacity, 2 * model_width), jnp.bfloat16)
        .at[target_rows]
        .set(both_copies)
    )
    both_recv = lax.all_to_all(
        both_send.reshape(experts, capacity, 2 * model_width),
        "expert",
        split_axis=0,
        concat_axis=0,
        tiled=True,
    ).reshape(experts * capacity, 2 * model_width)
    input_rows = both_recv[:, :model_width]
    cot_rows = both_recv[:, model_width:]
    weight_down = w_down[0]

    def cols(block):
        return lax.dynamic_slice_in_dim(input_rows, block * block_rows, block_rows, axis=1)

    gate_up = None
    for block, weight in weight_blocks:
        part = jnp.dot(cols(block), weight, preferred_element_type=jnp.float32)
        gate_up = part if gate_up is None else gate_up + part
    gate = gate_up[:, :hidden_units]
    upper = gate_up[:, hidden_units:]
    sigma = jax.nn.sigmoid(gate)
    active = gate * sigma
    hidden = (active * upper).astype(jnp.bfloat16)
    output_rows = jnp.dot(hidden, weight_down, preferred_element_type=jnp.float32).astype(
        jnp.bfloat16
    )
    hidden_grad = lax.dot_general(
        cot_rows, weight_down, (((1,), (1,)), ((), ())), preferred_element_type=jnp.float32
    )
    gate_cot = hidden_grad * upper * sigma * (1.0 + gate * (1.0 - sigma))
    upper_cot = hidden_grad * active
    pair_cot = jnp.concatenate([gate_cot, upper_cot], axis=1).astype(jnp.bfloat16)
    input_cot = jnp.zeros((experts * capacity, model_width), jnp.bfloat16)
    for block, weight in weight_blocks:
        part = lax.dot_general(
            pair_cot, weight, (((1,), (1,)), ((), ())), preferred_element_type=jnp.float32
        ).astype(jnp.bfloat16)
        input_cot = lax.dynamic_update_slice_in_dim(input_cot, part, block * block_rows, axis=1)
    back = lax.all_to_all(
        jnp.concatenate([output_rows, input_cot], axis=1).reshape(
            experts, capacity, 2 * model_width
        ),
        "expert",
        split_axis=0,
        concat_axis=0,
        tiled=True,
    ).reshape(experts * capacity, 2 * model_width)
    slot_both = back[target_rows].reshape(token_count, top_count, 2 * model_width)
    slot_out = slot_both[:, :, :model_width]
    slot_in = slot_both[:, :, model_width:]
    layer_out = jnp.sum(gate_probs[:, :, None] * slot_out.astype(jnp.float32), axis=1).astype(
        jnp.bfloat16
    )
    input_grad = jnp.sum(slot_in.astype(jnp.float32), axis=1).astype(jnp.bfloat16)
    prob_grad = jnp.einsum("td,tkd->tk", cotangent, slot_out, preferred_element_type=jnp.float32)
    grad_rows = None
    for shift in range(replicas):
        block = (me_dp + shift) % replicas
        partial = lax.dot_general(
            cols(block), pair_cot, (((0,), (0,)), ((), ())), preferred_element_type=jnp.float32
        ).astype(jnp.bfloat16)
        if shift:
            partial = lax.ppermute(
                partial, "dp", [(i, (i + shift) % replicas) for i in range(replicas)]
            )
        grad_rows = (
            partial.astype(jnp.float32)
            if grad_rows is None
            else grad_rows + partial.astype(jnp.float32)
        )
    return (layer_out, input_grad, prob_grad, grad_rows.astype(jnp.bfloat16)[None])


def solution(mesh):
    placed = (
        P(("dp", "expert"), None),
        P(("dp", "expert"), None),
        P(("dp", "expert"), None),
        P(("dp", "expert"), None),
        P("expert", "dp", None),
        P("expert", None, None),
    )
    return jax.shard_map(
        local,
        mesh=mesh,
        in_specs=placed,
        out_specs=(
            P(("dp", "expert"), None),
            P(("dp", "expert"), None),
            P(("dp", "expert"), None),
            P("expert", "dp", None),
        ),
        check_vma=False,
    )
```

time: 167 us -> 150 us (0.90)
  between operations: 14.2 us -> 0.81 us
  starting transfers between devices: 20.9 us -> 13.9 us
  waiting for transfers between devices: 79.7 us -> 84.6 us
  matrix products: 23.1 us -> 18.4 us
  other arithmetic: 9.39 us -> 13.1 us
    ppermute x0 -> x2, waiting for transfers between devices: none -> 31.9 us  [the longest x1 31.9 us: local(): lax.ppermute(partial, 'dp', [(i, (i + shift) % replicas) for i in range(r...]
    all_gather x1 -> x0, waiting for transfers between devices: 15 us -> none  [local(): weight_fwd = lax.all_gather(w_gate_up, 'dp', axis=1, tiled=True)[0]]
    all_to_all x4 -> x2, waiting for transfers between devices: 64 us -> 52.7 us  [the longest x1 46.2 us: local(): lax.all_to_all(both_send.reshape(experts, capacity, 2 * model_width), 'ex...]
    all_to_all x4 -> x2, starting transfers between devices: 20.8 us -> 11.5 us  [the longest x1 6.55 us: local(): lax.all_to_all(both_send.reshape(experts, capacity, 2 * model_width), 'ex...]
    scatter x1 -> x0, local copies, waits for them, and re-layouts: 3.09 us -> none  [local(): jnp.zeros((experts * capacity, model_width), jnp.bfloat16).at[target_rows]]
    dot_general x1, matrix products: 3.98 us -> 1.08 us  [local(): jnp.dot(hidden, weight_down, preferred_element_type=jnp.float32)]
    ppermute x0 -> x2, starting transfers between devices: none -> 2.48 us  [the longest x1 1.24 us: gather_rows(): lax.ppermute(own, axis_name, [(i, (i + shift) % count) for i in range(cou...]
    gather x2 -> x1, local copies, waits for them, and re-layouts: 5.36 us -> 3.13 us  [local(): back[target_rows].reshape(token_count, top_count, 2 * model_width)]
  transfers between devices with their start and end apart: 6 -> 4, of which waited for: 5 -> 3; matrix products, arithmetic and copies ran while one was open for 21% -> 6% of each run, Pallas kernels for 0% -> 0%
where the time goes in v1:
time: 150 us
  waiting for transfers between devices  84.6 us (56%)
  local copies, waits for them, and re-layouts  18.8 us (13%)
  matrix products  18.4 us (12%)
  starting transfers between devices  13.9 us (9%)
  other arithmetic  13.1 us (9%)
    all_to_all x1, waiting for transfers between devices, local(): lax.all_to_all(both_send.reshape(experts, capacity, 2 * model_width), 'ex...  46.2 us
    ppermute x1, waiting for transfers between devices, local(): lax.ppermute(partial, 'dp', [(i, (i + shift) % replicas) for i in range(r...  31.9 us
    dot_general x2, matrix products, local(): lax.dot_general(cols(block), pair_cot, (((0,), (0,)), ((), ())), preferre...  7.77 us
    all_to_all x1, starting transfers between devices, local(): lax.all_to_all(both_send.reshape(experts, capacity, 2 * model_width), 'ex...  6.55 us
    all_to_all x1, waiting for transfers between devices, local(): lax.all_to_all(jnp.concatenate([output_rows, input_cot], axis=1).reshape(...  6.52 us
    scatter x1, other arithmetic, local(): both_send = jnp.zeros((experts * capacity, 2 * model_width), jnp.bfloat16...  5.26 us
    all_to_all x1, starting transfers between devices, local(): lax.all_to_all(jnp.concatenate([output_rows, input_cot], axis=1).reshape(...  4.9 us
    unnamed x22, local copies, waits for them, and re-layouts  3.84 us
  transfers between devices with their start and end apart: 4, of which 3 were waited for; matrix products, arithmetic and copies ran while one was open for 6% of the time, Pallas kernels for 0%

profile of v1, /device:TPU:11, one launch (start us, length us, event | category | flops | bytes accessed | tf_op | source)
XLA Modules:
  0.0 149.7 jit_solution(8133635513909234119)
XLA Ops:
  0.6 0.0 copy-start
  0.6 0.9 copy.17
  1.5 0.1 eq.33
  1.7 0.1 eq.29
  1.8 0.7 broadcast_multiply_fusion
  2.5 0.9 reduce-window.6
  3.4 0.0 copy-start.5
  3.4 0.2 slice_reduce_fusion.1
  3.6 0.1 copy.16
  3.7 0.3 copy-done.5
  4.0 0.1 mul.83
  4.1 0.8 copy.15
  4.9 0.0 copy-start.4
  4.9 0.6 copy-done.4
  5.5 0.1 mul.85
  5.7 1.2 mul.87
  6.8 1.4 mul.88
  8.2 0.0 copy-start.6
  8.2 0.0 copy-start.1
  8.2 2.1 %broadcast_in_dim.9 = bf16[64,6,1024]{2,1,0:T(8,128)(2,1)} broadcast(bf16[64,1024]{1,0:T(8,128)(2,1)} %param.6), dimensions={0,2} | broadcast | bytes 917504 | tf_op jit(solution)/shard_map/broadcast_in_dim | solution.py:35
  10.4 2.2 %reshape.80 = bf16[384,1024]{1,0:T(8,128)(2,1)} reshape(bf16[64,6,1024]{2,1,0:T(8,128)(2,1)} %broadcast_in_dim.9) | data formatting | bytes 1572864 | tf_op jit(solution)/shard_map/reshape | solution.py:36
  12.5 0.0 copy-done.6
  12.5 0.1 fusion.27
  12.6 0.0 copy-done.1
  12.7 1.0 multiply_convert_fusion.3
  13.7 5.3 %scatter_custom_fusion = bf16[512,2048]{1,0:T(8,128)(2,1)} fusion(s32[384]{0:T(512)S(1)} %fusion.29, bf16[384,1024]{1,0:T(8,128)(2,1)} %multiply_convert_fusion.3, bf16[]{:T(256)} %constant.55, bf16[384,1024]{1,0:T(8,128)(2,1)} %reshape.80, bf16[]{:T(256)} %constant.39.clone.1), kind=kCustom, calls=%fused_computation.9 | custom fusion | flops 3145728 | bytes 3670020 | tf_op jit(solution)/shard_map/scatter | solution.py:45
  18.9 6.6 %all-to-all-start = ((bf16[16,32,2048]{2,1,0:T(8,128)(2,1)}), bf16[16,32,2048]{2,1,0:T(8,128)(2,1)S(1)}, u32[]{:S(2)}, u32[]{:S(2)}) async-start(bf16[16,32,2048]{2,1,0:T(8,128)(2,1)} %bitcast.1), calls=%async_computation | async-start | bytes 4194304 | tf_op jit(solution)/shard_map/all_to_all | solution.py:47
  25.5 1.2 collective-permute-start
  26.7 46.2 %all-to-all-done = bf16[16,32,2048]{2,1,0:T(8,128)(2,1)S(1)} async-done(((bf16[16,32,2048]{2,1,0:T(8,128)(2,1)}), bf16[16,32,2048]{2,1,0:T(8,128)(2,1)S(1)}, u32[]{:S(2)}, u32[]{:S(2)}) %all-to-all-start) | async-done | bytes 2097184 | tf_op jit(solution)/shard_map/all_to_all | solution.py:47
  72.9 0.0 copy-start.3
  72.9 0.1 slice.35
  73.0 1.3 copy-done.3
  74.3 0.0 copy-start.2
  74.3 1.0 fusion.21
  75.3 0.0 collective-permute-done
  75.3 0.0 copy-done.2
  75.3 2.4 %convolution_add_fusion = f32[512,1408]{1,0:T(8,128)S(1)} fusion(f32[512,1408]{1,0:T(8,128)S(1)} %fusion.21, bf16[512,1408]{1,0:T(8,128)(2,1)} %collective-permute-done, bf16[512,1024]{1,0:T(8,128)(2,1)S(1)} %slice.35, s32[]{:T(128)S(6)} %select_n.43), kind=kOutput, calls=%fused_computation.2 | convolution fusion | flops 738918400 | bytes 7733252 | tf_op jit(solution)/shard_map/dot_general | solution.py:63
  77.7 0.0 copy-done
  77.7 1.5 multiply_convert_fusion.1
  79.2 0.0 copy-start.8
  79.2 0.0 copy-start.9
  79.2 1.1 convolution_convert_fusion.2
  80.3 0.1 broadcast_in_dim.10
  80.4 1.0 fusion.10
  81.4 0.0 copy-done.8
  81.4 0.0 copy-done.9
  81.5 2.4 %fusion.11 = bf16[512,1024]{1,0:T(8,128)(2,1)S(1)} fusion(bf16[512,1024]{1,0:T(8,128)(2,1)S(1)} %fusion.10, s32[]{:T(128)S(6)} %select_n.43, bf16[512,1408]{1,0:T(8,128)(2,1)} %collective-permute-done, bf16[512,704]{1,0:T(8,128)(2,1)S(1)} %get-tuple-element.5, bf16[512,704]{1,0:T(8,128)(2,1)S(1)} %get-tuple-element.4), kind=kOutput, calls=%fused_computation.28 | convolution fusion | flops 741343232 | bytes 3538948 | tf_op jit(solution)/shard_map/dot_general | solution.py:81
  83.8 1.5 %pad_maximum_fusion = bf16[512,2048]{1,0:T(8,128)(2,1)} fusion(bf16[512,1024]{1,0:T(8,128)(2,1)S(1)} %fusion.11, bf16[512,1024]{1,0:T(8,128)(2,1)S(1)} %convolution_convert_fusion.2), kind=kLoop, calls=%fused_computation.7 | loop fusion | flops 4194304 | bytes 4194304 | tf_op jit(solution)/shard_map/concatenate | solution.py:86
  85.4 4.9 %all-to-all-start.1 = ((bf16[16,32,2048]{2,1,0:T(8,128)(2,1)}), bf16[16,32,2048]{2,1,0:T(8,128)(2,1)S(1)}, u32[]{:S(2)}, u32[]{:S(2)}) async-start(bf16[16,32,2048]{2,1,0:T(8,128)(2,1)} %bitcast.43), calls=%async_computation.1 | async-start | bytes 4194304 | tf_op jit(solution)/shard_map/all_to_all | solution.py:85
  90.3 3.6 %convolution_convert_fusion = bf16[512,1408]{1,0:T(8,128)(2,1)} fusion(bf16[512,1024]{1,0:T(8,128)(2,1)} %copy-done.2, s32[]{:T(128)S(6)} %select_n.47, bf16[512,704]{1,0:T(8,128)(2,1)} %copy-done.9, bf16[512,704]{1,0:T(8,128)(2,1)} %copy-done.8), kind=kOutput, calls=%fused_computation.3 | convolution fusion | flops 741801984 | bytes 3538948 | tf_op jit(solution)/shard_map/dot_general | solution.py:105
  93.9 1.2 collective-permute-start.1
  95.2 31.9 %collective-permute-done.1 = bf16[512,1408]{1,0:T(8,128)(2,1)} collective-permute-done((bf16[512,1408]{1,0:T(8,128)(2,1)}, bf16[512,1408]{1,0:T(8,128)(2,1)}, u32[]{:S(2)}, u32[]{:S(2)}) %collective-permute-start.1) | collective-permute-done | bytes 1441824 | tf_op jit(solution)/shard_map/ppermute | solution.py:109
  127.1 4.1 %fusion.6 = bf16[1,512,1408]{2,1,0:T(8,128)(2,1)} fusion(bf16[512,1408]{1,0:T(8,128)(2,1)} %collective-permute-done.1, bf16[512,1024]{1,0:T(8,128)(2,1)} %copy-done.2, s32[]{:T(128)S(6)} %select_n.45, bf16[512,704]{1,0:T(8,128)(2,1)} %copy-done.9, bf16[512,704]{1,0:T(8,128)(2,1)} %copy-done.8), kind=kOutput, calls=%fused_computation.20 | convolution fusion | flops 744685568 | bytes 4980740 | tf_op jit(solution)/shard_map/dot_general | solution.py:105
  131.2 6.5 %all-to-all-done.1 = bf16[16,32,2048]{2,1,0:T(8,128)(2,1)S(1)} async-done(((bf16[16,32,2048]{2,1,0:T(8,128)(2,1)}), bf16[16,32,2048]{2,1,0:T(8,128)(2,1)S(1)}, u32[]{:S(2)}, u32[]{:S(2)}) %all-to-all-start.1) | async-done | bytes 2097184 | tf_op jit(solution)/shard_map/all_to_all | solution.py:85
  137.7 3.1 %gather_fusion = bf16[384,2048]{1,0:T(8,128)(2,1)} fusion(bf16[512,2048]{1,0:T(8,128)(2,1)S(1)} %bitcast.42, s32[1024]{0:T(1024)S(1)} %pad_clamp_fusion), kind=kCustom, calls=%fused_computation | custom fusion | bytes 3147264 | tf_op jit(solution)/shard_map/gather | solution.py:94
  140.8 2.5 %reshape.85 = bf16[64,6,2048]{2,1,0:T(8,128)(2,1)S(1)} reshape(bf16[384,2048]{1,0:T(8,128)(2,1)} %gather_fusion) | data formatting | bytes 3145728 | tf_op jit(solution)/shard_map/reshape | solution.py:94
  143.3 0.0 copy-start.7
  143.3 2.2 %multiply_reduce_fusion = bf16[64,1024]{1,0:T(8,128)(2,1)} fusion(f32[64,6]{1,0:T(8,128)} %copy-done.4, bf16[64,6,2048]{2,1,0:T(8,128)(2,1)S(1)} %reshape.85), kind=kLoop, calls=%fused_computation.8 | loop fusion | flops 1114112 | bytes 919040 | tf_op jit(solution)/shard_map/reduce_sum | solution.py:97
  145.6 1.4 slice_reduce_fusion
  146.9 0.0 copy-done.7
  146.9 1.3 fusion.14
  148.3 1.4 copy.29
  (4 shorter events, 0.1 us)
Async XLA Ops:
  0.6 77.0 %copy-start = (bf16[1,704,1024]{2,1,0:T(8,128)(2,1)S(1)}, bf16[1,704,1024]{2,1,0:T(8,128)(2,1)}, u32[]{:S(2)}) copy-start(bf16[1,704,1024]{2,1,0:T(8,128)(2,1)} %param.11) | copy-start | bytes 4325380
  3.4 0.6 copy-start.5
  4.9 0.6 copy-start.4
  8.2 4.3 %copy-start.6 = (s32[16,3,128]{2,0,1:T(8,128)S(1)}, s32[16,3,128]{2,0,1:T(8,128)}, u32[]{:S(2)}) copy-start(s32[16,3,128]{2,0,1:T(8,128)} %copy-done.5) | copy-start | bytes 73732
  8.2 4.4 %copy-start.1 = (f32[384,1024]{1,0:T(8,128)S(1)}, f32[384,1024]{1,0:T(8,128)}, u32[]{:S(2)}) copy-start(f32[384,1024]{1,0:T(8,128)} %mul.88) | copy-start | bytes 4718596
  18.9 54.0 %all-to-all-start = ((bf16[16,32,2048]{2,1,0:T(8,128)(2,1)}), bf16[16,32,2048]{2,1,0:T(8,128)(2,1)S(1)}, u32[]{:S(2)}, u32[]{:S(2)}) async-start(bf16[16,32,2048]{2,1,0:T(8,128)(2,1)} %bitcast.1), calls=%async_computation | async-start | bytes 4194304 | tf_op jit(solution)/shard_map/all_to_all | solution.py:47
  25.5 49.8 %collective-permute-start = (bf16[512,1408]{1,0:T(8,128)(2,1)}, bf16[512,1408]{1,0:T(8,128)(2,1)}, u32[]{:S(2)}, u32[]{:S(2)}) collective-permute-start(bf16[512,1408]{1,0:T(8,128)(2,1)} %bitcast.46), channel_id=1, source_target_pairs={{0,16},{16,0},{1,17},{17,1},{2,18},{18,2},{3,19},{19,3},{4,20},{20... | collective-permute-start | bytes 4325384 | tf_op jit(solution)/shard_map/ppermute | solution.py:12
  72.9 1.4 copy-start.3
  74.3 1.0 copy-start.2
  79.2 2.3 %copy-start.8 = (bf16[512,704]{1,0:T(8,128)(2,1)}, bf16[512,704]{1,0:T(8,128)(2,1)S(1)}, u32[]{:S(2)}) copy-start(bf16[512,704]{1,0:T(8,128)(2,1)S(1)} %get-tuple-element.4) | copy-start | bytes 2162692
  79.2 2.3 %copy-start.9 = (bf16[512,704]{1,0:T(8,128)(2,1)}, bf16[512,704]{1,0:T(8,128)(2,1)S(1)}, u32[]{:S(2)}) copy-start(bf16[512,704]{1,0:T(8,128)(2,1)S(1)} %get-tuple-element.5) | copy-start | bytes 2162692
  85.4 52.3 %all-to-all-start.1 = ((bf16[16,32,2048]{2,1,0:T(8,128)(2,1)}), bf16[16,32,2048]{2,1,0:T(8,128)(2,1)S(1)}, u32[]{:S(2)}, u32[]{:S(2)}) async-start(bf16[16,32,2048]{2,1,0:T(8,128)(2,1)} %bitcast.43), calls=%async_computation.1 | async-start | bytes 4194304 | tf_op jit(solution)/shard_map/all_to_all | solution.py:85
  93.9 33.1 %collective-permute-start.1 = (bf16[512,1408]{1,0:T(8,128)(2,1)}, bf16[512,1408]{1,0:T(8,128)(2,1)}, u32[]{:S(2)}, u32[]{:S(2)}) collective-permute-start(bf16[512,1408]{1,0:T(8,128)(2,1)} %convolution_convert_fusion), channel_id=1, source_target_pairs={{0,16},{16,0},{1,17},{17,1},{2,18},{18,2},{3,19},{19,3},{4,20},{20... | collective-permute-start | bytes 4325384 | tf_op jit(solution)/shard_map/ppermute | solution.py:109
  143.3 3.6 %copy-start.7 = (bf16[64,1024]{1,0:T(8,128)(2,1)S(1)}, bf16[64,1024]{1,0:T(8,128)(2,1)}, u32[]{:S(2)}) copy-start(bf16[64,1024]{1,0:T(8,128)(2,1)} %param.7) | copy-start | bytes 393220

commit v2 on v1

--- a/solution.py
+++ b/solution.py
@@ -32,18 +32,14 @@
     before = jnp.cumsum(onehot, axis=0) - onehot
     slot_rank = jnp.sum(before * onehot, axis=1)
     target_rows = flat_routes * capacity + slot_rank
-    token_copies = jnp.broadcast_to(tokens[:, None, :], (token_count, top_count, model_width))
-    token_copies = token_copies.reshape(token_count * top_count, model_width)
-    cot_copies = (gate_probs[:, :, None] * cotangent[:, None, :].astype(jnp.float32)).astype(
-        jnp.bfloat16
-    )
-    cot_copies = cot_copies.reshape(token_count * top_count, model_width)
-    both_copies = jnp.concatenate([token_copies, cot_copies], axis=1)
-    both_send = (
-        jnp.zeros((experts * capacity, 2 * model_width), jnp.bfloat16)
-        .at[target_rows]
-        .set(both_copies)
-    )
+    slots = jnp.arange(experts * capacity, dtype=jnp.int32)
+    chosen = target_rows.reshape(token_count, top_count)[None, :, :] == slots[:, None, None]
+    pick = jnp.any(chosen, axis=2).astype(jnp.bfloat16)
+    slot_prob = jnp.sum(jnp.where(chosen, gate_probs[None, :, :], 0.0), axis=(1, 2))
+    token_send = jnp.dot(pick, tokens, preferred_element_type=jnp.float32).astype(jnp.bfloat16)
+    cot_pick = jnp.dot(pick, cotangent, preferred_element_type=jnp.float32)
+    cot_send = (slot_prob[:, None] * cot_pick).astype(jnp.bfloat16)
+    both_send = jnp.concatenate([token_send, cot_send], axis=1)
     both_recv = lax.all_to_all(
         both_send.reshape(experts, capacity, 2 * model_width),
         "expert",
@@ -91,14 +87,24 @@
         concat_axis=0,
         tiled=True,
     ).reshape(experts * capacity, 2 * model_width)
-    slot_both = back[target_rows].reshape(token_count, top_count, 2 * model_width)
-    slot_out = slot_both[:, :, :model_width]
-    slot_in = slot_both[:, :, model_width:]
-    layer_out = jnp.sum(gate_probs[:, :, None] * slot_out.astype(jnp.float32), axis=1).astype(
+    back_out = back[:, :model_width]
+    back_in = back[:, model_width:]
+    owned = target_rows.reshape(token_count, top_count)[:, :, None] == slots[None, None, :]
+    weights = jnp.sum(jnp.where(owned, gate_probs[:, :, None], 0.0), axis=1)
+    layer_out = jnp.dot(
+        weights,
+        back_out.astype(jnp.float32),
+        precision=lax.Precision.HIGHEST,
+        preferred_element_type=jnp.float32,
+    ).astype(jnp.bfloat16)
+    gathered = jnp.any(owned, axis=1).astype(jnp.bfloat16)
+    input_grad = jnp.dot(gathered, back_in, preferred_element_type=jnp.float32).astype(
         jnp.bfloat16
     )
-    input_grad = jnp.sum(slot_in.astype(jnp.float32), axis=1).astype(jnp.bfloat16)
-    prob_grad = jnp.einsum("td,tkd->tk", cotangent, slot_out, preferred_element_type=jnp.float32)
+    inner = lax.dot_general(
+        cotangent, back_out, (((1,), (1,)), ((), ())), preferred_element_type=jnp.float32
+    )
+    prob_grad = jnp.sum(jnp.where(owned, inner[:, None, :], 0.0), axis=2)
     grad_rows = None
     for shift in range(replicas):
         block = (me_dp + shift) % replicas

time: 150 us -> 133 us (0.89)
  local copies, waits for them, and re-layouts: 18.8 us -> 3.11 us
  other arithmetic: 13.1 us -> 7.53 us
  matrix products: 18.4 us -> 23.4 us
    scatter x1 -> x0, other arithmetic: 5.26 us -> none  [local(): both_send = jnp.zeros((experts * capacity, 2 * model_width), jnp.bfloat16...]
    dot_general x1 -> x5, matrix products: 1.33 us -> 6.28 us  [the longest x1 1.72 us: local(): jnp.dot(gathered, back_in, preferred_element_type=jnp.float32)]
    reshape x2 -> x0, local copies, waits for them, and re-layouts: 4.65 us -> none  [the longest x1 2.48 us: local(): back[target_rows].reshape(token_count, top_count, 2 * model_width)]
    gather x1 -> x0, local copies, waits for them, and re-layouts: 3.13 us -> none  [local(): back[target_rows].reshape(token_count, top_count, 2 * model_width)]
    mul x5 -> x0, local copies, waits for them, and re-layouts: 2.9 us -> none  [the longest x2 2.54 us: local(): gate_probs[:, :, None] * cotangent[:, None, :].astype(jnp.float32)]
    broadcast_in_dim x1 -> x0, local copies, waits for them, and re-layouts: 2.15 us -> none  [local(): jnp.broadcast_to(tokens[:, None, :], (token_count, top_count, model_width))]
    reduce_sum x2, other arithmetic: 3.58 us -> 1.78 us  [the longest x1 0.91 us: local(): prob_grad = jnp.sum(jnp.where(owned, inner[:, None, :], 0.0), axis=2)]
    unnamed x22 -> x15, local copies, waits for them, and re-layouts: 3.84 us -> 2.2 us
  transfers between devices with their start and end apart: 4 -> 4, of which waited for: 3 -> 3; matrix products, arithmetic and copies ran while one was open for 6% -> 7% of each run, Pallas kernels for 0% -> 0%
where the time goes in v2:
time: 133 us
  waiting for transfers between devices  83.8 us (63%)
  matrix products  23.4 us (18%)
  starting transfers between devices  13.9 us (10%)
  other arithmetic  7.53 us (6%)
  local copies, waits for them, and re-layouts  3.11 us (2%)
    all_to_all x1, waiting for transfers between devices, local(): lax.all_to_all(both_send.reshape(experts, capacity, 2 * model_width), 'ex...  46.2 us
    ppermute x1, waiting for transfers between devices, local(): lax.ppermute(partial, 'dp', [(i, (i + shift) % replicas) for i in range(r...  31.1 us
    dot_general x2, matrix products, local(): lax.dot_general(cols(block), pair_cot, (((0,), (0,)), ((), ())), preferre...  7.77 us
    all_to_all x1, starting transfers between devices, local(): lax.all_to_all(both_send.reshape(experts, capacity, 2 * model_width), 'ex...  6.55 us
    all_to_all x1, waiting for transfers between devices, local(): lax.all_to_all(jnp.concatenate([output_rows, input_cot], axis=1).reshape(...  6.52 us
    all_to_all x1, starting transfers between devices, local(): lax.all_to_all(jnp.concatenate([output_rows, input_cot], axis=1).reshape(...  4.91 us
    dot_general x2, matrix products, local(): lax.dot_general(pair_cot, weight, (((1,), (1,)), ((), ())), preferred_ele...  3.41 us
    dot_general x2, matrix products, local(): part = jnp.dot(cols(block), weight, preferred_element_type=jnp.float32)  3.34 us
  transfers between devices with their start and end apart: 4, of which 3 were waited for; matrix products, arithmetic and copies ran while one was open for 7% of the time, Pallas kernels for 0%

profile of v2, /device:TPU:11, one launch (start us, length us, event | category | flops | bytes accessed | tf_op | source)
XLA Modules:
  0.0 132.6 jit_solution(11520535629752906421)
XLA Ops:
  0.6 0.0 copy-start
  0.6 0.0 copy-start.3
  0.7 0.9 copy.40
  1.6 0.1 eq.59
  1.7 0.1 eq.55
  1.9 0.9 reduce-window.6
  2.7 0.2 slice_reduce_fusion
  3.0 0.1 fusion.24
  3.1 0.1 reduce_sum.39
  3.2 0.1 copy.43
  3.3 0.7 multiply_add_fusion
  4.0 0.2 fusion.12
  4.2 0.9 select_reduce_fusion.1
  5.0 1.4 %convolution_convert_fusion.3 = bf16[512,1024]{1,0:T(8,128)(2,1)S(1)} fusion(pred[512,64]{0,1:T(8,128)(4,1)S(1)} %fusion.12, bf16[64,1024]{1,0:T(8,128)(2,1)} %param.6), kind=kOutput, calls=%fused_computation.14 | convolution fusion | flops 67633152 | bytes 1212416 | tf_op jit(solution)/shard_map/dot_general | solution.py:39
  6.4 0.0 copy-done.3
  6.5 0.5 multiply_convert_fusion
  6.9 1.5 %pad_maximum_fusion = bf16[512,2048]{1,0:T(8,128)(2,1)} fusion(bf16[512,1024]{1,0:T(8,128)(2,1)S(1)} %multiply_convert_fusion, bf16[512,1024]{1,0:T(8,128)(2,1)S(1)} %convolution_convert_fusion.3), kind=kLoop, calls=%fused_computation.5 | loop fusion | flops 4194304 | bytes 4194304 | tf_op jit(solution)/shard_map/concatenate | solution.py:42
  8.5 6.6 %all-to-all-start = ((bf16[16,32,2048]{2,1,0:T(8,128)(2,1)}), bf16[16,32,2048]{2,1,0:T(8,128)(2,1)S(1)}, u32[]{:S(2)}, u32[]{:S(2)}) async-start(bf16[16,32,2048]{2,1,0:T(8,128)(2,1)} %bitcast.1), calls=%async_computation | async-start | bytes 4194304 | tf_op jit(solution)/shard_map/all_to_all | solution.py:43
  15.0 1.2 collective-permute-start
  16.3 46.2 %all-to-all-done = bf16[16,32,2048]{2,1,0:T(8,128)(2,1)S(1)} async-done(((bf16[16,32,2048]{2,1,0:T(8,128)(2,1)}), bf16[16,32,2048]{2,1,0:T(8,128)(2,1)S(1)}, u32[]{:S(2)}, u32[]{:S(2)}) %all-to-all-start) | async-done | bytes 2097184 | tf_op jit(solution)/shard_map/all_to_all | solution.py:43
  62.5 0.0 copy-start.2
  62.5 0.1 slice.33
  62.6 1.3 copy-done.2
  63.8 0.0 copy-start.1
  63.8 1.0 fusion.19
  64.8 0.0 collective-permute-done
  64.8 0.0 copy-done.1
  64.8 2.4 %convolution_add_fusion = f32[512,1408]{1,0:T(8,128)S(1)} fusion(f32[512,1408]{1,0:T(8,128)S(1)} %fusion.19, bf16[512,1408]{1,0:T(8,128)(2,1)} %collective-permute-done, bf16[512,1024]{1,0:T(8,128)(2,1)S(1)} %slice.33, s32[]{:T(128)S(6)} %select_n.45), kind=kOutput, calls=%fused_computation | convolution fusion | flops 738918400 | bytes 7733252 | tf_op jit(solution)/shard_map/dot_general | solution.py:59
  67.2 0.0 copy-done
  67.2 1.5 %multiply_convert_fusion.2 = (bf16[512,704]{1,0:T(8,128)(2,1)S(1)}, bf16[512,704]{1,0:T(8,128)(2,1)S(1)}) fusion(f32[512,1408]{1,0:T(8,128)S(1)} %convolution_add_fusion, bf16[1,704,1024]{2,1,0:T(8,128)(2,1)S(1)} %copy-done, bf16[512,2048]{1,0:T(8,128)(2,1)S(1)} %bitcast.53), kind=kOutput, calls=%fused_computation.9 | convolution fusion | flops 742883328 | bytes 7077888 | tf_op jit(solution)/shard_map/dot_general | solution.py:69
  68.7 0.0 copy-start.5
  68.7 0.0 copy-start.6
  68.7 1.1 convolution_convert_fusion.2
  69.8 0.1 broadcast_in_dim.51
  69.9 1.0 fusion.6
  70.9 0.0 copy-done.5
  71.0 0.0 copy-done.6
  71.0 2.4 %fusion.7 = bf16[512,1024]{1,0:T(8,128)(2,1)S(1)} fusion(bf16[512,1024]{1,0:T(8,128)(2,1)S(1)} %fusion.6, s32[]{:T(128)S(6)} %select_n.45, bf16[512,1408]{1,0:T(8,128)(2,1)} %collective-permute-done, bf16[512,704]{1,0:T(8,128)(2,1)S(1)} %get-tuple-element.7, bf16[512,704]{1,0:T(8,128)(2,1)S(1)} %get-tuple-element.6), kind=kOutput, calls=%fused_computation.23 | convolution fusion | flops 741343232 | bytes 3538948 | tf_op jit(solution)/shard_map/dot_general | solution.py:77
  73.4 1.5 %pad_maximum_fusion.1 = bf16[512,2048]{1,0:T(8,128)(2,1)} fusion(bf16[512,1024]{1,0:T(8,128)(2,1)S(1)} %fusion.7, bf16[512,1024]{1,0:T(8,128)(2,1)S(1)} %convolution_convert_fusion.2), kind=kLoop, calls=%fused_computation.6 | loop fusion | flops 4194304 | bytes 4194304 | tf_op jit(solution)/shard_map/concatenate | solution.py:82
  74.9 4.9 %all-to-all-start.1 = ((bf16[16,32,2048]{2,1,0:T(8,128)(2,1)}), bf16[16,32,2048]{2,1,0:T(8,128)(2,1)S(1)}, u32[]{:S(2)}, u32[]{:S(2)}) async-start(bf16[16,32,2048]{2,1,0:T(8,128)(2,1)} %bitcast.5), calls=%async_computation.1 | async-start | bytes 4194304 | tf_op jit(solution)/shard_map/all_to_all | solution.py:81
  79.8 3.6 %convolution_convert_fusion = bf16[512,1408]{1,0:T(8,128)(2,1)} fusion(bf16[512,1024]{1,0:T(8,128)(2,1)} %copy-done.1, s32[]{:T(128)S(6)} %select_n.50, bf16[512,704]{1,0:T(8,128)(2,1)} %copy-done.6, bf16[512,704]{1,0:T(8,128)(2,1)} %copy-done.5), kind=kOutput, calls=%fused_computation.1 | convolution fusion | flops 741801984 | bytes 3538948 | tf_op jit(solution)/shard_map/dot_general | solution.py:111
  83.5 1.2 collective-permute-start.1
  84.7 0.8 fusion.13
  85.5 31.1 %collective-permute-done.1 = bf16[512,1408]{1,0:T(8,128)(2,1)} collective-permute-done((bf16[512,1408]{1,0:T(8,128)(2,1)}, bf16[512,1408]{1,0:T(8,128)(2,1)}, u32[]{:S(2)}, u32[]{:S(2)}) %collective-permute-start.1) | collective-permute-done | bytes 1441824 | tf_op jit(solution)/shard_map/ppermute | solution.py:115
  116.6 4.1 %fusion.2 = bf16[1,512,1408]{2,1,0:T(8,128)(2,1)} fusion(bf16[512,1408]{1,0:T(8,128)(2,1)} %collective-permute-done.1, bf16[512,1024]{1,0:T(8,128)(2,1)} %copy-done.1, s32[]{:T(128)S(6)} %select_n.48, bf16[512,704]{1,0:T(8,128)(2,1)} %copy-done.6, bf16[512,704]{1,0:T(8,128)(2,1)} %copy-done.5), kind=kOutput, calls=%fused_computation.15 | convolution fusion | flops 744685568 | bytes 4980740 | tf_op jit(solution)/shard_map/dot_general | solution.py:111
  120.7 0.0 copy-start.4
  120.7 6.5 %all-to-all-done.1 = bf16[16,32,2048]{2,1,0:T(8,128)(2,1)S(1)} async-done(((bf16[16,32,2048]{2,1,0:T(8,128)(2,1)}), bf16[16,32,2048]{2,1,0:T(8,128)(2,1)S(1)}, u32[]{:S(2)}, u32[]{:S(2)}) %all-to-all-start.1) | async-done | bytes 2097184 | tf_op jit(solution)/shard_map/all_to_all | solution.py:81
  127.2 1.4 %convolution_bitcast_fusion = f32[64,512]{1,0:T(8,128)S(1)} fusion(bf16[64,1024]{1,0:T(8,128)(2,1)} %param.7, bf16[512,2048]{1,0:T(8,128)(2,1)S(1)} %bitcast.49), kind=kOutput, calls=%fused_computation.26 | convolution fusion | flops 67108864 | bytes 1310720 | tf_op jit(solution)/shard_map/dot_general | solution.py:104
  128.6 1.7 %convolution_convert_fusion.6 = bf16[64,1024]{1,0:T(8,128)(2,1)} fusion(pred[64,512]{1,0:T(8,128)(4,1)} %fusion.13, bf16[512,2048]{1,0:T(8,128)(2,1)S(1)} %bitcast.50), kind=kOutput, calls=%fused_computation.24 | convolution fusion | flops 67174400 | bytes 1212416 | tf_op jit(solution)/shard_map/dot_general | solution.py:101
  130.3 0.0 copy-done.4
  130.3 0.9 select_reduce_fusion
  131.2 1.3 %convolution_convert_fusion.7 = bf16[64,1024]{1,0:T(8,128)(2,1)} fusion(f32[64,512]{1,0:T(8,128)S(1)} %get-tuple-element.5, bf16[512,2048]{1,0:T(8,128)(2,1)S(1)} %bitcast.51), kind=kOutput, calls=%fused_computation.25 | convolution fusion | flops 402718720 | bytes 1310720 | tf_op jit(solution)/shard_map/dot_general | solution.py:94
  (2 shorter events, 0.0 us)
Async XLA Ops:
  0.6 66.6 %copy-start = (bf16[1,704,1024]{2,1,0:T(8,128)(2,1)S(1)}, bf16[1,704,1024]{2,1,0:T(8,128)(2,1)}, u32[]{:S(2)}) copy-start(bf16[1,704,1024]{2,1,0:T(8,128)(2,1)} %param.11) | copy-start | bytes 4325380
  0.6 5.8 %copy-start.3 = (bf16[64,1024]{1,0:T(8,128)(2,1)S(1)}, bf16[64,1024]{1,0:T(8,128)(2,1)}, u32[]{:S(2)}) copy-start(bf16[64,1024]{1,0:T(8,128)(2,1)} %param.7) | copy-start | bytes 393220
  8.5 54.0 %all-to-all-start = ((bf16[16,32,2048]{2,1,0:T(8,128)(2,1)}), bf16[16,32,2048]{2,1,0:T(8,128)(2,1)S(1)}, u32[]{:S(2)}, u32[]{:S(2)}) async-start(bf16[16,32,2048]{2,1,0:T(8,128)(2,1)} %bitcast.1), calls=%async_computation | async-start | bytes 4194304 | tf_op jit(solution)/shard_map/all_to_all | solution.py:43
  15.0 49.8 %collective-permute-start = (bf16[512,1408]{1,0:T(8,128)(2,1)}, bf16[512,1408]{1,0:T(8,128)(2,1)}, u32[]{:S(2)}, u32[]{:S(2)}) collective-permute-start(bf16[512,1408]{1,0:T(8,128)(2,1)} %bitcast.54), channel_id=1, source_target_pairs={{0,16},{16,0},{1,17},{17,1},{2,18},{18,2},{3,19},{19,3},{4,20},{20... | collective-permute-start | bytes 4325384 | tf_op jit(solution)/shard_map/ppermute | solution.py:12
  62.5 1.4 %copy-start.2 = (bf16[1,512,1408]{2,1,0:T(8,128)(2,1)S(1)}, bf16[1,512,1408]{2,1,0:T(8,128)(2,1)}, u32[]{:S(2)}) copy-start(bf16[1,512,1408]{2,1,0:T(8,128)(2,1)} %param.10) | copy-start | bytes 4325380
  63.8 1.0 copy-start.1
  68.7 2.2 %copy-start.5 = (bf16[512,704]{1,0:T(8,128)(2,1)}, bf16[512,704]{1,0:T(8,128)(2,1)S(1)}, u32[]{:S(2)}) copy-start(bf16[512,704]{1,0:T(8,128)(2,1)S(1)} %get-tuple-element.6) | copy-start | bytes 2162692
  68.7 2.2 %copy-start.6 = (bf16[512,704]{1,0:T(8,128)(2,1)}, bf16[512,704]{1,0:T(8,128)(2,1)S(1)}, u32[]{:S(2)}) copy-start(bf16[512,704]{1,0:T(8,128)(2,1)S(1)} %get-tuple-element.7) | copy-start | bytes 2162692
  74.9 52.3 %all-to-all-start.1 = ((bf16[16,32,2048]{2,1,0:T(8,128)(2,1)}), bf16[16,32,2048]{2,1,0:T(8,128)(2,1)S(1)}, u32[]{:S(2)}, u32[]{:S(2)}) async-start(bf16[16,32,2048]{2,1,0:T(8,128)(2,1)} %bitcast.5), calls=%async_computation.1 | async-start | bytes 4194304 | tf_op jit(solution)/shard_map/all_to_all | solution.py:81
  83.5 33.1 %collective-permute-start.1 = (bf16[512,1408]{1,0:T(8,128)(2,1)}, bf16[512,1408]{1,0:T(8,128)(2,1)}, u32[]{:S(2)}, u32[]{:S(2)}) collective-permute-start(bf16[512,1408]{1,0:T(8,128)(2,1)} %convolution_convert_fusion), channel_id=1, source_target_pairs={{0,16},{16,0},{1,17},{17,1},{2,18},{18,2},{3,19},{19,3},{4,20},{20... | collective-permute-start | bytes 4325384 | tf_op jit(solution)/shard_map/ppermute | solution.py:115
  120.7 9.6 %copy-start.4 = (f32[64,6]{0,1:T(8,128)S(1)}, f32[64,6]{0,1:T(8,128)}, u32[]{:S(2)}) copy-start(f32[64,6]{0,1:T(8,128)} %param.9) | copy-start | bytes 4612

commit v3 on v2

v3 whole, which is shorter than its diff:
```python
import jax
import jax.numpy as jnp
from jax import lax
from jax.sharding import PartitionSpec as P

CHUNKS = 2


def gather_rows(own, axis_name):
    count = lax.axis_size(axis_name)
    me = lax.axis_index(axis_name)
    pieces = [(me, own)]
    for shift in range(1, count):
        moved = lax.ppermute(own, axis_name, [(i, (i + shift) % count) for i in range(count)])
        pieces.append(((me - shift) % count, moved))
    return pieces


def local(tokens, cotangent, expert_ids, gate_probs, w_gate_up, w_down):
    experts = lax.axis_size("expert")
    replicas = lax.axis_size("dp")
    me_dp = lax.axis_index("dp")
    token_count = tokens.shape[0]
    model_width = tokens.shape[1]
    top_count = expert_ids.shape[1]
    hidden_units = w_down.shape[1]
    block_rows = w_gate_up.shape[1]
    capacity = 4 * token_count * top_count // (3 * experts)
    chunks = CHUNKS if capacity % CHUNKS == 0 else 1
    part_cap = capacity // chunks
    weight_blocks = gather_rows(w_gate_up[0], "dp")
    weight_down = w_down[0]
    flat_routes = expert_ids.reshape(token_count * top_count)
    onehot = (flat_routes[:, None] == jnp.arange(experts, dtype=jnp.int32)[None, :]).astype(
        jnp.int32
    )
    before = jnp.cumsum(onehot, axis=0) - onehot
    slot_rank = jnp.sum(before * onehot, axis=1)
    target_rows = (flat_routes * capacity + slot_rank).reshape(token_count, top_count)
    slots = jnp.arange(experts * capacity, dtype=jnp.int32)
    chosen = target_rows[None, :, :] == slots[:, None, None]
    pick = jnp.any(chosen, axis=2).astype(jnp.bfloat16)
    slot_prob = jnp.sum(jnp.where(chosen, gate_probs[None, :, :], 0.0), axis=(1, 2))
    picked = jnp.dot(
        pick, jnp.concatenate([tokens, cotangent], axis=1), preferred_element_type=jnp.float32
    )
    both_send = jnp.concatenate(
        [picked[:, :model_width], slot_prob[:, None] * picked[:, model_width:]], axis=1
    ).astype(jnp.bfloat16)
    both_send = both_send.reshape(experts, capacity, 2 * model_width)

    def exchange(block):
        return lax.all_to_all(block, "expert", split_axis=0, concat_axis=0, tiled=True)

    def cols(rows, block):
        return lax.dynamic_slice_in_dim(rows, block * block_rows, block_rows, axis=1)

    received = [
        exchange(both_send[:, c * part_cap : (c + 1) * part_cap]).reshape(
            experts * part_cap, 2 * model_width
        )
        for c in range(chunks)
    ]
    returned = []
    grads = [None] * replicas
    for recv in received:
        input_rows = recv[:, :model_width]
        cot_rows = recv[:, model_width:]
        gate_up = None
        for block, weight in weight_blocks:
            part = jnp.dot(cols(input_rows, block), weight, preferred_element_type=jnp.float32)
            gate_up = part if gate_up is None else gate_up + part
        gate = gate_up[:, :hidden_units]
        upper = gate_up[:, hidden_units:]
        sigma = jax.nn.sigmoid(gate)
        active = gate * sigma
        hidden = (active * upper).astype(jnp.bfloat16)
        output_rows = jnp.dot(hidden, weight_down, preferred_element_type=jnp.float32).astype(
            jnp.bfloat16
        )
        hidden_grad = lax.dot_general(
            cot_rows, weight_down, (((1,), (1,)), ((), ())), preferred_element_type=jnp.float32
        )
        gate_cot = hidden_grad * upper * sigma * (1.0 + gate * (1.0 - sigma))
        upper_cot = hidden_grad * active
        pair_cot = jnp.concatenate([gate_cot, upper_cot], axis=1).astype(jnp.bfloat16)
        input_cot = jnp.zeros((experts * part_cap, model_width), jnp.bfloat16)
        for block, weight in weight_blocks:
            part = lax.dot_general(
                pair_cot, weight, (((1,), (1,)), ((), ())), preferred_element_type=jnp.float32
            ).astype(jnp.bfloat16)
            input_cot = lax.dynamic_update_slice_in_dim(
                input_cot, part, block * block_rows, axis=1
            )
        back = exchange(
            jnp.concatenate([output_rows, input_cot], axis=1).reshape(
                experts, part_cap, 2 * model_width
            )
        )
        returned.append(back)
        for shift in range(replicas):
            block = (me_dp + shift) % replicas
            partial = lax.dot_general(
                cols(input_rows, block),
                pair_cot,
                (((0,), (0,)), ((), ())),
                preferred_element_type=jnp.float32,
            )
            grads[shift] = partial if grads[shift] is None else grads[shift] + partial
    grad_rows = lax.optimization_barrier(grads[0])
    for shift in range(1, replicas):
        moved = lax.ppermute(
            grads[shift].astype(jnp.bfloat16),
            "dp",
            [(i, (i + shift) % replicas) for i in range(replicas)],
        )
        grad_rows = grad_rows + moved.astype(jnp.float32)
    back = jnp.concatenate(returned, axis=1).reshape(experts * capacity, 2 * model_width)
    back_out = back[:, :model_width]
    back_in = back[:, model_width:]
    owned = target_rows[:, :, None] == slots[None, None, :]
    weights = jnp.sum(jnp.where(owned, gate_probs[:, :, None], 0.0), axis=1)
    layer_out = jnp.dot(
        weights,
        back_out.astype(jnp.float32),
        precision=lax.Precision.HIGHEST,
        preferred_element_type=jnp.float32,
    ).astype(jnp.bfloat16)
    gathered = jnp.any(owned, axis=1).astype(jnp.bfloat16)
    input_grad = jnp.dot(gathered, back_in, preferred_element_type=jnp.float32).astype(
        jnp.bfloat16
    )
    inner = lax.dot_general(
        cotangent, back_out, (((1,), (1,)), ((), ())), preferred_element_type=jnp.float32
    )
    prob_grad = jnp.sum(jnp.where(owned, inner[:, None, :], 0.0), axis=2)
    return (layer_out, input_grad, prob_grad, grad_rows.astype(jnp.bfloat16)[None])


def solution(mesh):
    placed = (
        P(("dp", "expert"), None),
        P(("dp", "expert"), None),
        P(("dp", "expert"), None),
        P(("dp", "expert"), None),
        P("expert", "dp", None),
        P("expert", None, None),
    )
    return jax.shard_map(
        local,
        mesh=mesh,
        in_specs=placed,
        out_specs=(
            P(("dp", "expert"), None),
            P(("dp", "expert"), None),
            P(("dp", "expert"), None),
            P("expert", "dp", None),
        ),
        check_vma=False,
    )
```

time: 133 us -> 136 us (1.023)
  waiting for transfers between devices: 83.8 us -> 72.4 us
  starting transfers between devices: 13.9 us -> 23.4 us
  other arithmetic: 7.53 us -> 11.5 us
  local copies, waits for them, and re-layouts: 3.11 us -> 5.96 us
  matrix products: 23.4 us -> 20.9 us
    ppermute x1, waiting for transfers between devices: 31.1 us -> 10.1 us  [local(): lax.ppermute(grads[shift].astype(jnp.bfloat16), 'dp', [(i, (i + shift) %...]
    all_to_all x2 -> x4, starting transfers between devices: 11.5 us -> 20.9 us  [exchange(): lax.all_to_all(block, 'expert', split_axis=0, concat_axis=0, tiled=True)]
    all_to_all x2 -> x4, waiting for transfers between devices: 52.7 us -> 62.1 us  [exchange(): lax.all_to_all(block, 'expert', split_axis=0, concat_axis=0, tiled=True)]
    broadcast_in_dim x0 -> x1, other arithmetic: none -> 2.82 us  [local(): grad_rows.astype(jnp.bfloat16)[None]]
    dot_general x6 -> x9, matrix products: 13 us -> 10.6 us  [the longest x4 5.24 us: local(): jnp.dot(cols(input_rows, block), weight, preferred_element_type=jnp.float32)]
    dot_general x1 -> x2, matrix products: 1.49 us -> 3.82 us  [local(): lax.dot_general(cot_rows, weight_down, (((1,), (1,)), ((), ())), preferre...]
    slice x2 -> x4, local copies, waits for them, and re-layouts: 0.3 us -> 2.52 us  [the longest x2 2.15 us: local(): input_rows = recv[:, :model_width]]
    concatenate x1 -> x2, other arithmetic: 1.54 us -> 3.28 us  [the longest x1 1.78 us: local(): jnp.concatenate(returned, axis=1)]
  transfers between devices with their start and end apart: 4 -> 6, of which waited for: 3 -> 6; matrix products, arithmetic and copies ran while one was open for 7% -> 18% of each run, Pallas kernels for 0% -> 0%
where the time goes in v3:
time: 136 us; the launch traced here: 135 us
  waiting for transfers between devices  72.4 us (53%)
  starting transfers between devices  23.4 us (17%)
  matrix products  20.9 us (15%)
  other arithmetic  11.5 us (8%)
  local copies, waits for them, and re-layouts  5.96 us (4%)
    all_to_all x4, waiting for transfers between devices, exchange(): lax.all_to_all(block, 'expert', split_axis=0, concat_axis=0, tiled=True)  62.1 us
    all_to_all x4, starting transfers between devices, exchange(): lax.all_to_all(block, 'expert', split_axis=0, concat_axis=0, tiled=True)  20.9 us
    ppermute x1, waiting for transfers between devices, local(): lax.ppermute(grads[shift].astype(jnp.bfloat16), 'dp', [(i, (i + shift) %...  10.1 us
    dot_general x4, matrix products, local(): jnp.dot(cols(input_rows, block), weight, preferred_element_type=jnp.float32)  5.24 us
    dot_general x2, matrix products, local(): lax.dot_general(cot_rows, weight_down, (((1,), (1,)), ((), ())), preferre...  3.82 us
    dot_general x4, matrix products, local(): lax.dot_general(cols(input_rows, block), pair_cot, (((0,), (0,)), ((), ()...  3.62 us
    unnamed x35, local copies, waits for them, and re-layouts  2.85 us
    broadcast_in_dim x1, other arithmetic, local(): grad_rows.astype(jnp.bfloat16)[None]  2.82 us
  transfers between devices with their start and end apart: 6, of which 6 were waited for; matrix products, arithmetic and copies ran while one was open for 18% of the time, Pallas kernels for 0%

profile of v3, /device:TPU:11, one launch (start us, length us, event | category | flops | bytes accessed | tf_op | source)
XLA Modules:
  0.0 135.2 jit_solution(960685696545293713)
XLA Ops:
  0.6 0.0 copy-start
  0.6 0.9 copy.40
  1.5 0.1 eq.57
  1.7 0.1 eq.61
  1.8 0.9 reduce-window.6
  2.7 0.2 slice_reduce_fusion
  3.0 0.1 fusion.51
  3.1 0.1 reduce_sum.39
  3.2 0.1 copy.43
  3.3 0.7 multiply_add_fusion
  4.0 0.2 fusion.27
  4.1 1.7 %fusion.31 = f32[512,2048]{1,0:T(8,128)S(1)} fusion(pred[512,64]{0,1:T(8,128)(4,1)S(1)} %fusion.27, bf16[64,1024]{1,0:T(8,128)(2,1)} %param.7, bf16[64,1024]{1,0:T(8,128)(2,1)} %param.6), kind=kOutput, calls=%fused_computation.62 | convolution fusion | flops 134742016 | bytes 4489216 | tf_op jit(solution)/shard_map/dot_general | solution.py:44
  5.9 0.2 slice.121
  6.0 0.5 copy-done.16
  6.6 0.2 select_reduce_fusion.1
  6.7 0.2 fusion.1
  6.9 1.5 %fusion.21 = (bf16[16,16,2048]{2,1,0:T(8,128)(2,1)}, bf16[16,16,2048]{2,1,0:T(8,128)(2,1)}) fusion(bf16[16,32,1024]{2,1,0:T(8,128)(2,1)S(1)} %bitcast.71, bf16[16,32,1024]{2,1,0:T(8,128)(2,1)S(1)} %bitcast.72), kind=kLoop, calls=%fused_computation.34 | loop fusion | flops 4194304 | bytes 4194304 | tf_op jit(solution)/shard_map/concatenate | solution.py:47
  8.4 6.6 %all-to-all-start.2 = ((bf16[16,16,2048]{2,1,0:T(8,128)(2,1)}), bf16[16,16,2048]{2,1,0:T(8,128)(2,1)}, u32[]{:S(2)}, u32[]{:S(2)}) async-start(bf16[16,16,2048]{2,1,0:T(8,128)(2,1)} %get-tuple-element.11), calls=%async_computation.2 | async-start | bytes 2097152 | tf_op jit(solution)/shard_map/all_to_all | solution.py:53
  15.0 1.2 collective-permute-start
  16.2 23.9 %all-to-all-done.2 = bf16[16,16,2048]{2,1,0:T(8,128)(2,1)} async-done(((bf16[16,16,2048]{2,1,0:T(8,128)(2,1)}), bf16[16,16,2048]{2,1,0:T(8,128)(2,1)}, u32[]{:S(2)}, u32[]{:S(2)}) %all-to-all-start.2) | async-done | bytes 1048608 | tf_op jit(solution)/shard_map/all_to_all | solution.py:53
  40.2 4.7 %all-to-all-start = ((bf16[16,16,2048]{2,1,0:T(8,128)(2,1)}), bf16[16,16,2048]{2,1,0:T(8,128)(2,1)}, u32[]{:S(2)}, u32[]{:S(2)}) async-start(bf16[16,16,2048]{2,1,0:T(8,128)(2,1)} %get-tuple-element.10), calls=%async_computation | async-start | bytes 2097152 | tf_op jit(solution)/shard_map/all_to_all | solution.py:53
  44.9 1.1 slice.74
  46.0 1.9 %fusion.42 = f32[256,1408]{1,0:T(8,128)S(1)} fusion(bf16[256,1024]{1,0:T(8,128)(2,1)S(1)} %slice.74, s32[]{:T(128)S(6)} %select_n.53, bf16[1,512,1408]{2,1,0:T(8,128)(2,1)} %param.10), kind=kOutput, calls=%fused_computation.73 | convolution fusion | flops 369098752 | bytes 3145732 | tf_op jit(solution)/shard_map/dot_general | solution.py:71
  47.9 0.2 collective-permute-done
  48.1 0.6 convolution_add_fusion.2
  48.7 2.0 %multiply_convert_fusion.1 = (bf16[256,704]{1,0:T(8,128)(2,1)S(1)}, bf16[256,704]{1,0:T(8,128)(2,1)S(1)}) fusion(f32[256,1408]{1,0:T(8,128)S(1)} %convolution_add_fusion.2, bf16[1,704,1024]{2,1,0:T(8,128)(2,1)S(1)} %copy-done, bf16[256,2048]{1,0:T(8,128)(2,1)} %bitcast.7), kind=kOutput, calls=%fused_computation.43 | convolution fusion | flops 371441664 | bytes 4128768 | tf_op jit(solution)/shard_map/dot_general | solution.py:81
  50.7 0.1 broadcast.36.clone
  50.8 0.6 fusion.19
  51.4 0.1 copy-done.9
  51.5 0.1 copy-done.12
  51.6 0.6 fusion.20
  52.2 0.7 fusion.14
  52.9 1.1 pad_maximum_fusion.3
  54.0 15.9 %all-to-all-done = bf16[16,16,2048]{2,1,0:T(8,128)(2,1)} async-done(((bf16[16,16,2048]{2,1,0:T(8,128)(2,1)}), bf16[16,16,2048]{2,1,0:T(8,128)(2,1)}, u32[]{:S(2)}, u32[]{:S(2)}) %all-to-all-start) | async-done | bytes 1048608 | tf_op jit(solution)/shard_map/all_to_all | solution.py:53
  69.9 4.9 %all-to-all-start.3 = ((bf16[16,16,2048]{2,1,0:T(8,128)(2,1)}), bf16[16,16,2048]{2,1,0:T(8,128)(2,1)}, u32[]{:S(2)}, u32[]{:S(2)}) async-start(bf16[16,16,2048]{2,1,0:T(8,128)(2,1)} %bitcast.70), calls=%async_computation.3 | async-start | bytes 2097152 | tf_op jit(solution)/shard_map/all_to_all | solution.py:53
  74.8 1.1 slice.70
  75.9 2.1 %fusion.45 = f32[256,1408]{1,0:T(8,128)S(1)} fusion(bf16[256,1024]{1,0:T(8,128)(2,1)S(1)} %slice.70, s32[]{:T(128)S(6)} %select_n.53, bf16[1,512,1408]{2,1,0:T(8,128)(2,1)} %param.10), kind=kOutput, calls=%fused_computation.76 | convolution fusion | flops 369098752 | bytes 3145732 | tf_op jit(solution)/shard_map/dot_general | solution.py:71
  78.1 0.6 convolution_add_fusion.3
  78.6 1.9 %multiply_convert_fusion.4 = (bf16[256,704]{1,0:T(8,128)(2,1)S(1)}, bf16[256,704]{1,0:T(8,128)(2,1)S(1)}) fusion(f32[256,1408]{1,0:T(8,128)S(1)} %convolution_add_fusion.3, bf16[1,704,1024]{2,1,0:T(8,128)(2,1)S(1)} %copy-done, bf16[256,2048]{1,0:T(8,128)(2,1)} %bitcast.3), kind=kOutput, calls=%fused_computation.48 | convolution fusion | flops 371441664 | bytes 4128768 | tf_op jit(solution)/shard_map/dot_general | solution.py:81
  80.6 0.6 fusion.36
  81.2 0.6 copy-done.10
  81.8 0.1 copy-done.13
  81.9 1.7 %fusion = bf16[512,1408]{1,0:T(8,128)(2,1)} fusion(f32[512,1408]{1,0:T(8,128)S(1)} %fusion.36, bf16[256,1024]{1,0:T(8,128)(2,1)S(1)} %slice.74, s32[]{:T(128)S(6)} %select_n.60, bf16[256,704]{1,0:T(8,128)(2,1)S(1)} %copy-done.13, bf16[256,704]{1,0:T(8,128)(2,1)S(1)} %copy-done.10), kind=kOutput, calls=%fused_computation.2 | convolution fusion | flops 371982336 | bytes 5373956 | tf_op jit(solution)/shard_map/dot_general | solution.py:103
  83.7 1.3 collective-permute-start.1
  84.9 0.1 broadcast.36.clone.1
  85.0 0.6 fusion.17
  85.6 0.6 fusion.18
  86.3 0.7 fusion.11
  86.9 1.1 pad_maximum_fusion.2
  88.0 12.1 %all-to-all-done.3 = bf16[16,16,2048]{2,1,0:T(8,128)(2,1)} async-done(((bf16[16,16,2048]{2,1,0:T(8,128)(2,1)}), bf16[16,16,2048]{2,1,0:T(8,128)(2,1)}, u32[]{:S(2)}, u32[]{:S(2)}) %all-to-all-start.3) | async-done | bytes 1048608 | tf_op jit(solution)/shard_map/all_to_all | solution.py:53
  100.1 4.6 %all-to-all-start.1 = ((bf16[16,16,2048]{2,1,0:T(8,128)(2,1)}), bf16[16,16,2048]{2,1,0:T(8,128)(2,1)}, u32[]{:S(2)}, u32[]{:S(2)}) async-start(bf16[16,16,2048]{2,1,0:T(8,128)(2,1)} %bitcast.69), calls=%async_computation.1 | async-start | bytes 2097152 | tf_op jit(solution)/shard_map/all_to_all | solution.py:53
  104.7 0.2 fusion.28
  105.0 0.6 fusion.39
  105.6 0.3 copy-done.11
  105.9 0.1 copy-done.14
  106.1 0.6 convolution_add_fusion.1
  106.7 10.1 %collective-permute-done.1 = bf16[512,1408]{1,0:T(8,128)(2,1)} collective-permute-done((bf16[512,1408]{1,0:T(8,128)(2,1)}, bf16[512,1408]{1,0:T(8,128)(2,1)}, u32[]{:S(2)}, u32[]{:S(2)}) %collective-permute-start.1) | collective-permute-done | bytes 1441824 | tf_op jit(solution)/shard_map/ppermute | solution.py:112
  116.8 2.8 %fusion.2 = bf16[1,512,1408]{2,1,0:T(8,128)(2,1)} fusion(f32[512,1408]{1,0:T(8,128)S(1)} %convolution_add_fusion.1, bf16[512,1408]{1,0:T(8,128)(2,1)} %collective-permute-done.1), kind=kLoop, calls=%fused_computation.12 | loop fusion | flops 2162688 | bytes 5767168 | tf_op jit(solution)/shard_map/broadcast_in_dim | solution.py:137
  119.6 10.1 %all-to-all-done.1 = bf16[16,16,2048]{2,1,0:T(8,128)(2,1)} async-done(((bf16[16,16,2048]{2,1,0:T(8,128)(2,1)}), bf16[16,16,2048]{2,1,0:T(8,128)(2,1)}, u32[]{:S(2)}, u32[]{:S(2)}) %all-to-all-start.1) | async-done | bytes 1048608 | tf_op jit(solution)/shard_map/all_to_all | solution.py:53
  129.7 1.8 %pad_maximum_fusion = bf16[16,32,2048]{2,1,0:T(8,128)(2,1)S(1)} fusion(bf16[16,16,2048]{2,1,0:T(8,128)(2,1)} %all-to-all-done.3, bf16[16,16,2048]{2,1,0:T(8,128)(2,1)} %all-to-all-done.1), kind=kLoop, calls=%fused_computation.11 | loop fusion | flops 4194304 | bytes 4194304 | tf_op jit(solution)/shard_map/concatenate | solution.py:118
  131.5 0.4 convolution_bitcast_fusion
  132.0 0.9 select_reduce_fusion
  132.9 1.3 convolution_convert_fusion.5
  134.2 1.0 convolution_convert_fusion.4
  (28 shorter events, 0.1 us)
Async XLA Ops:
  0.6 48.1 %copy-start = (bf16[1,704,1024]{2,1,0:T(8,128)(2,1)S(1)}, bf16[1,704,1024]{2,1,0:T(8,128)(2,1)}, u32[]{:S(2)}) copy-start(bf16[1,704,1024]{2,1,0:T(8,128)(2,1)} %param.11) | copy-start | bytes 4325380
  5.9 0.7 copy-start.16
  8.4 31.7 %all-to-all-start.2 = ((bf16[16,16,2048]{2,1,0:T(8,128)(2,1)}), bf16[16,16,2048]{2,1,0:T(8,128)(2,1)}, u32[]{:S(2)}, u32[]{:S(2)}) async-start(bf16[16,16,2048]{2,1,0:T(8,128)(2,1)} %get-tuple-element.11), calls=%async_computation.2 | async-start | bytes 2097152 | tf_op jit(solution)/shard_map/all_to_all | solution.py:53
  15.0 33.1 %collective-permute-start = (bf16[512,1408]{1,0:T(8,128)(2,1)}, bf16[512,1408]{1,0:T(8,128)(2,1)S(1)}, u32[]{:S(2)}, u32[]{:S(2)}) collective-permute-start(bf16[512,1408]{1,0:T(8,128)(2,1)} %bitcast.65), channel_id=1, source_target_pairs={{0,16},{16,0},{1,17},{17,1},{2,18},{18,2},{3,19},{19,3},{4,20},{20... | collective-permute-start | bytes 4325384 | tf_op jit(solution)/shard_map/ppermute | solution.py:14
  40.2 29.7 %all-to-all-start = ((bf16[16,16,2048]{2,1,0:T(8,128)(2,1)}), bf16[16,16,2048]{2,1,0:T(8,128)(2,1)}, u32[]{:S(2)}, u32[]{:S(2)}) async-start(bf16[16,16,2048]{2,1,0:T(8,128)(2,1)} %get-tuple-element.10), calls=%async_computation | async-start | bytes 2097152 | tf_op jit(solution)/shard_map/all_to_all | solution.py:53
  48.7 2.1 %copy-start.1 = (bf16[1,512,1408]{2,1,0:T(8,128)(2,1)S(1)}, bf16[1,512,1408]{2,1,0:T(8,128)(2,1)}, u32[]{:S(2)}) copy-start(bf16[1,512,1408]{2,1,0:T(8,128)(2,1)} %param.10) | copy-start | bytes 4325380
  50.7 0.8 copy-start.9
  50.7 0.9 copy-start.12
  69.9 30.2 %all-to-all-start.3 = ((bf16[16,16,2048]{2,1,0:T(8,128)(2,1)}), bf16[16,16,2048]{2,1,0:T(8,128)(2,1)}, u32[]{:S(2)}, u32[]{:S(2)}) async-start(bf16[16,16,2048]{2,1,0:T(8,128)(2,1)} %bitcast.70), calls=%async_computation.3 | async-start | bytes 2097152 | tf_op jit(solution)/shard_map/all_to_all | solution.py:53
  75.9 4.6 %copy-start.3 = (bf16[256,1024]{1,0:T(8,128)(2,1)}, bf16[256,1024]{1,0:T(8,128)(2,1)S(1)}, u32[]{:S(2)}) copy-start(bf16[256,1024]{1,0:T(8,128)(2,1)S(1)} %slice.70) | copy-start | bytes 1572868
  80.5 5.1 %copy-start.5 = (bf16[256,704]{1,0:T(8,128)(2,1)}, bf16[256,704]{1,0:T(8,128)(2,1)S(1)}, u32[]{:S(2)}) copy-start(bf16[256,704]{1,0:T(8,128)(2,1)S(1)} %get-tuple-element.6) | copy-start | bytes 1081348
  80.5 5.1 %copy-start.7 = (bf16[256,704]{1,0:T(8,128)(2,1)}, bf16[256,704]{1,0:T(8,128)(2,1)S(1)}, u32[]{:S(2)}) copy-start(bf16[256,704]{1,0:T(8,128)(2,1)S(1)} %get-tuple-element.7) | copy-start | bytes 1081348
  80.5 1.3 copy-start.10
  80.5 1.4 %copy-start.13 = (bf16[256,704]{1,0:T(8,128)(2,1)S(1)}, bf16[256,704]{1,0:T(8,128)(2,1)}, u32[]{:S(2)}) copy-start(bf16[256,704]{1,0:T(8,128)(2,1)} %copy-done.12) | copy-start | bytes 1081348
  81.9 3.1 %copy-start.2 = (bf16[1,512,1408]{2,1,0:T(8,128)(2,1)S(1)}, bf16[1,512,1408]{2,1,0:T(8,128)(2,1)}, u32[]{:S(2)}) copy-start(bf16[1,512,1408]{2,1,0:T(8,128)(2,1)} %param.10) | copy-start | bytes 4325380
  83.7 33.1 %collective-permute-start.1 = (bf16[512,1408]{1,0:T(8,128)(2,1)}, bf16[512,1408]{1,0:T(8,128)(2,1)}, u32[]{:S(2)}, u32[]{:S(2)}) collective-permute-start(bf16[512,1408]{1,0:T(8,128)(2,1)} %fusion), channel_id=1, source_target_pairs={{0,16},{16,0},{1,17},{17,1},{2,18},{18,2},{3,19},{19,3},{4,20},{20... | collective-permute-start | bytes 4325384 | tf_op jit(solution)/shard_map/ppermute | solution.py:112
  88.0 16.9 %copy-start.4 = (bf16[256,1024]{1,0:T(8,128)(2,1)S(1)}, bf16[256,1024]{1,0:T(8,128)(2,1)}, u32[]{:S(2)}) copy-start(bf16[256,1024]{1,0:T(8,128)(2,1)} %copy-done.3) | copy-start | bytes 1572868
  88.0 16.9 %copy-start.6 = (bf16[256,704]{1,0:T(8,128)(2,1)S(1)}, bf16[256,704]{1,0:T(8,128)(2,1)}, u32[]{:S(2)}) copy-start(bf16[256,704]{1,0:T(8,128)(2,1)} %copy-done.5) | copy-start | bytes 1081348
  88.0 16.9 %copy-start.8 = (bf16[256,704]{1,0:T(8,128)(2,1)S(1)}, bf16[256,704]{1,0:T(8,128)(2,1)}, u32[]{:S(2)}) copy-start(bf16[256,704]{1,0:T(8,128)(2,1)} %copy-done.7) | copy-start | bytes 1081348
  100.1 29.6 %all-to-all-start.1 = ((bf16[16,16,2048]{2,1,0:T(8,128)(2,1)}), bf16[16,16,2048]{2,1,0:T(8,128)(2,1)}, u32[]{:S(2)}, u32[]{:S(2)}) async-start(bf16[16,16,2048]{2,1,0:T(8,128)(2,1)} %bitcast.69), calls=%async_computation.1 | async-start | bytes 2097152 | tf_op jit(solution)/shard_map/all_to_all | solution.py:53
  104.9 1.0 copy-start.11
  105.0 1.1 copy-start.14
  119.6 11.9 %copy-start.15 = (bf16[64,1024]{1,0:T(8,128)(2,1)S(1)}, bf16[64,1024]{1,0:T(8,128)(2,1)}, u32[]{:S(2)}) copy-start(bf16[64,1024]{1,0:T(8,128)(2,1)} %param.7) | copy-start | bytes 393220

commit v4 on v2

--- a/solution.py
+++ b/solution.py
@@ -25,6 +25,9 @@
     block_rows = w_gate_up.shape[1]
     capacity = 4 * token_count * top_count // (3 * experts)
     weight_blocks = gather_rows(w_gate_up[0], "dp", block_rows)
+    stacked = jnp.stack([weight for _, weight in weight_blocks])
+    order = (me_dp - jnp.arange(replicas, dtype=jnp.int32)) % replicas
+    weight_fwd = jnp.take(stacked, order, axis=0).reshape(replicas * block_rows, -1)
     flat_routes = expert_ids.reshape(token_count * top_count)
     onehot = (flat_routes[:, None] == jnp.arange(experts, dtype=jnp.int32)[None, :]).astype(
         jnp.int32
@@ -51,13 +54,7 @@
     cot_rows = both_recv[:, model_width:]
     weight_down = w_down[0]
 
-    def cols(block):
-        return lax.dynamic_slice_in_dim(input_rows, block * block_rows, block_rows, axis=1)
-
-    gate_up = None
-    for block, weight in weight_blocks:
-        part = jnp.dot(cols(block), weight, preferred_element_type=jnp.float32)
-        gate_up = part if gate_up is None else gate_up + part
+    gate_up = jnp.dot(input_rows, weight_fwd, preferred_element_type=jnp.float32)
     gate = gate_up[:, :hidden_units]
     upper = gate_up[:, hidden_units:]
     sigma = jax.nn.sigmoid(gate)
@@ -72,12 +69,9 @@
     gate_cot = hidden_grad * upper * sigma * (1.0 + gate * (1.0 - sigma))
     upper_cot = hidden_grad * active
     pair_cot = jnp.concatenate([gate_cot, upper_cot], axis=1).astype(jnp.bfloat16)
-    input_cot = jnp.zeros((experts * capacity, model_width), jnp.bfloat16)
-    for block, weight in weight_blocks:
-        part = lax.dot_general(
-            pair_cot, weight, (((1,), (1,)), ((), ())), preferred_element_type=jnp.float32
-        ).astype(jnp.bfloat16)
-        input_cot = lax.dynamic_update_slice_in_dim(input_cot, part, block * block_rows, axis=1)
+    input_cot = lax.dot_general(
+        pair_cot, weight_fwd, (((1,), (1,)), ((), ())), preferred_element_type=jnp.float32
+    ).astype(jnp.bfloat16)
     back = lax.all_to_all(
         jnp.concatenate([output_rows, input_cot], axis=1).reshape(
             experts, capacity, 2 * model_width
@@ -87,39 +81,32 @@
         concat_axis=0,
         tiled=True,
     ).reshape(experts * capacity, 2 * model_width)
-    back_out = back[:, :model_width]
-    back_in = back[:, model_width:]
-    owned = target_rows.reshape(token_count, top_count)[:, :, None] == slots[None, None, :]
-    weights = jnp.sum(jnp.where(owned, gate_probs[:, :, None], 0.0), axis=1)
-    layer_out = jnp.dot(
-        weights,
-        back_out.astype(jnp.float32),
-        precision=lax.Precision.HIGHEST,
-        preferred_element_type=jnp.float32,
-    ).astype(jnp.bfloat16)
-    gathered = jnp.any(owned, axis=1).astype(jnp.bfloat16)
-    input_grad = jnp.dot(gathered, back_in, preferred_element_type=jnp.float32).astype(
+    owned = (target_rows.reshape(token_count * top_count)[:, None] == slots[None, :]).astype(
         jnp.bfloat16
     )
-    inner = lax.dot_general(
-        cotangent, back_out, (((1,), (1,)), ((), ())), preferred_element_type=jnp.float32
+    slot_both = jnp.dot(owned, back, preferred_element_type=jnp.float32).reshape(
+        token_count, top_count, 2 * model_width
     )
-    prob_grad = jnp.sum(jnp.where(owned, inner[:, None, :], 0.0), axis=2)
-    grad_rows = None
-    for shift in range(replicas):
-        block = (me_dp + shift) % replicas
-        partial = lax.dot_general(
-            cols(block), pair_cot, (((0,), (0,)), ((), ())), preferred_element_type=jnp.float32
-        ).astype(jnp.bfloat16)
-        if shift:
-            partial = lax.ppermute(
-                partial, "dp", [(i, (i + shift) % replicas) for i in range(replicas)]
-            )
-        grad_rows = (
-            partial.astype(jnp.float32)
-            if grad_rows is None
-            else grad_rows + partial.astype(jnp.float32)
+    slot_out = slot_both[:, :, :model_width]
+    slot_in = slot_both[:, :, model_width:]
+    layer_out = jnp.sum(gate_probs[:, :, None] * slot_out, axis=1).astype(jnp.bfloat16)
+    input_grad = jnp.sum(slot_in, axis=1).astype(jnp.bfloat16)
+    prob_grad = jnp.sum(cotangent[:, None, :].astype(jnp.float32) * slot_out, axis=2)
+    weight_cot = lax.dot_general(
+        input_rows, pair_cot, (((0,), (0,)), ((), ())), preferred_element_type=jnp.float32
+    )
+
+    def grad_block(block):
+        return lax.dynamic_slice_in_dim(weight_cot, block * block_rows, block_rows, axis=0)
+
+    grad_rows = grad_block(me_dp)
+    for shift in range(1, replicas):
+        moved = lax.ppermute(
+            grad_block((me_dp + shift) % replicas).astype(jnp.bfloat16),
+            "dp",
+            [(i, (i + shift) % replicas) for i in range(replicas)],
         )
+        grad_rows = grad_rows + moved.astype(jnp.float32)
     return (layer_out, input_grad, prob_grad, grad_rows.astype(jnp.bfloat16)[None])
 
 

time: 133 us -> 130 us (0.977)
  waiting for transfers between devices: 83.8 us -> 68.9 us
  other arithmetic: 7.53 us -> 18.6 us
  local copies, waits for them, and re-layouts: 3.11 us -> 11 us
  matrix products: 23.4 us -> 16.1 us
    all_to_all x1, waiting for transfers between devices: 46.2 us -> 2.55 us  [local(): lax.all_to_all(both_send.reshape(experts, capacity, 2 * model_width), 'ex...]
    ppermute x1, waiting for transfers between devices: 0.01 us -> 31.7 us  [gather_rows(): lax.ppermute(own, axis_name, [(i, (i + shift) % count) for i in range(cou...]
    dot_general x9 -> x4, matrix products: 18.9 us -> 10.7 us  [the longest x1 4.36 us: local(): jnp.dot(input_rows, weight_fwd, preferred_element_type=jnp.float32)]
    gather x0 -> x1, local copies, waits for them, and re-layouts: none -> 4.29 us  [local(): jnp.take(stacked, order, axis=0).reshape(replicas * block_rows, -1)]
    select_n x0 -> x2, other arithmetic: none -> 3.8 us  [local(): jnp.take(stacked, order, axis=0).reshape(replicas * block_rows, -1)]
    another operation x2 -> x3, other arithmetic: 0.91 us -> 4.57 us  [the longest x1 3.66 us: local(): stacked = jnp.stack([weight for _, weight in weight_blocks])]
    broadcast_in_dim x0 -> x1, other arithmetic: none -> 3.6 us  [local(): grad_rows.astype(jnp.bfloat16)[None]]
    all_to_all x1, waiting for transfers between devices: 6.52 us -> 3.43 us  [local(): lax.all_to_all(jnp.concatenate([output_rows, input_cot], axis=1).reshape(...]
  transfers between devices with their start and end apart: 4 -> 4, of which waited for: 3 -> 4; matrix products, arithmetic and copies ran while one was open for 7% -> 16% of each run, Pallas kernels for 0% -> 0%
where the time goes in v4:
time: 130 us; the launch traced here: 129 us
  waiting for transfers between devices  68.9 us (53%)
  other arithmetic  18.6 us (14%)
  matrix products  16.1 us (12%)
  starting transfers between devices  14 us (11%)
  local copies, waits for them, and re-layouts  11 us (8%)
    ppermute x1, waiting for transfers between devices, gather_rows(): lax.ppermute(own, axis_name, [(i, (i + shift) % count) for i in range(cou...  31.7 us
    ppermute x1, waiting for transfers between devices, local(): lax.ppermute(grad_block((me_dp + shift) % replicas).astype(jnp.bfloat16),...  31.1 us
    all_to_all x1, starting transfers between devices, local(): lax.all_to_all(both_send.reshape(experts, capacity, 2 * model_width), 'ex...  6.56 us
    all_to_all x1, starting transfers between devices, local(): lax.all_to_all(jnp.concatenate([output_rows, input_cot], axis=1).reshape(...  4.9 us
    unnamed x19, local copies, waits for them, and re-layouts  4.66 us
    dot_general x1, matrix products, local(): jnp.dot(input_rows, weight_fwd, preferred_element_type=jnp.float32)  4.36 us
    gather x1, local copies, waits for them, and re-layouts, local(): jnp.take(stacked, order, axis=0).reshape(replicas * block_rows, -1)  4.29 us
    select_n x2, other arithmetic, local(): jnp.take(stacked, order, axis=0).reshape(replicas * block_rows, -1)  3.8 us
  transfers between devices with their start and end apart: 4, of which 4 were waited for; matrix products, arithmetic and copies ran while one was open for 16% of the time, Pallas kernels for 0%

profile of v4, /device:TPU:11, one launch (start us, length us, event | category | flops | bytes accessed | tf_op | source)
XLA Modules:
  0.0 129.3 jit_solution(8898742106600630090)
XLA Ops:
  0.6 0.0 copy-start
  0.6 0.9 copy.32
  1.5 0.1 eq.71
  1.7 0.1 eq.75
  1.8 0.9 reduce-window.6
  2.7 0.2 slice_reduce_fusion.1
  3.0 0.1 fusion.18
  3.1 0.1 reduce_sum.48
  3.2 0.1 copy.35
  3.3 0.7 multiply_add_fusion
  4.0 0.2 fusion.10
  4.1 0.9 select_reduce_fusion
  5.0 1.4 %convolution_convert_fusion.2 = bf16[512,1024]{1,0:T(8,128)(2,1)S(1)} fusion(pred[512,64]{0,1:T(8,128)(4,1)S(1)} %fusion.10, bf16[64,1024]{1,0:T(8,128)(2,1)} %param.6), kind=kOutput, calls=%fused_computation.18 | convolution fusion | flops 67633152 | bytes 1212416 | tf_op jit(solution)/shard_map/dot_general | solution.py:42
  6.4 1.4 %multiply_convert_fusion = bf16[512,1024]{1,0:T(8,128)(2,1)S(1)} fusion(pred[512,64]{0,1:T(8,128)(4,1)S(1)} %fusion.10, bf16[64,1024]{1,0:T(8,128)(2,1)} %param.7, f32[512]{0:T(512)S(1)} %select_reduce_fusion), kind=kOutput, calls=%fused_computation.7 | convolution fusion | flops 68157440 | bytes 1214464 | tf_op jit(solution)/shard_map/dot_general | solution.py:43
  7.8 1.5 %pad_maximum_fusion.1 = bf16[512,2048]{1,0:T(8,128)(2,1)} fusion(bf16[512,1024]{1,0:T(8,128)(2,1)S(1)} %multiply_convert_fusion, bf16[512,1024]{1,0:T(8,128)(2,1)S(1)} %convolution_convert_fusion.2), kind=kLoop, calls=%fused_computation.5 | loop fusion | flops 4194304 | bytes 4194304 | tf_op jit(solution)/shard_map/concatenate | solution.py:45
  9.3 6.6 %all-to-all-start = ((bf16[16,32,2048]{2,1,0:T(8,128)(2,1)}), bf16[16,32,2048]{2,1,0:T(8,128)(2,1)S(1)}, u32[]{:S(2)}, u32[]{:S(2)}) async-start(bf16[16,32,2048]{2,1,0:T(8,128)(2,1)} %bitcast.2), calls=%async_computation | async-start | bytes 4194304 | tf_op jit(solution)/shard_map/all_to_all | solution.py:46
  15.9 1.2 collective-permute-start
  17.1 0.1 broadcast_in_dim.39
  17.3 31.7 %collective-permute-done = bf16[512,1408]{1,0:T(8,128)(2,1)} collective-permute-done((bf16[512,1408]{1,0:T(8,128)(2,1)}, bf16[512,1408]{1,0:T(8,128)(2,1)}, u32[]{:S(2)}, u32[]{:S(2)}) %collective-permute-start) | collective-permute-done | bytes 1441824 | tf_op jit(solution)/shard_map/ppermute | solution.py:12
  49.0 3.7 %pad_maximum_fusion = bf16[2,512,1408]{2,1,0:T(8,128)(2,1)} fusion(bf16[1,512,1408]{2,1,0:T(8,128)(2,1)} %bitcast.5, bf16[1,512,1408]{2,1,0:T(8,128)(2,1)} %param.10), kind=kLoop, calls=%fused_computation.1 | loop fusion | flops 1441792 | bytes 5767168 | tf_op jit(solution)/shard_map/stack | solution.py:28
  52.7 4.3 %gather_fusion = bf16[2,512,1408]{2,1,0:T(8,128)(2,1)} fusion(bf16[2,512,1408]{2,1,0:T(8,128)(2,1)} %pad_maximum_fusion, s32[1024]{0:T(1024)S(1)} %pad_clamp_fusion), kind=kCustom, calls=%fused_computation | custom fusion | bytes 5767176 | tf_op jit(solution)/shard_map/jit(_take)/gather | solution.py:30
  57.0 3.8 %bitcast_select_fusion = bf16[1024,1408]{1,0:T(8,128)(2,1)} fusion(bf16[2,512,1408]{2,1,0:T(8,128)(2,1)} %gather_fusion, pred[1024]{0:T(1024)(128)(4,1)S(1)} %broadcast_in_dim.40), kind=kLoop, calls=%fused_computation.2 | loop fusion | flops 1441792 | bytes 5768192 | tf_op jit(solution)/shard_map/jit(_take)/select_n | solution.py:30
  60.7 2.6 %all-to-all-done = bf16[16,32,2048]{2,1,0:T(8,128)(2,1)S(1)} async-done(((bf16[16,32,2048]{2,1,0:T(8,128)(2,1)}), bf16[16,32,2048]{2,1,0:T(8,128)(2,1)S(1)}, u32[]{:S(2)}, u32[]{:S(2)}) %all-to-all-start) | async-done | bytes 2097184 | tf_op jit(solution)/shard_map/all_to_all | solution.py:46
  63.3 0.0 copy-start.2
  63.3 4.4 %fusion.8 = f32[512,1408]{1,0:T(8,128)S(1)} fusion(bf16[1024,1408]{1,0:T(8,128)(2,1)} %bitcast_select_fusion, bf16[512,2048]{1,0:T(8,128)(2,1)S(1)} %bitcast.53), kind=kOutput, calls=%fused_computation.27 | convolution fusion | flops 1476395008 | bytes 6815744 | tf_op jit(solution)/shard_map/dot_general | solution.py:57
  67.7 0.0 copy-done.2
  67.7 0.0 copy-done
  67.7 1.5 %multiply_convert_fusion.2 = (bf16[512,704]{1,0:T(8,128)(2,1)S(1)}, bf16[512,704]{1,0:T(8,128)(2,1)S(1)}) fusion(f32[512,1408]{1,0:T(8,128)S(1)} %fusion.8, bf16[1,704,1024]{2,1,0:T(8,128)(2,1)S(1)} %copy-done, bf16[512,2048]{1,0:T(8,128)(2,1)S(1)} %bitcast.54), kind=kOutput, calls=%fused_computation.12 | convolution fusion | flops 742883328 | bytes 7077888 | tf_op jit(solution)/shard_map/dot_general | solution.py:66
  69.2 0.0 copy-start.5
  69.2 0.0 copy-start.6
  69.2 0.0 copy-start.3
  69.2 1.1 convolution_convert_fusion.1
  70.3 0.0 copy-done.5
  70.3 0.0 copy-done.6
  70.3 1.3 copy-done.3
  71.6 1.8 %convolution_convert_fusion = bf16[512,1024]{1,0:T(8,128)(2,1)S(1)} fusion(bf16[1024,1408]{1,0:T(8,128)(2,1)S(1)} %copy-done.3, bf16[512,704]{1,0:T(8,128)(2,1)S(1)} %get-tuple-element.8, bf16[512,704]{1,0:T(8,128)(2,1)S(1)} %get-tuple-element.7), kind=kOutput, calls=%fused_computation.16 | convolution fusion | flops 1479802880 | bytes 5373952 | tf_op jit(solution)/shard_map/dot_general | solution.py:72
  73.4 1.5 %pad_maximum_fusion.2 = bf16[512,2048]{1,0:T(8,128)(2,1)} fusion(bf16[512,1024]{1,0:T(8,128)(2,1)S(1)} %convolution_convert_fusion, bf16[512,1024]{1,0:T(8,128)(2,1)S(1)} %convolution_convert_fusion.1), kind=kLoop, calls=%fused_computation.6 | loop fusion | flops 4194304 | bytes 4194304 | tf_op jit(solution)/shard_map/concatenate | solution.py:76
  74.9 4.9 %all-to-all-start.1 = ((bf16[16,32,2048]{2,1,0:T(8,128)(2,1)}), bf16[16,32,2048]{2,1,0:T(8,128)(2,1)S(1)}, u32[]{:S(2)}, u32[]{:S(2)}) async-start(bf16[16,32,2048]{2,1,0:T(8,128)(2,1)} %bitcast.52), calls=%async_computation.1 | async-start | bytes 4194304 | tf_op jit(solution)/shard_map/all_to_all | solution.py:75
  79.8 3.5 %fusion.6 = f32[1024,1408]{1,0:T(8,128)S(1)} fusion(bf16[512,2048]{1,0:T(8,128)(2,1)} %bitcast.55, bf16[512,704]{1,0:T(8,128)(2,1)} %copy-done.6, bf16[512,704]{1,0:T(8,128)(2,1)} %copy-done.5), kind=kOutput, calls=%fused_computation.25 | convolution fusion | flops 1479278592 | bytes 8388608 | tf_op jit(solution)/shard_map/dot_general | solution.py:95
  83.4 0.0 copy-start.1
  83.4 2.5 %copy-done.1 = f32[1024,1408]{1,0:T(8,128)} copy-done((f32[1024,1408]{1,0:T(8,128)}, f32[1024,1408]{1,0:T(8,128)S(1)}, u32[]{:S(2)}) %copy-start.1) | copy-done | bytes 5767192
  85.8 0.0 copy-start.7
  85.8 1.2 dynamic-slice_convert_fusion
  87.1 1.3 collective-permute-start.1
  88.3 0.0 copy-done.7
  88.3 0.7 convert_element_type.53
  89.1 31.1 %collective-permute-done.1 = bf16[512,1408]{1,0:T(8,128)(2,1)} collective-permute-done((bf16[512,1408]{1,0:T(8,128)(2,1)}, bf16[512,1408]{1,0:T(8,128)(2,1)}, u32[]{:S(2)}, u32[]{:S(2)}) %collective-permute-start.1) | collective-permute-done | bytes 1441824 | tf_op jit(solution)/shard_map/ppermute | solution.py:104
  120.2 3.6 %fusion.1 = bf16[1,512,1408]{2,1,0:T(8,128)(2,1)} fusion(bf16[512,1408]{1,0:T(8,128)(2,1)} %collective-permute-done.1, f32[1024,1408]{1,0:T(8,128)} %copy-done.1, s32[]{:T(128)S(6)} %select_n.61), kind=kLoop, calls=%fused_computation.19 | loop fusion | flops 2162688 | bytes 5767172 | tf_op jit(solution)/shard_map/broadcast_in_dim | solution.py:110
  123.8 3.4 %all-to-all-done.1 = bf16[16,32,2048]{2,1,0:T(8,128)(2,1)S(1)} async-done(((bf16[16,32,2048]{2,1,0:T(8,128)(2,1)}), bf16[16,32,2048]{2,1,0:T(8,128)(2,1)S(1)}, u32[]{:S(2)}, u32[]{:S(2)}) %all-to-all-start.1) | async-done | bytes 2097184 | tf_op jit(solution)/shard_map/all_to_all | solution.py:75
  127.2 0.0 copy-start.4
  127.2 0.0 copy-start.8
  127.2 1.0 fusion.12
  128.3 0.0 copy-done.4
  128.3 0.0 copy-done.8
  128.3 1.0 multiply_reduce_fusion
  (6 shorter events, 0.1 us)
Async XLA Ops:
  0.6 67.0 %copy-start = (bf16[1,704,1024]{2,1,0:T(8,128)(2,1)S(1)}, bf16[1,704,1024]{2,1,0:T(8,128)(2,1)}, u32[]{:S(2)}) copy-start(bf16[1,704,1024]{2,1,0:T(8,128)(2,1)} %param.11) | copy-start | bytes 4325380
  9.3 54.0 %all-to-all-start = ((bf16[16,32,2048]{2,1,0:T(8,128)(2,1)}), bf16[16,32,2048]{2,1,0:T(8,128)(2,1)S(1)}, u32[]{:S(2)}, u32[]{:S(2)}) async-start(bf16[16,32,2048]{2,1,0:T(8,128)(2,1)} %bitcast.2), calls=%async_computation | async-start | bytes 4194304 | tf_op jit(solution)/shard_map/all_to_all | solution.py:46
  15.9 33.1 %collective-permute-start = (bf16[512,1408]{1,0:T(8,128)(2,1)}, bf16[512,1408]{1,0:T(8,128)(2,1)}, u32[]{:S(2)}, u32[]{:S(2)}) collective-permute-start(bf16[512,1408]{1,0:T(8,128)(2,1)} %bitcast.56), channel_id=1, source_target_pairs={{0,16},{16,0},{1,17},{17,1},{2,18},{18,2},{3,19},{19,3},{4,20},{20... | collective-permute-start | bytes 4325384 | tf_op jit(solution)/shard_map/ppermute | solution.py:12
  63.3 4.4 %copy-start.2 = (bf16[16,32,2048]{2,1,0:T(8,128)(2,1)}, bf16[16,32,2048]{2,1,0:T(8,128)(2,1)S(1)}, u32[]{:S(2)}) copy-start(bf16[16,32,2048]{2,1,0:T(8,128)(2,1)S(1)} %all-to-all-done) | copy-start | bytes 6291460
  69.2 1.1 copy-start.5
  69.2 1.1 copy-start.6
  69.2 2.4 %copy-start.3 = (bf16[1024,1408]{1,0:T(8,128)(2,1)S(1)}, bf16[1024,1408]{1,0:T(8,128)(2,1)}, u32[]{:S(2)}) copy-start(bf16[1024,1408]{1,0:T(8,128)(2,1)} %bitcast_select_fusion) | copy-start | bytes 8650756
  74.9 52.3 %all-to-all-start.1 = ((bf16[16,32,2048]{2,1,0:T(8,128)(2,1)}), bf16[16,32,2048]{2,1,0:T(8,128)(2,1)S(1)}, u32[]{:S(2)}, u32[]{:S(2)}) async-start(bf16[16,32,2048]{2,1,0:T(8,128)(2,1)} %bitcast.52), calls=%async_computation.1 | async-start | bytes 4194304 | tf_op jit(solution)/shard_map/all_to_all | solution.py:75
  83.4 2.5 %copy-start.1 = (f32[1024,1408]{1,0:T(8,128)}, f32[1024,1408]{1,0:T(8,128)S(1)}, u32[]{:S(2)}) copy-start(f32[1024,1408]{1,0:T(8,128)S(1)} %fusion.6) | copy-start | bytes 17301508
  85.8 2.5 %copy-start.7 = (bf16[64,1024]{1,0:T(8,128)(2,1)S(1)}, bf16[64,1024]{1,0:T(8,128)(2,1)}, u32[]{:S(2)}) copy-start(bf16[64,1024]{1,0:T(8,128)(2,1)} %param.7) | copy-start | bytes 393220
  87.1 33.1 %collective-permute-start.1 = (bf16[512,1408]{1,0:T(8,128)(2,1)}, bf16[512,1408]{1,0:T(8,128)(2,1)}, u32[]{:S(2)}, u32[]{:S(2)}) collective-permute-start(bf16[512,1408]{1,0:T(8,128)(2,1)} %dynamic-slice_convert_fusion), channel_id=1, source_target_pairs={{0,16},{16,0},{1,17},{17,1},{2,18},{18,2},{3,19},{19,3},{4,20},{20... | collective-permute-start | bytes 4325384 | tf_op jit(solution)/shard_map/ppermute | solution.py:104
  127.2 1.0 copy-start.4
  127.2 1.0 copy-start.8

commit v5 on v4

--- a/solution.py
+++ b/solution.py
@@ -25,9 +25,6 @@
     block_rows = w_gate_up.shape[1]
     capacity = 4 * token_count * top_count // (3 * experts)
     weight_blocks = gather_rows(w_gate_up[0], "dp", block_rows)
-    stacked = jnp.stack([weight for _, weight in weight_blocks])
-    order = (me_dp - jnp.arange(replicas, dtype=jnp.int32)) % replicas
-    weight_fwd = jnp.take(stacked, order, axis=0).reshape(replicas * block_rows, -1)
     flat_routes = expert_ids.reshape(token_count * top_count)
     onehot = (flat_routes[:, None] == jnp.arange(experts, dtype=jnp.int32)[None, :]).astype(
         jnp.int32
@@ -54,7 +51,14 @@
     cot_rows = both_recv[:, model_width:]
     weight_down = w_down[0]
 
-    gate_up = jnp.dot(input_rows, weight_fwd, preferred_element_type=jnp.float32)
+
+    def cols(block):
+        return lax.dynamic_slice_in_dim(input_rows, block * block_rows, block_rows, axis=1)
+
+    gate_up = None
+    for block, weight in weight_blocks:
+        part = jnp.dot(cols(block), weight, preferred_element_type=jnp.float32)
+        gate_up = part if gate_up is None else gate_up + part
     gate = gate_up[:, :hidden_units]
     upper = gate_up[:, hidden_units:]
     sigma = jax.nn.sigmoid(gate)
@@ -69,9 +73,12 @@
     gate_cot = hidden_grad * upper * sigma * (1.0 + gate * (1.0 - sigma))
     upper_cot = hidden_grad * active
     pair_cot = jnp.concatenate([gate_cot, upper_cot], axis=1).astype(jnp.bfloat16)
-    input_cot = lax.dot_general(
-        pair_cot, weight_fwd, (((1,), (1,)), ((), ())), preferred_element_type=jnp.float32
-    ).astype(jnp.bfloat16)
+    input_cot = jnp.zeros((experts * capacity, model_width), jnp.bfloat16)
+    for block, weight in weight_blocks:
+        part = lax.dot_general(
+            pair_cot, weight, (((1,), (1,)), ((), ())), preferred_element_type=jnp.float32
+        ).astype(jnp.bfloat16)
+        input_cot = lax.dynamic_update_slice_in_dim(input_cot, part, block * block_rows, axis=1)
     back = lax.all_to_all(
         jnp.concatenate([output_rows, input_cot], axis=1).reshape(
             experts, capacity, 2 * model_width

time: 130 us -> 131 us (level)
  waiting for transfers between devices: 68.9 us -> 86.5 us
  other arithmetic: 18.6 us -> 8.91 us
  local copies, waits for them, and re-layouts: 11 us -> 4.04 us
    all_to_all x1, waiting for transfers between devices: 2.55 us -> 46.2 us  [local(): lax.all_to_all(both_send.reshape(experts, capacity, 2 * model_width), 'ex...]
    ppermute x1, waiting for transfers between devices: 31.7 us -> 0.01 us  [gather_rows(): lax.ppermute(own, axis_name, [(i, (i + shift) % count) for i in range(cou...]
    all_to_all x1, waiting for transfers between devices: 3.43 us -> 9.45 us  [local(): lax.all_to_all(jnp.concatenate([output_rows, input_cot], axis=1).reshape(...]
    gather x1 -> x0, local copies, waits for them, and re-layouts: 4.29 us -> none  [local(): jnp.take(stacked, order, axis=0).reshape(replicas * block_rows, -1)]
    select_n x2 -> x0, other arithmetic: 3.8 us -> none  [local(): jnp.take(stacked, order, axis=0).reshape(replicas * block_rows, -1)]
    another operation x3 -> x2, other arithmetic: 4.57 us -> 0.91 us  [the longest x1 3.66 us: local(): stacked = jnp.stack([weight for _, weight in weight_blocks])]
    broadcast_in_dim x1, other arithmetic: 3.6 us -> 1.36 us  [local(): grad_rows.astype(jnp.bfloat16)[None]]
    unnamed x19, local copies, waits for them, and re-layouts: 4.66 us -> 2.97 us
  transfers between devices with their start and end apart: 4 -> 4, of which waited for: 4 -> 3; matrix products, arithmetic and copies ran while one was open for 16% -> 5% of each run, Pallas kernels for 0% -> 0%
where the time goes in v5:
time: 131 us; the launch traced here: 130 us
  waiting for transfers between devices  86.5 us (66%)
  matrix products  15.8 us (12%)
  starting transfers between devices  14 us (11%)
  other arithmetic  8.91 us (7%)
  local copies, waits for them, and re-layouts  4.04 us (3%)
    all_to_all x1, waiting for transfers between devices, local(): lax.all_to_all(both_send.reshape(experts, capacity, 2 * model_width), 'ex...  46.2 us
    ppermute x1, waiting for transfers between devices, local(): lax.ppermute(grad_block((me_dp + shift) % replicas).astype(jnp.bfloat16),...  30.8 us
    all_to_all x1, waiting for transfers between devices, local(): lax.all_to_all(jnp.concatenate([output_rows, input_cot], axis=1).reshape(...  9.45 us
    all_to_all x1, starting transfers between devices, local(): lax.all_to_all(both_send.reshape(experts, capacity, 2 * model_width), 'ex...  6.55 us
    all_to_all x1, starting transfers between devices, local(): lax.all_to_all(jnp.concatenate([output_rows, input_cot], axis=1).reshape(...  4.91 us
    dot_general x1, matrix products, local(): lax.dot_general(input_rows, pair_cot, (((0,), (0,)), ((), ())), preferred...  3.54 us
    dot_general x2, matrix products, local(): lax.dot_general(pair_cot, weight, (((1,), (1,)), ((), ())), preferred_ele...  3.4 us
    dot_general x2, matrix products, local(): part = jnp.dot(cols(block), weight, preferred_element_type=jnp.float32)  3.35 us
  transfers between devices with their start and end apart: 4, of which 3 were waited for; matrix products, arithmetic and copies ran while one was open for 5% of the time, Pallas kernels for 0%

profile of v5, /device:TPU:11, one launch (start us, length us, event | category | flops | bytes accessed | tf_op | source)
XLA Modules:
  0.0 130.0 jit_solution(13681527682199118214)
XLA Ops:
  0.6 0.0 copy-start
  0.6 0.0 copy-start.6
  0.7 0.9 copy.38
  1.6 0.1 eq.70
  1.7 0.1 eq.74
  1.9 0.9 reduce-window.6
  2.7 0.2 slice_reduce_fusion.1
  3.0 0.1 fusion.20
  3.1 0.1 reduce_sum.48
  3.2 0.1 copy.41
  3.3 0.7 multiply_add_fusion
  4.0 0.2 fusion.8
  4.2 0.9 select_reduce_fusion
  5.0 1.4 %convolution_convert_fusion.1 = bf16[512,1024]{1,0:T(8,128)(2,1)S(1)} fusion(pred[512,64]{0,1:T(8,128)(4,1)S(1)} %fusion.8, bf16[64,1024]{1,0:T(8,128)(2,1)} %param.6), kind=kOutput, calls=%fused_computation.15 | convolution fusion | flops 67633152 | bytes 1212416 | tf_op jit(solution)/shard_map/dot_general | solution.py:39
  6.4 0.0 copy-done.6
  6.5 0.5 multiply_convert_fusion
  6.9 1.5 %pad_maximum_fusion = bf16[512,2048]{1,0:T(8,128)(2,1)} fusion(bf16[512,1024]{1,0:T(8,128)(2,1)S(1)} %multiply_convert_fusion, bf16[512,1024]{1,0:T(8,128)(2,1)S(1)} %convolution_convert_fusion.1), kind=kLoop, calls=%fused_computation.3 | loop fusion | flops 4194304 | bytes 4194304 | tf_op jit(solution)/shard_map/concatenate | solution.py:42
  8.4 6.6 %all-to-all-start = ((bf16[16,32,2048]{2,1,0:T(8,128)(2,1)}), bf16[16,32,2048]{2,1,0:T(8,128)(2,1)S(1)}, u32[]{:S(2)}, u32[]{:S(2)}) async-start(bf16[16,32,2048]{2,1,0:T(8,128)(2,1)} %bitcast.2), calls=%async_computation | async-start | bytes 4194304 | tf_op jit(solution)/shard_map/all_to_all | solution.py:43
  15.0 1.2 collective-permute-start
  16.2 46.2 %all-to-all-done = bf16[16,32,2048]{2,1,0:T(8,128)(2,1)S(1)} async-done(((bf16[16,32,2048]{2,1,0:T(8,128)(2,1)}), bf16[16,32,2048]{2,1,0:T(8,128)(2,1)S(1)}, u32[]{:S(2)}, u32[]{:S(2)}) %all-to-all-start) | async-done | bytes 2097184 | tf_op jit(solution)/shard_map/all_to_all | solution.py:43
  62.4 0.0 copy-start.1
  62.4 0.0 copy-start.2
  62.4 0.1 slice.33
  62.5 2.0 %copy-done.2 = bf16[1,512,1408]{2,1,0:T(8,128)(2,1)S(1)} copy-done((bf16[1,512,1408]{2,1,0:T(8,128)(2,1)S(1)}, bf16[1,512,1408]{2,1,0:T(8,128)(2,1)}, u32[]{:S(2)}) %copy-start.2) | copy-done | bytes 1441816
  64.5 1.0 fusion.13
  65.5 0.0 collective-permute-done
  65.5 2.4 %convolution_add_fusion = f32[512,1408]{1,0:T(8,128)S(1)} fusion(f32[512,1408]{1,0:T(8,128)S(1)} %fusion.13, bf16[512,1408]{1,0:T(8,128)(2,1)} %collective-permute-done, bf16[512,1024]{1,0:T(8,128)(2,1)S(1)} %slice.33, s32[]{:T(128)S(6)} %select_n.30), kind=kOutput, calls=%fused_computation | convolution fusion | flops 738918400 | bytes 7733252 | tf_op jit(solution)/shard_map/dot_general | solution.py:60
  67.9 0.0 copy-done.1
  67.9 0.0 copy-done
  67.9 1.5 %multiply_convert_fusion.2 = (bf16[512,704]{1,0:T(8,128)(2,1)S(1)}, bf16[512,704]{1,0:T(8,128)(2,1)S(1)}) fusion(f32[512,1408]{1,0:T(8,128)S(1)} %convolution_add_fusion, bf16[1,704,1024]{2,1,0:T(8,128)(2,1)S(1)} %copy-done, bf16[512,2048]{1,0:T(8,128)(2,1)S(1)} %bitcast.53), kind=kOutput, calls=%fused_computation.10 | convolution fusion | flops 742883328 | bytes 7077888 | tf_op jit(solution)/shard_map/dot_general | solution.py:70
  69.4 0.0 copy-start.4
  69.4 0.0 copy-start.5
  69.4 1.1 convolution_convert_fusion
  70.5 0.1 broadcast_in_dim.28
  70.6 1.0 fusion.5
  71.7 0.0 copy-done.4
  71.7 0.0 copy-done.5
  71.7 2.4 %fusion.6 = bf16[512,1024]{1,0:T(8,128)(2,1)S(1)} fusion(bf16[512,1024]{1,0:T(8,128)(2,1)S(1)} %fusion.5, s32[]{:T(128)S(6)} %select_n.30, bf16[512,1408]{1,0:T(8,128)(2,1)} %collective-permute-done, bf16[512,704]{1,0:T(8,128)(2,1)S(1)} %get-tuple-element.8, bf16[512,704]{1,0:T(8,128)(2,1)S(1)} %get-tuple-element.7), kind=kOutput, calls=%fused_computation.24 | convolution fusion | flops 741343232 | bytes 3538948 | tf_op jit(solution)/shard_map/dot_general | solution.py:78
  74.1 1.5 %pad_maximum_fusion.1 = bf16[512,2048]{1,0:T(8,128)(2,1)} fusion(bf16[512,1024]{1,0:T(8,128)(2,1)S(1)} %fusion.6, bf16[512,1024]{1,0:T(8,128)(2,1)S(1)} %convolution_convert_fusion), kind=kLoop, calls=%fused_computation.4 | loop fusion | flops 4194304 | bytes 4194304 | tf_op jit(solution)/shard_map/concatenate | solution.py:83
  75.6 4.9 %all-to-all-start.1 = ((bf16[16,32,2048]{2,1,0:T(8,128)(2,1)}), bf16[16,32,2048]{2,1,0:T(8,128)(2,1)S(1)}, u32[]{:S(2)}, u32[]{:S(2)}) async-start(bf16[16,32,2048]{2,1,0:T(8,128)(2,1)} %bitcast.51), calls=%async_computation.1 | async-start | bytes 4194304 | tf_op jit(solution)/shard_map/all_to_all | solution.py:82
  80.5 3.5 %fusion.16 = f32[1024,1408]{1,0:T(8,128)S(1)} fusion(bf16[512,704]{1,0:T(8,128)(2,1)} %copy-done.5, bf16[512,704]{1,0:T(8,128)(2,1)} %copy-done.4, bf16[512,2048]{1,0:T(8,128)(2,1)} %bitcast.54), kind=kOutput, calls=%fused_computation.36 | convolution fusion | flops 1479278592 | bytes 8388608 | tf_op jit(solution)/shard_map/dot_general | solution.py:102
  84.1 0.0 copy-start.7
  84.1 0.2 dynamic-slice_convert_fusion
  84.3 1.3 %collective-permute-start.1 = (bf16[512,1408]{1,0:T(8,128)(2,1)S(1)}, bf16[512,1408]{1,0:T(8,128)(2,1)S(1)}, u32[]{:S(2)}, u32[]{:S(2)}) collective-permute-start(bf16[512,1408]{1,0:T(8,128)(2,1)S(1)} %dynamic-slice_convert_fusion), channel_id=1, source_target_pairs={{0,16},{16,0},{1,17},{17,1},{2,18},{18,2},{3,19},{19,3},{4,20},{20... | collective-permute-start | bytes 4325384 | tf_op jit(solution)/shard_map/ppermute | solution.py:111
  85.6 0.0 copy-done.7
  85.6 0.7 convert_element_type.57
  86.3 30.8 %collective-permute-done.1 = bf16[512,1408]{1,0:T(8,128)(2,1)S(1)} collective-permute-done((bf16[512,1408]{1,0:T(8,128)(2,1)S(1)}, bf16[512,1408]{1,0:T(8,128)(2,1)S(1)}, u32[]{:S(2)}, u32[]{:S(2)}) %collective-permute-start.1) | collective-permute-done | bytes 1441824 | tf_op jit(solution)/shard_map/ppermute | solution.py:111
  117.1 1.4 %fusion.1 = bf16[1,512,1408]{2,1,0:T(8,128)(2,1)} fusion(bf16[512,1408]{1,0:T(8,128)(2,1)S(1)} %collective-permute-done.1, f32[1024,1408]{1,0:T(8,128)S(1)} %fusion.16, s32[]{:T(128)S(6)} %select_n.28), kind=kLoop, calls=%fused_computation.16 | loop fusion | flops 2162688 | bytes 5767172 | tf_op jit(solution)/shard_map/broadcast_in_dim | solution.py:117
  118.5 9.5 %all-to-all-done.1 = bf16[16,32,2048]{2,1,0:T(8,128)(2,1)S(1)} async-done(((bf16[16,32,2048]{2,1,0:T(8,128)(2,1)}), bf16[16,32,2048]{2,1,0:T(8,128)(2,1)S(1)}, u32[]{:S(2)}, u32[]{:S(2)}) %all-to-all-start.1) | async-done | bytes 2097184 | tf_op jit(solution)/shard_map/all_to_all | solution.py:82
  128.0 0.0 copy-start.3
  128.0 0.0 copy-start.8
  128.0 1.0 fusion.10
  129.0 0.0 copy-done.3
  129.0 0.0 copy-done.8
  129.0 1.0 multiply_reduce_fusion
  (2 shorter events, 0.0 us)
Async XLA Ops:
  0.6 67.3 %copy-start = (bf16[1,704,1024]{2,1,0:T(8,128)(2,1)S(1)}, bf16[1,704,1024]{2,1,0:T(8,128)(2,1)}, u32[]{:S(2)}) copy-start(bf16[1,704,1024]{2,1,0:T(8,128)(2,1)} %param.11) | copy-start | bytes 4325380
  0.6 5.8 %copy-start.6 = (bf16[64,1024]{1,0:T(8,128)(2,1)S(1)}, bf16[64,1024]{1,0:T(8,128)(2,1)}, u32[]{:S(2)}) copy-start(bf16[64,1024]{1,0:T(8,128)(2,1)} %param.7) | copy-start | bytes 393220
  8.4 54.0 %all-to-all-start = ((bf16[16,32,2048]{2,1,0:T(8,128)(2,1)}), bf16[16,32,2048]{2,1,0:T(8,128)(2,1)S(1)}, u32[]{:S(2)}, u32[]{:S(2)}) async-start(bf16[16,32,2048]{2,1,0:T(8,128)(2,1)} %bitcast.2), calls=%async_computation | async-start | bytes 4194304 | tf_op jit(solution)/shard_map/all_to_all | solution.py:43
  15.0 50.5 %collective-permute-start = (bf16[512,1408]{1,0:T(8,128)(2,1)}, bf16[512,1408]{1,0:T(8,128)(2,1)}, u32[]{:S(2)}, u32[]{:S(2)}) collective-permute-start(bf16[512,1408]{1,0:T(8,128)(2,1)} %bitcast.55), channel_id=1, source_target_pairs={{0,16},{16,0},{1,17},{17,1},{2,18},{18,2},{3,19},{19,3},{4,20},{20... | collective-permute-start | bytes 4325384 | tf_op jit(solution)/shard_map/ppermute | solution.py:12
  62.4 5.5 %copy-start.1 = (bf16[16,32,2048]{2,1,0:T(8,128)(2,1)}, bf16[16,32,2048]{2,1,0:T(8,128)(2,1)S(1)}, u32[]{:S(2)}) copy-start(bf16[16,32,2048]{2,1,0:T(8,128)(2,1)S(1)} %all-to-all-done) | copy-start | bytes 6291460
  62.4 2.1 %copy-start.2 = (bf16[1,512,1408]{2,1,0:T(8,128)(2,1)S(1)}, bf16[1,512,1408]{2,1,0:T(8,128)(2,1)}, u32[]{:S(2)}) copy-start(bf16[1,512,1408]{2,1,0:T(8,128)(2,1)} %param.10) | copy-start | bytes 4325380
  69.4 2.3 %copy-start.4 = (bf16[512,704]{1,0:T(8,128)(2,1)}, bf16[512,704]{1,0:T(8,128)(2,1)S(1)}, u32[]{:S(2)}) copy-start(bf16[512,704]{1,0:T(8,128)(2,1)S(1)} %get-tuple-element.7) | copy-start | bytes 2162692
  69.4 2.3 %copy-start.5 = (bf16[512,704]{1,0:T(8,128)(2,1)}, bf16[512,704]{1,0:T(8,128)(2,1)S(1)}, u32[]{:S(2)}) copy-start(bf16[512,704]{1,0:T(8,128)(2,1)S(1)} %get-tuple-element.8) | copy-start | bytes 2162692
  75.6 52.3 %all-to-all-start.1 = ((bf16[16,32,2048]{2,1,0:T(8,128)(2,1)}), bf16[16,32,2048]{2,1,0:T(8,128)(2,1)S(1)}, u32[]{:S(2)}, u32[]{:S(2)}) async-start(bf16[16,32,2048]{2,1,0:T(8,128)(2,1)} %bitcast.51), calls=%async_computation.1 | async-start | bytes 4194304 | tf_op jit(solution)/shard_map/all_to_all | solution.py:82
  84.1 1.5 %copy-start.7 = (bf16[64,1024]{1,0:T(8,128)(2,1)S(1)}, bf16[64,1024]{1,0:T(8,128)(2,1)}, u32[]{:S(2)}) copy-start(bf16[64,1024]{1,0:T(8,128)(2,1)} %param.7) | copy-start | bytes 393220
  84.3 32.9 %collective-permute-start.1 = (bf16[512,1408]{1,0:T(8,128)(2,1)S(1)}, bf16[512,1408]{1,0:T(8,128)(2,1)S(1)}, u32[]{:S(2)}, u32[]{:S(2)}) collective-permute-start(bf16[512,1408]{1,0:T(8,128)(2,1)S(1)} %dynamic-slice_convert_fusion), channel_id=1, source_target_pairs={{0,16},{16,0},{1,17},{17,1},{2,18},{18,2},{3,19},{19,3},{4,20},{20... | collective-permute-start | bytes 4325384 | tf_op jit(solution)/shard_map/ppermute | solution.py:111
  128.0 1.0 copy-start.3
  128.0 1.0 copy-start.8

commit v6 on v5

--- a/solution.py
+++ b/solution.py
@@ -39,7 +39,9 @@
     token_send = jnp.dot(pick, tokens, preferred_element_type=jnp.float32).astype(jnp.bfloat16)
     cot_pick = jnp.dot(pick, cotangent, preferred_element_type=jnp.float32)
     cot_send = (slot_prob[:, None] * cot_pick).astype(jnp.bfloat16)
-    both_send = jnp.concatenate([token_send, cot_send], axis=1)
+    both_send = jnp.zeros((experts * capacity, 2 * model_width), jnp.bfloat16)
+    both_send = lax.dynamic_update_slice_in_dim(both_send, token_send, 0, axis=1)
+    both_send = lax.dynamic_update_slice_in_dim(both_send, cot_send, model_width, axis=1)
     both_recv = lax.all_to_all(
         both_send.reshape(experts, capacity, 2 * model_width),
         "expert",
@@ -73,14 +75,17 @@
     gate_cot = hidden_grad * upper * sigma * (1.0 + gate * (1.0 - sigma))
     upper_cot = hidden_grad * active
     pair_cot = jnp.concatenate([gate_cot, upper_cot], axis=1).astype(jnp.bfloat16)
-    input_cot = jnp.zeros((experts * capacity, model_width), jnp.bfloat16)
+    send_back = jnp.zeros((experts * capacity, 2 * model_width), jnp.bfloat16)
+    send_back = lax.dynamic_update_slice_in_dim(send_back, output_rows, 0, axis=1)
     for block, weight in weight_blocks:
         part = lax.dot_general(
             pair_cot, weight, (((1,), (1,)), ((), ())), preferred_element_type=jnp.float32
         ).astype(jnp.bfloat16)
-        input_cot = lax.dynamic_update_slice_in_dim(input_cot, part, block * block_rows, axis=1)
+        send_back = lax.dynamic_update_slice_in_dim(
+            send_back, part, model_width + block * block_rows, axis=1
+        )
     back = lax.all_to_all(
-        jnp.concatenate([output_rows, input_cot], axis=1).reshape(
+        send_back.reshape(
             experts, capacity, 2 * model_width
         ),
         "expert",

time: 131 us -> 130 us (level)
  other arithmetic: 8.91 us -> 7.37 us
  local copies, waits for them, and re-layouts: 4.04 us -> 5.5 us
    concatenate x2 -> x0, other arithmetic: 3.03 us -> none  [the longest x1 1.54 us: local(): jnp.concatenate([output_rows, input_cot], axis=1)]
    dynamic_update_slice x0 -> x1, other arithmetic: none -> 1.49 us  [local(): lax.dynamic_update_slice_in_dim(both_send, cot_send, model_width, axis=1)]
    unnamed x19 -> x21, local copies, waits for them, and re-layouts: 2.97 us -> 4.32 us
where the time goes in v6:
time: 130 us
  waiting for transfers between devices  86.5 us (67%)
  matrix products  15.8 us (12%)
  starting transfers between devices  14 us (11%)
  other arithmetic  7.37 us (6%)
  local copies, waits for them, and re-layouts  5.5 us (4%)
    all_to_all x1, waiting for transfers between devices, local(): lax.all_to_all(both_send.reshape(experts, capacity, 2 * model_width), 'ex...  46.2 us
    ppermute x1, waiting for transfers between devices, local(): lax.ppermute(grad_block((me_dp + shift) % replicas).astype(jnp.bfloat16),...  30.8 us
    all_to_all x1, waiting for transfers between devices, local(): lax.all_to_all(send_back.reshape(experts, capacity, 2 * model_width), 'ex...  9.46 us
    all_to_all x1, starting transfers between devices, local(): lax.all_to_all(both_send.reshape(experts, capacity, 2 * model_width), 'ex...  6.55 us
    all_to_all x1, starting transfers between devices, local(): lax.all_to_all(send_back.reshape(experts, capacity, 2 * model_width), 'ex...  4.91 us
    unnamed x21, local copies, waits for them, and re-layouts  4.32 us
    dot_general x1, matrix products, local(): lax.dot_general(input_rows, pair_cot, (((0,), (0,)), ((), ())), preferred...  3.54 us
    dot_general x2, matrix products, local(): lax.dot_general(pair_cot, weight, (((1,), (1,)), ((), ())), preferred_ele...  3.4 us
  transfers between devices with their start and end apart: 4, of which 3 were waited for; matrix products, arithmetic and copies ran while one was open for 5% of the time, Pallas kernels for 0%

profile of v6, /device:TPU:11, one launch (start us, length us, event | category | flops | bytes accessed | tf_op | source)
XLA Modules:
  0.0 130.0 jit_solution(8626291894743989200)
XLA Ops:
  0.6 0.0 copy-start
  0.6 0.0 copy-start.7
  0.7 0.9 copy.32
  1.6 0.1 eq.74
  1.7 0.1 eq.70
  1.9 0.9 reduce-window.6
  2.7 0.2 slice_reduce_fusion.1
  3.0 0.1 fusion.20
  3.1 0.1 reduce_sum.48
  3.2 0.1 copy.35
  3.3 0.7 multiply_add_fusion
  4.0 0.2 fusion.8
  4.2 0.9 select_reduce_fusion
  5.0 1.4 %convolution_convert_fusion.1 = bf16[512,1024]{1,0:T(8,128)(2,1)S(1)} fusion(pred[512,64]{0,1:T(8,128)(4,1)S(1)} %fusion.8, bf16[64,1024]{1,0:T(8,128)(2,1)} %param.6), kind=kOutput, calls=%fused_computation.14 | convolution fusion | flops 67633152 | bytes 1212416 | tf_op jit(solution)/shard_map/dot_general | solution.py:39
  6.4 0.0 copy-done.7
  6.5 0.5 multiply_convert_fusion
  6.9 1.5 %pad_maximum_fusion = bf16[512,2048]{1,0:T(8,128)(2,1)} fusion(bf16[512,1024]{1,0:T(8,128)(2,1)S(1)} %multiply_convert_fusion, bf16[512,1024]{1,0:T(8,128)(2,1)S(1)} %convolution_convert_fusion.1), kind=kLoop, calls=%fused_computation.3 | loop fusion | flops 4194304 | bytes 4194304 | tf_op jit(solution)/shard_map/dynamic_update_slice | solution.py:44
  8.4 6.6 %all-to-all-start = ((bf16[16,32,2048]{2,1,0:T(8,128)(2,1)}), bf16[16,32,2048]{2,1,0:T(8,128)(2,1)S(1)}, u32[]{:S(2)}, u32[]{:S(2)}) async-start(bf16[16,32,2048]{2,1,0:T(8,128)(2,1)} %bitcast.2), calls=%async_computation | async-start | bytes 4194304 | tf_op jit(solution)/shard_map/all_to_all | solution.py:45
  15.0 1.2 collective-permute-start
  16.2 46.2 %all-to-all-done = bf16[16,32,2048]{2,1,0:T(8,128)(2,1)S(1)} async-done(((bf16[16,32,2048]{2,1,0:T(8,128)(2,1)}), bf16[16,32,2048]{2,1,0:T(8,128)(2,1)S(1)}, u32[]{:S(2)}, u32[]{:S(2)}) %all-to-all-start) | async-done | bytes 2097184 | tf_op jit(solution)/shard_map/all_to_all | solution.py:45
  62.4 0.0 copy-start.2
  62.4 0.0 copy-start.3
  62.4 0.1 slice.33
  62.5 2.0 %copy-done.3 = bf16[1,512,1408]{2,1,0:T(8,128)(2,1)S(1)} copy-done((bf16[1,512,1408]{2,1,0:T(8,128)(2,1)S(1)}, bf16[1,512,1408]{2,1,0:T(8,128)(2,1)}, u32[]{:S(2)}) %copy-start.3) | copy-done | bytes 1441816
  64.5 1.0 fusion.13
  65.5 0.0 collective-permute-done
  65.5 2.4 %convolution_add_fusion = f32[512,1408]{1,0:T(8,128)S(1)} fusion(f32[512,1408]{1,0:T(8,128)S(1)} %fusion.13, bf16[512,1408]{1,0:T(8,128)(2,1)} %collective-permute-done, bf16[512,1024]{1,0:T(8,128)(2,1)S(1)} %slice.33, s32[]{:T(128)S(6)} %select_n.34), kind=kOutput, calls=%fused_computation | convolution fusion | flops 738918400 | bytes 7733252 | tf_op jit(solution)/shard_map/dot_general | solution.py:62
  67.9 0.0 copy-done
  67.9 1.1 convolution_convert_fusion
  69.0 0.0 copy-done.2
  69.0 1.5 %multiply_convert_fusion.2 = (bf16[512,704]{1,0:T(8,128)(2,1)S(1)}, bf16[512,704]{1,0:T(8,128)(2,1)S(1)}) fusion(f32[512,1408]{1,0:T(8,128)S(1)} %convolution_add_fusion, bf16[1,704,1024]{2,1,0:T(8,128)(2,1)S(1)} %copy-done, bf16[512,2048]{1,0:T(8,128)(2,1)S(1)} %bitcast.53), kind=kOutput, calls=%fused_computation.9 | convolution fusion | flops 742883328 | bytes 7077888 | tf_op jit(solution)/shard_map/dot_general | solution.py:72
  70.5 0.0 copy-start.5
  70.5 0.0 copy-start.6
  70.5 0.2 dynamic_update_slice.14
  70.8 1.0 fusion.5
  71.8 0.0 copy-done.5
  71.8 0.0 copy-done.6
  71.8 2.4 %fusion.6 = bf16[512,2048]{1,0:T(8,128)(2,1)S(1)} fusion(bf16[512,2048]{1,0:T(8,128)(2,1)S(1)} %fusion.5, s32[]{:T(128)S(6)} %select_n.36, bf16[512,1408]{1,0:T(8,128)(2,1)} %collective-permute-done, bf16[512,704]{1,0:T(8,128)(2,1)S(1)} %get-tuple-element.8, bf16[512,704]{1,0:T(8,128)(2,1)S(1)} %get-tuple-element.7), kind=kOutput, calls=%fused_computation.23 | convolution fusion | flops 741343232 | bytes 3538948 | tf_op jit(solution)/shard_map/dot_general | solution.py:81
  74.2 0.0 copy-start.1
  74.2 1.3 %copy-done.1 = bf16[512,2048]{1,0:T(8,128)(2,1)} copy-done((bf16[512,2048]{1,0:T(8,128)(2,1)}, bf16[512,2048]{1,0:T(8,128)(2,1)S(1)}, u32[]{:S(2)}) %copy-start.1) | copy-done | bytes 2097176
  75.6 4.9 %all-to-all-start.1 = ((bf16[16,32,2048]{2,1,0:T(8,128)(2,1)}), bf16[16,32,2048]{2,1,0:T(8,128)(2,1)S(1)}, u32[]{:S(2)}, u32[]{:S(2)}) async-start(bf16[16,32,2048]{2,1,0:T(8,128)(2,1)} %bitcast.51), calls=%async_computation.1 | async-start | bytes 4194304 | tf_op jit(solution)/shard_map/all_to_all | solution.py:87
  80.5 3.5 %fusion.16 = f32[1024,1408]{1,0:T(8,128)S(1)} fusion(bf16[512,704]{1,0:T(8,128)(2,1)} %copy-done.6, bf16[512,704]{1,0:T(8,128)(2,1)} %copy-done.5, bf16[512,2048]{1,0:T(8,128)(2,1)} %bitcast.54), kind=kOutput, calls=%fused_computation.35 | convolution fusion | flops 1479278592 | bytes 8388608 | tf_op jit(solution)/shard_map/dot_general | solution.py:107
  84.0 0.0 copy-start.8
  84.0 0.2 dynamic-slice_convert_fusion
  84.2 1.3 %collective-permute-start.1 = (bf16[512,1408]{1,0:T(8,128)(2,1)S(1)}, bf16[512,1408]{1,0:T(8,128)(2,1)S(1)}, u32[]{:S(2)}, u32[]{:S(2)}) collective-permute-start(bf16[512,1408]{1,0:T(8,128)(2,1)S(1)} %dynamic-slice_convert_fusion), channel_id=1, source_target_pairs={{0,16},{16,0},{1,17},{17,1},{2,18},{18,2},{3,19},{19,3},{4,20},{20... | collective-permute-start | bytes 4325384 | tf_op jit(solution)/shard_map/ppermute | solution.py:116
  85.5 0.0 copy-done.8
  85.5 0.7 convert_element_type.57
  86.3 30.8 %collective-permute-done.1 = bf16[512,1408]{1,0:T(8,128)(2,1)S(1)} collective-permute-done((bf16[512,1408]{1,0:T(8,128)(2,1)S(1)}, bf16[512,1408]{1,0:T(8,128)(2,1)S(1)}, u32[]{:S(2)}, u32[]{:S(2)}) %collective-permute-start.1) | collective-permute-done | bytes 1441824 | tf_op jit(solution)/shard_map/ppermute | solution.py:116
  117.1 1.4 %fusion.1 = bf16[1,512,1408]{2,1,0:T(8,128)(2,1)} fusion(bf16[512,1408]{1,0:T(8,128)(2,1)S(1)} %collective-permute-done.1, f32[1024,1408]{1,0:T(8,128)S(1)} %fusion.16, s32[]{:T(128)S(6)} %select_n.32), kind=kLoop, calls=%fused_computation.15 | loop fusion | flops 2162688 | bytes 5767172 | tf_op jit(solution)/shard_map/broadcast_in_dim | solution.py:122
  118.4 9.5 %all-to-all-done.1 = bf16[16,32,2048]{2,1,0:T(8,128)(2,1)S(1)} async-done(((bf16[16,32,2048]{2,1,0:T(8,128)(2,1)}), bf16[16,32,2048]{2,1,0:T(8,128)(2,1)S(1)}, u32[]{:S(2)}, u32[]{:S(2)}) %all-to-all-start.1) | async-done | bytes 2097184 | tf_op jit(solution)/shard_map/all_to_all | solution.py:87
  127.9 0.0 copy-start.4
  127.9 0.0 copy-start.9
  127.9 1.0 fusion.10
  128.9 0.0 copy-done.4
  128.9 0.0 copy-done.9
  128.9 1.0 multiply_reduce_fusion
  (2 shorter events, 0.0 us)
Async XLA Ops:
  0.6 67.3 %copy-start = (bf16[1,704,1024]{2,1,0:T(8,128)(2,1)S(1)}, bf16[1,704,1024]{2,1,0:T(8,128)(2,1)}, u32[]{:S(2)}) copy-start(bf16[1,704,1024]{2,1,0:T(8,128)(2,1)} %param.11) | copy-start | bytes 4325380
  0.6 5.8 %copy-start.7 = (bf16[64,1024]{1,0:T(8,128)(2,1)S(1)}, bf16[64,1024]{1,0:T(8,128)(2,1)}, u32[]{:S(2)}) copy-start(bf16[64,1024]{1,0:T(8,128)(2,1)} %param.7) | copy-start | bytes 393220
  8.4 54.0 %all-to-all-start = ((bf16[16,32,2048]{2,1,0:T(8,128)(2,1)}), bf16[16,32,2048]{2,1,0:T(8,128)(2,1)S(1)}, u32[]{:S(2)}, u32[]{:S(2)}) async-start(bf16[16,32,2048]{2,1,0:T(8,128)(2,1)} %bitcast.2), calls=%async_computation | async-start | bytes 4194304 | tf_op jit(solution)/shard_map/all_to_all | solution.py:45
  15.0 50.5 %collective-permute-start = (bf16[512,1408]{1,0:T(8,128)(2,1)}, bf16[512,1408]{1,0:T(8,128)(2,1)}, u32[]{:S(2)}, u32[]{:S(2)}) collective-permute-start(bf16[512,1408]{1,0:T(8,128)(2,1)} %bitcast.55), channel_id=1, source_target_pairs={{0,16},{16,0},{1,17},{17,1},{2,18},{18,2},{3,19},{19,3},{4,20},{20... | collective-permute-start | bytes 4325384 | tf_op jit(solution)/shard_map/ppermute | solution.py:12
  62.4 6.6 %copy-start.2 = (bf16[16,32,2048]{2,1,0:T(8,128)(2,1)}, bf16[16,32,2048]{2,1,0:T(8,128)(2,1)S(1)}, u32[]{:S(2)}) copy-start(bf16[16,32,2048]{2,1,0:T(8,128)(2,1)S(1)} %all-to-all-done) | copy-start | bytes 6291460
  62.4 2.1 %copy-start.3 = (bf16[1,512,1408]{2,1,0:T(8,128)(2,1)S(1)}, bf16[1,512,1408]{2,1,0:T(8,128)(2,1)}, u32[]{:S(2)}) copy-start(bf16[1,512,1408]{2,1,0:T(8,128)(2,1)} %param.10) | copy-start | bytes 4325380
  70.5 1.3 copy-start.5
  70.5 1.3 copy-start.6
  74.2 1.4 %copy-start.1 = (bf16[512,2048]{1,0:T(8,128)(2,1)}, bf16[512,2048]{1,0:T(8,128)(2,1)S(1)}, u32[]{:S(2)}) copy-start(bf16[512,2048]{1,0:T(8,128)(2,1)S(1)} %fusion.6) | copy-start | bytes 6291460
  75.6 52.3 %all-to-all-start.1 = ((bf16[16,32,2048]{2,1,0:T(8,128)(2,1)}), bf16[16,32,2048]{2,1,0:T(8,128)(2,1)S(1)}, u32[]{:S(2)}, u32[]{:S(2)}) async-start(bf16[16,32,2048]{2,1,0:T(8,128)(2,1)} %bitcast.51), calls=%async_computation.1 | async-start | bytes 4194304 | tf_op jit(solution)/shard_map/all_to_all | solution.py:87
  84.0 1.5 %copy-start.8 = (bf16[64,1024]{1,0:T(8,128)(2,1)S(1)}, bf16[64,1024]{1,0:T(8,128)(2,1)}, u32[]{:S(2)}) copy-start(bf16[64,1024]{1,0:T(8,128)(2,1)} %param.7) | copy-start | bytes 393220
  84.2 32.9 %collective-permute-start.1 = (bf16[512,1408]{1,0:T(8,128)(2,1)S(1)}, bf16[512,1408]{1,0:T(8,128)(2,1)S(1)}, u32[]{:S(2)}, u32[]{:S(2)}) collective-permute-start(bf16[512,1408]{1,0:T(8,128)(2,1)S(1)} %dynamic-slice_convert_fusion), channel_id=1, source_target_pairs={{0,16},{16,0},{1,17},{17,1},{2,18},{18,2},{3,19},{19,3},{4,20},{20... | collective-permute-start | bytes 4325384 | tf_op jit(solution)/shard_map/ppermute | solution.py:116
  127.9 1.0 copy-start.4
  127.9 1.0 copy-start.9

commit v7 on v6

--- a/solution.py
+++ b/solution.py
@@ -36,12 +36,12 @@
     chosen = target_rows.reshape(token_count, top_count)[None, :, :] == slots[:, None, None]
     pick = jnp.any(chosen, axis=2).astype(jnp.bfloat16)
     slot_prob = jnp.sum(jnp.where(chosen, gate_probs[None, :, :], 0.0), axis=(1, 2))
-    token_send = jnp.dot(pick, tokens, preferred_element_type=jnp.float32).astype(jnp.bfloat16)
-    cot_pick = jnp.dot(pick, cotangent, preferred_element_type=jnp.float32)
-    cot_send = (slot_prob[:, None] * cot_pick).astype(jnp.bfloat16)
-    both_send = jnp.zeros((experts * capacity, 2 * model_width), jnp.bfloat16)
-    both_send = lax.dynamic_update_slice_in_dim(both_send, token_send, 0, axis=1)
-    both_send = lax.dynamic_update_slice_in_dim(both_send, cot_send, model_width, axis=1)
+    picked = jnp.dot(
+        pick, jnp.concatenate([tokens, cotangent], axis=1), preferred_element_type=jnp.float32
+    )
+    columns = lax.broadcasted_iota(jnp.int32, picked.shape, 1)
+    scale = jnp.where(columns < model_width, 1.0, slot_prob[:, None])
+    both_send = (picked * scale).astype(jnp.bfloat16)
     both_recv = lax.all_to_all(
         both_send.reshape(experts, capacity, 2 * model_width),
         "expert",

time: 130 us -> 130 us (level)
  other arithmetic: 7.37 us -> 5.89 us
    dynamic_update_slice x1 -> x0, other arithmetic: 1.49 us -> none  [local(): lax.dynamic_update_slice_in_dim(both_send, cot_send, model_width, axis=1)]
    dot_general x2 -> x1, matrix products: 1.87 us -> 3.03 us  [local(): jnp.dot(pick, jnp.concatenate([tokens, cotangent], axis=1), preferred_ele...]
    unnamed x21 -> x19, local copies, waits for them, and re-layouts: 4.32 us -> 4.29 us
where the time goes in v7:
time: 130 us
  waiting for transfers between devices  86.5 us (67%)
  matrix products  16.9 us (13%)
  starting transfers between devices  14 us (11%)
  other arithmetic  5.89 us (5%)
  local copies, waits for them, and re-layouts  5.48 us (4%)
    all_to_all x1, waiting for transfers between devices, local(): lax.all_to_all(both_send.reshape(experts, capacity, 2 * model_width), 'ex...  46.2 us
    ppermute x1, waiting for transfers between devices, local(): lax.ppermute(grad_block((me_dp + shift) % replicas).astype(jnp.bfloat16),...  30.8 us
    all_to_all x1, waiting for transfers between devices, local(): lax.all_to_all(send_back.reshape(experts, capacity, 2 * model_width), 'ex...  9.44 us
    all_to_all x1, starting transfers between devices, local(): lax.all_to_all(both_send.reshape(experts, capacity, 2 * model_width), 'ex...  6.55 us
    all_to_all x1, starting transfers between devices, local(): lax.all_to_all(send_back.reshape(experts, capacity, 2 * model_width), 'ex...  4.91 us
    unnamed x19, local copies, waits for them, and re-layouts  4.29 us
    dot_general x1, matrix products, local(): lax.dot_general(input_rows, pair_cot, (((0,), (0,)), ((), ())), preferred...  3.54 us
    dot_general x2, matrix products, local(): lax.dot_general(pair_cot, weight, (((1,), (1,)), ((), ())), preferred_ele...  3.4 us
  transfers between devices with their start and end apart: 4, of which 3 were waited for; matrix products, arithmetic and copies ran while one was open for 5% of the time, Pallas kernels for 0%

profile of v7, /device:TPU:11, one launch (start us, length us, event | category | flops | bytes accessed | tf_op | source)
XLA Modules:
  0.0 129.6 jit_solution(18097086380595420839)
XLA Ops:
  0.6 0.0 copy-start
  0.7 0.9 copy.32
  1.5 0.1 eq.74
  1.7 0.1 eq.70
  1.8 0.9 reduce-window.6
  2.7 0.2 slice_reduce_fusion.1
  3.0 0.1 fusion.23
  3.1 0.1 reduce_sum.48
  3.2 0.1 copy.35
  3.3 0.7 multiply_add_fusion
  4.0 0.2 fusion.8
  4.2 0.9 select_reduce_fusion
  5.0 3.0 %multiply_convert_fusion = bf16[512,2048]{1,0:T(8,128)(2,1)} fusion(pred[512,64]{0,1:T(8,128)(4,1)S(1)} %fusion.8, f32[512]{0:T(512)S(1)} %select_reduce_fusion, pred[2048]{0:T(1024)(128)(4,1)S(1)} %iota_compare_fusion.4, bf16[64,1024]{1,0:T(8,128)(2,1)} %param.7, bf16[64,1024]{1,0:T(8,128)(2,1)} %param.6), kind=kOutput, calls=%fused_computation | convolution fusion | flops 137887744 | bytes 2396160 | tf_op jit(solution)/shard_map/dot_general | solution.py:39
  8.1 6.6 %all-to-all-start = ((bf16[16,32,2048]{2,1,0:T(8,128)(2,1)}), bf16[16,32,2048]{2,1,0:T(8,128)(2,1)S(1)}, u32[]{:S(2)}, u32[]{:S(2)}) async-start(bf16[16,32,2048]{2,1,0:T(8,128)(2,1)} %bitcast.52), calls=%async_computation | async-start | bytes 4194304 | tf_op jit(solution)/shard_map/all_to_all | solution.py:45
  14.6 1.2 collective-permute-start
  15.9 46.2 %all-to-all-done = bf16[16,32,2048]{2,1,0:T(8,128)(2,1)S(1)} async-done(((bf16[16,32,2048]{2,1,0:T(8,128)(2,1)}), bf16[16,32,2048]{2,1,0:T(8,128)(2,1)S(1)}, u32[]{:S(2)}, u32[]{:S(2)}) %all-to-all-start) | async-done | bytes 2097184 | tf_op jit(solution)/shard_map/all_to_all | solution.py:45
  62.0 0.0 copy-start.2
  62.0 0.0 copy-start.3
  62.0 0.1 slice.33
  62.1 2.0 %copy-done.3 = bf16[1,512,1408]{2,1,0:T(8,128)(2,1)S(1)} copy-done((bf16[1,512,1408]{2,1,0:T(8,128)(2,1)S(1)}, bf16[1,512,1408]{2,1,0:T(8,128)(2,1)}, u32[]{:S(2)}) %copy-start.3) | copy-done | bytes 1441816
  64.2 1.0 fusion.13
  65.1 0.0 collective-permute-done
  65.1 2.4 %convolution_add_fusion = f32[512,1408]{1,0:T(8,128)S(1)} fusion(f32[512,1408]{1,0:T(8,128)S(1)} %fusion.13, bf16[512,1408]{1,0:T(8,128)(2,1)} %collective-permute-done, bf16[512,1024]{1,0:T(8,128)(2,1)S(1)} %slice.33, s32[]{:T(128)S(6)} %select_n.39), kind=kOutput, calls=%fused_computation.1 | convolution fusion | flops 738918400 | bytes 7733252 | tf_op jit(solution)/shard_map/dot_general | solution.py:62
  67.5 0.0 copy-done
  67.5 1.1 convolution_convert_fusion
  68.6 0.0 copy-done.2
  68.6 1.5 %multiply_convert_fusion.2 = (bf16[512,704]{1,0:T(8,128)(2,1)S(1)}, bf16[512,704]{1,0:T(8,128)(2,1)S(1)}) fusion(f32[512,1408]{1,0:T(8,128)S(1)} %convolution_add_fusion, bf16[1,704,1024]{2,1,0:T(8,128)(2,1)S(1)} %copy-done, bf16[512,2048]{1,0:T(8,128)(2,1)S(1)} %bitcast.50), kind=kOutput, calls=%fused_computation.8 | convolution fusion | flops 742883328 | bytes 7077888 | tf_op jit(solution)/shard_map/dot_general | solution.py:72
  70.1 0.0 copy-start.5
  70.1 0.0 copy-start.6
  70.2 0.2 dynamic_update_slice.9
  70.4 1.0 fusion.5
  71.4 0.0 copy-done.5
  71.4 0.0 copy-done.6
  71.5 2.4 %fusion.6 = bf16[512,2048]{1,0:T(8,128)(2,1)S(1)} fusion(bf16[512,2048]{1,0:T(8,128)(2,1)S(1)} %fusion.5, s32[]{:T(128)S(6)} %select_n.41, bf16[512,1408]{1,0:T(8,128)(2,1)} %collective-permute-done, bf16[512,704]{1,0:T(8,128)(2,1)S(1)} %get-tuple-element.8, bf16[512,704]{1,0:T(8,128)(2,1)S(1)} %get-tuple-element.7), kind=kOutput, calls=%fused_computation.21 | convolution fusion | flops 741343232 | bytes 3538948 | tf_op jit(solution)/shard_map/dot_general | solution.py:81
  73.8 0.0 copy-start.1
  73.9 1.3 %copy-done.1 = bf16[512,2048]{1,0:T(8,128)(2,1)} copy-done((bf16[512,2048]{1,0:T(8,128)(2,1)}, bf16[512,2048]{1,0:T(8,128)(2,1)S(1)}, u32[]{:S(2)}) %copy-start.1) | copy-done | bytes 2097176
  75.2 4.9 %all-to-all-start.1 = ((bf16[16,32,2048]{2,1,0:T(8,128)(2,1)}), bf16[16,32,2048]{2,1,0:T(8,128)(2,1)S(1)}, u32[]{:S(2)}, u32[]{:S(2)}) async-start(bf16[16,32,2048]{2,1,0:T(8,128)(2,1)} %bitcast.48), calls=%async_computation.1 | async-start | bytes 4194304 | tf_op jit(solution)/shard_map/all_to_all | solution.py:87
  80.1 3.5 %fusion.16 = f32[1024,1408]{1,0:T(8,128)S(1)} fusion(bf16[512,704]{1,0:T(8,128)(2,1)} %copy-done.6, bf16[512,704]{1,0:T(8,128)(2,1)} %copy-done.5, bf16[512,2048]{1,0:T(8,128)(2,1)} %bitcast.51), kind=kOutput, calls=%fused_computation.33 | convolution fusion | flops 1479278592 | bytes 8388608 | tf_op jit(solution)/shard_map/dot_general | solution.py:107
  83.7 0.0 copy-start.7
  83.7 0.2 dynamic-slice_convert_fusion
  83.8 1.3 %collective-permute-start.1 = (bf16[512,1408]{1,0:T(8,128)(2,1)S(1)}, bf16[512,1408]{1,0:T(8,128)(2,1)S(1)}, u32[]{:S(2)}, u32[]{:S(2)}) collective-permute-start(bf16[512,1408]{1,0:T(8,128)(2,1)S(1)} %dynamic-slice_convert_fusion), channel_id=1, source_target_pairs={{0,16},{16,0},{1,17},{17,1},{2,18},{18,2},{3,19},{19,3},{4,20},{20... | collective-permute-start | bytes 4325384 | tf_op jit(solution)/shard_map/ppermute | solution.py:116
  85.1 0.0 copy-done.7
  85.1 0.7 convert_element_type.53
  85.9 30.8 %collective-permute-done.1 = bf16[512,1408]{1,0:T(8,128)(2,1)S(1)} collective-permute-done((bf16[512,1408]{1,0:T(8,128)(2,1)S(1)}, bf16[512,1408]{1,0:T(8,128)(2,1)S(1)}, u32[]{:S(2)}, u32[]{:S(2)}) %collective-permute-start.1) | collective-permute-done | bytes 1441824 | tf_op jit(solution)/shard_map/ppermute | solution.py:116
  116.7 1.4 %fusion.1 = bf16[1,512,1408]{2,1,0:T(8,128)(2,1)} fusion(bf16[512,1408]{1,0:T(8,128)(2,1)S(1)} %collective-permute-done.1, f32[1024,1408]{1,0:T(8,128)S(1)} %fusion.16, s32[]{:T(128)S(6)} %select_n.37), kind=kLoop, calls=%fused_computation.13 | loop fusion | flops 2162688 | bytes 5767172 | tf_op jit(solution)/shard_map/broadcast_in_dim | solution.py:122
  118.1 9.4 %all-to-all-done.1 = bf16[16,32,2048]{2,1,0:T(8,128)(2,1)S(1)} async-done(((bf16[16,32,2048]{2,1,0:T(8,128)(2,1)}), bf16[16,32,2048]{2,1,0:T(8,128)(2,1)S(1)}, u32[]{:S(2)}, u32[]{:S(2)}) %all-to-all-start.1) | async-done | bytes 2097184 | tf_op jit(solution)/shard_map/all_to_all | solution.py:87
  127.5 0.0 copy-start.4
  127.5 0.0 copy-start.8
  127.5 1.0 fusion.10
  128.6 0.0 copy-done.4
  128.6 0.0 copy-done.8
  128.6 1.0 multiply_reduce_fusion
  (3 shorter events, 0.0 us)
Async XLA Ops:
  0.6 66.9 %copy-start = (bf16[1,704,1024]{2,1,0:T(8,128)(2,1)S(1)}, bf16[1,704,1024]{2,1,0:T(8,128)(2,1)}, u32[]{:S(2)}) copy-start(bf16[1,704,1024]{2,1,0:T(8,128)(2,1)} %param.11) | copy-start | bytes 4325380
  8.1 54.0 %all-to-all-start = ((bf16[16,32,2048]{2,1,0:T(8,128)(2,1)}), bf16[16,32,2048]{2,1,0:T(8,128)(2,1)S(1)}, u32[]{:S(2)}, u32[]{:S(2)}) async-start(bf16[16,32,2048]{2,1,0:T(8,128)(2,1)} %bitcast.52), calls=%async_computation | async-start | bytes 4194304 | tf_op jit(solution)/shard_map/all_to_all | solution.py:45
  14.6 50.5 %collective-permute-start = (bf16[512,1408]{1,0:T(8,128)(2,1)}, bf16[512,1408]{1,0:T(8,128)(2,1)}, u32[]{:S(2)}, u32[]{:S(2)}) collective-permute-start(bf16[512,1408]{1,0:T(8,128)(2,1)} %bitcast.53), channel_id=1, source_target_pairs={{0,16},{16,0},{1,17},{17,1},{2,18},{18,2},{3,19},{19,3},{4,20},{20... | collective-permute-start | bytes 4325384 | tf_op jit(solution)/shard_map/ppermute | solution.py:12
  62.0 6.6 %copy-start.2 = (bf16[16,32,2048]{2,1,0:T(8,128)(2,1)}, bf16[16,32,2048]{2,1,0:T(8,128)(2,1)S(1)}, u32[]{:S(2)}) copy-start(bf16[16,32,2048]{2,1,0:T(8,128)(2,1)S(1)} %all-to-all-done) | copy-start | bytes 6291460
  62.0 2.1 %copy-start.3 = (bf16[1,512,1408]{2,1,0:T(8,128)(2,1)S(1)}, bf16[1,512,1408]{2,1,0:T(8,128)(2,1)}, u32[]{:S(2)}) copy-start(bf16[1,512,1408]{2,1,0:T(8,128)(2,1)} %param.10) | copy-start | bytes 4325380
  70.1 1.3 %copy-start.5 = (bf16[512,704]{1,0:T(8,128)(2,1)}, bf16[512,704]{1,0:T(8,128)(2,1)S(1)}, u32[]{:S(2)}) copy-start(bf16[512,704]{1,0:T(8,128)(2,1)S(1)} %get-tuple-element.7) | copy-start | bytes 2162692
  70.1 1.3 %copy-start.6 = (bf16[512,704]{1,0:T(8,128)(2,1)}, bf16[512,704]{1,0:T(8,128)(2,1)S(1)}, u32[]{:S(2)}) copy-start(bf16[512,704]{1,0:T(8,128)(2,1)S(1)} %get-tuple-element.8) | copy-start | bytes 2162692
  73.8 1.4 %copy-start.1 = (bf16[512,2048]{1,0:T(8,128)(2,1)}, bf16[512,2048]{1,0:T(8,128)(2,1)S(1)}, u32[]{:S(2)}) copy-start(bf16[512,2048]{1,0:T(8,128)(2,1)S(1)} %fusion.6) | copy-start | bytes 6291460
  75.2 52.3 %all-to-all-start.1 = ((bf16[16,32,2048]{2,1,0:T(8,128)(2,1)}), bf16[16,32,2048]{2,1,0:T(8,128)(2,1)S(1)}, u32[]{:S(2)}, u32[]{:S(2)}) async-start(bf16[16,32,2048]{2,1,0:T(8,128)(2,1)} %bitcast.48), calls=%async_computation.1 | async-start | bytes 4194304 | tf_op jit(solution)/shard_map/all_to_all | solution.py:87
  83.7 1.5 %copy-start.7 = (bf16[64,1024]{1,0:T(8,128)(2,1)S(1)}, bf16[64,1024]{1,0:T(8,128)(2,1)}, u32[]{:S(2)}) copy-start(bf16[64,1024]{1,0:T(8,128)(2,1)} %param.7) | copy-start | bytes 393220
  83.8 32.9 %collective-permute-start.1 = (bf16[512,1408]{1,0:T(8,128)(2,1)S(1)}, bf16[512,1408]{1,0:T(8,128)(2,1)S(1)}, u32[]{:S(2)}, u32[]{:S(2)}) collective-permute-start(bf16[512,1408]{1,0:T(8,128)(2,1)S(1)} %dynamic-slice_convert_fusion), channel_id=1, source_target_pairs={{0,16},{16,0},{1,17},{17,1},{2,18},{18,2},{3,19},{19,3},{4,20},{20... | collective-permute-start | bytes 4325384 | tf_op jit(solution)/shard_map/ppermute | solution.py:116
  127.5 1.0 copy-start.4
  127.5 1.0 copy-start.8

commit v8 on v7

--- a/solution.py
+++ b/solution.py
@@ -25,6 +25,13 @@
     block_rows = w_gate_up.shape[1]
     capacity = 4 * token_count * top_count // (3 * experts)
     weight_blocks = gather_rows(w_gate_up[0], "dp", block_rows)
+    ordered = []
+    for block in range(replicas):
+        chosen_block = weight_blocks[0][1]
+        for index, weight in weight_blocks[1:]:
+            chosen_block = jnp.where(index == block, weight, chosen_block)
+        ordered.append(chosen_block)
+    weight_fwd = jnp.concatenate(ordered, axis=0)
     flat_routes = expert_ids.reshape(token_count * top_count)
     onehot = (flat_routes[:, None] == jnp.arange(experts, dtype=jnp.int32)[None, :]).astype(
         jnp.int32
@@ -54,13 +61,7 @@
     weight_down = w_down[0]
 
 
-    def cols(block):
-        return lax.dynamic_slice_in_dim(input_rows, block * block_rows, block_rows, axis=1)
-
-    gate_up = None
-    for block, weight in weight_blocks:
-        part = jnp.dot(cols(block), weight, preferred_element_type=jnp.float32)
-        gate_up = part if gate_up is None else gate_up + part
+    gate_up = jnp.dot(input_rows, weight_fwd, preferred_element_type=jnp.float32)
     gate = gate_up[:, :hidden_units]
     upper = gate_up[:, hidden_units:]
     sigma = jax.nn.sigmoid(gate)
@@ -77,13 +78,12 @@
     pair_cot = jnp.concatenate([gate_cot, upper_cot], axis=1).astype(jnp.bfloat16)
     send_back = jnp.zeros((experts * capacity, 2 * model_width), jnp.bfloat16)
     send_back = lax.dynamic_update_slice_in_dim(send_back, output_rows, 0, axis=1)
-    for block, weight in weight_blocks:
-        part = lax.dot_general(
-            pair_cot, weight, (((1,), (1,)), ((), ())), preferred_element_type=jnp.float32
-        ).astype(jnp.bfloat16)
-        send_back = lax.dynamic_update_slice_in_dim(
-            send_back, part, model_width + block * block_rows, axis=1
-        )
+    input_cot = lax.dot_general(
+        pair_cot, weight_fwd, (((1,), (1,)), ((), ())), preferred_element_type=jnp.float32
+    ).astype(jnp.bfloat16)
+    send_back = lax.dynamic_update_slice_in_dim(
+        send_back, input_cot, model_width + jnp.minimum(me_dp, 0), axis=1
+    )
     back = lax.all_to_all(
         send_back.reshape(
             experts, capacity, 2 * model_width

time: 130 us -> 141 us (1.085)
  local copies, waits for them, and re-layouts: 5.48 us -> 19.1 us
  waiting for transfers between devices: 86.5 us -> 76.2 us
  other arithmetic: 5.89 us -> 12.6 us
    all_to_all x1, waiting for transfers between devices: 46.2 us -> 10.7 us  [local(): lax.all_to_all(both_send.reshape(experts, capacity, 2 * model_width), 'ex...]
    ppermute x1, waiting for transfers between devices: 0.01 us -> 31.9 us  [gather_rows(): lax.ppermute(own, axis_name, [(i, (i + shift) % count) for i in range(cou...]
    dynamic_update_slice x0 -> x1, local copies, waits for them, and re-layouts: none -> 11.9 us  [local(): lax.dynamic_update_slice_in_dim(send_back, input_cot, model_width + jnp.m...]
    all_to_all x1, waiting for transfers between devices: 9.44 us -> 3.42 us  [local(): lax.all_to_all(send_back.reshape(experts, capacity, 2 * model_width), 'ex...]
    select_n x0 -> x1, other arithmetic: none -> 3.62 us  [local(): chosen_block = jnp.where(index == block, weight, chosen_block)]
    broadcast_in_dim x1, other arithmetic: 1.36 us -> 3.6 us  [local(): grad_rows.astype(jnp.bfloat16)[None]]
    unnamed x19 -> x21, local copies, waits for them, and re-layouts: 4.29 us -> 4.96 us
    dot_general x4 -> x2, matrix products: 6.76 us -> 7.13 us  [the longest x1 4.34 us: local(): jnp.dot(input_rows, weight_fwd, preferred_element_type=jnp.float32)]
  transfers between devices with their start and end apart: 4 -> 4, of which waited for: 3 -> 4; matrix products, arithmetic and copies ran while one was open for 5% -> 10% of each run, Pallas kernels for 0% -> 0%
where the time goes in v8:
time: 141 us; the launch traced here: 140 us
  waiting for transfers between devices  76.2 us (54%)
  local copies, waits for them, and re-layouts  19.1 us (14%)
  matrix products  17.3 us (12%)
  starting transfers between devices  13.9 us (10%)
  other arithmetic  12.6 us (9%)
    ppermute x1, waiting for transfers between devices, gather_rows(): lax.ppermute(own, axis_name, [(i, (i + shift) % count) for i in range(cou...  31.9 us
    ppermute x1, waiting for transfers between devices, local(): lax.ppermute(grad_block((me_dp + shift) % replicas).astype(jnp.bfloat16),...  30.2 us
    dynamic_update_slice x1, local copies, waits for them, and re-layouts, local(): lax.dynamic_update_slice_in_dim(send_back, input_cot, model_width + jnp.m...  11.9 us
    all_to_all x1, waiting for transfers between devices, local(): lax.all_to_all(both_send.reshape(experts, capacity, 2 * model_width), 'ex...  10.7 us
    all_to_all x1, starting transfers between devices, local(): lax.all_to_all(both_send.reshape(experts, capacity, 2 * model_width), 'ex...  6.55 us
    unnamed x21, local copies, waits for them, and re-layouts  4.96 us
    all_to_all x1, starting transfers between devices, local(): lax.all_to_all(send_back.reshape(experts, capacity, 2 * model_width), 'ex...  4.91 us
    dot_general x1, matrix products, local(): jnp.dot(input_rows, weight_fwd, preferred_element_type=jnp.float32)  4.34 us
  transfers between devices with their start and end apart: 4, of which 4 were waited for; matrix products, arithmetic and copies ran while one was open for 10% of the time, Pallas kernels for 0%

profile of v8, /device:TPU:11, one launch (start us, length us, event | category | flops | bytes accessed | tf_op | source)
XLA Modules:
  0.0 140.1 jit_solution(5207109704128031605)
XLA Ops:
  0.6 0.0 copy-start
  0.7 0.9 copy.32
  1.5 0.1 eq.80
  1.7 0.1 eq.76
  1.8 0.9 reduce-window.6
  2.7 0.2 slice_reduce_fusion.1
  3.0 0.1 fusion.23
  3.1 0.1 reduce_sum.48
  3.2 0.1 copy.35
  3.3 0.7 multiply_add_fusion
  4.0 0.2 fusion.12
  4.2 0.9 select_reduce_fusion
  5.0 3.1 %multiply_convert_fusion = bf16[512,2048]{1,0:T(8,128)(2,1)} fusion(pred[512,64]{0,1:T(8,128)(4,1)S(1)} %fusion.12, f32[512]{0:T(512)S(1)} %select_reduce_fusion, pred[2048]{0:T(1024)(128)(4,1)S(1)} %iota_compare_fusion.4, bf16[64,1024]{1,0:T(8,128)(2,1)} %param.7, bf16[64,1024]{1,0:T(8,128)(2,1)} %param.6), kind=kOutput, calls=%fused_computation | convolution fusion | flops 137887744 | bytes 2396160 | tf_op jit(solution)/shard_map/dot_general | solution.py:46
  8.1 6.6 %all-to-all-start = ((bf16[16,32,2048]{2,1,0:T(8,128)(2,1)}), bf16[16,32,2048]{2,1,0:T(8,128)(2,1)S(1)}, u32[]{:S(2)}, u32[]{:S(2)}) async-start(bf16[16,32,2048]{2,1,0:T(8,128)(2,1)} %bitcast.48), calls=%async_computation | async-start | bytes 4194304 | tf_op jit(solution)/shard_map/all_to_all | solution.py:52
  14.7 1.2 collective-permute-start
  15.9 31.9 %collective-permute-done = bf16[512,1408]{1,0:T(8,128)(2,1)} collective-permute-done((bf16[512,1408]{1,0:T(8,128)(2,1)}, bf16[512,1408]{1,0:T(8,128)(2,1)}, u32[]{:S(2)}, u32[]{:S(2)}) %collective-permute-start) | collective-permute-done | bytes 1441824 | tf_op jit(solution)/shard_map/ppermute | solution.py:12
  47.8 3.6 %broadcast_select_fusion.1 = (bf16[512,1408]{1,0:T(8,128)(2,1)}, bf16[512,1408]{1,0:T(8,128)(2,1)}) fusion(bf16[512,1408]{1,0:T(8,128)(2,1)} %collective-permute-done, pred[]{:T(512)S(6)} %eq.91, bf16[1,512,1408]{2,1,0:T(8,128)(2,1)} %param.10, pred[]{:T(512)S(6)} %eq.92), kind=kLoop, calls=%fused_computation.22 | loop fusion | flops 1441792 | bytes 5767170 | tf_op jit(solution)/shard_map/jit(_where)/select_n | solution.py:32
  51.4 10.7 %all-to-all-done = bf16[16,32,2048]{2,1,0:T(8,128)(2,1)S(1)} async-done(((bf16[16,32,2048]{2,1,0:T(8,128)(2,1)}), bf16[16,32,2048]{2,1,0:T(8,128)(2,1)S(1)}, u32[]{:S(2)}, u32[]{:S(2)}) %all-to-all-start) | async-done | bytes 2097184 | tf_op jit(solution)/shard_map/all_to_all | solution.py:52
  62.1 0.0 copy-start.3
  62.1 4.3 %fusion.1 = f32[512,1408]{1,0:T(8,128)S(1)} fusion(bf16[512,1408]{1,0:T(8,128)(2,1)} %get-tuple-element.10, bf16[512,1408]{1,0:T(8,128)(2,1)} %get-tuple-element.9, bf16[512,2048]{1,0:T(8,128)(2,1)S(1)} %bitcast.45), kind=kOutput, calls=%fused_computation.5 | convolution fusion | flops 1482162176 | bytes 6815744 | tf_op jit(solution)/shard_map/dot_general | solution.py:64
  66.4 0.0 copy-done
  66.4 1.1 convolution_convert_fusion
  67.5 0.0 copy-done.3
  67.5 0.0 copy-start.4
  67.5 0.0 copy-start.5
  67.6 1.5 %multiply_convert_fusion.2 = (bf16[512,704]{1,0:T(8,128)(2,1)S(1)}, bf16[512,704]{1,0:T(8,128)(2,1)S(1)}) fusion(f32[512,1408]{1,0:T(8,128)S(1)} %fusion.1, bf16[1,704,1024]{2,1,0:T(8,128)(2,1)S(1)} %copy-done, bf16[512,2048]{1,0:T(8,128)(2,1)S(1)} %bitcast.46), kind=kOutput, calls=%fused_computation.10 | convolution fusion | flops 742883328 | bytes 7077888 | tf_op jit(solution)/shard_map/dot_general | solution.py:73
  69.1 0.0 copy-start.7
  69.1 0.0 copy-start.8
  69.1 0.0 copy-done.4
  69.1 0.2 copy-done.5
  69.3 2.8 %fusion.3 = bf16[512,1024]{1,0:T(8,128)(2,1)} fusion(bf16[512,1408]{1,0:T(8,128)(2,1)S(1)} %copy-done.5, bf16[512,1408]{1,0:T(8,128)(2,1)S(1)} %copy-done.4, bf16[512,704]{1,0:T(8,128)(2,1)S(1)} %get-tuple-element.8, bf16[512,704]{1,0:T(8,128)(2,1)S(1)} %get-tuple-element.7), kind=kOutput, calls=%fused_computation.15 | convolution fusion | flops 1485570048 | bytes 5373952 | tf_op jit(solution)/shard_map/dot_general | solution.py:81
  72.1 0.0 copy-done.7
  72.1 0.0 copy-done.8
  72.1 0.2 dynamic_update_slice.6
  72.4 11.9 %dynamic_update_slice.7 = bf16[512,2048]{1,0:T(8,128)(2,1)S(1)} dynamic-update-slice(bf16[512,2048]{1,0:T(8,128)(2,1)S(1)} %dynamic_update_slice.6, bf16[512,1024]{1,0:T(8,128)(2,1)} %fusion.3, s32[]{:T(128)} %constant.37.clone.1, s32[]{:T(128)S(6)} %select_n.49) | dynamic-update-slice | bytes 2097156 | tf_op jit(solution)/shard_map/dynamic_update_slice | solution.py:84
  84.3 0.0 copy-start.2
  84.3 1.3 copy-done.2
  85.6 4.9 %all-to-all-start.1 = ((bf16[16,32,2048]{2,1,0:T(8,128)(2,1)}), bf16[16,32,2048]{2,1,0:T(8,128)(2,1)S(1)}, u32[]{:S(2)}, u32[]{:S(2)}) async-start(bf16[16,32,2048]{2,1,0:T(8,128)(2,1)} %bitcast.44), calls=%async_computation.1 | async-start | bytes 4194304 | tf_op jit(solution)/shard_map/all_to_all | solution.py:87
  90.6 3.5 %fusion.9 = f32[1024,1408]{1,0:T(8,128)S(1)} fusion(bf16[512,2048]{1,0:T(8,128)(2,1)} %bitcast.47, bf16[512,704]{1,0:T(8,128)(2,1)} %copy-done.8, bf16[512,704]{1,0:T(8,128)(2,1)} %copy-done.7), kind=kOutput, calls=%fused_computation.24 | convolution fusion | flops 1479278592 | bytes 8388608 | tf_op jit(solution)/shard_map/dot_general | solution.py:107
  94.1 0.0 copy-start.1
  94.1 2.5 %copy-done.1 = f32[1024,1408]{1,0:T(8,128)} copy-done((f32[1024,1408]{1,0:T(8,128)}, f32[1024,1408]{1,0:T(8,128)S(1)}, u32[]{:S(2)}) %copy-start.1) | copy-done | bytes 5767192
  96.6 1.2 dynamic-slice_convert_fusion
  97.8 1.2 collective-permute-start.1
  99.1 1.6 %convert_element_type.49 = f32[64,1024]{1,0:T(8,128)} convert(bf16[64,1024]{1,0:T(8,128)(2,1)} %param.7) | non-fusion elementwise | flops 65536 | bytes 393216 | tf_op jit(solution)/shard_map/convert_element_type | solution.py:106
  100.7 30.2 %collective-permute-done.1 = bf16[512,1408]{1,0:T(8,128)(2,1)} collective-permute-done((bf16[512,1408]{1,0:T(8,128)(2,1)}, bf16[512,1408]{1,0:T(8,128)(2,1)}, u32[]{:S(2)}, u32[]{:S(2)}) %collective-permute-start.1) | collective-permute-done | bytes 1441824 | tf_op jit(solution)/shard_map/ppermute | solution.py:116
  131.0 3.6 %fusion.4 = bf16[1,512,1408]{2,1,0:T(8,128)(2,1)} fusion(bf16[512,1408]{1,0:T(8,128)(2,1)} %collective-permute-done.1, f32[1024,1408]{1,0:T(8,128)} %copy-done.1, s32[]{:T(128)S(6)} %select_n.50), kind=kLoop, calls=%fused_computation.16 | loop fusion | flops 2162688 | bytes 5767172 | tf_op jit(solution)/shard_map/broadcast_in_dim | solution.py:122
  134.6 3.4 %all-to-all-done.1 = bf16[16,32,2048]{2,1,0:T(8,128)(2,1)S(1)} async-done(((bf16[16,32,2048]{2,1,0:T(8,128)(2,1)}), bf16[16,32,2048]{2,1,0:T(8,128)(2,1)S(1)}, u32[]{:S(2)}, u32[]{:S(2)}) %all-to-all-start.1) | async-done | bytes 2097184 | tf_op jit(solution)/shard_map/all_to_all | solution.py:87
  138.0 0.0 copy-start.6
  138.0 0.0 copy-start.9
  138.0 1.0 fusion.14
  139.0 0.0 copy-done.6
  139.0 0.0 copy-done.9
  139.0 1.0 multiply_reduce_fusion
  (3 shorter events, 0.0 us)
Async XLA Ops:
  0.6 65.8 %copy-start = (bf16[1,704,1024]{2,1,0:T(8,128)(2,1)S(1)}, bf16[1,704,1024]{2,1,0:T(8,128)(2,1)}, u32[]{:S(2)}) copy-start(bf16[1,704,1024]{2,1,0:T(8,128)(2,1)} %param.11) | copy-start | bytes 4325380
  8.1 54.0 %all-to-all-start = ((bf16[16,32,2048]{2,1,0:T(8,128)(2,1)}), bf16[16,32,2048]{2,1,0:T(8,128)(2,1)S(1)}, u32[]{:S(2)}, u32[]{:S(2)}) async-start(bf16[16,32,2048]{2,1,0:T(8,128)(2,1)} %bitcast.48), calls=%async_computation | async-start | bytes 4194304 | tf_op jit(solution)/shard_map/all_to_all | solution.py:52
  14.7 33.1 %collective-permute-start = (bf16[512,1408]{1,0:T(8,128)(2,1)}, bf16[512,1408]{1,0:T(8,128)(2,1)}, u32[]{:S(2)}, u32[]{:S(2)}) collective-permute-start(bf16[512,1408]{1,0:T(8,128)(2,1)} %bitcast.49), channel_id=1, source_target_pairs={{0,16},{16,0},{1,17},{17,1},{2,18},{18,2},{3,19},{19,3},{4,20},{20... | collective-permute-start | bytes 4325384 | tf_op jit(solution)/shard_map/ppermute | solution.py:12
  62.1 5.4 %copy-start.3 = (bf16[16,32,2048]{2,1,0:T(8,128)(2,1)}, bf16[16,32,2048]{2,1,0:T(8,128)(2,1)S(1)}, u32[]{:S(2)}) copy-start(bf16[16,32,2048]{2,1,0:T(8,128)(2,1)S(1)} %all-to-all-done) | copy-start | bytes 6291460
  67.5 1.5 %copy-start.4 = (bf16[512,1408]{1,0:T(8,128)(2,1)S(1)}, bf16[512,1408]{1,0:T(8,128)(2,1)}, u32[]{:S(2)}) copy-start(bf16[512,1408]{1,0:T(8,128)(2,1)} %get-tuple-element.9) | copy-start | bytes 4325380
  67.5 1.8 %copy-start.5 = (bf16[512,1408]{1,0:T(8,128)(2,1)S(1)}, bf16[512,1408]{1,0:T(8,128)(2,1)}, u32[]{:S(2)}) copy-start(bf16[512,1408]{1,0:T(8,128)(2,1)} %get-tuple-element.10) | copy-start | bytes 4325380
  69.1 3.1 %copy-start.7 = (bf16[512,704]{1,0:T(8,128)(2,1)}, bf16[512,704]{1,0:T(8,128)(2,1)S(1)}, u32[]{:S(2)}) copy-start(bf16[512,704]{1,0:T(8,128)(2,1)S(1)} %get-tuple-element.7) | copy-start | bytes 2162692
  69.1 3.1 %copy-start.8 = (bf16[512,704]{1,0:T(8,128)(2,1)}, bf16[512,704]{1,0:T(8,128)(2,1)S(1)}, u32[]{:S(2)}) copy-start(bf16[512,704]{1,0:T(8,128)(2,1)S(1)} %get-tuple-element.8) | copy-start | bytes 2162692
  84.3 1.3 copy-start.2
  85.6 52.3 %all-to-all-start.1 = ((bf16[16,32,2048]{2,1,0:T(8,128)(2,1)}), bf16[16,32,2048]{2,1,0:T(8,128)(2,1)S(1)}, u32[]{:S(2)}, u32[]{:S(2)}) async-start(bf16[16,32,2048]{2,1,0:T(8,128)(2,1)} %bitcast.44), calls=%async_computation.1 | async-start | bytes 4194304 | tf_op jit(solution)/shard_map/all_to_all | solution.py:87
  94.1 2.5 %copy-start.1 = (f32[1024,1408]{1,0:T(8,128)}, f32[1024,1408]{1,0:T(8,128)S(1)}, u32[]{:S(2)}) copy-start(f32[1024,1408]{1,0:T(8,128)S(1)} %fusion.9) | copy-start | bytes 17301508
  97.8 33.1 %collective-permute-start.1 = (bf16[512,1408]{1,0:T(8,128)(2,1)}, bf16[512,1408]{1,0:T(8,128)(2,1)}, u32[]{:S(2)}, u32[]{:S(2)}) collective-permute-start(bf16[512,1408]{1,0:T(8,128)(2,1)} %dynamic-slice_convert_fusion), channel_id=1, source_target_pairs={{0,16},{16,0},{1,17},{17,1},{2,18},{18,2},{3,19},{19,3},{4,20},{20... | collective-permute-start | bytes 4325384 | tf_op jit(solution)/shard_map/ppermute | solution.py:116
  138.0 1.0 copy-start.6
  138.0 1.0 copy-start.9

commit v9 on v7

--- a/solution.py
+++ b/solution.py
@@ -25,6 +25,13 @@
     block_rows = w_gate_up.shape[1]
     capacity = 4 * token_count * top_count // (3 * experts)
     weight_blocks = gather_rows(w_gate_up[0], "dp", block_rows)
+    ordered = []
+    for block in range(replicas):
+        chosen_block = weight_blocks[0][1]
+        for index, weight in weight_blocks[1:]:
+            chosen_block = jnp.where(index == block, weight, chosen_block)
+        ordered.append(chosen_block)
+    weight_fwd = lax.optimization_barrier(jnp.concatenate(ordered, axis=0))
     flat_routes = expert_ids.reshape(token_count * top_count)
     onehot = (flat_routes[:, None] == jnp.arange(experts, dtype=jnp.int32)[None, :]).astype(
         jnp.int32
@@ -54,13 +61,7 @@
     weight_down = w_down[0]
 
 
-    def cols(block):
-        return lax.dynamic_slice_in_dim(input_rows, block * block_rows, block_rows, axis=1)
-
-    gate_up = None
-    for block, weight in weight_blocks:
-        part = jnp.dot(cols(block), weight, preferred_element_type=jnp.float32)
-        gate_up = part if gate_up is None else gate_up + part
+    gate_up = jnp.dot(input_rows, weight_fwd, preferred_element_type=jnp.float32)
     gate = gate_up[:, :hidden_units]
     upper = gate_up[:, hidden_units:]
     sigma = jax.nn.sigmoid(gate)

time: 130 us -> 131 us (level)
  waiting for transfers between devices: 86.5 us -> 76 us
  other arithmetic: 5.89 us -> 12.9 us
  local copies, waits for them, and re-layouts: 5.48 us -> 8.56 us
    all_to_all x1, waiting for transfers between devices: 46.2 us -> 10.4 us  [local(): lax.all_to_all(both_send.reshape(experts, capacity, 2 * model_width), 'ex...]
    ppermute x1, waiting for transfers between devices: 0.01 us -> 31.9 us  [gather_rows(): lax.ppermute(own, axis_name, [(i, (i + shift) % count) for i in range(cou...]
    all_to_all x1, waiting for transfers between devices: 9.44 us -> 3.43 us  [local(): lax.all_to_all(send_back.reshape(experts, capacity, 2 * model_width), 'ex...]
    broadcast_in_dim x1, other arithmetic: 1.36 us -> 3.6 us  [local(): grad_rows.astype(jnp.bfloat16)[None]]
    unnamed x19, local copies, waits for them, and re-layouts: 4.29 us -> 6.38 us
    select_n x0 -> x1, other arithmetic: none -> 2.05 us  [local(): chosen_block = jnp.where(index == block, weight, chosen_block)]
    concatenate x0 -> x1, other arithmetic: none -> 1.79 us  [local(): weight_fwd = lax.optimization_barrier(jnp.concatenate(ordered, axis=0))]
    dot_general x2 -> x1, matrix products: 3.35 us -> 4.36 us  [local(): jnp.dot(input_rows, weight_fwd, preferred_element_type=jnp.float32)]
  transfers between devices with their start and end apart: 4 -> 4, of which waited for: 3 -> 4; matrix products, arithmetic and copies ran while one was open for 5% -> 11% of each run, Pallas kernels for 0% -> 0%
where the time goes in v9:
time: 131 us; the launch traced here: 130 us
  waiting for transfers between devices  76 us (58%)
  matrix products  18 us (14%)
  starting transfers between devices  13.9 us (11%)
  other arithmetic  12.9 us (10%)
  local copies, waits for them, and re-layouts  8.56 us (7%)
    ppermute x1, waiting for transfers between devices, gather_rows(): lax.ppermute(own, axis_name, [(i, (i + shift) % count) for i in range(cou...  31.9 us
    ppermute x1, waiting for transfers between devices, local(): lax.ppermute(grad_block((me_dp + shift) % replicas).astype(jnp.bfloat16),...  30.2 us
    all_to_all x1, waiting for transfers between devices, local(): lax.all_to_all(both_send.reshape(experts, capacity, 2 * model_width), 'ex...  10.4 us
    all_to_all x1, starting transfers between devices, local(): lax.all_to_all(both_send.reshape(experts, capacity, 2 * model_width), 'ex...  6.55 us
    unnamed x19, local copies, waits for them, and re-layouts  6.38 us
    all_to_all x1, starting transfers between devices, local(): lax.all_to_all(send_back.reshape(experts, capacity, 2 * model_width), 'ex...  4.9 us
    dot_general x1, matrix products, local(): jnp.dot(input_rows, weight_fwd, preferred_element_type=jnp.float32)  4.36 us
    broadcast_in_dim x1, other arithmetic, local(): grad_rows.astype(jnp.bfloat16)[None]  3.6 us
  transfers between devices with their start and end apart: 4, of which 4 were waited for; matrix products, arithmetic and copies ran while one was open for 11% of the time, Pallas kernels for 0%

profile of v9, /device:TPU:11, one launch (start us, length us, event | category | flops | bytes accessed | tf_op | source)
XLA Modules:
  0.0 130.1 jit_solution(6627130104462389281)
XLA Ops:
  0.6 0.0 copy-start
  0.7 0.9 copy.32
  1.5 0.1 eq.80
  1.7 0.1 eq.76
  1.8 0.9 reduce-window.6
  2.7 0.2 slice_reduce_fusion.1
  3.0 0.1 fusion.23
  3.1 0.1 reduce_sum.48
  3.2 0.1 copy.35
  3.3 0.7 multiply_add_fusion
  4.0 0.2 fusion.12
  4.2 0.9 select_reduce_fusion
  5.0 3.1 %multiply_convert_fusion = bf16[512,2048]{1,0:T(8,128)(2,1)} fusion(pred[512,64]{0,1:T(8,128)(4,1)S(1)} %fusion.12, f32[512]{0:T(512)S(1)} %select_reduce_fusion, pred[2048]{0:T(1024)(128)(4,1)S(1)} %iota_compare_fusion.4, bf16[64,1024]{1,0:T(8,128)(2,1)} %param.7, bf16[64,1024]{1,0:T(8,128)(2,1)} %param.6), kind=kOutput, calls=%fused_computation | convolution fusion | flops 137887744 | bytes 2396160 | tf_op jit(solution)/shard_map/dot_general | solution.py:46
  8.1 6.6 %all-to-all-start = ((bf16[16,32,2048]{2,1,0:T(8,128)(2,1)}), bf16[16,32,2048]{2,1,0:T(8,128)(2,1)S(1)}, u32[]{:S(2)}, u32[]{:S(2)}) async-start(bf16[16,32,2048]{2,1,0:T(8,128)(2,1)} %bitcast.52), calls=%async_computation | async-start | bytes 4194304 | tf_op jit(solution)/shard_map/all_to_all | solution.py:52
  14.7 1.2 collective-permute-start
  15.9 31.9 %collective-permute-done = bf16[512,1408]{1,0:T(8,128)(2,1)} collective-permute-done((bf16[512,1408]{1,0:T(8,128)(2,1)}, bf16[512,1408]{1,0:T(8,128)(2,1)}, u32[]{:S(2)}, u32[]{:S(2)}) %collective-permute-start) | collective-permute-done | bytes 1441824 | tf_op jit(solution)/shard_map/ppermute | solution.py:12
  47.8 2.1 %broadcast_select_fusion.1 = (bf16[512,1408]{1,0:T(8,128)(2,1)S(1)}, bf16[512,1408]{1,0:T(8,128)(2,1)S(1)}) fusion(bf16[512,1408]{1,0:T(8,128)(2,1)} %collective-permute-done, pred[]{:T(512)S(6)} %eq.91, bf16[1,512,1408]{2,1,0:T(8,128)(2,1)} %param.10, pred[]{:T(512)S(6)} %eq.92), kind=kLoop, calls=%fused_computation.19 | loop fusion | flops 1441792 | bytes 5767170 | tf_op jit(solution)/shard_map/jit(_where)/select_n | solution.py:32
  49.8 1.8 %pad_maximum_fusion = bf16[1024,1408]{1,0:T(8,128)(2,1)} fusion(bf16[512,1408]{1,0:T(8,128)(2,1)S(1)} %get-tuple-element.10, bf16[512,1408]{1,0:T(8,128)(2,1)S(1)} %get-tuple-element.9), kind=kLoop, calls=%fused_computation.1 | loop fusion | flops 5767168 | bytes 5767168 | tf_op jit(solution)/shard_map/concatenate | solution.py:34
  51.6 10.4 %all-to-all-done = bf16[16,32,2048]{2,1,0:T(8,128)(2,1)S(1)} async-done(((bf16[16,32,2048]{2,1,0:T(8,128)(2,1)}), bf16[16,32,2048]{2,1,0:T(8,128)(2,1)S(1)}, u32[]{:S(2)}, u32[]{:S(2)}) %all-to-all-start) | async-done | bytes 2097184 | tf_op jit(solution)/shard_map/all_to_all | solution.py:52
  62.1 0.0 copy-start.3
  62.1 4.4 %fusion.10 = f32[512,1408]{1,0:T(8,128)S(1)} fusion(bf16[1024,1408]{1,0:T(8,128)(2,1)} %pad_maximum_fusion, bf16[512,2048]{1,0:T(8,128)(2,1)S(1)} %bitcast.49), kind=kOutput, calls=%fused_computation.27 | convolution fusion | flops 1476395008 | bytes 6815744 | tf_op jit(solution)/shard_map/dot_general | solution.py:64
  66.4 0.0 copy-done
  66.5 1.1 convolution_convert_fusion
  67.5 0.0 copy-done.3
  67.6 1.5 %multiply_convert_fusion.2 = (bf16[512,704]{1,0:T(8,128)(2,1)S(1)}, bf16[512,704]{1,0:T(8,128)(2,1)S(1)}) fusion(f32[512,1408]{1,0:T(8,128)S(1)} %fusion.10, bf16[1,704,1024]{2,1,0:T(8,128)(2,1)S(1)} %copy-done, bf16[512,2048]{1,0:T(8,128)(2,1)S(1)} %bitcast.50), kind=kOutput, calls=%fused_computation.8 | convolution fusion | flops 742883328 | bytes 7077888 | tf_op jit(solution)/shard_map/dot_general | solution.py:73
  69.0 0.0 copy-start.6
  69.1 0.0 copy-start.7
  69.1 0.0 copy-start.4
  69.1 0.2 dynamic_update_slice.9
  69.3 1.7 %copy-done.4 = bf16[1,512,1408]{2,1,0:T(8,128)(2,1)S(1)} copy-done((bf16[1,512,1408]{2,1,0:T(8,128)(2,1)S(1)}, bf16[1,512,1408]{2,1,0:T(8,128)(2,1)}, u32[]{:S(2)}) %copy-start.4) | copy-done | bytes 1441816
  71.0 1.0 fusion.5
  72.0 0.0 copy-done.6
  72.0 0.0 copy-done.7
  72.0 2.4 %fusion.6 = bf16[512,2048]{1,0:T(8,128)(2,1)S(1)} fusion(bf16[512,2048]{1,0:T(8,128)(2,1)S(1)} %fusion.5, s32[]{:T(128)S(6)} %select_n.53, bf16[512,1408]{1,0:T(8,128)(2,1)} %collective-permute-done, bf16[512,704]{1,0:T(8,128)(2,1)S(1)} %get-tuple-element.8, bf16[512,704]{1,0:T(8,128)(2,1)S(1)} %get-tuple-element.7), kind=kOutput, calls=%fused_computation.23 | convolution fusion | flops 741343232 | bytes 3538948 | tf_op jit(solution)/shard_map/dot_general | solution.py:82
  74.4 0.0 copy-start.2
  74.4 1.3 %copy-done.2 = bf16[512,2048]{1,0:T(8,128)(2,1)} copy-done((bf16[512,2048]{1,0:T(8,128)(2,1)}, bf16[512,2048]{1,0:T(8,128)(2,1)S(1)}, u32[]{:S(2)}) %copy-start.2) | copy-done | bytes 2097176
  75.7 4.9 %all-to-all-start.1 = ((bf16[16,32,2048]{2,1,0:T(8,128)(2,1)}), bf16[16,32,2048]{2,1,0:T(8,128)(2,1)S(1)}, u32[]{:S(2)}, u32[]{:S(2)}) async-start(bf16[16,32,2048]{2,1,0:T(8,128)(2,1)} %bitcast.48), calls=%async_computation.1 | async-start | bytes 4194304 | tf_op jit(solution)/shard_map/all_to_all | solution.py:88
  80.6 3.5 %fusion.8 = f32[1024,1408]{1,0:T(8,128)S(1)} fusion(bf16[512,2048]{1,0:T(8,128)(2,1)} %bitcast.51, bf16[512,704]{1,0:T(8,128)(2,1)} %copy-done.7, bf16[512,704]{1,0:T(8,128)(2,1)} %copy-done.6), kind=kOutput, calls=%fused_computation.25 | convolution fusion | flops 1479278592 | bytes 8388608 | tf_op jit(solution)/shard_map/dot_general | solution.py:108
  84.2 0.0 copy-start.1
  84.2 2.5 %copy-done.1 = f32[1024,1408]{1,0:T(8,128)} copy-done((f32[1024,1408]{1,0:T(8,128)}, f32[1024,1408]{1,0:T(8,128)S(1)}, u32[]{:S(2)}) %copy-start.1) | copy-done | bytes 5767192
  86.7 1.2 dynamic-slice_convert_fusion
  87.9 1.2 collective-permute-start.1
  89.2 1.6 %convert_element_type.53 = f32[64,1024]{1,0:T(8,128)} convert(bf16[64,1024]{1,0:T(8,128)(2,1)} %param.7) | non-fusion elementwise | flops 65536 | bytes 393216 | tf_op jit(solution)/shard_map/convert_element_type | solution.py:107
  90.8 30.2 %collective-permute-done.1 = bf16[512,1408]{1,0:T(8,128)(2,1)} collective-permute-done((bf16[512,1408]{1,0:T(8,128)(2,1)}, bf16[512,1408]{1,0:T(8,128)(2,1)}, u32[]{:S(2)}, u32[]{:S(2)}) %collective-permute-start.1) | collective-permute-done | bytes 1441824 | tf_op jit(solution)/shard_map/ppermute | solution.py:117
  121.0 3.6 %fusion.1 = bf16[1,512,1408]{2,1,0:T(8,128)(2,1)} fusion(bf16[512,1408]{1,0:T(8,128)(2,1)} %collective-permute-done.1, f32[1024,1408]{1,0:T(8,128)} %copy-done.1, s32[]{:T(128)S(6)} %select_n.54), kind=kLoop, calls=%fused_computation.13 | loop fusion | flops 2162688 | bytes 5767172 | tf_op jit(solution)/shard_map/broadcast_in_dim | solution.py:123
  124.6 3.4 %all-to-all-done.1 = bf16[16,32,2048]{2,1,0:T(8,128)(2,1)S(1)} async-done(((bf16[16,32,2048]{2,1,0:T(8,128)(2,1)}), bf16[16,32,2048]{2,1,0:T(8,128)(2,1)S(1)}, u32[]{:S(2)}, u32[]{:S(2)}) %all-to-all-start.1) | async-done | bytes 2097184 | tf_op jit(solution)/shard_map/all_to_all | solution.py:88
  128.1 0.0 copy-start.5
  128.1 0.0 copy-start.8
  128.1 1.0 fusion.14
  129.1 0.0 copy-done.5
  129.1 0.0 copy-done.8
  129.1 1.0 multiply_reduce_fusion
  (3 shorter events, 0.0 us)
Async XLA Ops:
  0.6 65.8 %copy-start = (bf16[1,704,1024]{2,1,0:T(8,128)(2,1)S(1)}, bf16[1,704,1024]{2,1,0:T(8,128)(2,1)}, u32[]{:S(2)}) copy-start(bf16[1,704,1024]{2,1,0:T(8,128)(2,1)} %param.11) | copy-start | bytes 4325380
  8.1 54.0 %all-to-all-start = ((bf16[16,32,2048]{2,1,0:T(8,128)(2,1)}), bf16[16,32,2048]{2,1,0:T(8,128)(2,1)S(1)}, u32[]{:S(2)}, u32[]{:S(2)}) async-start(bf16[16,32,2048]{2,1,0:T(8,128)(2,1)} %bitcast.52), calls=%async_computation | async-start | bytes 4194304 | tf_op jit(solution)/shard_map/all_to_all | solution.py:52
  14.7 33.1 %collective-permute-start = (bf16[512,1408]{1,0:T(8,128)(2,1)}, bf16[512,1408]{1,0:T(8,128)(2,1)}, u32[]{:S(2)}, u32[]{:S(2)}) collective-permute-start(bf16[512,1408]{1,0:T(8,128)(2,1)} %bitcast.53), channel_id=1, source_target_pairs={{0,16},{16,0},{1,17},{17,1},{2,18},{18,2},{3,19},{19,3},{4,20},{20... | collective-permute-start | bytes 4325384 | tf_op jit(solution)/shard_map/ppermute | solution.py:12
  62.1 5.5 %copy-start.3 = (bf16[16,32,2048]{2,1,0:T(8,128)(2,1)}, bf16[16,32,2048]{2,1,0:T(8,128)(2,1)S(1)}, u32[]{:S(2)}) copy-start(bf16[16,32,2048]{2,1,0:T(8,128)(2,1)S(1)} %all-to-all-done) | copy-start | bytes 6291460
  69.0 3.0 %copy-start.6 = (bf16[512,704]{1,0:T(8,128)(2,1)}, bf16[512,704]{1,0:T(8,128)(2,1)S(1)}, u32[]{:S(2)}) copy-start(bf16[512,704]{1,0:T(8,128)(2,1)S(1)} %get-tuple-element.7) | copy-start | bytes 2162692
  69.1 3.0 %copy-start.7 = (bf16[512,704]{1,0:T(8,128)(2,1)}, bf16[512,704]{1,0:T(8,128)(2,1)S(1)}, u32[]{:S(2)}) copy-start(bf16[512,704]{1,0:T(8,128)(2,1)S(1)} %get-tuple-element.8) | copy-start | bytes 2162692
  69.1 1.9 %copy-start.4 = (bf16[1,512,1408]{2,1,0:T(8,128)(2,1)S(1)}, bf16[1,512,1408]{2,1,0:T(8,128)(2,1)}, u32[]{:S(2)}) copy-start(bf16[1,512,1408]{2,1,0:T(8,128)(2,1)} %param.10) | copy-start | bytes 4325380
  74.4 1.3 %copy-start.2 = (bf16[512,2048]{1,0:T(8,128)(2,1)}, bf16[512,2048]{1,0:T(8,128)(2,1)S(1)}, u32[]{:S(2)}) copy-start(bf16[512,2048]{1,0:T(8,128)(2,1)S(1)} %fusion.6) | copy-start | bytes 6291460
  75.7 52.3 %all-to-all-start.1 = ((bf16[16,32,2048]{2,1,0:T(8,128)(2,1)}), bf16[16,32,2048]{2,1,0:T(8,128)(2,1)S(1)}, u32[]{:S(2)}, u32[]{:S(2)}) async-start(bf16[16,32,2048]{2,1,0:T(8,128)(2,1)} %bitcast.48), calls=%async_computation.1 | async-start | bytes 4194304 | tf_op jit(solution)/shard_map/all_to_all | solution.py:88
  84.2 2.5 %copy-start.1 = (f32[1024,1408]{1,0:T(8,128)}, f32[1024,1408]{1,0:T(8,128)S(1)}, u32[]{:S(2)}) copy-start(f32[1024,1408]{1,0:T(8,128)S(1)} %fusion.8) | copy-start | bytes 17301508
  87.9 33.1 %collective-permute-start.1 = (bf16[512,1408]{1,0:T(8,128)(2,1)}, bf16[512,1408]{1,0:T(8,128)(2,1)}, u32[]{:S(2)}, u32[]{:S(2)}) collective-permute-start(bf16[512,1408]{1,0:T(8,128)(2,1)} %dynamic-slice_convert_fusion), channel_id=1, source_target_pairs={{0,16},{16,0},{1,17},{17,1},{2,18},{18,2},{3,19},{19,3},{4,20},{20... | collective-permute-start | bytes 4325384 | tf_op jit(solution)/shard_map/ppermute | solution.py:117
  128.1 1.0 copy-start.5
  128.1 1.0 copy-start.8

commit v10 on v7

--- a/solution.py
+++ b/solution.py
@@ -25,17 +25,26 @@
     block_rows = w_gate_up.shape[1]
     capacity = 4 * token_count * top_count // (3 * experts)
     weight_blocks = gather_rows(w_gate_up[0], "dp", block_rows)
-    flat_routes = expert_ids.reshape(token_count * top_count)
-    onehot = (flat_routes[:, None] == jnp.arange(experts, dtype=jnp.int32)[None, :]).astype(
-        jnp.int32
+    hit = expert_ids[:, :, None] == jnp.arange(experts, dtype=jnp.int32)[None, None, :]
+    token_hit = jnp.any(hit, axis=1)
+    token_prob = jnp.sum(jnp.where(hit, gate_probs[:, :, None], 0.0), axis=1)
+    earlier = (
+        lax.broadcasted_iota(jnp.int32, (token_count, token_count), 0)
+        > lax.broadcasted_iota(jnp.int32, (token_count, token_count), 1)
+    ).astype(jnp.bfloat16)
+    rank = jnp.dot(
+        earlier, token_hit.astype(jnp.bfloat16), preferred_element_type=jnp.float32
+    ).astype(jnp.int32)
+    slot_rank = jnp.sum(jnp.where(hit, rank[:, None, :], 0), axis=2)
+    target_rows = expert_ids * capacity + slot_rank
+    slots = jnp.arange(experts * capacity, dtype=jnp.int32)
+    chosen = token_hit.T[:, None, :] & (
+        rank.T[:, None, :] == jnp.arange(capacity, dtype=jnp.int32)[None, :, None]
     )
-    before = jnp.cumsum(onehot, axis=0) - onehot
-    slot_rank = jnp.sum(before * onehot, axis=1)
-    target_rows = flat_routes * capacity + slot_rank
-    slots = jnp.arange(experts * capacity, dtype=jnp.int32)
-    chosen = target_rows.reshape(token_count, top_count)[None, :, :] == slots[:, None, None]
-    pick = jnp.any(chosen, axis=2).astype(jnp.bfloat16)
-    slot_prob = jnp.sum(jnp.where(chosen, gate_probs[None, :, :], 0.0), axis=(1, 2))
+    pick = chosen.reshape(experts * capacity, token_count).astype(jnp.bfloat16)
+    slot_prob = jnp.sum(jnp.where(chosen, token_prob.T[:, None, :], 0.0), axis=2).reshape(
+        experts * capacity
+    )
     picked = jnp.dot(
         pick, jnp.concatenate([tokens, cotangent], axis=1), preferred_element_type=jnp.float32
     )

time: 130 us -> 128 us (0.985)
  local copies, waits for them, and re-layouts: 5.48 us -> 4.06 us
    unnamed x19 -> x20, local copies, waits for them, and re-layouts: 4.29 us -> 3.41 us
where the time goes in v10:
time: 128 us; the launch traced here: 127 us
  waiting for transfers between devices  86.4 us (68%)
  matrix products  17 us (13%)
  starting transfers between devices  14 us (11%)
  other arithmetic  4.98 us (4%)
  local copies, waits for them, and re-layouts  4.06 us (3%)
    all_to_all x1, waiting for transfers between devices, local(): lax.all_to_all(both_send.reshape(experts, capacity, 2 * model_width), 'ex...  46.2 us
    ppermute x1, waiting for transfers between devices, local(): lax.ppermute(grad_block((me_dp + shift) % replicas).astype(jnp.bfloat16),...  30.8 us
    all_to_all x1, waiting for transfers between devices, local(): lax.all_to_all(send_back.reshape(experts, capacity, 2 * model_width), 'ex...  9.44 us
    all_to_all x1, starting transfers between devices, local(): lax.all_to_all(both_send.reshape(experts, capacity, 2 * model_width), 'ex...  6.55 us
    all_to_all x1, starting transfers between devices, local(): lax.all_to_all(send_back.reshape(experts, capacity, 2 * model_width), 'ex...  4.91 us
    dot_general x1, matrix products, local(): lax.dot_general(input_rows, pair_cot, (((0,), (0,)), ((), ())), preferred...  3.54 us
    unnamed x20, local copies, waits for them, and re-layouts  3.41 us
    dot_general x2, matrix products, local(): lax.dot_general(pair_cot, weight, (((1,), (1,)), ((), ())), preferred_ele...  3.41 us
  transfers between devices with their start and end apart: 4, of which 3 were waited for; matrix products, arithmetic and copies ran while one was open for 5% of the time, Pallas kernels for 0%

profile of v10, /device:TPU:11, one launch (start us, length us, event | category | flops | bytes accessed | tf_op | source)
XLA Modules:
  0.0 127.3 jit_solution(16304736334885462569)
XLA Ops:
  0.6 0.0 copy-start
  0.7 0.8 fusion.22
  1.5 0.1 convolution_convert_fusion.3
  1.6 0.7 select_reduce_fusion.1
  2.3 0.1 select_reduce_fusion
  2.5 0.1 broadcast_in_dim.72
  2.6 0.1 eq.79
  2.6 0.1 fusion.20
  2.8 3.0 %multiply_convert_fusion = bf16[512,2048]{1,0:T(8,128)(2,1)} fusion(pred[512,64]{1,0:T(32,128)(4,1)S(1)} %fusion.20, f32[512]{0:T(512)S(1)} %broadcast_in_dim.72, pred[2048]{0:T(1024)(128)(4,1)S(1)} %iota_compare_fusion.5, bf16[64,1024]{1,0:T(8,128)(2,1)} %param.7, bf16[64,1024]{1,0:T(8,128)(2,1)} %param.6), kind=kOutput, calls=%fused_computation | convolution fusion | flops 137887744 | bytes 2396160 | tf_op jit(solution)/shard_map/dot_general | solution.py:48
  5.8 6.6 %all-to-all-start = ((bf16[16,32,2048]{2,1,0:T(8,128)(2,1)}), bf16[16,32,2048]{2,1,0:T(8,128)(2,1)S(1)}, u32[]{:S(2)}, u32[]{:S(2)}) async-start(bf16[16,32,2048]{2,1,0:T(8,128)(2,1)} %bitcast.42), calls=%async_computation | async-start | bytes 4194304 | tf_op jit(solution)/shard_map/all_to_all | solution.py:54
  12.3 1.2 collective-permute-start
  13.6 46.2 %all-to-all-done = bf16[16,32,2048]{2,1,0:T(8,128)(2,1)S(1)} async-done(((bf16[16,32,2048]{2,1,0:T(8,128)(2,1)}), bf16[16,32,2048]{2,1,0:T(8,128)(2,1)S(1)}, u32[]{:S(2)}, u32[]{:S(2)}) %all-to-all-start) | async-done | bytes 2097184 | tf_op jit(solution)/shard_map/all_to_all | solution.py:54
  59.7 0.0 copy-start.2
  59.7 0.0 copy-start.3
  59.7 0.1 slice.24
  59.8 2.0 %copy-done.3 = bf16[1,512,1408]{2,1,0:T(8,128)(2,1)S(1)} copy-done((bf16[1,512,1408]{2,1,0:T(8,128)(2,1)S(1)}, bf16[1,512,1408]{2,1,0:T(8,128)(2,1)}, u32[]{:S(2)}) %copy-start.3) | copy-done | bytes 1441816
  61.9 1.0 fusion.12
  62.8 0.0 collective-permute-done
  62.8 2.4 %convolution_add_fusion = f32[512,1408]{1,0:T(8,128)S(1)} fusion(f32[512,1408]{1,0:T(8,128)S(1)} %fusion.12, bf16[512,1408]{1,0:T(8,128)(2,1)} %collective-permute-done, bf16[512,1024]{1,0:T(8,128)(2,1)S(1)} %slice.24, s32[]{:T(128)S(6)} %select_n.49), kind=kOutput, calls=%fused_computation.1 | convolution fusion | flops 738918400 | bytes 7733252 | tf_op jit(solution)/shard_map/dot_general | solution.py:71
  65.2 0.0 copy-done
  65.2 1.1 convolution_convert_fusion
  66.3 0.0 copy-done.2
  66.3 1.5 %multiply_convert_fusion.2 = (bf16[512,704]{1,0:T(8,128)(2,1)S(1)}, bf16[512,704]{1,0:T(8,128)(2,1)S(1)}) fusion(f32[512,1408]{1,0:T(8,128)S(1)} %convolution_add_fusion, bf16[1,704,1024]{2,1,0:T(8,128)(2,1)S(1)} %copy-done, bf16[512,2048]{1,0:T(8,128)(2,1)S(1)} %bitcast.40), kind=kOutput, calls=%fused_computation.8 | convolution fusion | flops 742883328 | bytes 7077888 | tf_op jit(solution)/shard_map/dot_general | solution.py:81
  67.8 0.0 copy-start.5
  67.8 0.0 copy-start.6
  67.9 0.2 dynamic_update_slice.9
  68.1 1.0 fusion.5
  69.1 0.0 copy-done.5
  69.1 0.0 copy-done.6
  69.1 2.4 %fusion.6 = bf16[512,2048]{1,0:T(8,128)(2,1)S(1)} fusion(bf16[512,2048]{1,0:T(8,128)(2,1)S(1)} %fusion.5, s32[]{:T(128)S(6)} %select_n.51, bf16[512,1408]{1,0:T(8,128)(2,1)} %collective-permute-done, bf16[512,704]{1,0:T(8,128)(2,1)S(1)} %get-tuple-element.8, bf16[512,704]{1,0:T(8,128)(2,1)S(1)} %get-tuple-element.7), kind=kOutput, calls=%fused_computation.21 | convolution fusion | flops 741343232 | bytes 3538948 | tf_op jit(solution)/shard_map/dot_general | solution.py:90
  71.5 0.0 copy-start.1
  71.6 1.3 %copy-done.1 = bf16[512,2048]{1,0:T(8,128)(2,1)} copy-done((bf16[512,2048]{1,0:T(8,128)(2,1)}, bf16[512,2048]{1,0:T(8,128)(2,1)S(1)}, u32[]{:S(2)}) %copy-start.1) | copy-done | bytes 2097176
  72.9 4.9 %all-to-all-start.1 = ((bf16[16,32,2048]{2,1,0:T(8,128)(2,1)}), bf16[16,32,2048]{2,1,0:T(8,128)(2,1)S(1)}, u32[]{:S(2)}, u32[]{:S(2)}) async-start(bf16[16,32,2048]{2,1,0:T(8,128)(2,1)} %bitcast.38), calls=%async_computation.1 | async-start | bytes 4194304 | tf_op jit(solution)/shard_map/all_to_all | solution.py:96
  77.8 3.5 %fusion.15 = f32[1024,1408]{1,0:T(8,128)S(1)} fusion(bf16[512,704]{1,0:T(8,128)(2,1)} %copy-done.6, bf16[512,704]{1,0:T(8,128)(2,1)} %copy-done.5, bf16[512,2048]{1,0:T(8,128)(2,1)} %bitcast.41), kind=kOutput, calls=%fused_computation.31 | convolution fusion | flops 1479278592 | bytes 8388608 | tf_op jit(solution)/shard_map/dot_general | solution.py:116
  81.4 0.0 copy-start.7
  81.4 0.0 copy-start.8
  81.4 0.2 dynamic-slice_convert_fusion
  81.5 1.3 %collective-permute-start.1 = (bf16[512,1408]{1,0:T(8,128)(2,1)S(1)}, bf16[512,1408]{1,0:T(8,128)(2,1)S(1)}, u32[]{:S(2)}, u32[]{:S(2)}) collective-permute-start(bf16[512,1408]{1,0:T(8,128)(2,1)S(1)} %dynamic-slice_convert_fusion), channel_id=1, source_target_pairs={{0,16},{16,0},{1,17},{17,1},{2,18},{18,2},{3,19},{19,3},{4,20},{20... | collective-permute-start | bytes 4325384 | tf_op jit(solution)/shard_map/ppermute | solution.py:125
  82.8 0.0 copy-done.7
  82.9 0.7 convert_element_type.55
  83.6 0.0 copy-done.8
  83.6 30.8 %collective-permute-done.1 = bf16[512,1408]{1,0:T(8,128)(2,1)S(1)} collective-permute-done((bf16[512,1408]{1,0:T(8,128)(2,1)S(1)}, bf16[512,1408]{1,0:T(8,128)(2,1)S(1)}, u32[]{:S(2)}, u32[]{:S(2)}) %collective-permute-start.1) | collective-permute-done | bytes 1441824 | tf_op jit(solution)/shard_map/ppermute | solution.py:125
  114.4 1.4 %fusion.1 = bf16[1,512,1408]{2,1,0:T(8,128)(2,1)} fusion(bf16[512,1408]{1,0:T(8,128)(2,1)S(1)} %collective-permute-done.1, f32[1024,1408]{1,0:T(8,128)S(1)} %fusion.15, s32[]{:T(128)S(6)} %select_n.47), kind=kLoop, calls=%fused_computation.13 | loop fusion | flops 2162688 | bytes 5767172 | tf_op jit(solution)/shard_map/broadcast_in_dim | solution.py:131
  115.8 9.4 %all-to-all-done.1 = bf16[16,32,2048]{2,1,0:T(8,128)(2,1)S(1)} async-done(((bf16[16,32,2048]{2,1,0:T(8,128)(2,1)}), bf16[16,32,2048]{2,1,0:T(8,128)(2,1)S(1)}, u32[]{:S(2)}, u32[]{:S(2)}) %all-to-all-start.1) | async-done | bytes 2097184 | tf_op jit(solution)/shard_map/all_to_all | solution.py:96
  125.2 0.0 copy-start.4
  125.2 0.0 copy-start.9
  125.2 1.0 fusion.9
  126.3 0.0 copy-done.4
  126.3 0.0 copy-done.9
  126.3 1.0 multiply_reduce_fusion
  (4 shorter events, 0.0 us)
Async XLA Ops:
  0.6 64.6 %copy-start = (bf16[1,704,1024]{2,1,0:T(8,128)(2,1)S(1)}, bf16[1,704,1024]{2,1,0:T(8,128)(2,1)}, u32[]{:S(2)}) copy-start(bf16[1,704,1024]{2,1,0:T(8,128)(2,1)} %param.11) | copy-start | bytes 4325380
  5.8 54.0 %all-to-all-start = ((bf16[16,32,2048]{2,1,0:T(8,128)(2,1)}), bf16[16,32,2048]{2,1,0:T(8,128)(2,1)S(1)}, u32[]{:S(2)}, u32[]{:S(2)}) async-start(bf16[16,32,2048]{2,1,0:T(8,128)(2,1)} %bitcast.42), calls=%async_computation | async-start | bytes 4194304 | tf_op jit(solution)/shard_map/all_to_all | solution.py:54
  12.3 50.5 %collective-permute-start = (bf16[512,1408]{1,0:T(8,128)(2,1)}, bf16[512,1408]{1,0:T(8,128)(2,1)}, u32[]{:S(2)}, u32[]{:S(2)}) collective-permute-start(bf16[512,1408]{1,0:T(8,128)(2,1)} %bitcast.43), channel_id=1, source_target_pairs={{0,16},{16,0},{1,17},{17,1},{2,18},{18,2},{3,19},{19,3},{4,20},{20... | collective-permute-start | bytes 4325384 | tf_op jit(solution)/shard_map/ppermute | solution.py:12
  59.7 6.6 %copy-start.2 = (bf16[16,32,2048]{2,1,0:T(8,128)(2,1)}, bf16[16,32,2048]{2,1,0:T(8,128)(2,1)S(1)}, u32[]{:S(2)}) copy-start(bf16[16,32,2048]{2,1,0:T(8,128)(2,1)S(1)} %all-to-all-done) | copy-start | bytes 6291460
  59.7 2.1 %copy-start.3 = (bf16[1,512,1408]{2,1,0:T(8,128)(2,1)S(1)}, bf16[1,512,1408]{2,1,0:T(8,128)(2,1)}, u32[]{:S(2)}) copy-start(bf16[1,512,1408]{2,1,0:T(8,128)(2,1)} %param.10) | copy-start | bytes 4325380
  67.8 1.3 %copy-start.5 = (bf16[512,704]{1,0:T(8,128)(2,1)}, bf16[512,704]{1,0:T(8,128)(2,1)S(1)}, u32[]{:S(2)}) copy-start(bf16[512,704]{1,0:T(8,128)(2,1)S(1)} %get-tuple-element.7) | copy-start | bytes 2162692
  67.8 1.3 %copy-start.6 = (bf16[512,704]{1,0:T(8,128)(2,1)}, bf16[512,704]{1,0:T(8,128)(2,1)S(1)}, u32[]{:S(2)}) copy-start(bf16[512,704]{1,0:T(8,128)(2,1)S(1)} %get-tuple-element.8) | copy-start | bytes 2162692
  71.5 1.4 %copy-start.1 = (bf16[512,2048]{1,0:T(8,128)(2,1)}, bf16[512,2048]{1,0:T(8,128)(2,1)S(1)}, u32[]{:S(2)}) copy-start(bf16[512,2048]{1,0:T(8,128)(2,1)S(1)} %fusion.6) | copy-start | bytes 6291460
  72.9 52.3 %all-to-all-start.1 = ((bf16[16,32,2048]{2,1,0:T(8,128)(2,1)}), bf16[16,32,2048]{2,1,0:T(8,128)(2,1)S(1)}, u32[]{:S(2)}, u32[]{:S(2)}) async-start(bf16[16,32,2048]{2,1,0:T(8,128)(2,1)} %bitcast.38), calls=%async_computation.1 | async-start | bytes 4194304 | tf_op jit(solution)/shard_map/all_to_all | solution.py:96
  81.4 1.5 %copy-start.7 = (bf16[64,1024]{1,0:T(8,128)(2,1)S(1)}, bf16[64,1024]{1,0:T(8,128)(2,1)}, u32[]{:S(2)}) copy-start(bf16[64,1024]{1,0:T(8,128)(2,1)} %param.7) | copy-start | bytes 393220
  81.4 2.2 %copy-start.8 = (s32[64,6]{0,1:T(8,128)S(1)}, s32[64,6]{0,1:T(8,128)}, u32[]{:S(2)}) copy-start(s32[64,6]{0,1:T(8,128)} %param.8) | copy-start | bytes 4612
  81.5 32.9 %collective-permute-start.1 = (bf16[512,1408]{1,0:T(8,128)(2,1)S(1)}, bf16[512,1408]{1,0:T(8,128)(2,1)S(1)}, u32[]{:S(2)}, u32[]{:S(2)}) collective-permute-start(bf16[512,1408]{1,0:T(8,128)(2,1)S(1)} %dynamic-slice_convert_fusion), channel_id=1, source_target_pairs={{0,16},{16,0},{1,17},{17,1},{2,18},{18,2},{3,19},{19,3},{4,20},{20... | collective-permute-start | bytes 4325384 | tf_op jit(solution)/shard_map/ppermute | solution.py:125
  125.2 1.0 copy-start.4
  125.2 1.0 copy-start.9

commit v11 on v10

--- a/solution.py
+++ b/solution.py
@@ -7,11 +7,12 @@
 def gather_rows(own, axis_name, width):
     count = lax.axis_size(axis_name)
     me = lax.axis_index(axis_name)
-    pieces = [(me, own)]
-    for shift in range(1, count):
-        moved = lax.ppermute(own, axis_name, [(i, (i + shift) % count) for i in range(count)])
-        pieces.append(((me - shift) % count, moved))
-    return pieces
+    moved = [
+        lax.ppermute(own, axis_name, [(i, (i + shift) % count) for i in range(count)])
+        for shift in range(1, count)
+    ]
+    held = lax.optimization_barrier((own, *moved))
+    return [((me - shift) % count, block) for shift, block in enumerate(held)]
 
 
 def local(tokens, cotangent, expert_ids, gate_probs, w_gate_up, w_down):

time: 128 us -> 126 us (0.984)
  waiting for transfers between devices: 86.4 us -> 79.8 us
  other arithmetic: 4.98 us -> 8.12 us
  local copies, waits for them, and re-layouts: 4.06 us -> 5.56 us
    all_to_all x1, waiting for transfers between devices: 46.2 us -> 14.3 us  [local(): lax.all_to_all(both_send.reshape(experts, capacity, 2 * model_width), 'ex...]
    ppermute x1, waiting for transfers between devices: 0.01 us -> 31.9 us  [gather_rows(): lax.ppermute(own, axis_name, [(i, (i + shift) % count) for i in range(cou...]
    all_to_all x1, waiting for transfers between devices: 9.44 us -> 3.42 us  [local(): lax.all_to_all(send_back.reshape(experts, capacity, 2 * model_width), 'ex...]
    broadcast_in_dim x1, other arithmetic: 1.36 us -> 3.6 us  [local(): grad_rows.astype(jnp.bfloat16)[None]]
  transfers between devices with their start and end apart: 4 -> 4, of which waited for: 3 -> 4; matrix products, arithmetic and copies ran while one was open for 5% -> 8% of each run, Pallas kernels for 0% -> 0%
where the time goes in v11:
time: 126 us
  waiting for transfers between devices  79.8 us (63%)
  matrix products  17.7 us (14%)
  starting transfers between devices  13.9 us (11%)
  other arithmetic  8.12 us (6%)
  local copies, waits for them, and re-layouts  5.56 us (4%)
    ppermute x1, waiting for transfers between devices, gather_rows(): lax.ppermute(own, axis_name, [(i, (i + shift) % count) for i in range(cou...  31.9 us
    ppermute x1, waiting for transfers between devices, local(): lax.ppermute(grad_block((me_dp + shift) % replicas).astype(jnp.bfloat16),...  30.2 us
    all_to_all x1, waiting for transfers between devices, local(): lax.all_to_all(both_send.reshape(experts, capacity, 2 * model_width), 'ex...  14.3 us
    all_to_all x1, starting transfers between devices, local(): lax.all_to_all(both_send.reshape(experts, capacity, 2 * model_width), 'ex...  6.55 us
    all_to_all x1, starting transfers between devices, local(): lax.all_to_all(send_back.reshape(experts, capacity, 2 * model_width), 'ex...  4.91 us
    dot_general x2, matrix products, local(): part = jnp.dot(cols(block), weight, preferred_element_type=jnp.float32)  4.05 us
    unnamed x20, local copies, waits for them, and re-layouts  3.82 us
    broadcast_in_dim x1, other arithmetic, local(): grad_rows.astype(jnp.bfloat16)[None]  3.6 us
  transfers between devices with their start and end apart: 4, of which 4 were waited for; matrix products, arithmetic and copies ran while one was open for 8% of the time, Pallas kernels for 0%

profile of v11, /device:TPU:11, one launch (start us, length us, event | category | flops | bytes accessed | tf_op | source)
XLA Modules:
  0.0 126.0 jit_solution(1195176678030903593)
XLA Ops:
  0.6 0.0 copy-start
  0.7 0.8 fusion.22
  1.5 0.1 convolution_convert_fusion.3
  1.6 0.7 select_reduce_fusion.1
  2.3 0.1 select_reduce_fusion
  2.5 0.1 broadcast_in_dim.72
  2.6 0.1 eq.80
  2.6 0.1 fusion.20
  2.8 3.0 %multiply_convert_fusion = bf16[512,2048]{1,0:T(8,128)(2,1)} fusion(pred[512,64]{1,0:T(32,128)(4,1)S(1)} %fusion.20, f32[512]{0:T(512)S(1)} %broadcast_in_dim.72, pred[2048]{0:T(1024)(128)(4,1)S(1)} %iota_compare_fusion.5, bf16[64,1024]{1,0:T(8,128)(2,1)} %param.7, bf16[64,1024]{1,0:T(8,128)(2,1)} %param.6), kind=kOutput, calls=%fused_computation | convolution fusion | flops 137887744 | bytes 2396160 | tf_op jit(solution)/shard_map/dot_general | solution.py:49
  5.8 6.6 %all-to-all-start = ((bf16[16,32,2048]{2,1,0:T(8,128)(2,1)}), bf16[16,32,2048]{2,1,0:T(8,128)(2,1)S(1)}, u32[]{:S(2)}, u32[]{:S(2)}) async-start(bf16[16,32,2048]{2,1,0:T(8,128)(2,1)} %bitcast.40), calls=%async_computation | async-start | bytes 4194304 | tf_op jit(solution)/shard_map/all_to_all | solution.py:55
  12.4 1.2 collective-permute-start
  13.6 31.9 %collective-permute-done = bf16[512,1408]{1,0:T(8,128)(2,1)} collective-permute-done((bf16[512,1408]{1,0:T(8,128)(2,1)}, bf16[512,1408]{1,0:T(8,128)(2,1)}, u32[]{:S(2)}, u32[]{:S(2)}) %collective-permute-start) | collective-permute-done | bytes 1441824 | tf_op jit(solution)/shard_map/ppermute | solution.py:11
  45.5 14.3 %all-to-all-done = bf16[16,32,2048]{2,1,0:T(8,128)(2,1)S(1)} async-done(((bf16[16,32,2048]{2,1,0:T(8,128)(2,1)}), bf16[16,32,2048]{2,1,0:T(8,128)(2,1)S(1)}, u32[]{:S(2)}, u32[]{:S(2)}) %all-to-all-start) | async-done | bytes 2097184 | tf_op jit(solution)/shard_map/all_to_all | solution.py:55
  59.8 0.0 copy-start.3
  59.8 0.1 slice.24
  59.9 0.0 copy-start.4
  59.9 3.0 %fusion.11 = f32[512,1408]{1,0:T(8,128)S(1)} fusion(bf16[512,1408]{1,0:T(8,128)(2,1)} %collective-permute-done, bf16[512,1024]{1,0:T(8,128)(2,1)S(1)} %slice.24, s32[]{:T(128)S(6)} %select_n.56), kind=kOutput, calls=%fused_computation.27 | convolution fusion | flops 738197504 | bytes 4849668 | tf_op jit(solution)/shard_map/dot_general | solution.py:72
  62.9 0.0 copy-done.4
  63.0 1.0 convolution_add_fusion
  64.0 0.0 copy-done
  64.0 1.1 convolution_convert_fusion
  65.1 0.0 copy-done.3
  65.1 1.5 %multiply_convert_fusion.2 = (bf16[512,704]{1,0:T(8,128)(2,1)S(1)}, bf16[512,704]{1,0:T(8,128)(2,1)S(1)}) fusion(f32[512,1408]{1,0:T(8,128)S(1)} %convolution_add_fusion, bf16[1,704,1024]{2,1,0:T(8,128)(2,1)S(1)} %copy-done, bf16[512,2048]{1,0:T(8,128)(2,1)S(1)} %bitcast.38), kind=kOutput, calls=%fused_computation.8 | convolution fusion | flops 742883328 | bytes 7077888 | tf_op jit(solution)/shard_map/dot_general | solution.py:82
  66.6 0.0 copy-start.6
  66.6 0.0 copy-start.7
  66.6 0.2 dynamic_update_slice.9
  66.8 1.0 fusion.5
  67.9 0.0 copy-done.6
  67.9 0.0 copy-done.7
  67.9 2.4 %fusion.6 = bf16[512,2048]{1,0:T(8,128)(2,1)S(1)} fusion(bf16[512,2048]{1,0:T(8,128)(2,1)S(1)} %fusion.5, s32[]{:T(128)S(6)} %select_n.58, bf16[512,1408]{1,0:T(8,128)(2,1)} %collective-permute-done, bf16[512,704]{1,0:T(8,128)(2,1)S(1)} %get-tuple-element.12, bf16[512,704]{1,0:T(8,128)(2,1)S(1)} %get-tuple-element.11), kind=kOutput, calls=%fused_computation.21 | convolution fusion | flops 741343232 | bytes 3538948 | tf_op jit(solution)/shard_map/dot_general | solution.py:91
  70.3 0.0 copy-start.2
  70.3 1.3 %copy-done.2 = bf16[512,2048]{1,0:T(8,128)(2,1)} copy-done((bf16[512,2048]{1,0:T(8,128)(2,1)}, bf16[512,2048]{1,0:T(8,128)(2,1)S(1)}, u32[]{:S(2)}) %copy-start.2) | copy-done | bytes 2097176
  71.6 4.9 %all-to-all-start.1 = ((bf16[16,32,2048]{2,1,0:T(8,128)(2,1)}), bf16[16,32,2048]{2,1,0:T(8,128)(2,1)S(1)}, u32[]{:S(2)}, u32[]{:S(2)}) async-start(bf16[16,32,2048]{2,1,0:T(8,128)(2,1)} %bitcast.36), calls=%async_computation.1 | async-start | bytes 4194304 | tf_op jit(solution)/shard_map/all_to_all | solution.py:97
  76.5 3.5 %fusion.15 = f32[1024,1408]{1,0:T(8,128)S(1)} fusion(bf16[512,704]{1,0:T(8,128)(2,1)} %copy-done.7, bf16[512,704]{1,0:T(8,128)(2,1)} %copy-done.6, bf16[512,2048]{1,0:T(8,128)(2,1)} %bitcast.39), kind=kOutput, calls=%fused_computation.31 | convolution fusion | flops 1479278592 | bytes 8388608 | tf_op jit(solution)/shard_map/dot_general | solution.py:117
  80.1 0.0 copy-start.1
  80.1 2.5 %copy-done.1 = f32[1024,1408]{1,0:T(8,128)} copy-done((f32[1024,1408]{1,0:T(8,128)}, f32[1024,1408]{1,0:T(8,128)S(1)}, u32[]{:S(2)}) %copy-start.1) | copy-done | bytes 5767192
  82.5 0.0 copy-start.8
  82.5 1.2 dynamic-slice_convert_fusion
  83.8 1.2 collective-permute-start.1
  85.0 1.6 %convert_element_type.55 = f32[64,1024]{1,0:T(8,128)} convert(bf16[64,1024]{1,0:T(8,128)(2,1)} %param.7) | non-fusion elementwise | flops 65536 | bytes 393216 | tf_op jit(solution)/shard_map/convert_element_type | solution.py:116
  86.7 0.0 copy-done.8
  86.7 30.2 %collective-permute-done.1 = bf16[512,1408]{1,0:T(8,128)(2,1)} collective-permute-done((bf16[512,1408]{1,0:T(8,128)(2,1)}, bf16[512,1408]{1,0:T(8,128)(2,1)}, u32[]{:S(2)}, u32[]{:S(2)}) %collective-permute-start.1) | collective-permute-done | bytes 1441824 | tf_op jit(solution)/shard_map/ppermute | solution.py:126
  116.9 3.6 %fusion.1 = bf16[1,512,1408]{2,1,0:T(8,128)(2,1)} fusion(bf16[512,1408]{1,0:T(8,128)(2,1)} %collective-permute-done.1, f32[1024,1408]{1,0:T(8,128)} %copy-done.1, s32[]{:T(128)S(6)} %select_n.59), kind=kLoop, calls=%fused_computation.13 | loop fusion | flops 2162688 | bytes 5767172 | tf_op jit(solution)/shard_map/broadcast_in_dim | solution.py:132
  120.5 3.4 %all-to-all-done.1 = bf16[16,32,2048]{2,1,0:T(8,128)(2,1)S(1)} async-done(((bf16[16,32,2048]{2,1,0:T(8,128)(2,1)}), bf16[16,32,2048]{2,1,0:T(8,128)(2,1)S(1)}, u32[]{:S(2)}, u32[]{:S(2)}) %all-to-all-start.1) | async-done | bytes 2097184 | tf_op jit(solution)/shard_map/all_to_all | solution.py:97
  123.9 0.0 copy-start.5
  123.9 0.0 copy-start.9
  123.9 1.0 fusion.9
  125.0 0.0 copy-done.5
  125.0 0.0 copy-done.9
  125.0 1.0 multiply_reduce_fusion
  (4 shorter events, 0.0 us)
Async XLA Ops:
  0.6 63.3 %copy-start = (bf16[1,704,1024]{2,1,0:T(8,128)(2,1)S(1)}, bf16[1,704,1024]{2,1,0:T(8,128)(2,1)}, u32[]{:S(2)}) copy-start(bf16[1,704,1024]{2,1,0:T(8,128)(2,1)} %param.11) | copy-start | bytes 4325380
  5.8 54.0 %all-to-all-start = ((bf16[16,32,2048]{2,1,0:T(8,128)(2,1)}), bf16[16,32,2048]{2,1,0:T(8,128)(2,1)S(1)}, u32[]{:S(2)}, u32[]{:S(2)}) async-start(bf16[16,32,2048]{2,1,0:T(8,128)(2,1)} %bitcast.40), calls=%async_computation | async-start | bytes 4194304 | tf_op jit(solution)/shard_map/all_to_all | solution.py:55
  12.4 33.1 %collective-permute-start = (bf16[512,1408]{1,0:T(8,128)(2,1)}, bf16[512,1408]{1,0:T(8,128)(2,1)}, u32[]{:S(2)}, u32[]{:S(2)}) collective-permute-start(bf16[512,1408]{1,0:T(8,128)(2,1)} %bitcast.41), channel_id=1, source_target_pairs={{0,16},{16,0},{1,17},{17,1},{2,18},{18,2},{3,19},{19,3},{4,20},{20... | collective-permute-start | bytes 4325384 | tf_op jit(solution)/shard_map/ppermute | solution.py:11
  59.8 5.3 %copy-start.3 = (bf16[16,32,2048]{2,1,0:T(8,128)(2,1)}, bf16[16,32,2048]{2,1,0:T(8,128)(2,1)S(1)}, u32[]{:S(2)}) copy-start(bf16[16,32,2048]{2,1,0:T(8,128)(2,1)S(1)} %all-to-all-done) | copy-start | bytes 6291460
  59.9 3.1 %copy-start.4 = (bf16[1,512,1408]{2,1,0:T(8,128)(2,1)S(1)}, bf16[1,512,1408]{2,1,0:T(8,128)(2,1)}, u32[]{:S(2)}) copy-start(bf16[1,512,1408]{2,1,0:T(8,128)(2,1)} %param.10) | copy-start | bytes 4325380
  66.6 1.3 %copy-start.6 = (bf16[512,704]{1,0:T(8,128)(2,1)}, bf16[512,704]{1,0:T(8,128)(2,1)S(1)}, u32[]{:S(2)}) copy-start(bf16[512,704]{1,0:T(8,128)(2,1)S(1)} %get-tuple-element.11) | copy-start | bytes 2162692
  66.6 1.3 %copy-start.7 = (bf16[512,704]{1,0:T(8,128)(2,1)}, bf16[512,704]{1,0:T(8,128)(2,1)S(1)}, u32[]{:S(2)}) copy-start(bf16[512,704]{1,0:T(8,128)(2,1)S(1)} %get-tuple-element.12) | copy-start | bytes 2162692
  70.3 1.3 %copy-start.2 = (bf16[512,2048]{1,0:T(8,128)(2,1)}, bf16[512,2048]{1,0:T(8,128)(2,1)S(1)}, u32[]{:S(2)}) copy-start(bf16[512,2048]{1,0:T(8,128)(2,1)S(1)} %fusion.6) | copy-start | bytes 6291460
  71.6 52.3 %all-to-all-start.1 = ((bf16[16,32,2048]{2,1,0:T(8,128)(2,1)}), bf16[16,32,2048]{2,1,0:T(8,128)(2,1)S(1)}, u32[]{:S(2)}, u32[]{:S(2)}) async-start(bf16[16,32,2048]{2,1,0:T(8,128)(2,1)} %bitcast.36), calls=%async_computation.1 | async-start | bytes 4194304 | tf_op jit(solution)/shard_map/all_to_all | solution.py:97
  80.1 2.5 %copy-start.1 = (f32[1024,1408]{1,0:T(8,128)}, f32[1024,1408]{1,0:T(8,128)S(1)}, u32[]{:S(2)}) copy-start(f32[1024,1408]{1,0:T(8,128)S(1)} %fusion.15) | copy-start | bytes 17301508
  82.5 4.1 %copy-start.8 = (s32[64,6]{0,1:T(8,128)S(1)}, s32[64,6]{0,1:T(8,128)}, u32[]{:S(2)}) copy-start(s32[64,6]{0,1:T(8,128)} %param.8) | copy-start | bytes 4612
  83.8 33.1 %collective-permute-start.1 = (bf16[512,1408]{1,0:T(8,128)(2,1)}, bf16[512,1408]{1,0:T(8,128)(2,1)}, u32[]{:S(2)}, u32[]{:S(2)}) collective-permute-start(bf16[512,1408]{1,0:T(8,128)(2,1)} %dynamic-slice_convert_fusion), channel_id=1, source_target_pairs={{0,16},{16,0},{1,17},{17,1},{2,18},{18,2},{3,19},{19,3},{4,20},{20... | collective-permute-start | bytes 4325384 | tf_op jit(solution)/shard_map/ppermute | solution.py:126
  123.9 1.0 copy-start.5
  123.9 1.0 copy-start.9

commit v12 on v11

--- a/solution.py
+++ b/solution.py
@@ -12,7 +12,11 @@
         for shift in range(1, count)
     ]
     held = lax.optimization_barrier((own, *moved))
-    return [((me - shift) % count, block) for shift, block in enumerate(held)]
+    keep = me >= 0
+    fresh = lax.optimization_barrier(
+        tuple(jnp.where(keep, block, jnp.zeros_like(block)) for block in held)
+    )
+    return [((me - shift) % count, block) for shift, block in enumerate(fresh)]
 
 
 def local(tokens, cotangent, expert_ids, gate_probs, w_gate_up, w_down):

time: 126 us -> 125 us (level)
  waiting for transfers between devices: 79.8 us -> 76.2 us
  other arithmetic: 8.12 us -> 11.7 us
  matrix products: 17.7 us -> 14.3 us
  local copies, waits for them, and re-layouts: 5.56 us -> 7.95 us
    all_to_all x1, waiting for transfers between devices: 14.3 us -> 10.7 us  [local(): lax.all_to_all(both_send.reshape(experts, capacity, 2 * model_width), 'ex...]
    select_n x0 -> x1, other arithmetic: none -> 3.61 us  [gather_rows(): jnp.where(keep, block, jnp.zeros_like(block))]
    unnamed x20 -> x22, local copies, waits for them, and re-layouts: 3.82 us -> 6.21 us
    dot_general x2, matrix products: 4.05 us -> 1.98 us  [local(): part = jnp.dot(cols(block), weight, preferred_element_type=jnp.float32)]
    dot_general x2, matrix products: 3.4 us -> 2.03 us  [local(): lax.dot_general(pair_cot, weight, (((1,), (1,)), ((), ())), preferred_ele...]
  transfers between devices with their start and end apart: 4 -> 4, of which waited for: 4 -> 4; matrix products, arithmetic and copies ran while one was open for 8% -> 11% of each run, Pallas kernels for 0% -> 0%
where the time goes in v12:
time: 125 us
  waiting for transfers between devices  76.2 us (61%)
  matrix products  14.3 us (11%)
  starting transfers between devices  13.9 us (11%)
  other arithmetic  11.7 us (9%)
  local copies, waits for them, and re-layouts  7.95 us (6%)
    ppermute x1, waiting for transfers between devices, gather_rows(): lax.ppermute(own, axis_name, [(i, (i + shift) % count) for i in range(cou...  31.9 us
    ppermute x1, waiting for transfers between devices, local(): lax.ppermute(grad_block((me_dp + shift) % replicas).astype(jnp.bfloat16),...  30.2 us
    all_to_all x1, waiting for transfers between devices, local(): lax.all_to_all(both_send.reshape(experts, capacity, 2 * model_width), 'ex...  10.7 us
    all_to_all x1, starting transfers between devices, local(): lax.all_to_all(both_send.reshape(experts, capacity, 2 * model_width), 'ex...  6.55 us
    unnamed x22, local copies, waits for them, and re-layouts  6.21 us
    all_to_all x1, starting transfers between devices, local(): lax.all_to_all(send_back.reshape(experts, capacity, 2 * model_width), 'ex...  4.91 us
    select_n x1, other arithmetic, gather_rows(): jnp.where(keep, block, jnp.zeros_like(block))  3.61 us
    broadcast_in_dim x1, other arithmetic, local(): grad_rows.astype(jnp.bfloat16)[None]  3.6 us
  transfers between devices with their start and end apart: 4, of which 4 were waited for; matrix products, arithmetic and copies ran while one was open for 11% of the time, Pallas kernels for 0%

profile of v12, /device:TPU:11, one launch (start us, length us, event | category | flops | bytes accessed | tf_op | source)
XLA Modules:
  0.0 124.9 jit_solution(12450406921013468744)
XLA Ops:
  0.6 0.0 copy-start
  0.7 0.8 fusion.22
  1.5 0.1 convolution_convert_fusion.3
  1.6 0.7 select_reduce_fusion.1
  2.3 0.1 select_reduce_fusion
  2.5 0.1 broadcast_in_dim.72
  2.6 0.1 eq.80
  2.6 0.1 fusion.20
  2.8 3.0 %multiply_convert_fusion = bf16[512,2048]{1,0:T(8,128)(2,1)} fusion(pred[512,64]{1,0:T(32,128)(4,1)S(1)} %fusion.20, f32[512]{0:T(512)S(1)} %broadcast_in_dim.72, pred[2048]{0:T(1024)(128)(4,1)S(1)} %iota_compare_fusion.5, bf16[64,1024]{1,0:T(8,128)(2,1)} %param.7, bf16[64,1024]{1,0:T(8,128)(2,1)} %param.6), kind=kOutput, calls=%fused_computation | convolution fusion | flops 137887744 | bytes 2396160 | tf_op jit(solution)/shard_map/dot_general | solution.py:53
  5.8 6.6 %all-to-all-start = ((bf16[16,32,2048]{2,1,0:T(8,128)(2,1)}), bf16[16,32,2048]{2,1,0:T(8,128)(2,1)S(1)}, u32[]{:S(2)}, u32[]{:S(2)}) async-start(bf16[16,32,2048]{2,1,0:T(8,128)(2,1)} %bitcast.40), calls=%async_computation | async-start | bytes 4194304 | tf_op jit(solution)/shard_map/all_to_all | solution.py:59
  12.4 1.2 collective-permute-start
  13.6 31.9 %collective-permute-done = bf16[512,1408]{1,0:T(8,128)(2,1)} collective-permute-done((bf16[512,1408]{1,0:T(8,128)(2,1)}, bf16[512,1408]{1,0:T(8,128)(2,1)}, u32[]{:S(2)}, u32[]{:S(2)}) %collective-permute-start) | collective-permute-done | bytes 1441824 | tf_op jit(solution)/shard_map/ppermute | solution.py:11
  45.5 3.6 %broadcast_select_fusion = (bf16[512,1408]{1,0:T(8,128)(2,1)}, bf16[512,1408]{1,0:T(8,128)(2,1)}) fusion(bf16[512,1408]{1,0:T(8,128)(2,1)} %collective-permute-done, pred[]{:T(512)S(6)} %ge.3, bf16[512,1408]{1,0:T(8,128)(2,1)} %bitcast.42), kind=kLoop, calls=%fused_computation.18 | loop fusion | flops 1441792 | bytes 5767169 | tf_op jit(solution)/shard_map/jit(_where)/select_n | solution.py:17
  49.1 10.7 %all-to-all-done = bf16[16,32,2048]{2,1,0:T(8,128)(2,1)S(1)} async-done(((bf16[16,32,2048]{2,1,0:T(8,128)(2,1)}), bf16[16,32,2048]{2,1,0:T(8,128)(2,1)S(1)}, u32[]{:S(2)}, u32[]{:S(2)}) %all-to-all-start) | async-done | bytes 2097184 | tf_op jit(solution)/shard_map/all_to_all | solution.py:59
  59.8 0.0 copy-start.3
  59.8 0.0 copy-start.4
  59.8 0.1 slice.24
  59.9 2.0 %copy-done.4 = bf16[512,1408]{1,0:T(8,128)(2,1)S(1)} copy-done((bf16[512,1408]{1,0:T(8,128)(2,1)S(1)}, bf16[512,1408]{1,0:T(8,128)(2,1)}, u32[]{:S(2)}) %copy-start.4) | copy-done | bytes 1441816
  61.9 0.0 copy-start.5
  61.9 1.0 fusion.12
  62.9 0.4 copy-done.5
  63.3 1.0 convolution_add_fusion
  64.3 0.0 copy-done
  64.3 1.1 convolution_convert_fusion
  65.4 0.0 copy-done.3
  65.4 1.5 %multiply_convert_fusion.2 = (bf16[512,704]{1,0:T(8,128)(2,1)S(1)}, bf16[512,704]{1,0:T(8,128)(2,1)S(1)}) fusion(f32[512,1408]{1,0:T(8,128)S(1)} %convolution_add_fusion, bf16[1,704,1024]{2,1,0:T(8,128)(2,1)S(1)} %copy-done, bf16[512,2048]{1,0:T(8,128)(2,1)S(1)} %bitcast.38), kind=kOutput, calls=%fused_computation.8 | convolution fusion | flops 742883328 | bytes 7077888 | tf_op jit(solution)/shard_map/dot_general | solution.py:86
  66.9 0.0 copy-start.7
  66.9 0.0 copy-start.8
  66.9 0.2 dynamic_update_slice.9
  67.2 1.0 fusion.5
  68.2 0.0 copy-done.7
  68.2 0.0 copy-done.8
  68.2 1.0 fusion.6
  69.2 0.0 copy-start.2
  69.2 1.3 %copy-done.2 = bf16[512,2048]{1,0:T(8,128)(2,1)} copy-done((bf16[512,2048]{1,0:T(8,128)(2,1)}, bf16[512,2048]{1,0:T(8,128)(2,1)S(1)}, u32[]{:S(2)}) %copy-start.2) | copy-done | bytes 2097176
  70.5 4.9 %all-to-all-start.1 = ((bf16[16,32,2048]{2,1,0:T(8,128)(2,1)}), bf16[16,32,2048]{2,1,0:T(8,128)(2,1)S(1)}, u32[]{:S(2)}, u32[]{:S(2)}) async-start(bf16[16,32,2048]{2,1,0:T(8,128)(2,1)} %bitcast.36), calls=%async_computation.1 | async-start | bytes 4194304 | tf_op jit(solution)/shard_map/all_to_all | solution.py:101
  75.4 3.5 %fusion.15 = f32[1024,1408]{1,0:T(8,128)S(1)} fusion(bf16[512,704]{1,0:T(8,128)(2,1)} %copy-done.8, bf16[512,704]{1,0:T(8,128)(2,1)} %copy-done.7, bf16[512,2048]{1,0:T(8,128)(2,1)} %bitcast.39), kind=kOutput, calls=%fused_computation.33 | convolution fusion | flops 1479278592 | bytes 8388608 | tf_op jit(solution)/shard_map/dot_general | solution.py:121
  79.0 0.0 copy-start.1
  79.0 2.5 %copy-done.1 = f32[1024,1408]{1,0:T(8,128)} copy-done((f32[1024,1408]{1,0:T(8,128)}, f32[1024,1408]{1,0:T(8,128)S(1)}, u32[]{:S(2)}) %copy-start.1) | copy-done | bytes 5767192
  81.5 0.0 copy-start.9
  81.5 1.2 dynamic-slice_convert_fusion
  82.7 1.2 collective-permute-start.1
  84.0 1.6 %convert_element_type.55 = f32[64,1024]{1,0:T(8,128)} convert(bf16[64,1024]{1,0:T(8,128)(2,1)} %param.7) | non-fusion elementwise | flops 65536 | bytes 393216 | tf_op jit(solution)/shard_map/convert_element_type | solution.py:120
  85.6 0.0 copy-done.9
  85.7 30.2 %collective-permute-done.1 = bf16[512,1408]{1,0:T(8,128)(2,1)} collective-permute-done((bf16[512,1408]{1,0:T(8,128)(2,1)}, bf16[512,1408]{1,0:T(8,128)(2,1)}, u32[]{:S(2)}, u32[]{:S(2)}) %collective-permute-start.1) | collective-permute-done | bytes 1441824 | tf_op jit(solution)/shard_map/ppermute | solution.py:130
  115.9 3.6 %fusion.1 = bf16[1,512,1408]{2,1,0:T(8,128)(2,1)} fusion(bf16[512,1408]{1,0:T(8,128)(2,1)} %collective-permute-done.1, f32[1024,1408]{1,0:T(8,128)} %copy-done.1, s32[]{:T(128)S(6)} %select_n.74), kind=kLoop, calls=%fused_computation.13 | loop fusion | flops 2162688 | bytes 5767172 | tf_op jit(solution)/shard_map/broadcast_in_dim | solution.py:136
  119.5 3.4 %all-to-all-done.1 = bf16[16,32,2048]{2,1,0:T(8,128)(2,1)S(1)} async-done(((bf16[16,32,2048]{2,1,0:T(8,128)(2,1)}), bf16[16,32,2048]{2,1,0:T(8,128)(2,1)S(1)}, u32[]{:S(2)}, u32[]{:S(2)}) %all-to-all-start.1) | async-done | bytes 2097184 | tf_op jit(solution)/shard_map/all_to_all | solution.py:101
  122.9 0.0 copy-start.6
  122.9 0.0 copy-start.10
  122.9 1.0 fusion.9
  123.9 0.0 copy-done.6
  123.9 0.0 copy-done.10
  123.9 1.0 multiply_reduce_fusion
  (4 shorter events, 0.0 us)
Async XLA Ops:
  0.6 63.6 %copy-start = (bf16[1,704,1024]{2,1,0:T(8,128)(2,1)S(1)}, bf16[1,704,1024]{2,1,0:T(8,128)(2,1)}, u32[]{:S(2)}) copy-start(bf16[1,704,1024]{2,1,0:T(8,128)(2,1)} %param.11) | copy-start | bytes 4325380
  5.8 54.0 %all-to-all-start = ((bf16[16,32,2048]{2,1,0:T(8,128)(2,1)}), bf16[16,32,2048]{2,1,0:T(8,128)(2,1)S(1)}, u32[]{:S(2)}, u32[]{:S(2)}) async-start(bf16[16,32,2048]{2,1,0:T(8,128)(2,1)} %bitcast.40), calls=%async_computation | async-start | bytes 4194304 | tf_op jit(solution)/shard_map/all_to_all | solution.py:59
  12.4 33.1 %collective-permute-start = (bf16[512,1408]{1,0:T(8,128)(2,1)}, bf16[512,1408]{1,0:T(8,128)(2,1)}, u32[]{:S(2)}, u32[]{:S(2)}) collective-permute-start(bf16[512,1408]{1,0:T(8,128)(2,1)} %bitcast.41), channel_id=1, source_target_pairs={{0,16},{16,0},{1,17},{17,1},{2,18},{18,2},{3,19},{19,3},{4,20},{20... | collective-permute-start | bytes 4325384 | tf_op jit(solution)/shard_map/ppermute | solution.py:11
  59.8 5.6 %copy-start.3 = (bf16[16,32,2048]{2,1,0:T(8,128)(2,1)}, bf16[16,32,2048]{2,1,0:T(8,128)(2,1)S(1)}, u32[]{:S(2)}) copy-start(bf16[16,32,2048]{2,1,0:T(8,128)(2,1)S(1)} %all-to-all-done) | copy-start | bytes 6291460
  59.8 2.1 %copy-start.4 = (bf16[512,1408]{1,0:T(8,128)(2,1)S(1)}, bf16[512,1408]{1,0:T(8,128)(2,1)}, u32[]{:S(2)}) copy-start(bf16[512,1408]{1,0:T(8,128)(2,1)} %get-tuple-element.10) | copy-start | bytes 4325380
  61.9 1.4 %copy-start.5 = (bf16[512,1408]{1,0:T(8,128)(2,1)S(1)}, bf16[512,1408]{1,0:T(8,128)(2,1)}, u32[]{:S(2)}) copy-start(bf16[512,1408]{1,0:T(8,128)(2,1)} %get-tuple-element.11) | copy-start | bytes 4325380
  66.9 1.3 %copy-start.7 = (bf16[512,704]{1,0:T(8,128)(2,1)}, bf16[512,704]{1,0:T(8,128)(2,1)S(1)}, u32[]{:S(2)}) copy-start(bf16[512,704]{1,0:T(8,128)(2,1)S(1)} %get-tuple-element.15) | copy-start | bytes 2162692
  66.9 1.3 %copy-start.8 = (bf16[512,704]{1,0:T(8,128)(2,1)}, bf16[512,704]{1,0:T(8,128)(2,1)S(1)}, u32[]{:S(2)}) copy-start(bf16[512,704]{1,0:T(8,128)(2,1)S(1)} %get-tuple-element.16) | copy-start | bytes 2162692
  69.2 1.3 %copy-start.2 = (bf16[512,2048]{1,0:T(8,128)(2,1)}, bf16[512,2048]{1,0:T(8,128)(2,1)S(1)}, u32[]{:S(2)}) copy-start(bf16[512,2048]{1,0:T(8,128)(2,1)S(1)} %fusion.6) | copy-start | bytes 6291460
  70.5 52.3 %all-to-all-start.1 = ((bf16[16,32,2048]{2,1,0:T(8,128)(2,1)}), bf16[16,32,2048]{2,1,0:T(8,128)(2,1)S(1)}, u32[]{:S(2)}, u32[]{:S(2)}) async-start(bf16[16,32,2048]{2,1,0:T(8,128)(2,1)} %bitcast.36), calls=%async_computation.1 | async-start | bytes 4194304 | tf_op jit(solution)/shard_map/all_to_all | solution.py:101
  79.0 2.5 %copy-start.1 = (f32[1024,1408]{1,0:T(8,128)}, f32[1024,1408]{1,0:T(8,128)S(1)}, u32[]{:S(2)}) copy-start(f32[1024,1408]{1,0:T(8,128)S(1)} %fusion.15) | copy-start | bytes 17301508
  81.5 4.1 %copy-start.9 = (s32[64,6]{0,1:T(8,128)S(1)}, s32[64,6]{0,1:T(8,128)}, u32[]{:S(2)}) copy-start(s32[64,6]{0,1:T(8,128)} %param.8) | copy-start | bytes 4612
  82.7 33.1 %collective-permute-start.1 = (bf16[512,1408]{1,0:T(8,128)(2,1)}, bf16[512,1408]{1,0:T(8,128)(2,1)}, u32[]{:S(2)}, u32[]{:S(2)}) collective-permute-start(bf16[512,1408]{1,0:T(8,128)(2,1)} %dynamic-slice_convert_fusion), channel_id=1, source_target_pairs={{0,16},{16,0},{1,17},{17,1},{2,18},{18,2},{3,19},{19,3},{4,20},{20... | collective-permute-start | bytes 4325384 | tf_op jit(solution)/shard_map/ppermute | solution.py:130
  122.9 1.0 copy-start.6
  122.9 1.0 copy-start.10

commit v13 on v12

--- a/solution.py
+++ b/solution.py
@@ -71,6 +71,13 @@
     def cols(block):
         return lax.dynamic_slice_in_dim(input_rows, block * block_rows, block_rows, axis=1)
 
+    hidden_grad = lax.dot_general(
+        cot_rows, weight_down, (((1,), (1,)), ((), ())), preferred_element_type=jnp.float32
+    )
+    hidden_grad, held_weights = lax.optimization_barrier(
+        (hidden_grad, tuple(weight for _, weight in weight_blocks))
+    )
+    weight_blocks = [(index, weight) for (index, _), weight in zip(weight_blocks, held_weights)]
     gate_up = None
     for block, weight in weight_blocks:
         part = jnp.dot(cols(block), weight, preferred_element_type=jnp.float32)
@@ -82,9 +89,6 @@
     hidden = (active * upper).astype(jnp.bfloat16)
     output_rows = jnp.dot(hidden, weight_down, preferred_element_type=jnp.float32).astype(
         jnp.bfloat16
-    )
-    hidden_grad = lax.dot_general(
-        cot_rows, weight_down, (((1,), (1,)), ((), ())), preferred_element_type=jnp.float32
     )
     gate_cot = hidden_grad * upper * sigma * (1.0 + gate * (1.0 - sigma))
     upper_cot = hidden_grad * active

time: 125 us -> 125 us (level)
  no operation moved by 1% of the time
where the time goes in v13:
time: 125 us; the launch traced here: 124 us
  waiting for transfers between devices  76.2 us (61%)
  starting transfers between devices  13.9 us (11%)
  matrix products  13.7 us (11%)
  other arithmetic  12.7 us (10%)
  local copies, waits for them, and re-layouts  7.02 us (6%)
    ppermute x1, waiting for transfers between devices, gather_rows(): lax.ppermute(own, axis_name, [(i, (i + shift) % count) for i in range(cou...  31.9 us
    ppermute x1, waiting for transfers between devices, local(): lax.ppermute(grad_block((me_dp + shift) % replicas).astype(jnp.bfloat16),...  30.2 us
    all_to_all x1, waiting for transfers between devices, local(): lax.all_to_all(both_send.reshape(experts, capacity, 2 * model_width), 'ex...  10.7 us
    all_to_all x1, starting transfers between devices, local(): lax.all_to_all(both_send.reshape(experts, capacity, 2 * model_width), 'ex...  6.56 us
    unnamed x22, local copies, waits for them, and re-layouts  5.3 us
    all_to_all x1, starting transfers between devices, local(): lax.all_to_all(send_back.reshape(experts, capacity, 2 * model_width), 'ex...  4.91 us
    select_n x1, other arithmetic, gather_rows(): jnp.where(keep, block, jnp.zeros_like(block))  3.61 us
    broadcast_in_dim x1, other arithmetic, local(): grad_rows.astype(jnp.bfloat16)[None]  3.6 us
  transfers between devices with their start and end apart: 4, of which 4 were waited for; matrix products, arithmetic and copies ran while one was open for 11% of the time, Pallas kernels for 0%

profile of v13, /device:TPU:11, one launch (start us, length us, event | category | flops | bytes accessed | tf_op | source)
XLA Modules:
  0.0 124.4 jit_solution(2022945082213647832)
XLA Ops:
  0.6 0.0 copy-start
  0.7 0.8 fusion.22
  1.5 0.1 convolution_convert_fusion.3
  1.6 0.7 select_reduce_fusion.1
  2.3 0.1 select_reduce_fusion
  2.5 0.1 broadcast_in_dim.72
  2.6 0.1 eq.80
  2.6 0.1 fusion.20
  2.8 3.0 %multiply_convert_fusion = bf16[512,2048]{1,0:T(8,128)(2,1)} fusion(pred[512,64]{1,0:T(32,128)(4,1)S(1)} %fusion.20, f32[512]{0:T(512)S(1)} %broadcast_in_dim.72, pred[2048]{0:T(1024)(128)(4,1)S(1)} %iota_compare_fusion.5, bf16[64,1024]{1,0:T(8,128)(2,1)} %param.7, bf16[64,1024]{1,0:T(8,128)(2,1)} %param.6), kind=kOutput, calls=%fused_computation | convolution fusion | flops 137887744 | bytes 2396160 | tf_op jit(solution)/shard_map/dot_general | solution.py:53
  5.8 6.6 %all-to-all-start = ((bf16[16,32,2048]{2,1,0:T(8,128)(2,1)}), bf16[16,32,2048]{2,1,0:T(8,128)(2,1)S(1)}, u32[]{:S(2)}, u32[]{:S(2)}) async-start(bf16[16,32,2048]{2,1,0:T(8,128)(2,1)} %bitcast.38), calls=%async_computation | async-start | bytes 4194304 | tf_op jit(solution)/shard_map/all_to_all | solution.py:59
  12.4 1.2 collective-permute-start
  13.6 31.9 %collective-permute-done = bf16[512,1408]{1,0:T(8,128)(2,1)} collective-permute-done((bf16[512,1408]{1,0:T(8,128)(2,1)}, bf16[512,1408]{1,0:T(8,128)(2,1)}, u32[]{:S(2)}, u32[]{:S(2)}) %collective-permute-start) | collective-permute-done | bytes 1441824 | tf_op jit(solution)/shard_map/ppermute | solution.py:11
  45.5 3.6 %broadcast_select_fusion = (bf16[512,1408]{1,0:T(8,128)(2,1)}, bf16[512,1408]{1,0:T(8,128)(2,1)}) fusion(bf16[512,1408]{1,0:T(8,128)(2,1)} %collective-permute-done, pred[]{:T(512)S(6)} %ge.3, bf16[512,1408]{1,0:T(8,128)(2,1)} %bitcast.40), kind=kLoop, calls=%fused_computation.18 | loop fusion | flops 1441792 | bytes 5767169 | tf_op jit(solution)/shard_map/jit(_where)/select_n | solution.py:17
  49.1 10.7 %all-to-all-done = bf16[16,32,2048]{2,1,0:T(8,128)(2,1)S(1)} async-done(((bf16[16,32,2048]{2,1,0:T(8,128)(2,1)}), bf16[16,32,2048]{2,1,0:T(8,128)(2,1)S(1)}, u32[]{:S(2)}, u32[]{:S(2)}) %all-to-all-start) | async-done | bytes 2097184 | tf_op jit(solution)/shard_map/all_to_all | solution.py:59
  59.8 0.0 copy-start.3
  59.8 0.1 slice.24
  59.9 0.0 copy-done
  59.9 0.0 copy-start.4
  59.9 0.9 fusion.2
  60.8 0.3 copy-done.3
  61.1 0.8 copy-done.4
  61.9 0.0 copy-start.5
  61.9 1.0 fusion.12
  62.9 0.4 copy-done.5
  63.3 1.0 convolution_add_fusion
  64.2 1.1 convolution_convert_fusion
  65.4 0.9 multiply_convert_fusion.2
  66.3 0.0 copy-start.6
  66.3 0.0 copy-start.7
  66.3 0.2 dynamic_update_slice.9
  66.6 1.0 fusion.5
  67.6 0.0 copy-done.6
  67.6 0.0 copy-done.7
  67.6 1.0 fusion.6
  68.7 0.0 copy-start.2
  68.7 1.3 %copy-done.2 = bf16[512,2048]{1,0:T(8,128)(2,1)} copy-done((bf16[512,2048]{1,0:T(8,128)(2,1)}, bf16[512,2048]{1,0:T(8,128)(2,1)S(1)}, u32[]{:S(2)}) %copy-start.2) | copy-done | bytes 2097176
  70.0 4.9 %all-to-all-start.1 = ((bf16[16,32,2048]{2,1,0:T(8,128)(2,1)}), bf16[16,32,2048]{2,1,0:T(8,128)(2,1)S(1)}, u32[]{:S(2)}, u32[]{:S(2)}) async-start(bf16[16,32,2048]{2,1,0:T(8,128)(2,1)} %bitcast.34), calls=%async_computation.1 | async-start | bytes 4194304 | tf_op jit(solution)/shard_map/all_to_all | solution.py:105
  74.9 3.5 %fusion.14 = f32[1024,1408]{1,0:T(8,128)S(1)} fusion(bf16[512,704]{0,1:T(8,128)(2,1)} %copy-done.7, bf16[512,704]{0,1:T(8,128)(2,1)} %copy-done.6, bf16[512,2048]{1,0:T(8,128)(2,1)} %bitcast.37), kind=kOutput, calls=%fused_computation.32 | convolution fusion | flops 1479278592 | bytes 8257536 | tf_op jit(solution)/shard_map/dot_general | solution.py:125
  78.4 0.0 copy-start.1
  78.4 2.5 %copy-done.1 = f32[1024,1408]{1,0:T(8,128)} copy-done((f32[1024,1408]{1,0:T(8,128)}, f32[1024,1408]{1,0:T(8,128)S(1)}, u32[]{:S(2)}) %copy-start.1) | copy-done | bytes 5767192
  80.9 0.0 copy-start.9
  80.9 1.2 %dynamic-slice_convert_fusion = bf16[512,1408]{1,0:T(8,128)(2,1)} fusion(f32[1024,1408]{1,0:T(8,128)S(1)} %fusion.14, s32[]{:T(128)S(6)} %select_n.76), kind=kLoop, calls=%fused_computation.3 | loop fusion | bytes 2883588 | tf_op jit(solution)/shard_map/convert_element_type | solution.py:135
  82.1 1.2 %collective-permute-start.1 = (bf16[512,1408]{1,0:T(8,128)(2,1)}, bf16[512,1408]{1,0:T(8,128)(2,1)}, u32[]{:S(2)}, u32[]{:S(2)}) collective-permute-start(bf16[512,1408]{1,0:T(8,128)(2,1)} %dynamic-slice_convert_fusion), channel_id=1, source_target_pairs={{0,16},{16,0},{1,17},{17,1},{2,18},{18,2},{3,19},{19,3},{4,20},{20... | collective-permute-start | bytes 4325384 | tf_op jit(solution)/shard_map/ppermute | solution.py:134
  83.4 1.6 %convert_element_type.55 = f32[64,1024]{1,0:T(8,128)} convert(bf16[64,1024]{1,0:T(8,128)(2,1)} %param.7) | non-fusion elementwise | flops 65536 | bytes 393216 | tf_op jit(solution)/shard_map/convert_element_type | solution.py:124
  85.0 0.0 copy-done.9
  85.0 30.2 %collective-permute-done.1 = bf16[512,1408]{1,0:T(8,128)(2,1)} collective-permute-done((bf16[512,1408]{1,0:T(8,128)(2,1)}, bf16[512,1408]{1,0:T(8,128)(2,1)}, u32[]{:S(2)}, u32[]{:S(2)}) %collective-permute-start.1) | collective-permute-done | bytes 1441824 | tf_op jit(solution)/shard_map/ppermute | solution.py:134
  115.2 3.6 %fusion = bf16[1,512,1408]{2,1,0:T(8,128)(2,1)} fusion(bf16[512,1408]{1,0:T(8,128)(2,1)} %collective-permute-done.1, f32[1024,1408]{1,0:T(8,128)} %copy-done.1, s32[]{:T(128)S(6)} %select_n.74), kind=kLoop, calls=%fused_computation.8 | loop fusion | flops 2162688 | bytes 5767172 | tf_op jit(solution)/shard_map/broadcast_in_dim | solution.py:140
  118.8 3.5 %all-to-all-done.1 = bf16[16,32,2048]{2,1,0:T(8,128)(2,1)S(1)} async-done(((bf16[16,32,2048]{2,1,0:T(8,128)(2,1)}), bf16[16,32,2048]{2,1,0:T(8,128)(2,1)S(1)}, u32[]{:S(2)}, u32[]{:S(2)}) %all-to-all-start.1) | async-done | bytes 2097184 | tf_op jit(solution)/shard_map/all_to_all | solution.py:105
  122.3 0.0 copy-start.8
  122.3 0.0 copy-start.10
  122.3 1.0 fusion.9
  123.3 0.0 copy-done.8
  123.4 0.0 copy-done.10
  123.4 1.0 multiply_reduce_fusion
  (4 shorter events, 0.0 us)
Async XLA Ops:
  0.6 59.2 %copy-start = (bf16[1,704,1024]{2,1,0:T(8,128)(2,1)S(1)}, bf16[1,704,1024]{2,1,0:T(8,128)(2,1)}, u32[]{:S(2)}) copy-start(bf16[1,704,1024]{2,1,0:T(8,128)(2,1)} %param.11) | copy-start | bytes 4325380
  5.8 54.0 %all-to-all-start = ((bf16[16,32,2048]{2,1,0:T(8,128)(2,1)}), bf16[16,32,2048]{2,1,0:T(8,128)(2,1)S(1)}, u32[]{:S(2)}, u32[]{:S(2)}) async-start(bf16[16,32,2048]{2,1,0:T(8,128)(2,1)} %bitcast.38), calls=%async_computation | async-start | bytes 4194304 | tf_op jit(solution)/shard_map/all_to_all | solution.py:59
  12.4 33.1 %collective-permute-start = (bf16[512,1408]{1,0:T(8,128)(2,1)}, bf16[512,1408]{1,0:T(8,128)(2,1)}, u32[]{:S(2)}, u32[]{:S(2)}) collective-permute-start(bf16[512,1408]{1,0:T(8,128)(2,1)} %bitcast.39), channel_id=1, source_target_pairs={{0,16},{16,0},{1,17},{17,1},{2,18},{18,2},{3,19},{19,3},{4,20},{20... | collective-permute-start | bytes 4325384 | tf_op jit(solution)/shard_map/ppermute | solution.py:11
  59.8 1.4 %copy-start.3 = (bf16[16,32,2048]{2,1,0:T(8,128)(2,1)}, bf16[16,32,2048]{2,1,0:T(8,128)(2,1)S(1)}, u32[]{:S(2)}) copy-start(bf16[16,32,2048]{2,1,0:T(8,128)(2,1)S(1)} %all-to-all-done) | copy-start | bytes 6291460
  59.9 2.1 %copy-start.4 = (bf16[512,1408]{1,0:T(8,128)(2,1)S(1)}, bf16[512,1408]{1,0:T(8,128)(2,1)}, u32[]{:S(2)}) copy-start(bf16[512,1408]{1,0:T(8,128)(2,1)} %get-tuple-element.15) | copy-start | bytes 4325380
  61.9 1.4 %copy-start.5 = (bf16[512,1408]{1,0:T(8,128)(2,1)S(1)}, bf16[512,1408]{1,0:T(8,128)(2,1)}, u32[]{:S(2)}) copy-start(bf16[512,1408]{1,0:T(8,128)(2,1)} %get-tuple-element.16) | copy-start | bytes 4325380
  66.3 1.3 %copy-start.6 = (bf16[512,704]{0,1:T(8,128)(2,1)}, bf16[512,704]{0,1:T(8,128)(2,1)S(1)}, u32[]{:S(2)}) copy-start(bf16[512,704]{0,1:T(8,128)(2,1)S(1)} %get-tuple-element.21) | copy-start | bytes 2162692
  66.3 1.3 %copy-start.7 = (bf16[512,704]{0,1:T(8,128)(2,1)}, bf16[512,704]{0,1:T(8,128)(2,1)S(1)}, u32[]{:S(2)}) copy-start(bf16[512,704]{0,1:T(8,128)(2,1)S(1)} %get-tuple-element.22) | copy-start | bytes 2162692
  68.7 1.3 %copy-start.2 = (bf16[512,2048]{1,0:T(8,128)(2,1)}, bf16[512,2048]{1,0:T(8,128)(2,1)S(1)}, u32[]{:S(2)}) copy-start(bf16[512,2048]{1,0:T(8,128)(2,1)S(1)} %fusion.6) | copy-start | bytes 6291460
  70.0 52.3 %all-to-all-start.1 = ((bf16[16,32,2048]{2,1,0:T(8,128)(2,1)}), bf16[16,32,2048]{2,1,0:T(8,128)(2,1)S(1)}, u32[]{:S(2)}, u32[]{:S(2)}) async-start(bf16[16,32,2048]{2,1,0:T(8,128)(2,1)} %bitcast.34), calls=%async_computation.1 | async-start | bytes 4194304 | tf_op jit(solution)/shard_map/all_to_all | solution.py:105
  78.4 2.5 %copy-start.1 = (f32[1024,1408]{1,0:T(8,128)}, f32[1024,1408]{1,0:T(8,128)S(1)}, u32[]{:S(2)}) copy-start(f32[1024,1408]{1,0:T(8,128)S(1)} %fusion.14) | copy-start | bytes 17301508
  80.9 4.1 %copy-start.9 = (s32[64,6]{0,1:T(8,128)S(1)}, s32[64,6]{0,1:T(8,128)}, u32[]{:S(2)}) copy-start(s32[64,6]{0,1:T(8,128)} %param.8) | copy-start | bytes 4612
  82.1 33.1 %collective-permute-start.1 = (bf16[512,1408]{1,0:T(8,128)(2,1)}, bf16[512,1408]{1,0:T(8,128)(2,1)}, u32[]{:S(2)}, u32[]{:S(2)}) collective-permute-start(bf16[512,1408]{1,0:T(8,128)(2,1)} %dynamic-slice_convert_fusion), channel_id=1, source_target_pairs={{0,16},{16,0},{1,17},{17,1},{2,18},{18,2},{3,19},{19,3},{4,20},{20... | collective-permute-start | bytes 4325384 | tf_op jit(solution)/shard_map/ppermute | solution.py:134
  122.3 1.0 copy-start.8
  122.3 1.0 copy-start.10

commit v14 on v13

--- a/solution.py
+++ b/solution.py
@@ -13,8 +13,8 @@
     ]
     held = lax.optimization_barrier((own, *moved))
     keep = me >= 0
-    fresh = lax.optimization_barrier(
-        tuple(jnp.where(keep, block, jnp.zeros_like(block)) for block in held)
+    fresh = (held[0],) + lax.optimization_barrier(
+        tuple(jnp.where(keep, block, jnp.zeros_like(block)) for block in held[1:])
     )
     return [((me - shift) % count, block) for shift, block in enumerate(fresh)]
 

time: 125 us -> 125 us (level)
  transfers between devices with their start and end apart: 4 -> 4, of which waited for: 4 -> 4; matrix products, arithmetic and copies ran while one was open for 11% -> 10% of each run, Pallas kernels for 0% -> 0%
where the time goes in v14:
time: 125 us; the launch traced here: 124 us
  waiting for transfers between devices  77.3 us (62%)
  starting transfers between devices  13.9 us (11%)
  matrix products  13.7 us (11%)
  other arithmetic  11.6 us (9%)
  local copies, waits for them, and re-layouts  7.02 us (6%)
    ppermute x1, waiting for transfers between devices, gather_rows(): lax.ppermute(own, axis_name, [(i, (i + shift) % count) for i in range(cou...  31.9 us
    ppermute x1, waiting for transfers between devices, local(): lax.ppermute(grad_block((me_dp + shift) % replicas).astype(jnp.bfloat16),...  30.2 us
    all_to_all x1, waiting for transfers between devices, local(): lax.all_to_all(both_send.reshape(experts, capacity, 2 * model_width), 'ex...  11.7 us
    all_to_all x1, starting transfers between devices, local(): lax.all_to_all(both_send.reshape(experts, capacity, 2 * model_width), 'ex...  6.56 us
    unnamed x22, local copies, waits for them, and re-layouts  5.3 us
    all_to_all x1, starting transfers between devices, local(): lax.all_to_all(send_back.reshape(experts, capacity, 2 * model_width), 'ex...  4.91 us
    broadcast_in_dim x1, other arithmetic, local(): grad_rows.astype(jnp.bfloat16)[None]  3.6 us
    all_to_all x1, waiting for transfers between devices, local(): lax.all_to_all(send_back.reshape(experts, capacity, 2 * model_width), 'ex...  3.48 us
  transfers between devices with their start and end apart: 4, of which 4 were waited for; matrix products, arithmetic and copies ran while one was open for 10% of the time, Pallas kernels for 0%

profile of v14, /device:TPU:11, one launch (start us, length us, event | category | flops | bytes accessed | tf_op | source)
XLA Modules:
  0.0 124.4 jit_solution(5180250077413904805)
XLA Ops:
  0.6 0.0 copy-start
  0.7 0.8 fusion.22
  1.5 0.1 convolution_convert_fusion.3
  1.6 0.7 select_reduce_fusion.1
  2.3 0.1 select_reduce_fusion
  2.5 0.1 broadcast_in_dim.75
  2.6 0.1 eq.80
  2.6 0.1 fusion.20
  2.8 3.0 %multiply_convert_fusion = bf16[512,2048]{1,0:T(8,128)(2,1)} fusion(pred[512,64]{1,0:T(32,128)(4,1)S(1)} %fusion.20, f32[512]{0:T(512)S(1)} %broadcast_in_dim.75, pred[2048]{0:T(1024)(128)(4,1)S(1)} %iota_compare_fusion.5, bf16[64,1024]{1,0:T(8,128)(2,1)} %param.7, bf16[64,1024]{1,0:T(8,128)(2,1)} %param.6), kind=kOutput, calls=%fused_computation | convolution fusion | flops 137887744 | bytes 2396160 | tf_op jit(solution)/shard_map/dot_general | solution.py:53
  5.8 6.6 %all-to-all-start = ((bf16[16,32,2048]{2,1,0:T(8,128)(2,1)}), bf16[16,32,2048]{2,1,0:T(8,128)(2,1)S(1)}, u32[]{:S(2)}, u32[]{:S(2)}) async-start(bf16[16,32,2048]{2,1,0:T(8,128)(2,1)} %bitcast.38), calls=%async_computation | async-start | bytes 4194304 | tf_op jit(solution)/shard_map/all_to_all | solution.py:59
  12.4 1.2 collective-permute-start
  13.6 31.9 %collective-permute-done = bf16[512,1408]{1,0:T(8,128)(2,1)} collective-permute-done((bf16[512,1408]{1,0:T(8,128)(2,1)}, bf16[512,1408]{1,0:T(8,128)(2,1)}, u32[]{:S(2)}, u32[]{:S(2)}) %collective-permute-start) | collective-permute-done | bytes 1441824 | tf_op jit(solution)/shard_map/ppermute | solution.py:11
  45.5 2.6 %broadcast_select_fusion = bf16[512,1408]{1,0:T(8,128)(2,1)} fusion(bf16[512,1408]{1,0:T(8,128)(2,1)} %collective-permute-done, pred[]{:T(512)S(6)} %ge.3), kind=kLoop, calls=%fused_computation.18 | loop fusion | flops 720896 | bytes 2883585 | tf_op jit(solution)/shard_map/jit(_where)/select_n | solution.py:17
  48.1 11.7 %all-to-all-done = bf16[16,32,2048]{2,1,0:T(8,128)(2,1)S(1)} async-done(((bf16[16,32,2048]{2,1,0:T(8,128)(2,1)}), bf16[16,32,2048]{2,1,0:T(8,128)(2,1)S(1)}, u32[]{:S(2)}, u32[]{:S(2)}) %all-to-all-start) | async-done | bytes 2097184 | tf_op jit(solution)/shard_map/all_to_all | solution.py:59
  59.8 0.0 copy-start.3
  59.8 0.1 slice.24
  59.9 0.0 copy-done
  59.9 0.0 copy-start.7
  59.9 0.9 fusion.2
  60.8 0.3 copy-done.3
  61.1 0.8 copy-done.7
  61.9 0.0 copy-start.4
  61.9 1.0 fusion.12
  62.9 0.4 copy-done.4
  63.3 1.0 convolution_add_fusion
  64.2 1.1 convolution_convert_fusion
  65.3 0.9 multiply_convert_fusion.2
  66.3 0.0 copy-start.5
  66.3 0.0 copy-start.6
  66.3 0.2 dynamic_update_slice.9
  66.6 1.0 fusion.5
  67.6 0.0 copy-done.5
  67.6 0.0 copy-done.6
  67.6 1.0 fusion.6
  68.7 0.0 copy-start.2
  68.7 1.3 %copy-done.2 = bf16[512,2048]{1,0:T(8,128)(2,1)} copy-done((bf16[512,2048]{1,0:T(8,128)(2,1)}, bf16[512,2048]{1,0:T(8,128)(2,1)S(1)}, u32[]{:S(2)}) %copy-start.2) | copy-done | bytes 2097176
  70.0 4.9 %all-to-all-start.1 = ((bf16[16,32,2048]{2,1,0:T(8,128)(2,1)}), bf16[16,32,2048]{2,1,0:T(8,128)(2,1)S(1)}, u32[]{:S(2)}, u32[]{:S(2)}) async-start(bf16[16,32,2048]{2,1,0:T(8,128)(2,1)} %bitcast.34), calls=%async_computation.1 | async-start | bytes 4194304 | tf_op jit(solution)/shard_map/all_to_all | solution.py:105
  74.9 3.5 %fusion.14 = f32[1024,1408]{1,0:T(8,128)S(1)} fusion(bf16[512,704]{0,1:T(8,128)(2,1)} %copy-done.6, bf16[512,704]{0,1:T(8,128)(2,1)} %copy-done.5, bf16[512,2048]{1,0:T(8,128)(2,1)} %bitcast.37), kind=kOutput, calls=%fused_computation.31 | convolution fusion | flops 1479278592 | bytes 8257536 | tf_op jit(solution)/shard_map/dot_general | solution.py:125
  78.4 0.0 copy-start.1
  78.4 2.5 %copy-done.1 = f32[1024,1408]{1,0:T(8,128)} copy-done((f32[1024,1408]{1,0:T(8,128)}, f32[1024,1408]{1,0:T(8,128)S(1)}, u32[]{:S(2)}) %copy-start.1) | copy-done | bytes 5767192
  80.9 0.0 copy-start.9
  80.9 1.2 %dynamic-slice_convert_fusion = bf16[512,1408]{1,0:T(8,128)(2,1)} fusion(f32[1024,1408]{1,0:T(8,128)S(1)} %fusion.14, s32[]{:T(128)S(6)} %select_n.71), kind=kLoop, calls=%fused_computation.3 | loop fusion | bytes 2883588 | tf_op jit(solution)/shard_map/convert_element_type | solution.py:135
  82.1 1.2 collective-permute-start.1
  83.3 1.6 %convert_element_type.55 = f32[64,1024]{1,0:T(8,128)} convert(bf16[64,1024]{1,0:T(8,128)(2,1)} %param.7) | non-fusion elementwise | flops 65536 | bytes 393216 | tf_op jit(solution)/shard_map/convert_element_type | solution.py:124
  85.0 0.0 copy-done.9
  85.0 30.2 %collective-permute-done.1 = bf16[512,1408]{1,0:T(8,128)(2,1)} collective-permute-done((bf16[512,1408]{1,0:T(8,128)(2,1)}, bf16[512,1408]{1,0:T(8,128)(2,1)}, u32[]{:S(2)}, u32[]{:S(2)}) %collective-permute-start.1) | collective-permute-done | bytes 1441824 | tf_op jit(solution)/shard_map/ppermute | solution.py:134
  115.2 3.6 %fusion = bf16[1,512,1408]{2,1,0:T(8,128)(2,1)} fusion(bf16[512,1408]{1,0:T(8,128)(2,1)} %collective-permute-done.1, f32[1024,1408]{1,0:T(8,128)} %copy-done.1, s32[]{:T(128)S(6)} %select_n.69), kind=kLoop, calls=%fused_computation.8 | loop fusion | flops 2162688 | bytes 5767172 | tf_op jit(solution)/shard_map/broadcast_in_dim | solution.py:140
  118.8 3.5 %all-to-all-done.1 = bf16[16,32,2048]{2,1,0:T(8,128)(2,1)S(1)} async-done(((bf16[16,32,2048]{2,1,0:T(8,128)(2,1)}), bf16[16,32,2048]{2,1,0:T(8,128)(2,1)S(1)}, u32[]{:S(2)}, u32[]{:S(2)}) %all-to-all-start.1) | async-done | bytes 2097184 | tf_op jit(solution)/shard_map/all_to_all | solution.py:105
  122.3 0.0 copy-start.8
  122.3 0.0 copy-start.10
  122.3 1.0 fusion.9
  123.3 0.0 copy-done.8
  123.4 0.0 copy-done.10
  123.4 1.0 multiply_reduce_fusion
  (4 shorter events, 0.0 us)
Async XLA Ops:
  0.6 59.2 %copy-start = (bf16[1,704,1024]{2,1,0:T(8,128)(2,1)S(1)}, bf16[1,704,1024]{2,1,0:T(8,128)(2,1)}, u32[]{:S(2)}) copy-start(bf16[1,704,1024]{2,1,0:T(8,128)(2,1)} %param.11) | copy-start | bytes 4325380
  5.8 54.0 %all-to-all-start = ((bf16[16,32,2048]{2,1,0:T(8,128)(2,1)}), bf16[16,32,2048]{2,1,0:T(8,128)(2,1)S(1)}, u32[]{:S(2)}, u32[]{:S(2)}) async-start(bf16[16,32,2048]{2,1,0:T(8,128)(2,1)} %bitcast.38), calls=%async_computation | async-start | bytes 4194304 | tf_op jit(solution)/shard_map/all_to_all | solution.py:59
  12.4 33.1 %collective-permute-start = (bf16[512,1408]{1,0:T(8,128)(2,1)}, bf16[512,1408]{1,0:T(8,128)(2,1)}, u32[]{:S(2)}, u32[]{:S(2)}) collective-permute-start(bf16[512,1408]{1,0:T(8,128)(2,1)} %bitcast.39), channel_id=1, source_target_pairs={{0,16},{16,0},{1,17},{17,1},{2,18},{18,2},{3,19},{19,3},{4,20},{20... | collective-permute-start | bytes 4325384 | tf_op jit(solution)/shard_map/ppermute | solution.py:11
  59.8 1.4 %copy-start.3 = (bf16[16,32,2048]{2,1,0:T(8,128)(2,1)}, bf16[16,32,2048]{2,1,0:T(8,128)(2,1)S(1)}, u32[]{:S(2)}) copy-start(bf16[16,32,2048]{2,1,0:T(8,128)(2,1)S(1)} %all-to-all-done) | copy-start | bytes 6291460
  59.9 2.0 %copy-start.7 = (bf16[1,512,1408]{2,1,0:T(8,128)(2,1)S(1)}, bf16[1,512,1408]{2,1,0:T(8,128)(2,1)}, u32[]{:S(2)}) copy-start(bf16[1,512,1408]{2,1,0:T(8,128)(2,1)} %param.10) | copy-start | bytes 4325380
  61.9 1.4 %copy-start.4 = (bf16[512,1408]{1,0:T(8,128)(2,1)S(1)}, bf16[512,1408]{1,0:T(8,128)(2,1)}, u32[]{:S(2)}) copy-start(bf16[512,1408]{1,0:T(8,128)(2,1)} %broadcast_select_fusion) | copy-start | bytes 4325380
  66.3 1.3 %copy-start.5 = (bf16[512,704]{0,1:T(8,128)(2,1)}, bf16[512,704]{0,1:T(8,128)(2,1)S(1)}, u32[]{:S(2)}) copy-start(bf16[512,704]{0,1:T(8,128)(2,1)S(1)} %get-tuple-element.17) | copy-start | bytes 2162692
  66.3 1.3 %copy-start.6 = (bf16[512,704]{0,1:T(8,128)(2,1)}, bf16[512,704]{0,1:T(8,128)(2,1)S(1)}, u32[]{:S(2)}) copy-start(bf16[512,704]{0,1:T(8,128)(2,1)S(1)} %get-tuple-element.18) | copy-start | bytes 2162692
  68.7 1.3 %copy-start.2 = (bf16[512,2048]{1,0:T(8,128)(2,1)}, bf16[512,2048]{1,0:T(8,128)(2,1)S(1)}, u32[]{:S(2)}) copy-start(bf16[512,2048]{1,0:T(8,128)(2,1)S(1)} %fusion.6) | copy-start | bytes 6291460
  70.0 52.3 %all-to-all-start.1 = ((bf16[16,32,2048]{2,1,0:T(8,128)(2,1)}), bf16[16,32,2048]{2,1,0:T(8,128)(2,1)S(1)}, u32[]{:S(2)}, u32[]{:S(2)}) async-start(bf16[16,32,2048]{2,1,0:T(8,128)(2,1)} %bitcast.34), calls=%async_computation.1 | async-start | bytes 4194304 | tf_op jit(solution)/shard_map/all_to_all | solution.py:105
  78.4 2.5 %copy-start.1 = (f32[1024,1408]{1,0:T(8,128)}, f32[1024,1408]{1,0:T(8,128)S(1)}, u32[]{:S(2)}) copy-start(f32[1024,1408]{1,0:T(8,128)S(1)} %fusion.14) | copy-start | bytes 17301508
  80.9 4.1 %copy-start.9 = (s32[64,6]{0,1:T(8,128)S(1)}, s32[64,6]{0,1:T(8,128)}, u32[]{:S(2)}) copy-start(s32[64,6]{0,1:T(8,128)} %param.8) | copy-start | bytes 4612
  82.1 33.1 %collective-permute-start.1 = (bf16[512,1408]{1,0:T(8,128)(2,1)}, bf16[512,1408]{1,0:T(8,128)(2,1)}, u32[]{:S(2)}, u32[]{:S(2)}) collective-permute-start(bf16[512,1408]{1,0:T(8,128)(2,1)} %dynamic-slice_convert_fusion), channel_id=1, source_target_pairs={{0,16},{16,0},{1,17},{17,1},{2,18},{18,2},{3,19},{19,3},{4,20},{20... | collective-permute-start | bytes 4325384 | tf_op jit(solution)/shard_map/ppermute | solution.py:134
  122.3 1.0 copy-start.8
  122.3 1.0 copy-start.10

commit v15 on v13

--- a/solution.py
+++ b/solution.py
@@ -31,8 +31,8 @@
     capacity = 4 * token_count * top_count // (3 * experts)
     weight_blocks = gather_rows(w_gate_up[0], "dp", block_rows)
     hit = expert_ids[:, :, None] == jnp.arange(experts, dtype=jnp.int32)[None, None, :]
-    token_hit = jnp.any(hit, axis=1)
     token_prob = jnp.sum(jnp.where(hit, gate_probs[:, :, None], 0.0), axis=1)
+    token_hit = token_prob > 0.0
     earlier = (
         lax.broadcasted_iota(jnp.int32, (token_count, token_count), 0)
         > lax.broadcasted_iota(jnp.int32, (token_count, token_count), 1)

time: 125 us -> 124 us (level)
  no operation moved by 1% of the time
where the time goes in v15:
time: 124 us
  waiting for transfers between devices  76.2 us (61%)
  starting transfers between devices  13.9 us (11%)
  matrix products  13.7 us (11%)
  other arithmetic  12 us (10%)
  local copies, waits for them, and re-layouts  7.04 us (6%)
    ppermute x1, waiting for transfers between devices, gather_rows(): lax.ppermute(own, axis_name, [(i, (i + shift) % count) for i in range(cou...  31.9 us
    ppermute x1, waiting for transfers between devices, local(): lax.ppermute(grad_block((me_dp + shift) % replicas).astype(jnp.bfloat16),...  30.2 us
    all_to_all x1, waiting for transfers between devices, local(): lax.all_to_all(both_send.reshape(experts, capacity, 2 * model_width), 'ex...  10.7 us
    all_to_all x1, starting transfers between devices, local(): lax.all_to_all(both_send.reshape(experts, capacity, 2 * model_width), 'ex...  6.55 us
    unnamed x22, local copies, waits for them, and re-layouts  5.33 us
    all_to_all x1, starting transfers between devices, local(): lax.all_to_all(send_back.reshape(experts, capacity, 2 * model_width), 'ex...  4.91 us
    select_n x1, other arithmetic, gather_rows(): jnp.where(keep, block, jnp.zeros_like(block))  3.62 us
    broadcast_in_dim x1, other arithmetic, local(): grad_rows.astype(jnp.bfloat16)[None]  3.6 us
  transfers between devices with their start and end apart: 4, of which 4 were waited for; matrix products, arithmetic and copies ran while one was open for 11% of the time, Pallas kernels for 0%

profile of v15, /device:TPU:11, one launch (start us, length us, event | category | flops | bytes accessed | tf_op | source)
XLA Modules:
  0.0 123.7 jit_solution(2790844577399185499)
XLA Ops:
  0.6 0.0 copy-start
  0.7 0.8 select_reduce_fusion.2
  1.5 0.1 convolution_convert_fusion.3
  1.6 0.2 select_reduce_fusion
  1.8 0.1 broadcast_in_dim.72
  1.9 0.1 eq.80
  2.0 0.1 fusion.20
  2.1 3.0 %multiply_convert_fusion = bf16[512,2048]{1,0:T(8,128)(2,1)} fusion(pred[512,64]{1,0:T(32,128)(4,1)S(1)} %fusion.20, f32[512]{0:T(512)S(1)} %broadcast_in_dim.72, pred[2048]{0:T(1024)(128)(4,1)S(1)} %iota_compare_fusion.5, bf16[64,1024]{1,0:T(8,128)(2,1)} %param.7, bf16[64,1024]{1,0:T(8,128)(2,1)} %param.6), kind=kOutput, calls=%fused_computation | convolution fusion | flops 137887744 | bytes 2396160 | tf_op jit(solution)/shard_map/dot_general | solution.py:53
  5.1 6.6 %all-to-all-start = ((bf16[16,32,2048]{2,1,0:T(8,128)(2,1)}), bf16[16,32,2048]{2,1,0:T(8,128)(2,1)S(1)}, u32[]{:S(2)}, u32[]{:S(2)}) async-start(bf16[16,32,2048]{2,1,0:T(8,128)(2,1)} %bitcast.37), calls=%async_computation | async-start | bytes 4194304 | tf_op jit(solution)/shard_map/all_to_all | solution.py:59
  11.7 1.2 %collective-permute-start = (bf16[512,1408]{1,0:T(8,128)(2,1)}, bf16[512,1408]{1,0:T(8,128)(2,1)}, u32[]{:S(2)}, u32[]{:S(2)}) collective-permute-start(bf16[512,1408]{1,0:T(8,128)(2,1)} %bitcast.38), channel_id=1, source_target_pairs={{0,16},{16,0},{1,17},{17,1},{2,18},{18,2},{3,19},{19,3},{4,20},{20... | collective-permute-start | bytes 4325384 | tf_op jit(solution)/shard_map/ppermute | solution.py:11
  12.9 31.9 %collective-permute-done = bf16[512,1408]{1,0:T(8,128)(2,1)} collective-permute-done((bf16[512,1408]{1,0:T(8,128)(2,1)}, bf16[512,1408]{1,0:T(8,128)(2,1)}, u32[]{:S(2)}, u32[]{:S(2)}) %collective-permute-start) | collective-permute-done | bytes 1441824 | tf_op jit(solution)/shard_map/ppermute | solution.py:11
  44.8 3.6 %broadcast_select_fusion = (bf16[512,1408]{1,0:T(8,128)(2,1)}, bf16[512,1408]{1,0:T(8,128)(2,1)}) fusion(bf16[512,1408]{1,0:T(8,128)(2,1)} %collective-permute-done, pred[]{:T(512)S(6)} %ge.3, bf16[512,1408]{1,0:T(8,128)(2,1)} %bitcast.39), kind=kLoop, calls=%fused_computation.18 | loop fusion | flops 1441792 | bytes 5767169 | tf_op jit(solution)/shard_map/jit(_where)/select_n | solution.py:17
  48.4 10.7 %all-to-all-done = bf16[16,32,2048]{2,1,0:T(8,128)(2,1)S(1)} async-done(((bf16[16,32,2048]{2,1,0:T(8,128)(2,1)}), bf16[16,32,2048]{2,1,0:T(8,128)(2,1)S(1)}, u32[]{:S(2)}, u32[]{:S(2)}) %all-to-all-start) | async-done | bytes 2097184 | tf_op jit(solution)/shard_map/all_to_all | solution.py:59
  59.1 0.0 copy-start.3
  59.1 0.1 slice.24
  59.2 0.0 copy-done
  59.2 0.0 copy-start.4
  59.2 0.9 fusion.2
  60.1 0.3 copy-done.3
  60.4 0.8 copy-done.4
  61.2 0.0 copy-start.5
  61.2 1.0 fusion.12
  62.2 0.4 copy-done.5
  62.6 1.0 convolution_add_fusion
  63.5 1.1 convolution_convert_fusion
  64.6 0.9 multiply_convert_fusion.2
  65.6 0.0 copy-start.6
  65.6 0.0 copy-start.7
  65.6 0.2 dynamic_update_slice.9
  65.9 1.0 fusion.5
  66.9 0.0 copy-done.6
  66.9 0.0 copy-done.7
  66.9 1.0 fusion.6
  68.0 0.0 copy-start.2
  68.0 1.3 %copy-done.2 = bf16[512,2048]{1,0:T(8,128)(2,1)} copy-done((bf16[512,2048]{1,0:T(8,128)(2,1)}, bf16[512,2048]{1,0:T(8,128)(2,1)S(1)}, u32[]{:S(2)}) %copy-start.2) | copy-done | bytes 2097176
  69.3 4.9 %all-to-all-start.1 = ((bf16[16,32,2048]{2,1,0:T(8,128)(2,1)}), bf16[16,32,2048]{2,1,0:T(8,128)(2,1)S(1)}, u32[]{:S(2)}, u32[]{:S(2)}) async-start(bf16[16,32,2048]{2,1,0:T(8,128)(2,1)} %bitcast.33), calls=%async_computation.1 | async-start | bytes 4194304 | tf_op jit(solution)/shard_map/all_to_all | solution.py:105
  74.2 3.5 %fusion.14 = f32[1024,1408]{1,0:T(8,128)S(1)} fusion(bf16[512,704]{0,1:T(8,128)(2,1)} %copy-done.7, bf16[512,704]{0,1:T(8,128)(2,1)} %copy-done.6, bf16[512,2048]{1,0:T(8,128)(2,1)} %bitcast.36), kind=kOutput, calls=%fused_computation.32 | convolution fusion | flops 1479278592 | bytes 8257536 | tf_op jit(solution)/shard_map/dot_general | solution.py:125
  77.7 0.0 copy-start.1
  77.7 2.5 %copy-done.1 = f32[1024,1408]{1,0:T(8,128)} copy-done((f32[1024,1408]{1,0:T(8,128)}, f32[1024,1408]{1,0:T(8,128)S(1)}, u32[]{:S(2)}) %copy-start.1) | copy-done | bytes 5767192
  80.2 0.0 copy-start.9
  80.2 1.2 %dynamic-slice_convert_fusion = bf16[512,1408]{1,0:T(8,128)(2,1)} fusion(f32[1024,1408]{1,0:T(8,128)S(1)} %fusion.14, s32[]{:T(128)S(6)} %select_n.76), kind=kLoop, calls=%fused_computation.3 | loop fusion | bytes 2883588 | tf_op jit(solution)/shard_map/convert_element_type | solution.py:135
  81.4 1.2 collective-permute-start.1
  82.7 1.6 %convert_element_type.55 = f32[64,1024]{1,0:T(8,128)} convert(bf16[64,1024]{1,0:T(8,128)(2,1)} %param.7) | non-fusion elementwise | flops 65536 | bytes 393216 | tf_op jit(solution)/shard_map/convert_element_type | solution.py:124
  84.3 0.0 copy-done.9
  84.3 30.2 %collective-permute-done.1 = bf16[512,1408]{1,0:T(8,128)(2,1)} collective-permute-done((bf16[512,1408]{1,0:T(8,128)(2,1)}, bf16[512,1408]{1,0:T(8,128)(2,1)}, u32[]{:S(2)}, u32[]{:S(2)}) %collective-permute-start.1) | collective-permute-done | bytes 1441824 | tf_op jit(solution)/shard_map/ppermute | solution.py:134
  114.6 3.6 %fusion = bf16[1,512,1408]{2,1,0:T(8,128)(2,1)} fusion(bf16[512,1408]{1,0:T(8,128)(2,1)} %collective-permute-done.1, f32[1024,1408]{1,0:T(8,128)} %copy-done.1, s32[]{:T(128)S(6)} %select_n.74), kind=kLoop, calls=%fused_computation.8 | loop fusion | flops 2162688 | bytes 5767172 | tf_op jit(solution)/shard_map/broadcast_in_dim | solution.py:140
  118.2 3.5 %all-to-all-done.1 = bf16[16,32,2048]{2,1,0:T(8,128)(2,1)S(1)} async-done(((bf16[16,32,2048]{2,1,0:T(8,128)(2,1)}), bf16[16,32,2048]{2,1,0:T(8,128)(2,1)S(1)}, u32[]{:S(2)}, u32[]{:S(2)}) %all-to-all-start.1) | async-done | bytes 2097184 | tf_op jit(solution)/shard_map/all_to_all | solution.py:105
  121.6 0.0 copy-start.8
  121.6 0.0 copy-start.10
  121.6 1.0 fusion.9
  122.7 0.0 copy-done.8
  122.7 0.0 copy-done.10
  122.7 1.0 multiply_reduce_fusion
  (5 shorter events, 0.0 us)
Async XLA Ops:
  0.6 58.5 %copy-start = (bf16[1,704,1024]{2,1,0:T(8,128)(2,1)S(1)}, bf16[1,704,1024]{2,1,0:T(8,128)(2,1)}, u32[]{:S(2)}) copy-start(bf16[1,704,1024]{2,1,0:T(8,128)(2,1)} %param.11) | copy-start | bytes 4325380
  5.1 54.0 %all-to-all-start = ((bf16[16,32,2048]{2,1,0:T(8,128)(2,1)}), bf16[16,32,2048]{2,1,0:T(8,128)(2,1)S(1)}, u32[]{:S(2)}, u32[]{:S(2)}) async-start(bf16[16,32,2048]{2,1,0:T(8,128)(2,1)} %bitcast.37), calls=%async_computation | async-start | bytes 4194304 | tf_op jit(solution)/shard_map/all_to_all | solution.py:59
  11.7 33.1 %collective-permute-start = (bf16[512,1408]{1,0:T(8,128)(2,1)}, bf16[512,1408]{1,0:T(8,128)(2,1)}, u32[]{:S(2)}, u32[]{:S(2)}) collective-permute-start(bf16[512,1408]{1,0:T(8,128)(2,1)} %bitcast.38), channel_id=1, source_target_pairs={{0,16},{16,0},{1,17},{17,1},{2,18},{18,2},{3,19},{19,3},{4,20},{20... | collective-permute-start | bytes 4325384 | tf_op jit(solution)/shard_map/ppermute | solution.py:11
  59.1 1.3 %copy-start.3 = (bf16[16,32,2048]{2,1,0:T(8,128)(2,1)}, bf16[16,32,2048]{2,1,0:T(8,128)(2,1)S(1)}, u32[]{:S(2)}) copy-start(bf16[16,32,2048]{2,1,0:T(8,128)(2,1)S(1)} %all-to-all-done) | copy-start | bytes 6291460
  59.2 2.1 %copy-start.4 = (bf16[512,1408]{1,0:T(8,128)(2,1)S(1)}, bf16[512,1408]{1,0:T(8,128)(2,1)}, u32[]{:S(2)}) copy-start(bf16[512,1408]{1,0:T(8,128)(2,1)} %get-tuple-element.15) | copy-start | bytes 4325380
  61.2 1.4 %copy-start.5 = (bf16[512,1408]{1,0:T(8,128)(2,1)S(1)}, bf16[512,1408]{1,0:T(8,128)(2,1)}, u32[]{:S(2)}) copy-start(bf16[512,1408]{1,0:T(8,128)(2,1)} %get-tuple-element.16) | copy-start | bytes 4325380
  65.6 1.3 %copy-start.6 = (bf16[512,704]{0,1:T(8,128)(2,1)}, bf16[512,704]{0,1:T(8,128)(2,1)S(1)}, u32[]{:S(2)}) copy-start(bf16[512,704]{0,1:T(8,128)(2,1)S(1)} %get-tuple-element.21) | copy-start | bytes 2162692
  65.6 1.3 %copy-start.7 = (bf16[512,704]{0,1:T(8,128)(2,1)}, bf16[512,704]{0,1:T(8,128)(2,1)S(1)}, u32[]{:S(2)}) copy-start(bf16[512,704]{0,1:T(8,128)(2,1)S(1)} %get-tuple-element.22) | copy-start | bytes 2162692
  68.0 1.3 %copy-start.2 = (bf16[512,2048]{1,0:T(8,128)(2,1)}, bf16[512,2048]{1,0:T(8,128)(2,1)S(1)}, u32[]{:S(2)}) copy-start(bf16[512,2048]{1,0:T(8,128)(2,1)S(1)} %fusion.6) | copy-start | bytes 6291460
  69.3 52.3 %all-to-all-start.1 = ((bf16[16,32,2048]{2,1,0:T(8,128)(2,1)}), bf16[16,32,2048]{2,1,0:T(8,128)(2,1)S(1)}, u32[]{:S(2)}, u32[]{:S(2)}) async-start(bf16[16,32,2048]{2,1,0:T(8,128)(2,1)} %bitcast.33), calls=%async_computation.1 | async-start | bytes 4194304 | tf_op jit(solution)/shard_map/all_to_all | solution.py:105
  77.7 2.5 %copy-start.1 = (f32[1024,1408]{1,0:T(8,128)}, f32[1024,1408]{1,0:T(8,128)S(1)}, u32[]{:S(2)}) copy-start(f32[1024,1408]{1,0:T(8,128)S(1)} %fusion.14) | copy-start | bytes 17301508
  80.2 4.1 %copy-start.9 = (s32[64,6]{0,1:T(8,128)S(1)}, s32[64,6]{0,1:T(8,128)}, u32[]{:S(2)}) copy-start(s32[64,6]{0,1:T(8,128)} %param.8) | copy-start | bytes 4612
  81.4 33.1 %collective-permute-start.1 = (bf16[512,1408]{1,0:T(8,128)(2,1)}, bf16[512,1408]{1,0:T(8,128)(2,1)}, u32[]{:S(2)}, u32[]{:S(2)}) collective-permute-start(bf16[512,1408]{1,0:T(8,128)(2,1)} %dynamic-slice_convert_fusion), channel_id=1, source_target_pairs={{0,16},{16,0},{1,17},{17,1},{2,18},{18,2},{3,19},{19,3},{4,20},{20... | collective-permute-start | bytes 4325384 | tf_op jit(solution)/shard_map/ppermute | solution.py:134
  121.6 1.0 copy-start.8
  121.6 1.0 copy-start.10

commit v16 on v15

--- a/solution.py
+++ b/solution.py
@@ -50,9 +50,8 @@
     slot_prob = jnp.sum(jnp.where(chosen, token_prob.T[:, None, :], 0.0), axis=2).reshape(
         experts * capacity
     )
-    picked = jnp.dot(
-        pick, jnp.concatenate([tokens, cotangent], axis=1), preferred_element_type=jnp.float32
-    )
+    rows_both = lax.optimization_barrier(jnp.concatenate([tokens, cotangent], axis=1))
+    picked = jnp.dot(pick, rows_both, preferred_element_type=jnp.float32)
     columns = lax.broadcasted_iota(jnp.int32, picked.shape, 1)
     scale = jnp.where(columns < model_width, 1.0, slot_prob[:, None])
     both_send = (picked * scale).astype(jnp.bfloat16)

time: 124 us -> 124 us (level)
  no operation moved by 1% of the time
where the time goes in v16:
time: 124 us
  waiting for transfers between devices  76.2 us (61%)
  starting transfers between devices  13.9 us (11%)
  other arithmetic  13 us (10%)
  matrix products  12.7 us (10%)
  local copies, waits for them, and re-layouts  7.04 us (6%)
    ppermute x1, waiting for transfers between devices, gather_rows(): lax.ppermute(own, axis_name, [(i, (i + shift) % count) for i in range(cou...  31.9 us
    ppermute x1, waiting for transfers between devices, local(): lax.ppermute(grad_block((me_dp + shift) % replicas).astype(jnp.bfloat16),...  30.2 us
    all_to_all x1, waiting for transfers between devices, local(): lax.all_to_all(both_send.reshape(experts, capacity, 2 * model_width), 'ex...  10.7 us
    all_to_all x1, starting transfers between devices, local(): lax.all_to_all(both_send.reshape(experts, capacity, 2 * model_width), 'ex...  6.56 us
    unnamed x22, local copies, waits for them, and re-layouts  5.33 us
    all_to_all x1, starting transfers between devices, local(): lax.all_to_all(send_back.reshape(experts, capacity, 2 * model_width), 'ex...  4.91 us
    select_n x1, other arithmetic, gather_rows(): jnp.where(keep, block, jnp.zeros_like(block))  3.62 us
    broadcast_in_dim x1, other arithmetic, local(): grad_rows.astype(jnp.bfloat16)[None]  3.6 us
  transfers between devices with their start and end apart: 4, of which 4 were waited for; matrix products, arithmetic and copies ran while one was open for 11% of the time, Pallas kernels for 0%

profile of v16, /device:TPU:11, one launch (start us, length us, event | category | flops | bytes accessed | tf_op | source)
XLA Modules:
  0.0 123.7 jit_solution(10608397263417945749)
XLA Ops:
  0.6 0.0 copy-start
  0.7 0.8 select_reduce_fusion.2
  1.5 0.1 convolution_convert_fusion.3
  1.6 0.2 select_reduce_fusion
  1.8 0.1 broadcast_in_dim.72
  1.9 0.1 eq.80
  2.0 0.1 fusion.17
  2.1 1.0 pad_maximum_fusion.4
  3.1 2.0 %multiply_convert_fusion = bf16[512,2048]{1,0:T(8,128)(2,1)} fusion(pred[512,64]{1,0:T(32,128)(4,1)S(1)} %fusion.17, bf16[64,2048]{1,0:T(8,128)(2,1)S(1)} %pad_maximum_fusion.4, f32[512]{0:T(512)S(1)} %broadcast_in_dim.72, pred[2048]{0:T(1024)(128)(4,1)S(1)} %iota_compare_fusion.5), kind=kOutput, calls=%fused_computation | convolution fusion | flops 137363456 | bytes 2396160 | tf_op jit(solution)/shard_map/dot_general | solution.py:54
  5.1 6.6 %all-to-all-start = ((bf16[16,32,2048]{2,1,0:T(8,128)(2,1)}), bf16[16,32,2048]{2,1,0:T(8,128)(2,1)S(1)}, u32[]{:S(2)}, u32[]{:S(2)}) async-start(bf16[16,32,2048]{2,1,0:T(8,128)(2,1)} %bitcast.38), calls=%async_computation | async-start | bytes 4194304 | tf_op jit(solution)/shard_map/all_to_all | solution.py:58
  11.7 1.2 %collective-permute-start = (bf16[512,1408]{1,0:T(8,128)(2,1)}, bf16[512,1408]{1,0:T(8,128)(2,1)}, u32[]{:S(2)}, u32[]{:S(2)}) collective-permute-start(bf16[512,1408]{1,0:T(8,128)(2,1)} %bitcast.39), channel_id=1, source_target_pairs={{0,16},{16,0},{1,17},{17,1},{2,18},{18,2},{3,19},{19,3},{4,20},{20... | collective-permute-start | bytes 4325384 | tf_op jit(solution)/shard_map/ppermute | solution.py:11
  12.9 31.9 %collective-permute-done = bf16[512,1408]{1,0:T(8,128)(2,1)} collective-permute-done((bf16[512,1408]{1,0:T(8,128)(2,1)}, bf16[512,1408]{1,0:T(8,128)(2,1)}, u32[]{:S(2)}, u32[]{:S(2)}) %collective-permute-start) | collective-permute-done | bytes 1441824 | tf_op jit(solution)/shard_map/ppermute | solution.py:11
  44.8 3.6 %broadcast_select_fusion = (bf16[512,1408]{1,0:T(8,128)(2,1)}, bf16[512,1408]{1,0:T(8,128)(2,1)}) fusion(bf16[512,1408]{1,0:T(8,128)(2,1)} %collective-permute-done, pred[]{:T(512)S(6)} %ge.3, bf16[512,1408]{1,0:T(8,128)(2,1)} %bitcast.40), kind=kLoop, calls=%fused_computation.18 | loop fusion | flops 1441792 | bytes 5767169 | tf_op jit(solution)/shard_map/jit(_where)/select_n | solution.py:17
  48.4 10.7 %all-to-all-done = bf16[16,32,2048]{2,1,0:T(8,128)(2,1)S(1)} async-done(((bf16[16,32,2048]{2,1,0:T(8,128)(2,1)}), bf16[16,32,2048]{2,1,0:T(8,128)(2,1)S(1)}, u32[]{:S(2)}, u32[]{:S(2)}) %all-to-all-start) | async-done | bytes 2097184 | tf_op jit(solution)/shard_map/all_to_all | solution.py:58
  59.1 0.0 copy-start.3
  59.1 0.1 slice.24
  59.2 0.0 copy-done
  59.2 0.0 copy-start.4
  59.2 0.9 fusion.2
  60.1 0.3 copy-done.3
  60.4 0.8 copy-done.4
  61.2 0.0 copy-start.5
  61.2 1.0 fusion.12
  62.2 0.4 copy-done.5
  62.6 1.0 convolution_add_fusion
  63.6 1.1 convolution_convert_fusion
  64.7 0.9 multiply_convert_fusion.2
  65.6 0.0 copy-start.6
  65.6 0.0 copy-start.7
  65.6 0.2 dynamic_update_slice.9
  65.9 1.0 fusion.5
  66.9 0.0 copy-done.6
  66.9 0.0 copy-done.7
  66.9 1.0 fusion.6
  68.0 0.0 copy-start.2
  68.0 1.3 %copy-done.2 = bf16[512,2048]{1,0:T(8,128)(2,1)} copy-done((bf16[512,2048]{1,0:T(8,128)(2,1)}, bf16[512,2048]{1,0:T(8,128)(2,1)S(1)}, u32[]{:S(2)}) %copy-start.2) | copy-done | bytes 2097176
  69.3 4.9 %all-to-all-start.1 = ((bf16[16,32,2048]{2,1,0:T(8,128)(2,1)}), bf16[16,32,2048]{2,1,0:T(8,128)(2,1)S(1)}, u32[]{:S(2)}, u32[]{:S(2)}) async-start(bf16[16,32,2048]{2,1,0:T(8,128)(2,1)} %bitcast.34), calls=%async_computation.1 | async-start | bytes 4194304 | tf_op jit(solution)/shard_map/all_to_all | solution.py:104
  74.2 3.5 %fusion.14 = f32[1024,1408]{1,0:T(8,128)S(1)} fusion(bf16[512,704]{0,1:T(8,128)(2,1)} %copy-done.7, bf16[512,704]{0,1:T(8,128)(2,1)} %copy-done.6, bf16[512,2048]{1,0:T(8,128)(2,1)} %bitcast.37), kind=kOutput, calls=%fused_computation.32 | convolution fusion | flops 1479278592 | bytes 8257536 | tf_op jit(solution)/shard_map/dot_general | solution.py:124
  77.7 0.0 copy-start.1
  77.7 2.5 %copy-done.1 = f32[1024,1408]{1,0:T(8,128)} copy-done((f32[1024,1408]{1,0:T(8,128)}, f32[1024,1408]{1,0:T(8,128)S(1)}, u32[]{:S(2)}) %copy-start.1) | copy-done | bytes 5767192
  80.2 0.0 copy-start.9
  80.2 1.2 %dynamic-slice_convert_fusion = bf16[512,1408]{1,0:T(8,128)(2,1)} fusion(f32[1024,1408]{1,0:T(8,128)S(1)} %fusion.14, s32[]{:T(128)S(6)} %select_n.76), kind=kLoop, calls=%fused_computation.3 | loop fusion | bytes 2883588 | tf_op jit(solution)/shard_map/convert_element_type | solution.py:134
  81.5 1.2 collective-permute-start.1
  82.7 1.6 %convert_element_type.55 = f32[64,1024]{1,0:T(8,128)} convert(bf16[64,1024]{1,0:T(8,128)(2,1)} %param.7) | non-fusion elementwise | flops 65536 | bytes 393216 | tf_op jit(solution)/shard_map/convert_element_type | solution.py:123
  84.3 0.0 copy-done.9
  84.4 30.2 %collective-permute-done.1 = bf16[512,1408]{1,0:T(8,128)(2,1)} collective-permute-done((bf16[512,1408]{1,0:T(8,128)(2,1)}, bf16[512,1408]{1,0:T(8,128)(2,1)}, u32[]{:S(2)}, u32[]{:S(2)}) %collective-permute-start.1) | collective-permute-done | bytes 1441824 | tf_op jit(solution)/shard_map/ppermute | solution.py:133
  114.6 3.6 %fusion = bf16[1,512,1408]{2,1,0:T(8,128)(2,1)} fusion(bf16[512,1408]{1,0:T(8,128)(2,1)} %collective-permute-done.1, f32[1024,1408]{1,0:T(8,128)} %copy-done.1, s32[]{:T(128)S(6)} %select_n.74), kind=kLoop, calls=%fused_computation.8 | loop fusion | flops 2162688 | bytes 5767172 | tf_op jit(solution)/shard_map/broadcast_in_dim | solution.py:139
  118.2 3.5 %all-to-all-done.1 = bf16[16,32,2048]{2,1,0:T(8,128)(2,1)S(1)} async-done(((bf16[16,32,2048]{2,1,0:T(8,128)(2,1)}), bf16[16,32,2048]{2,1,0:T(8,128)(2,1)S(1)}, u32[]{:S(2)}, u32[]{:S(2)}) %all-to-all-start.1) | async-done | bytes 2097184 | tf_op jit(solution)/shard_map/all_to_all | solution.py:104
  121.6 0.0 copy-start.8
  121.6 0.0 copy-start.10
  121.6 1.0 fusion.9
  122.7 0.0 copy-done.8
  122.7 0.0 copy-done.10
  122.7 1.0 multiply_reduce_fusion
  (5 shorter events, 0.0 us)
Async XLA Ops:
  0.6 58.5 %copy-start = (bf16[1,704,1024]{2,1,0:T(8,128)(2,1)S(1)}, bf16[1,704,1024]{2,1,0:T(8,128)(2,1)}, u32[]{:S(2)}) copy-start(bf16[1,704,1024]{2,1,0:T(8,128)(2,1)} %param.11) | copy-start | bytes 4325380
  5.1 54.0 %all-to-all-start = ((bf16[16,32,2048]{2,1,0:T(8,128)(2,1)}), bf16[16,32,2048]{2,1,0:T(8,128)(2,1)S(1)}, u32[]{:S(2)}, u32[]{:S(2)}) async-start(bf16[16,32,2048]{2,1,0:T(8,128)(2,1)} %bitcast.38), calls=%async_computation | async-start | bytes 4194304 | tf_op jit(solution)/shard_map/all_to_all | solution.py:58
  11.7 33.1 %collective-permute-start = (bf16[512,1408]{1,0:T(8,128)(2,1)}, bf16[512,1408]{1,0:T(8,128)(2,1)}, u32[]{:S(2)}, u32[]{:S(2)}) collective-permute-start(bf16[512,1408]{1,0:T(8,128)(2,1)} %bitcast.39), channel_id=1, source_target_pairs={{0,16},{16,0},{1,17},{17,1},{2,18},{18,2},{3,19},{19,3},{4,20},{20... | collective-permute-start | bytes 4325384 | tf_op jit(solution)/shard_map/ppermute | solution.py:11
  59.1 1.3 %copy-start.3 = (bf16[16,32,2048]{2,1,0:T(8,128)(2,1)}, bf16[16,32,2048]{2,1,0:T(8,128)(2,1)S(1)}, u32[]{:S(2)}) copy-start(bf16[16,32,2048]{2,1,0:T(8,128)(2,1)S(1)} %all-to-all-done) | copy-start | bytes 6291460
  59.2 2.1 %copy-start.4 = (bf16[512,1408]{1,0:T(8,128)(2,1)S(1)}, bf16[512,1408]{1,0:T(8,128)(2,1)}, u32[]{:S(2)}) copy-start(bf16[512,1408]{1,0:T(8,128)(2,1)} %get-tuple-element.15) | copy-start | bytes 4325380
  61.2 1.4 %copy-start.5 = (bf16[512,1408]{1,0:T(8,128)(2,1)S(1)}, bf16[512,1408]{1,0:T(8,128)(2,1)}, u32[]{:S(2)}) copy-start(bf16[512,1408]{1,0:T(8,128)(2,1)} %get-tuple-element.16) | copy-start | bytes 4325380
  65.6 1.3 %copy-start.6 = (bf16[512,704]{0,1:T(8,128)(2,1)}, bf16[512,704]{0,1:T(8,128)(2,1)S(1)}, u32[]{:S(2)}) copy-start(bf16[512,704]{0,1:T(8,128)(2,1)S(1)} %get-tuple-element.21) | copy-start | bytes 2162692
  65.6 1.3 %copy-start.7 = (bf16[512,704]{0,1:T(8,128)(2,1)}, bf16[512,704]{0,1:T(8,128)(2,1)S(1)}, u32[]{:S(2)}) copy-start(bf16[512,704]{0,1:T(8,128)(2,1)S(1)} %get-tuple-element.22) | copy-start | bytes 2162692
  68.0 1.3 %copy-start.2 = (bf16[512,2048]{1,0:T(8,128)(2,1)}, bf16[512,2048]{1,0:T(8,128)(2,1)S(1)}, u32[]{:S(2)}) copy-start(bf16[512,2048]{1,0:T(8,128)(2,1)S(1)} %fusion.6) | copy-start | bytes 6291460
  69.3 52.3 %all-to-all-start.1 = ((bf16[16,32,2048]{2,1,0:T(8,128)(2,1)}), bf16[16,32,2048]{2,1,0:T(8,128)(2,1)S(1)}, u32[]{:S(2)}, u32[]{:S(2)}) async-start(bf16[16,32,2048]{2,1,0:T(8,128)(2,1)} %bitcast.34), calls=%async_computation.1 | async-start | bytes 4194304 | tf_op jit(solution)/shard_map/all_to_all | solution.py:104
  77.7 2.5 %copy-start.1 = (f32[1024,1408]{1,0:T(8,128)}, f32[1024,1408]{1,0:T(8,128)S(1)}, u32[]{:S(2)}) copy-start(f32[1024,1408]{1,0:T(8,128)S(1)} %fusion.14) | copy-start | bytes 17301508
  80.2 4.1 %copy-start.9 = (s32[64,6]{0,1:T(8,128)S(1)}, s32[64,6]{0,1:T(8,128)}, u32[]{:S(2)}) copy-start(s32[64,6]{0,1:T(8,128)} %param.8) | copy-start | bytes 4612
  81.5 33.1 %collective-permute-start.1 = (bf16[512,1408]{1,0:T(8,128)(2,1)}, bf16[512,1408]{1,0:T(8,128)(2,1)}, u32[]{:S(2)}, u32[]{:S(2)}) collective-permute-start(bf16[512,1408]{1,0:T(8,128)(2,1)} %dynamic-slice_convert_fusion), channel_id=1, source_target_pairs={{0,16},{16,0},{1,17},{17,1},{2,18},{18,2},{3,19},{19,3},{4,20},{20... | collective-permute-start | bytes 4325384 | tf_op jit(solution)/shard_map/ppermute | solution.py:133
  121.6 1.0 copy-start.8
  121.6 1.0 copy-start.10

commit v17 on v15

--- a/solution.py
+++ b/solution.py
@@ -31,7 +31,10 @@
     capacity = 4 * token_count * top_count // (3 * experts)
     weight_blocks = gather_rows(w_gate_up[0], "dp", block_rows)
     hit = expert_ids[:, :, None] == jnp.arange(experts, dtype=jnp.int32)[None, None, :]
-    token_prob = jnp.sum(jnp.where(hit, gate_probs[:, :, None], 0.0), axis=1)
+    token_prob = None
+    for choice in range(top_count):
+        term = jnp.where(hit[:, choice, :], gate_probs[:, choice : choice + 1], 0.0)
+        token_prob = term if token_prob is None else token_prob + term
     token_hit = token_prob > 0.0
     earlier = (
         lax.broadcasted_iota(jnp.int32, (token_count, token_count), 0)

time: 124 us -> 125 us (level)
  no operation moved by 1% of the time
where the time goes in v17:
time: 125 us
  waiting for transfers between devices  76.3 us (61%)
  starting transfers between devices  13.9 us (11%)
  matrix products  13.7 us (11%)
  other arithmetic  11.8 us (9%)
  local copies, waits for them, and re-layouts  7.93 us (6%)
    ppermute x1, waiting for transfers between devices, gather_rows(): lax.ppermute(own, axis_name, [(i, (i + shift) % count) for i in range(cou...  31.9 us
    ppermute x1, waiting for transfers between devices, local(): lax.ppermute(grad_block((me_dp + shift) % replicas).astype(jnp.bfloat16),...  30.2 us
    all_to_all x1, waiting for transfers between devices, local(): lax.all_to_all(both_send.reshape(experts, capacity, 2 * model_width), 'ex...  10.7 us
    all_to_all x1, starting transfers between devices, local(): lax.all_to_all(both_send.reshape(experts, capacity, 2 * model_width), 'ex...  6.55 us
    unnamed x22, local copies, waits for them, and re-layouts  5.3 us
    all_to_all x1, starting transfers between devices, local(): lax.all_to_all(send_back.reshape(experts, capacity, 2 * model_width), 'ex...  4.91 us
    select_n x1, other arithmetic, gather_rows(): jnp.where(keep, block, jnp.zeros_like(block))  3.61 us
    broadcast_in_dim x1, other arithmetic, local(): grad_rows.astype(jnp.bfloat16)[None]  3.6 us
  transfers between devices with their start and end apart: 4, of which 4 were waited for; matrix products, arithmetic and copies ran while one was open for 11% of the time, Pallas kernels for 0%

profile of v17, /device:TPU:11, one launch (start us, length us, event | category | flops | bytes accessed | tf_op | source)
XLA Modules:
  0.0 124.5 jit_solution(4732880195308440915)
XLA Ops:
  0.6 0.0 copy-start
  0.7 0.9 slice_bitcast_fusion.11
  1.6 0.7 iota_compare_fusion.2
  2.3 0.1 convolution_convert_fusion.3
  2.5 0.1 eq.80
  2.5 0.1 select_reduce_fusion
  2.7 0.1 broadcast_in_dim.124
  2.8 0.1 fusion.20
  2.9 3.0 %multiply_convert_fusion = bf16[512,2048]{1,0:T(8,128)(2,1)} fusion(pred[512,64]{1,0:T(32,128)(4,1)S(1)} %fusion.20, f32[512]{0:T(512)S(1)} %broadcast_in_dim.124, pred[2048]{0:T(1024)(128)(4,1)S(1)} %iota_compare_fusion.5, bf16[64,1024]{1,0:T(8,128)(2,1)} %param.7, bf16[64,1024]{1,0:T(8,128)(2,1)} %param.6), kind=kOutput, calls=%fused_computation | convolution fusion | flops 137887744 | bytes 2396160 | tf_op jit(solution)/shard_map/dot_general | solution.py:56
  5.9 6.6 %all-to-all-start = ((bf16[16,32,2048]{2,1,0:T(8,128)(2,1)}), bf16[16,32,2048]{2,1,0:T(8,128)(2,1)S(1)}, u32[]{:S(2)}, u32[]{:S(2)}) async-start(bf16[16,32,2048]{2,1,0:T(8,128)(2,1)} %bitcast.130), calls=%async_computation | async-start | bytes 4194304 | tf_op jit(solution)/shard_map/all_to_all | solution.py:62
  12.5 1.2 collective-permute-start
  13.7 31.9 %collective-permute-done = bf16[512,1408]{1,0:T(8,128)(2,1)} collective-permute-done((bf16[512,1408]{1,0:T(8,128)(2,1)}, bf16[512,1408]{1,0:T(8,128)(2,1)}, u32[]{:S(2)}, u32[]{:S(2)}) %collective-permute-start) | collective-permute-done | bytes 1441824 | tf_op jit(solution)/shard_map/ppermute | solution.py:11
  45.6 3.6 %broadcast_select_fusion = (bf16[512,1408]{1,0:T(8,128)(2,1)}, bf16[512,1408]{1,0:T(8,128)(2,1)}) fusion(bf16[512,1408]{1,0:T(8,128)(2,1)} %collective-permute-done, pred[]{:T(512)S(6)} %ge.3, bf16[512,1408]{1,0:T(8,128)(2,1)} %bitcast.132), kind=kLoop, calls=%fused_computation.18 | loop fusion | flops 1441792 | bytes 5767169 | tf_op jit(solution)/shard_map/jit(_where)/select_n | solution.py:17
  49.2 10.7 %all-to-all-done = bf16[16,32,2048]{2,1,0:T(8,128)(2,1)S(1)} async-done(((bf16[16,32,2048]{2,1,0:T(8,128)(2,1)}), bf16[16,32,2048]{2,1,0:T(8,128)(2,1)S(1)}, u32[]{:S(2)}, u32[]{:S(2)}) %all-to-all-start) | async-done | bytes 2097184 | tf_op jit(solution)/shard_map/all_to_all | solution.py:62
  59.9 0.0 copy-start.3
  59.9 0.1 slice.78
  60.0 0.0 copy-done
  60.0 0.0 copy-start.4
  60.0 0.9 fusion.2
  60.9 0.3 copy-done.3
  61.3 0.8 copy-done.4
  62.0 0.0 copy-start.5
  62.0 1.0 fusion.12
  63.0 0.4 copy-done.5
  63.4 1.0 convolution_add_fusion
  64.4 1.1 convolution_convert_fusion
  65.5 0.9 multiply_convert_fusion.2
  66.4 0.0 copy-start.6
  66.4 0.0 copy-start.7
  66.4 0.2 dynamic_update_slice.9
  66.7 1.0 fusion.5
  67.7 0.0 copy-done.6
  67.7 0.0 copy-done.7
  67.7 1.0 fusion.6
  68.8 0.0 copy-start.2
  68.8 1.3 %copy-done.2 = bf16[512,2048]{1,0:T(8,128)(2,1)} copy-done((bf16[512,2048]{1,0:T(8,128)(2,1)}, bf16[512,2048]{1,0:T(8,128)(2,1)S(1)}, u32[]{:S(2)}) %copy-start.2) | copy-done | bytes 2097176
  70.1 4.9 %all-to-all-start.1 = ((bf16[16,32,2048]{2,1,0:T(8,128)(2,1)}), bf16[16,32,2048]{2,1,0:T(8,128)(2,1)S(1)}, u32[]{:S(2)}, u32[]{:S(2)}) async-start(bf16[16,32,2048]{2,1,0:T(8,128)(2,1)} %bitcast.126), calls=%async_computation.1 | async-start | bytes 4194304 | tf_op jit(solution)/shard_map/all_to_all | solution.py:108
  75.0 3.5 %fusion.14 = f32[1024,1408]{1,0:T(8,128)S(1)} fusion(bf16[512,704]{0,1:T(8,128)(2,1)} %copy-done.7, bf16[512,704]{0,1:T(8,128)(2,1)} %copy-done.6, bf16[512,2048]{1,0:T(8,128)(2,1)} %bitcast.129), kind=kOutput, calls=%fused_computation.32 | convolution fusion | flops 1479278592 | bytes 8257536 | tf_op jit(solution)/shard_map/dot_general | solution.py:128
  78.5 0.0 copy-start.1
  78.5 2.5 %copy-done.1 = f32[1024,1408]{1,0:T(8,128)} copy-done((f32[1024,1408]{1,0:T(8,128)}, f32[1024,1408]{1,0:T(8,128)S(1)}, u32[]{:S(2)}) %copy-start.1) | copy-done | bytes 5767192
  81.0 0.0 copy-start.9
  81.0 1.2 %dynamic-slice_convert_fusion = bf16[512,1408]{1,0:T(8,128)(2,1)} fusion(f32[1024,1408]{1,0:T(8,128)S(1)} %fusion.14, s32[]{:T(128)S(6)} %select_n.96), kind=kLoop, calls=%fused_computation.3 | loop fusion | bytes 2883588 | tf_op jit(solution)/shard_map/convert_element_type | solution.py:138
  82.2 1.2 collective-permute-start.1
  83.5 1.6 %convert_element_type.55 = f32[64,1024]{1,0:T(8,128)} convert(bf16[64,1024]{1,0:T(8,128)(2,1)} %param.7) | non-fusion elementwise | flops 65536 | bytes 393216 | tf_op jit(solution)/shard_map/convert_element_type | solution.py:127
  85.1 0.0 copy-done.9
  85.1 30.2 %collective-permute-done.1 = bf16[512,1408]{1,0:T(8,128)(2,1)} collective-permute-done((bf16[512,1408]{1,0:T(8,128)(2,1)}, bf16[512,1408]{1,0:T(8,128)(2,1)}, u32[]{:S(2)}, u32[]{:S(2)}) %collective-permute-start.1) | collective-permute-done | bytes 1441824 | tf_op jit(solution)/shard_map/ppermute | solution.py:137
  115.4 3.6 %fusion = bf16[1,512,1408]{2,1,0:T(8,128)(2,1)} fusion(bf16[512,1408]{1,0:T(8,128)(2,1)} %collective-permute-done.1, f32[1024,1408]{1,0:T(8,128)} %copy-done.1, s32[]{:T(128)S(6)} %select_n.94), kind=kLoop, calls=%fused_computation.8 | loop fusion | flops 2162688 | bytes 5767172 | tf_op jit(solution)/shard_map/broadcast_in_dim | solution.py:143
  119.0 3.5 %all-to-all-done.1 = bf16[16,32,2048]{2,1,0:T(8,128)(2,1)S(1)} async-done(((bf16[16,32,2048]{2,1,0:T(8,128)(2,1)}), bf16[16,32,2048]{2,1,0:T(8,128)(2,1)S(1)}, u32[]{:S(2)}, u32[]{:S(2)}) %all-to-all-start.1) | async-done | bytes 2097184 | tf_op jit(solution)/shard_map/all_to_all | solution.py:108
  122.4 0.0 copy-start.8
  122.4 0.0 copy-start.10
  122.4 1.0 fusion.9
  123.5 0.0 copy-done.8
  123.5 0.0 copy-done.10
  123.5 1.0 multiply_reduce_fusion
  (6 shorter events, 0.1 us)
Async XLA Ops:
  0.6 59.3 %copy-start = (bf16[1,704,1024]{2,1,0:T(8,128)(2,1)S(1)}, bf16[1,704,1024]{2,1,0:T(8,128)(2,1)}, u32[]{:S(2)}) copy-start(bf16[1,704,1024]{2,1,0:T(8,128)(2,1)} %param.11) | copy-start | bytes 4325380
  5.9 54.0 %all-to-all-start = ((bf16[16,32,2048]{2,1,0:T(8,128)(2,1)}), bf16[16,32,2048]{2,1,0:T(8,128)(2,1)S(1)}, u32[]{:S(2)}, u32[]{:S(2)}) async-start(bf16[16,32,2048]{2,1,0:T(8,128)(2,1)} %bitcast.130), calls=%async_computation | async-start | bytes 4194304 | tf_op jit(solution)/shard_map/all_to_all | solution.py:62
  12.5 33.1 %collective-permute-start = (bf16[512,1408]{1,0:T(8,128)(2,1)}, bf16[512,1408]{1,0:T(8,128)(2,1)}, u32[]{:S(2)}, u32[]{:S(2)}) collective-permute-start(bf16[512,1408]{1,0:T(8,128)(2,1)} %bitcast.131), channel_id=1, source_target_pairs={{0,16},{16,0},{1,17},{17,1},{2,18},{18,2},{3,19},{19,3},{4,20},{20... | collective-permute-start | bytes 4325384 | tf_op jit(solution)/shard_map/ppermute | solution.py:11
  59.9 1.4 %copy-start.3 = (bf16[16,32,2048]{2,1,0:T(8,128)(2,1)}, bf16[16,32,2048]{2,1,0:T(8,128)(2,1)S(1)}, u32[]{:S(2)}) copy-start(bf16[16,32,2048]{2,1,0:T(8,128)(2,1)S(1)} %all-to-all-done) | copy-start | bytes 6291460
  60.0 2.1 %copy-start.4 = (bf16[512,1408]{1,0:T(8,128)(2,1)S(1)}, bf16[512,1408]{1,0:T(8,128)(2,1)}, u32[]{:S(2)}) copy-start(bf16[512,1408]{1,0:T(8,128)(2,1)} %get-tuple-element.15) | copy-start | bytes 4325380
  62.0 1.4 %copy-start.5 = (bf16[512,1408]{1,0:T(8,128)(2,1)S(1)}, bf16[512,1408]{1,0:T(8,128)(2,1)}, u32[]{:S(2)}) copy-start(bf16[512,1408]{1,0:T(8,128)(2,1)} %get-tuple-element.16) | copy-start | bytes 4325380
  66.4 1.3 %copy-start.6 = (bf16[512,704]{0,1:T(8,128)(2,1)}, bf16[512,704]{0,1:T(8,128)(2,1)S(1)}, u32[]{:S(2)}) copy-start(bf16[512,704]{0,1:T(8,128)(2,1)S(1)} %get-tuple-element.21) | copy-start | bytes 2162692
  66.4 1.3 %copy-start.7 = (bf16[512,704]{0,1:T(8,128)(2,1)}, bf16[512,704]{0,1:T(8,128)(2,1)S(1)}, u32[]{:S(2)}) copy-start(bf16[512,704]{0,1:T(8,128)(2,1)S(1)} %get-tuple-element.22) | copy-start | bytes 2162692
  68.8 1.3 %copy-start.2 = (bf16[512,2048]{1,0:T(8,128)(2,1)}, bf16[512,2048]{1,0:T(8,128)(2,1)S(1)}, u32[]{:S(2)}) copy-start(bf16[512,2048]{1,0:T(8,128)(2,1)S(1)} %fusion.6) | copy-start | bytes 6291460
  70.1 52.3 %all-to-all-start.1 = ((bf16[16,32,2048]{2,1,0:T(8,128)(2,1)}), bf16[16,32,2048]{2,1,0:T(8,128)(2,1)S(1)}, u32[]{:S(2)}, u32[]{:S(2)}) async-start(bf16[16,32,2048]{2,1,0:T(8,128)(2,1)} %bitcast.126), calls=%async_computation.1 | async-start | bytes 4194304 | tf_op jit(solution)/shard_map/all_to_all | solution.py:108
  78.5 2.5 %copy-start.1 = (f32[1024,1408]{1,0:T(8,128)}, f32[1024,1408]{1,0:T(8,128)S(1)}, u32[]{:S(2)}) copy-start(f32[1024,1408]{1,0:T(8,128)S(1)} %fusion.14) | copy-start | bytes 17301508
  81.0 4.1 %copy-start.9 = (s32[64,6]{0,1:T(8,128)S(1)}, s32[64,6]{0,1:T(8,128)}, u32[]{:S(2)}) copy-start(s32[64,6]{0,1:T(8,128)} %param.8) | copy-start | bytes 4612
  82.2 33.1 %collective-permute-start.1 = (bf16[512,1408]{1,0:T(8,128)(2,1)}, bf16[512,1408]{1,0:T(8,128)(2,1)}, u32[]{:S(2)}, u32[]{:S(2)}) collective-permute-start(bf16[512,1408]{1,0:T(8,128)(2,1)} %dynamic-slice_convert_fusion), channel_id=1, source_target_pairs={{0,16},{16,0},{1,17},{17,1},{2,18},{18,2},{3,19},{19,3},{4,20},{20... | collective-permute-start | bytes 4325384 | tf_op jit(solution)/shard_map/ppermute | solution.py:137
  122.4 1.0 copy-start.8
  122.4 1.0 copy-start.10

commit v18 on v15

--- a/solution.py
+++ b/solution.py
@@ -111,8 +111,10 @@
         concat_axis=0,
         tiled=True,
     ).reshape(experts * capacity, 2 * model_width)
-    owned = (target_rows.reshape(token_count * top_count)[:, None] == slots[None, :]).astype(
-        jnp.bfloat16
+    owned = lax.optimization_barrier(
+        (target_rows.reshape(token_count * top_count)[:, None] == slots[None, :]).astype(
+            jnp.bfloat16
+        )
     )
     slot_both = jnp.dot(owned, back, preferred_element_type=jnp.float32).reshape(
         token_count, top_count, 2 * model_width

time: 124 us -> 127 us (1.024)
  waiting for transfers between devices: 76.2 us -> 71.8 us
  local copies, waits for them, and re-layouts: 7.04 us -> 10.7 us
  matrix products: 13.7 us -> 16.4 us
    ppermute x1, waiting for transfers between devices: 30.2 us -> 25.8 us  [local(): lax.ppermute(grad_block((me_dp + shift) % replicas).astype(jnp.bfloat16),...]
    dot_general x0 -> x1, local copies, waits for them, and re-layouts: none -> 1.93 us  [local(): jnp.dot(owned, back, preferred_element_type=jnp.float32)]
    dot_general x2, matrix products: 2.06 us -> 3.74 us  [local(): lax.dot_general(pair_cot, weight, (((1,), (1,)), ((), ())), preferred_ele...]
    dynamic_update_slice x1, local copies, waits for them, and re-layouts: 0.24 us -> 1.74 us  [local(): lax.dynamic_update_slice_in_dim(send_back, output_rows, 0, axis=1)]
    unnamed x22 -> x20, local copies, waits for them, and re-layouts: 5.33 us -> 3.99 us
  transfers between devices with their start and end apart: 4 -> 4, of which waited for: 4 -> 4; matrix products, arithmetic and copies ran while one was open for 11% -> 14% of each run, Pallas kernels for 0% -> 0%
where the time goes in v18:
time: 127 us
  waiting for transfers between devices  71.8 us (57%)
  matrix products  16.4 us (13%)
  starting transfers between devices  13.9 us (11%)
  other arithmetic  12.9 us (10%)
  local copies, waits for them, and re-layouts  10.7 us (8%)
    ppermute x1, waiting for transfers between devices, gather_rows(): lax.ppermute(own, axis_name, [(i, (i + shift) % count) for i in range(cou...  31.9 us
    ppermute x1, waiting for transfers between devices, local(): lax.ppermute(grad_block((me_dp + shift) % replicas).astype(jnp.bfloat16),...  25.8 us
    all_to_all x1, waiting for transfers between devices, local(): lax.all_to_all(both_send.reshape(experts, capacity, 2 * model_width), 'ex...  10.7 us
    all_to_all x1, starting transfers between devices, local(): lax.all_to_all(both_send.reshape(experts, capacity, 2 * model_width), 'ex...  6.55 us
    all_to_all x1, starting transfers between devices, local(): lax.all_to_all(send_back.reshape(experts, capacity, 2 * model_width), 'ex...  4.91 us
    unnamed x20, local copies, waits for them, and re-layouts  3.99 us
    dot_general x2, matrix products, local(): lax.dot_general(pair_cot, weight, (((1,), (1,)), ((), ())), preferred_ele...  3.74 us
    select_n x1, other arithmetic, gather_rows(): jnp.where(keep, block, jnp.zeros_like(block))  3.62 us
  transfers between devices with their start and end apart: 4, of which 4 were waited for; matrix products, arithmetic and copies ran while one was open for 14% of the time, Pallas kernels for 0%

profile of v18, /device:TPU:11, one launch (start us, length us, event | category | flops | bytes accessed | tf_op | source)
XLA Modules:
  0.0 126.6 jit_solution(12232556342965022530)
XLA Ops:
  0.6 0.0 copy-start
  0.7 0.8 select_reduce_fusion.2
  1.5 0.1 convolution_convert_fusion.3
  1.6 0.2 select_reduce_fusion
  1.8 0.1 broadcast_in_dim.72
  1.9 0.1 eq.66
  2.0 0.1 fusion.19
  2.1 3.0 %multiply_convert_fusion = bf16[512,2048]{1,0:T(8,128)(2,1)} fusion(pred[512,64]{1,0:T(32,128)(4,1)S(1)} %fusion.19, f32[512]{0:T(512)S(1)} %broadcast_in_dim.72, pred[2048]{0:T(1024)(128)(4,1)S(1)} %iota_compare_fusion.5, bf16[64,1024]{1,0:T(8,128)(2,1)} %param.7, bf16[64,1024]{1,0:T(8,128)(2,1)} %param.6), kind=kOutput, calls=%fused_computation | convolution fusion | flops 137887744 | bytes 2396160 | tf_op jit(solution)/shard_map/dot_general | solution.py:53
  5.1 6.6 %all-to-all-start = ((bf16[16,32,2048]{2,1,0:T(8,128)(2,1)}), bf16[16,32,2048]{2,1,0:T(8,128)(2,1)S(1)}, u32[]{:S(2)}, u32[]{:S(2)}) async-start(bf16[16,32,2048]{2,1,0:T(8,128)(2,1)} %bitcast.33), calls=%async_computation | async-start | bytes 4194304 | tf_op jit(solution)/shard_map/all_to_all | solution.py:59
  11.7 1.2 collective-permute-start
  12.9 31.9 %collective-permute-done = bf16[512,1408]{1,0:T(8,128)(2,1)} collective-permute-done((bf16[512,1408]{1,0:T(8,128)(2,1)}, bf16[512,1408]{1,0:T(8,128)(2,1)}, u32[]{:S(2)}, u32[]{:S(2)}) %collective-permute-start) | collective-permute-done | bytes 1441824 | tf_op jit(solution)/shard_map/ppermute | solution.py:11
  44.8 3.6 %broadcast_select_fusion = (bf16[512,1408]{1,0:T(8,128)(2,1)}, bf16[512,1408]{1,0:T(8,128)(2,1)}) fusion(bf16[512,1408]{1,0:T(8,128)(2,1)} %collective-permute-done, pred[]{:T(512)S(6)} %ge.3, bf16[512,1408]{1,0:T(8,128)(2,1)} %bitcast.35), kind=kLoop, calls=%fused_computation.18 | loop fusion | flops 1441792 | bytes 5767169 | tf_op jit(solution)/shard_map/jit(_where)/select_n | solution.py:17
  48.4 10.7 %all-to-all-done = bf16[16,32,2048]{2,1,0:T(8,128)(2,1)S(1)} async-done(((bf16[16,32,2048]{2,1,0:T(8,128)(2,1)}), bf16[16,32,2048]{2,1,0:T(8,128)(2,1)S(1)}, u32[]{:S(2)}, u32[]{:S(2)}) %all-to-all-start) | async-done | bytes 2097184 | tf_op jit(solution)/shard_map/all_to_all | solution.py:59
  59.1 0.0 copy-start.2
  59.1 0.1 slice.24
  59.2 0.0 copy-done
  59.2 0.0 copy-start.3
  59.2 1.0 fusion.2
  60.1 0.3 copy-done.2
  60.4 0.8 copy-done.3
  61.2 0.0 copy-start.4
  61.2 1.0 fusion.10
  62.2 0.4 copy-done.4
  62.6 1.0 convolution_add_fusion
  63.5 1.1 convolution_convert_fusion
  64.7 0.9 multiply_convert_fusion.2
  65.6 0.0 copy-start.5
  65.6 0.0 copy-start.6
  65.6 1.7 %dynamic_update_slice.9 = bf16[512,2048]{1,0:T(8,128)(2,1)} pad(bf16[512,1024]{1,0:T(8,128)(2,1)S(1)} %convolution_convert_fusion, bf16[]{:T(256)} %constant.48.clone.1), padding=0_0x0_1024 | pad | bytes 3145730 | tf_op jit(solution)/shard_map/dynamic_update_slice | solution.py:97
  67.4 1.9 %fusion.5 = bf16[512,2048]{1,0:T(8,128)(2,1)} fusion(bf16[512,2048]{1,0:T(8,128)(2,1)} %dynamic_update_slice.9, s32[]{:T(128)S(6)} %select_n.72, bf16[512,1408]{1,0:T(8,128)(2,1)S(1)} %copy-done.3, bf16[512,704]{0,1:T(8,128)(2,1)S(1)} %get-tuple-element.22, bf16[512,704]{0,1:T(8,128)(2,1)S(1)} %get-tuple-element.21), kind=kOutput, calls=%fused_computation.22 | convolution fusion | flops 741343232 | bytes 3407876 | tf_op jit(solution)/shard_map/dot_general | solution.py:99
  69.2 0.0 copy-done.5
  69.2 0.0 copy-done.6
  69.2 1.9 %fusion.6 = bf16[512,2048]{1,0:T(8,128)(2,1)} fusion(bf16[512,2048]{1,0:T(8,128)(2,1)} %fusion.5, s32[]{:T(128)S(6)} %select_n.73, bf16[512,1408]{1,0:T(8,128)(2,1)S(1)} %copy-done.4, bf16[512,704]{0,1:T(8,128)(2,1)S(1)} %get-tuple-element.22, bf16[512,704]{0,1:T(8,128)(2,1)S(1)} %get-tuple-element.21), kind=kOutput, calls=%fused_computation.23 | convolution fusion | flops 741343232 | bytes 3407876 | tf_op jit(solution)/shard_map/dot_general | solution.py:99
  71.1 4.9 %all-to-all-start.1 = ((bf16[16,32,2048]{2,1,0:T(8,128)(2,1)}), bf16[16,32,2048]{2,1,0:T(8,128)(2,1)S(1)}, u32[]{:S(2)}, u32[]{:S(2)}) async-start(bf16[16,32,2048]{2,1,0:T(8,128)(2,1)} %bitcast.8), calls=%async_computation.1 | async-start | bytes 4194304 | tf_op jit(solution)/shard_map/all_to_all | solution.py:105
  76.0 3.5 %fusion.12 = f32[1024,1408]{1,0:T(8,128)S(1)} fusion(bf16[512,704]{0,1:T(8,128)(2,1)} %copy-done.6, bf16[512,704]{0,1:T(8,128)(2,1)} %copy-done.5, bf16[512,2048]{1,0:T(8,128)(2,1)} %bitcast.32), kind=kOutput, calls=%fused_computation.31 | convolution fusion | flops 1479278592 | bytes 8257536 | tf_op jit(solution)/shard_map/dot_general | solution.py:127
  79.5 0.0 copy-start.1
  79.5 2.5 %copy-done.1 = f32[1024,1408]{1,0:T(8,128)} copy-done((f32[1024,1408]{1,0:T(8,128)}, f32[1024,1408]{1,0:T(8,128)S(1)}, u32[]{:S(2)}) %copy-start.1) | copy-done | bytes 5767192
  82.0 0.0 copy-start.8
  82.0 1.2 dynamic-slice_convert_fusion
  83.2 1.2 collective-permute-start.1
  84.5 1.6 %convert_element_type.58 = f32[64,1024]{1,0:T(8,128)} convert(bf16[64,1024]{1,0:T(8,128)(2,1)} %param.7) | non-fusion elementwise | flops 65536 | bytes 393216 | tf_op jit(solution)/shard_map/convert_element_type | solution.py:126
  86.1 0.0 copy-done.8
  86.1 0.7 copy.26
  86.9 0.9 eq.59
  87.7 0.9 fusion.8
  88.7 1.9 %dot_general.33 = bf16[64,6,512]{2,1,0:T(8,128)(2,1)} reshape(bf16[384,512]{1,0:T(8,128)(2,1)} %fusion.8) | data formatting | bytes 786432 | tf_op jit(solution)/shard_map/dot_general | solution.py:119
  90.6 25.8 %collective-permute-done.1 = bf16[512,1408]{1,0:T(8,128)(2,1)} collective-permute-done((bf16[512,1408]{1,0:T(8,128)(2,1)}, bf16[512,1408]{1,0:T(8,128)(2,1)}, u32[]{:S(2)}, u32[]{:S(2)}) %collective-permute-start.1) | collective-permute-done | bytes 1441824 | tf_op jit(solution)/shard_map/ppermute | solution.py:136
  116.4 3.6 %fusion = bf16[1,512,1408]{2,1,0:T(8,128)(2,1)} fusion(bf16[512,1408]{1,0:T(8,128)(2,1)} %collective-permute-done.1, f32[1024,1408]{1,0:T(8,128)} %copy-done.1, s32[]{:T(128)S(6)} %select_n.74), kind=kLoop, calls=%fused_computation.8 | loop fusion | flops 2162688 | bytes 5767172 | tf_op jit(solution)/shard_map/broadcast_in_dim | solution.py:142
  120.0 3.5 %all-to-all-done.1 = bf16[16,32,2048]{2,1,0:T(8,128)(2,1)S(1)} async-done(((bf16[16,32,2048]{2,1,0:T(8,128)(2,1)}), bf16[16,32,2048]{2,1,0:T(8,128)(2,1)S(1)}, u32[]{:S(2)}, u32[]{:S(2)}) %all-to-all-start.1) | async-done | bytes 2097184 | tf_op jit(solution)/shard_map/all_to_all | solution.py:105
  123.4 0.0 copy-start.7
  123.4 0.0 copy-start.9
  123.4 2.1 %fusion.13 = f32[64,6,2048]{2,0,1:T(8,128)S(1)} fusion(bf16[512,2048,1]{1,0,2:T(8,128)(2,1)S(1)} %bitcast.29, bf16[64,6,512]{2,1,0:T(8,128)(2,1)} %dot_general.33), kind=kOutput, calls=%fused_computation.32 | convolution fusion | flops 805306368 | bytes 5636096 | tf_op jit(solution)/shard_map/dot_general | solution.py:119
  125.5 0.0 copy-done.7
  125.5 0.0 copy-done.9
  125.5 1.0 multiply_reduce_fusion
  (5 shorter events, 0.0 us)
Async XLA Ops:
  0.6 58.5 %copy-start = (bf16[1,704,1024]{2,1,0:T(8,128)(2,1)S(1)}, bf16[1,704,1024]{2,1,0:T(8,128)(2,1)}, u32[]{:S(2)}) copy-start(bf16[1,704,1024]{2,1,0:T(8,128)(2,1)} %param.11) | copy-start | bytes 4325380
  5.1 54.0 %all-to-all-start = ((bf16[16,32,2048]{2,1,0:T(8,128)(2,1)}), bf16[16,32,2048]{2,1,0:T(8,128)(2,1)S(1)}, u32[]{:S(2)}, u32[]{:S(2)}) async-start(bf16[16,32,2048]{2,1,0:T(8,128)(2,1)} %bitcast.33), calls=%async_computation | async-start | bytes 4194304 | tf_op jit(solution)/shard_map/all_to_all | solution.py:59
  11.7 33.1 %collective-permute-start = (bf16[512,1408]{1,0:T(8,128)(2,1)}, bf16[512,1408]{1,0:T(8,128)(2,1)}, u32[]{:S(2)}, u32[]{:S(2)}) collective-permute-start(bf16[512,1408]{1,0:T(8,128)(2,1)} %bitcast.34), channel_id=1, source_target_pairs={{0,16},{16,0},{1,17},{17,1},{2,18},{18,2},{3,19},{19,3},{4,20},{20... | collective-permute-start | bytes 4325384 | tf_op jit(solution)/shard_map/ppermute | solution.py:11
  59.1 1.3 %copy-start.2 = (bf16[16,32,2048]{2,1,0:T(8,128)(2,1)}, bf16[16,32,2048]{2,1,0:T(8,128)(2,1)S(1)}, u32[]{:S(2)}) copy-start(bf16[16,32,2048]{2,1,0:T(8,128)(2,1)S(1)} %all-to-all-done) | copy-start | bytes 6291460
  59.2 2.1 %copy-start.3 = (bf16[512,1408]{1,0:T(8,128)(2,1)S(1)}, bf16[512,1408]{1,0:T(8,128)(2,1)}, u32[]{:S(2)}) copy-start(bf16[512,1408]{1,0:T(8,128)(2,1)} %get-tuple-element.15) | copy-start | bytes 4325380
  61.2 1.4 %copy-start.4 = (bf16[512,1408]{1,0:T(8,128)(2,1)S(1)}, bf16[512,1408]{1,0:T(8,128)(2,1)}, u32[]{:S(2)}) copy-start(bf16[512,1408]{1,0:T(8,128)(2,1)} %get-tuple-element.16) | copy-start | bytes 4325380
  65.6 3.6 %copy-start.5 = (bf16[512,704]{0,1:T(8,128)(2,1)}, bf16[512,704]{0,1:T(8,128)(2,1)S(1)}, u32[]{:S(2)}) copy-start(bf16[512,704]{0,1:T(8,128)(2,1)S(1)} %get-tuple-element.21) | copy-start | bytes 2162692
  65.6 3.6 %copy-start.6 = (bf16[512,704]{0,1:T(8,128)(2,1)}, bf16[512,704]{0,1:T(8,128)(2,1)S(1)}, u32[]{:S(2)}) copy-start(bf16[512,704]{0,1:T(8,128)(2,1)S(1)} %get-tuple-element.22) | copy-start | bytes 2162692
  71.1 52.3 %all-to-all-start.1 = ((bf16[16,32,2048]{2,1,0:T(8,128)(2,1)}), bf16[16,32,2048]{2,1,0:T(8,128)(2,1)S(1)}, u32[]{:S(2)}, u32[]{:S(2)}) async-start(bf16[16,32,2048]{2,1,0:T(8,128)(2,1)} %bitcast.8), calls=%async_computation.1 | async-start | bytes 4194304 | tf_op jit(solution)/shard_map/all_to_all | solution.py:105
  79.5 2.5 %copy-start.1 = (f32[1024,1408]{1,0:T(8,128)}, f32[1024,1408]{1,0:T(8,128)S(1)}, u32[]{:S(2)}) copy-start(f32[1024,1408]{1,0:T(8,128)S(1)} %fusion.12) | copy-start | bytes 17301508
  82.0 4.1 %copy-start.8 = (s32[64,6]{0,1:T(8,128)S(1)}, s32[64,6]{0,1:T(8,128)}, u32[]{:S(2)}) copy-start(s32[64,6]{0,1:T(8,128)} %param.8) | copy-start | bytes 4612
  83.2 33.1 %collective-permute-start.1 = (bf16[512,1408]{1,0:T(8,128)(2,1)}, bf16[512,1408]{1,0:T(8,128)(2,1)}, u32[]{:S(2)}, u32[]{:S(2)}) collective-permute-start(bf16[512,1408]{1,0:T(8,128)(2,1)} %dynamic-slice_convert_fusion), channel_id=1, source_target_pairs={{0,16},{16,0},{1,17},{17,1},{2,18},{18,2},{3,19},{19,3},{4,20},{20... | collective-permute-start | bytes 4325384 | tf_op jit(solution)/shard_map/ppermute | solution.py:136
  123.4 2.1 %copy-start.7 = (f32[64,1024]{1,0:T(8,128)S(1)}, f32[64,1024]{1,0:T(8,128)}, u32[]{:S(2)}) copy-start(f32[64,1024]{1,0:T(8,128)} %convert_element_type.58) | copy-start | bytes 786436
  123.4 2.1 %copy-start.9 = (f32[64,6]{0,1:T(8,128)S(1)}, f32[64,6]{0,1:T(8,128)}, u32[]{:S(2)}) copy-start(f32[64,6]{0,1:T(8,128)} %param.9) | copy-start | bytes 4612

commit v19 on v14

--- a/solution.py
+++ b/solution.py
@@ -31,8 +31,8 @@
     capacity = 4 * token_count * top_count // (3 * experts)
     weight_blocks = gather_rows(w_gate_up[0], "dp", block_rows)
     hit = expert_ids[:, :, None] == jnp.arange(experts, dtype=jnp.int32)[None, None, :]
-    token_hit = jnp.any(hit, axis=1)
     token_prob = jnp.sum(jnp.where(hit, gate_probs[:, :, None], 0.0), axis=1)
+    token_hit = token_prob > 0.0
     earlier = (
         lax.broadcasted_iota(jnp.int32, (token_count, token_count), 0)
         > lax.broadcasted_iota(jnp.int32, (token_count, token_count), 1)

time: 125 us -> 124 us (level)
  no operation moved by 1% of the time
where the time goes in v19:
time: 124 us
  waiting for transfers between devices  77.3 us (62%)
  starting transfers between devices  14 us (11%)
  matrix products  13.7 us (11%)
  other arithmetic  10.9 us (9%)
  local copies, waits for them, and re-layouts  7.04 us (6%)
    ppermute x1, waiting for transfers between devices, gather_rows(): lax.ppermute(own, axis_name, [(i, (i + shift) % count) for i in range(cou...  31.9 us
    ppermute x1, waiting for transfers between devices, local(): lax.ppermute(grad_block((me_dp + shift) % replicas).astype(jnp.bfloat16),...  30.2 us
    all_to_all x1, waiting for transfers between devices, local(): lax.all_to_all(both_send.reshape(experts, capacity, 2 * model_width), 'ex...  11.7 us
    all_to_all x1, starting transfers between devices, local(): lax.all_to_all(both_send.reshape(experts, capacity, 2 * model_width), 'ex...  6.55 us
    unnamed x22, local copies, waits for them, and re-layouts  5.32 us
    all_to_all x1, starting transfers between devices, local(): lax.all_to_all(send_back.reshape(experts, capacity, 2 * model_width), 'ex...  4.91 us
    broadcast_in_dim x1, other arithmetic, local(): grad_rows.astype(jnp.bfloat16)[None]  3.6 us
    dot_general x1, matrix products, local(): lax.dot_general(input_rows, pair_cot, (((0,), (0,)), ((), ())), preferred...  3.48 us
  transfers between devices with their start and end apart: 4, of which 4 were waited for; matrix products, arithmetic and copies ran while one was open for 10% of the time, Pallas kernels for 0%

profile of v19, /device:TPU:11, one launch (start us, length us, event | category | flops | bytes accessed | tf_op | source)
XLA Modules:
  0.0 123.7 jit_solution(7818625986819937283)
XLA Ops:
  0.6 0.0 copy-start
  0.7 0.8 select_reduce_fusion.2
  1.5 0.1 convolution_convert_fusion.3
  1.6 0.2 select_reduce_fusion
  1.8 0.1 broadcast_in_dim.75
  1.9 0.1 eq.80
  2.0 0.1 fusion.20
  2.1 3.0 %multiply_convert_fusion = bf16[512,2048]{1,0:T(8,128)(2,1)} fusion(pred[512,64]{1,0:T(32,128)(4,1)S(1)} %fusion.20, f32[512]{0:T(512)S(1)} %broadcast_in_dim.75, pred[2048]{0:T(1024)(128)(4,1)S(1)} %iota_compare_fusion.5, bf16[64,1024]{1,0:T(8,128)(2,1)} %param.7, bf16[64,1024]{1,0:T(8,128)(2,1)} %param.6), kind=kOutput, calls=%fused_computation | convolution fusion | flops 137887744 | bytes 2396160 | tf_op jit(solution)/shard_map/dot_general | solution.py:53
  5.1 6.6 %all-to-all-start = ((bf16[16,32,2048]{2,1,0:T(8,128)(2,1)}), bf16[16,32,2048]{2,1,0:T(8,128)(2,1)S(1)}, u32[]{:S(2)}, u32[]{:S(2)}) async-start(bf16[16,32,2048]{2,1,0:T(8,128)(2,1)} %bitcast.37), calls=%async_computation | async-start | bytes 4194304 | tf_op jit(solution)/shard_map/all_to_all | solution.py:59
  11.7 1.2 %collective-permute-start = (bf16[512,1408]{1,0:T(8,128)(2,1)}, bf16[512,1408]{1,0:T(8,128)(2,1)}, u32[]{:S(2)}, u32[]{:S(2)}) collective-permute-start(bf16[512,1408]{1,0:T(8,128)(2,1)} %bitcast.38), channel_id=1, source_target_pairs={{0,16},{16,0},{1,17},{17,1},{2,18},{18,2},{3,19},{19,3},{4,20},{20... | collective-permute-start | bytes 4325384 | tf_op jit(solution)/shard_map/ppermute | solution.py:11
  12.9 31.9 %collective-permute-done = bf16[512,1408]{1,0:T(8,128)(2,1)} collective-permute-done((bf16[512,1408]{1,0:T(8,128)(2,1)}, bf16[512,1408]{1,0:T(8,128)(2,1)}, u32[]{:S(2)}, u32[]{:S(2)}) %collective-permute-start) | collective-permute-done | bytes 1441824 | tf_op jit(solution)/shard_map/ppermute | solution.py:11
  44.8 2.6 %broadcast_select_fusion = bf16[512,1408]{1,0:T(8,128)(2,1)} fusion(bf16[512,1408]{1,0:T(8,128)(2,1)} %collective-permute-done, pred[]{:T(512)S(6)} %ge.3), kind=kLoop, calls=%fused_computation.18 | loop fusion | flops 720896 | bytes 2883585 | tf_op jit(solution)/shard_map/jit(_where)/select_n | solution.py:17
  47.4 11.7 %all-to-all-done = bf16[16,32,2048]{2,1,0:T(8,128)(2,1)S(1)} async-done(((bf16[16,32,2048]{2,1,0:T(8,128)(2,1)}), bf16[16,32,2048]{2,1,0:T(8,128)(2,1)S(1)}, u32[]{:S(2)}, u32[]{:S(2)}) %all-to-all-start) | async-done | bytes 2097184 | tf_op jit(solution)/shard_map/all_to_all | solution.py:59
  59.1 0.0 copy-start.3
  59.1 0.1 slice.24
  59.2 0.0 copy-done
  59.2 0.0 copy-start.7
  59.2 0.9 fusion.2
  60.1 0.3 copy-done.3
  60.4 0.8 copy-done.7
  61.2 0.0 copy-start.4
  61.2 1.0 fusion.12
  62.2 0.4 copy-done.4
  62.6 1.0 convolution_add_fusion
  63.5 1.1 convolution_convert_fusion
  64.7 0.9 multiply_convert_fusion.2
  65.6 0.0 copy-start.5
  65.6 0.0 copy-start.6
  65.6 0.2 dynamic_update_slice.9
  65.9 1.0 fusion.5
  66.9 0.0 copy-done.5
  66.9 0.0 copy-done.6
  66.9 1.0 fusion.6
  68.0 0.0 copy-start.2
  68.0 1.3 %copy-done.2 = bf16[512,2048]{1,0:T(8,128)(2,1)} copy-done((bf16[512,2048]{1,0:T(8,128)(2,1)}, bf16[512,2048]{1,0:T(8,128)(2,1)S(1)}, u32[]{:S(2)}) %copy-start.2) | copy-done | bytes 2097176
  69.3 4.9 %all-to-all-start.1 = ((bf16[16,32,2048]{2,1,0:T(8,128)(2,1)}), bf16[16,32,2048]{2,1,0:T(8,128)(2,1)S(1)}, u32[]{:S(2)}, u32[]{:S(2)}) async-start(bf16[16,32,2048]{2,1,0:T(8,128)(2,1)} %bitcast.33), calls=%async_computation.1 | async-start | bytes 4194304 | tf_op jit(solution)/shard_map/all_to_all | solution.py:105
  74.2 3.5 %fusion.14 = f32[1024,1408]{1,0:T(8,128)S(1)} fusion(bf16[512,704]{0,1:T(8,128)(2,1)} %copy-done.6, bf16[512,704]{0,1:T(8,128)(2,1)} %copy-done.5, bf16[512,2048]{1,0:T(8,128)(2,1)} %bitcast.36), kind=kOutput, calls=%fused_computation.31 | convolution fusion | flops 1479278592 | bytes 8257536 | tf_op jit(solution)/shard_map/dot_general | solution.py:125
  77.7 0.0 copy-start.1
  77.7 2.5 %copy-done.1 = f32[1024,1408]{1,0:T(8,128)} copy-done((f32[1024,1408]{1,0:T(8,128)}, f32[1024,1408]{1,0:T(8,128)S(1)}, u32[]{:S(2)}) %copy-start.1) | copy-done | bytes 5767192
  80.2 0.0 copy-start.9
  80.2 1.2 %dynamic-slice_convert_fusion = bf16[512,1408]{1,0:T(8,128)(2,1)} fusion(f32[1024,1408]{1,0:T(8,128)S(1)} %fusion.14, s32[]{:T(128)S(6)} %select_n.71), kind=kLoop, calls=%fused_computation.3 | loop fusion | bytes 2883588 | tf_op jit(solution)/shard_map/convert_element_type | solution.py:135
  81.4 1.2 %collective-permute-start.1 = (bf16[512,1408]{1,0:T(8,128)(2,1)}, bf16[512,1408]{1,0:T(8,128)(2,1)}, u32[]{:S(2)}, u32[]{:S(2)}) collective-permute-start(bf16[512,1408]{1,0:T(8,128)(2,1)} %dynamic-slice_convert_fusion), channel_id=1, source_target_pairs={{0,16},{16,0},{1,17},{17,1},{2,18},{18,2},{3,19},{19,3},{4,20},{20... | collective-permute-start | bytes 4325384 | tf_op jit(solution)/shard_map/ppermute | solution.py:134
  82.7 1.6 %convert_element_type.55 = f32[64,1024]{1,0:T(8,128)} convert(bf16[64,1024]{1,0:T(8,128)(2,1)} %param.7) | non-fusion elementwise | flops 65536 | bytes 393216 | tf_op jit(solution)/shard_map/convert_element_type | solution.py:124
  84.3 0.0 copy-done.9
  84.3 30.2 %collective-permute-done.1 = bf16[512,1408]{1,0:T(8,128)(2,1)} collective-permute-done((bf16[512,1408]{1,0:T(8,128)(2,1)}, bf16[512,1408]{1,0:T(8,128)(2,1)}, u32[]{:S(2)}, u32[]{:S(2)}) %collective-permute-start.1) | collective-permute-done | bytes 1441824 | tf_op jit(solution)/shard_map/ppermute | solution.py:134
  114.6 3.6 %fusion = bf16[1,512,1408]{2,1,0:T(8,128)(2,1)} fusion(bf16[512,1408]{1,0:T(8,128)(2,1)} %collective-permute-done.1, f32[1024,1408]{1,0:T(8,128)} %copy-done.1, s32[]{:T(128)S(6)} %select_n.69), kind=kLoop, calls=%fused_computation.8 | loop fusion | flops 2162688 | bytes 5767172 | tf_op jit(solution)/shard_map/broadcast_in_dim | solution.py:140
  118.2 3.5 %all-to-all-done.1 = bf16[16,32,2048]{2,1,0:T(8,128)(2,1)S(1)} async-done(((bf16[16,32,2048]{2,1,0:T(8,128)(2,1)}), bf16[16,32,2048]{2,1,0:T(8,128)(2,1)S(1)}, u32[]{:S(2)}, u32[]{:S(2)}) %all-to-all-start.1) | async-done | bytes 2097184 | tf_op jit(solution)/shard_map/all_to_all | solution.py:105
  121.6 0.0 copy-start.8
  121.6 0.0 copy-start.10
  121.6 1.0 fusion.9
  122.7 0.0 copy-done.8
  122.7 0.0 copy-done.10
  122.7 1.0 multiply_reduce_fusion
  (5 shorter events, 0.0 us)
Async XLA Ops:
  0.6 58.5 %copy-start = (bf16[1,704,1024]{2,1,0:T(8,128)(2,1)S(1)}, bf16[1,704,1024]{2,1,0:T(8,128)(2,1)}, u32[]{:S(2)}) copy-start(bf16[1,704,1024]{2,1,0:T(8,128)(2,1)} %param.11) | copy-start | bytes 4325380
  5.1 54.0 %all-to-all-start = ((bf16[16,32,2048]{2,1,0:T(8,128)(2,1)}), bf16[16,32,2048]{2,1,0:T(8,128)(2,1)S(1)}, u32[]{:S(2)}, u32[]{:S(2)}) async-start(bf16[16,32,2048]{2,1,0:T(8,128)(2,1)} %bitcast.37), calls=%async_computation | async-start | bytes 4194304 | tf_op jit(solution)/shard_map/all_to_all | solution.py:59
  11.7 33.1 %collective-permute-start = (bf16[512,1408]{1,0:T(8,128)(2,1)}, bf16[512,1408]{1,0:T(8,128)(2,1)}, u32[]{:S(2)}, u32[]{:S(2)}) collective-permute-start(bf16[512,1408]{1,0:T(8,128)(2,1)} %bitcast.38), channel_id=1, source_target_pairs={{0,16},{16,0},{1,17},{17,1},{2,18},{18,2},{3,19},{19,3},{4,20},{20... | collective-permute-start | bytes 4325384 | tf_op jit(solution)/shard_map/ppermute | solution.py:11
  59.1 1.3 %copy-start.3 = (bf16[16,32,2048]{2,1,0:T(8,128)(2,1)}, bf16[16,32,2048]{2,1,0:T(8,128)(2,1)S(1)}, u32[]{:S(2)}) copy-start(bf16[16,32,2048]{2,1,0:T(8,128)(2,1)S(1)} %all-to-all-done) | copy-start | bytes 6291460
  59.2 2.0 %copy-start.7 = (bf16[1,512,1408]{2,1,0:T(8,128)(2,1)S(1)}, bf16[1,512,1408]{2,1,0:T(8,128)(2,1)}, u32[]{:S(2)}) copy-start(bf16[1,512,1408]{2,1,0:T(8,128)(2,1)} %param.10) | copy-start | bytes 4325380
  61.2 1.4 %copy-start.4 = (bf16[512,1408]{1,0:T(8,128)(2,1)S(1)}, bf16[512,1408]{1,0:T(8,128)(2,1)}, u32[]{:S(2)}) copy-start(bf16[512,1408]{1,0:T(8,128)(2,1)} %broadcast_select_fusion) | copy-start | bytes 4325380
  65.6 1.3 %copy-start.5 = (bf16[512,704]{0,1:T(8,128)(2,1)}, bf16[512,704]{0,1:T(8,128)(2,1)S(1)}, u32[]{:S(2)}) copy-start(bf16[512,704]{0,1:T(8,128)(2,1)S(1)} %get-tuple-element.17) | copy-start | bytes 2162692
  65.6 1.3 %copy-start.6 = (bf16[512,704]{0,1:T(8,128)(2,1)}, bf16[512,704]{0,1:T(8,128)(2,1)S(1)}, u32[]{:S(2)}) copy-start(bf16[512,704]{0,1:T(8,128)(2,1)S(1)} %get-tuple-element.18) | copy-start | bytes 2162692
  68.0 1.3 %copy-start.2 = (bf16[512,2048]{1,0:T(8,128)(2,1)}, bf16[512,2048]{1,0:T(8,128)(2,1)S(1)}, u32[]{:S(2)}) copy-start(bf16[512,2048]{1,0:T(8,128)(2,1)S(1)} %fusion.6) | copy-start | bytes 6291460
  69.3 52.3 %all-to-all-start.1 = ((bf16[16,32,2048]{2,1,0:T(8,128)(2,1)}), bf16[16,32,2048]{2,1,0:T(8,128)(2,1)S(1)}, u32[]{:S(2)}, u32[]{:S(2)}) async-start(bf16[16,32,2048]{2,1,0:T(8,128)(2,1)} %bitcast.33), calls=%async_computation.1 | async-start | bytes 4194304 | tf_op jit(solution)/shard_map/all_to_all | solution.py:105
  77.7 2.5 %copy-start.1 = (f32[1024,1408]{1,0:T(8,128)}, f32[1024,1408]{1,0:T(8,128)S(1)}, u32[]{:S(2)}) copy-start(f32[1024,1408]{1,0:T(8,128)S(1)} %fusion.14) | copy-start | bytes 17301508
  80.2 4.1 %copy-start.9 = (s32[64,6]{0,1:T(8,128)S(1)}, s32[64,6]{0,1:T(8,128)}, u32[]{:S(2)}) copy-start(s32[64,6]{0,1:T(8,128)} %param.8) | copy-start | bytes 4612
  81.4 33.1 %collective-permute-start.1 = (bf16[512,1408]{1,0:T(8,128)(2,1)}, bf16[512,1408]{1,0:T(8,128)(2,1)}, u32[]{:S(2)}, u32[]{:S(2)}) collective-permute-start(bf16[512,1408]{1,0:T(8,128)(2,1)} %dynamic-slice_convert_fusion), channel_id=1, source_target_pairs={{0,16},{16,0},{1,17},{17,1},{2,18},{18,2},{3,19},{19,3},{4,20},{20... | collective-permute-start | bytes 4325384 | tf_op jit(solution)/shard_map/ppermute | solution.py:134
  121.6 1.0 copy-start.8
  121.6 1.0 copy-start.10

commit v20 on v15

--- a/solution.py
+++ b/solution.py
@@ -129,7 +129,7 @@
     def grad_block(block):
         return lax.dynamic_slice_in_dim(weight_cot, block * block_rows, block_rows, axis=0)
 
-    grad_rows = grad_block(me_dp)
+    grad_rows = grad_block(me_dp).astype(jnp.bfloat16).astype(jnp.float32)
     for shift in range(1, replicas):
         moved = lax.ppermute(
             grad_block((me_dp + shift) % replicas).astype(jnp.bfloat16),

time: 124 us -> 127 us (1.024)
  waiting for transfers between devices: 76.2 us -> 78.8 us
    all_to_all x1, waiting for transfers between devices: 3.45 us -> 5.53 us  [local(): lax.all_to_all(send_back.reshape(experts, capacity, 2 * model_width), 'ex...]
    unnamed x22 -> x24, local copies, waits for them, and re-layouts: 5.33 us -> 4.09 us
  transfers between devices with their start and end apart: 4 -> 4, of which waited for: 4 -> 4; matrix products, arithmetic and copies ran while one was open for 11% -> 10% of each run, Pallas kernels for 0% -> 0%
where the time goes in v20:
time: 127 us
  waiting for transfers between devices  78.8 us (62%)
  matrix products  14.9 us (12%)
  starting transfers between devices  14.2 us (11%)
  other arithmetic  11.1 us (9%)
  local copies, waits for them, and re-layouts  7.1 us (6%)
    ppermute x1, waiting for transfers between devices, gather_rows(): lax.ppermute(own, axis_name, [(i, (i + shift) % count) for i in range(cou...  31.7 us
    ppermute x1, waiting for transfers between devices, local(): lax.ppermute(grad_block((me_dp + shift) % replicas).astype(jnp.bfloat16),...  30.2 us
    all_to_all x1, waiting for transfers between devices, local(): lax.all_to_all(both_send.reshape(experts, capacity, 2 * model_width), 'ex...  11.4 us
    all_to_all x1, starting transfers between devices, local(): lax.all_to_all(both_send.reshape(experts, capacity, 2 * model_width), 'ex...  6.69 us
    all_to_all x1, waiting for transfers between devices, local(): lax.all_to_all(send_back.reshape(experts, capacity, 2 * model_width), 'ex...  5.53 us
    all_to_all x1, starting transfers between devices, local(): lax.all_to_all(send_back.reshape(experts, capacity, 2 * model_width), 'ex...  4.91 us
    unnamed x24, local copies, waits for them, and re-layouts  4.09 us
    dot_general x1, matrix products, local(): lax.dot_general(input_rows, pair_cot, (((0,), (0,)), ((), ())), preferred...  3.48 us
  transfers between devices with their start and end apart: 4, of which 4 were waited for; matrix products, arithmetic and copies ran while one was open for 10% of the time, Pallas kernels for 0%

profile of v20, /device:TPU:11, one launch (start us, length us, event | category | flops | bytes accessed | tf_op | source)
XLA Modules:
  0.0 126.9 jit_solution(8341017604140966763)
XLA Ops:
  0.6 0.0 copy-start
  0.7 0.8 select_reduce_fusion.2
  1.5 0.1 convolution_convert_fusion.3
  1.6 0.2 select_reduce_fusion
  1.8 0.1 broadcast_in_dim.72
  1.9 0.1 eq.80
  2.0 0.1 fusion.20
  2.1 3.0 %multiply_convert_fusion = bf16[512,2048]{1,0:T(8,128)(2,1)} fusion(pred[512,64]{1,0:T(32,128)(4,1)S(1)} %fusion.20, f32[512]{0:T(512)S(1)} %broadcast_in_dim.72, pred[2048]{0:T(1024)(128)(4,1)S(1)} %iota_compare_fusion.5, bf16[64,1024]{1,0:T(8,128)(2,1)} %param.7, bf16[64,1024]{1,0:T(8,128)(2,1)} %param.6), kind=kOutput, calls=%fused_computation | convolution fusion | flops 137887744 | bytes 2396160 | tf_op jit(solution)/shard_map/dot_general | solution.py:53
  5.1 0.0 copy-start.6
  5.1 6.7 %all-to-all-start = ((bf16[16,32,2048]{2,1,0:T(8,128)(2,1)}), bf16[16,32,2048]{2,1,0:T(8,128)(2,1)}, u32[]{:S(2)}, u32[]{:S(2)}) async-start(bf16[16,32,2048]{2,1,0:T(8,128)(2,1)} %bitcast.5), calls=%async_computation | async-start | bytes 4194304 | tf_op jit(solution)/shard_map/all_to_all | solution.py:59
  11.8 0.0 copy-done.6
  11.8 1.3 %collective-permute-start = (bf16[512,1408]{1,0:T(8,128)(2,1)S(1)}, bf16[512,1408]{1,0:T(8,128)(2,1)}, u32[]{:S(2)}, u32[]{:S(2)}) collective-permute-start(bf16[512,1408]{1,0:T(8,128)(2,1)S(1)} %bitcast.35), channel_id=1, source_target_pairs={{0,16},{16,0},{1,17},{17,1},{2,18},{18,2},{3,19},{19,3},{4,20},{20... | collective-permute-start | bytes 4325384 | tf_op jit(solution)/shard_map/ppermute | solution.py:11
  13.1 31.7 %collective-permute-done = bf16[512,1408]{1,0:T(8,128)(2,1)} collective-permute-done((bf16[512,1408]{1,0:T(8,128)(2,1)S(1)}, bf16[512,1408]{1,0:T(8,128)(2,1)}, u32[]{:S(2)}, u32[]{:S(2)}) %collective-permute-start) | collective-permute-done | bytes 1441824 | tf_op jit(solution)/shard_map/ppermute | solution.py:11
  44.8 3.1 %broadcast_select_fusion = (bf16[512,1408]{1,0:T(8,128)(2,1)}, bf16[512,1408]{1,0:T(8,128)(2,1)S(1)}) fusion(bf16[512,1408]{1,0:T(8,128)(2,1)} %collective-permute-done, pred[]{:T(512)S(6)} %ge.3, bf16[512,1408]{1,0:T(8,128)(2,1)} %bitcast.34), kind=kLoop, calls=%fused_computation.19 | loop fusion | flops 1441792 | bytes 5767169 | tf_op jit(solution)/shard_map/jit(_where)/select_n | solution.py:17
  47.9 0.0 copy-start.2
  47.9 11.4 %all-to-all-done = bf16[16,32,2048]{2,1,0:T(8,128)(2,1)} async-done(((bf16[16,32,2048]{2,1,0:T(8,128)(2,1)}), bf16[16,32,2048]{2,1,0:T(8,128)(2,1)}, u32[]{:S(2)}, u32[]{:S(2)}) %all-to-all-start) | async-done | bytes 2097184 | tf_op jit(solution)/shard_map/all_to_all | solution.py:59
  59.3 1.3 %slice.24 = bf16[512,1024]{1,0:T(8,128)(2,1)S(1)} slice(bf16[512,2048]{1,0:T(8,128)(2,1)} %bitcast.6), slice={[0:512], [0:1024]} | slice | bytes 2097152 | tf_op jit(solution)/shard_map/slice | solution.py:66
  60.6 0.0 copy-done
  60.6 2.2 %fusion.2 = f32[512,704]{0,1:T(8,128)S(1)} fusion(bf16[1,704,1024]{2,1,0:T(8,128)(2,1)S(1)} %copy-done, bf16[512,2048]{1,0:T(8,128)(2,1)} %bitcast.6), kind=kOutput, calls=%fused_computation.12 | convolution fusion | flops 738197504 | bytes 3932160 | tf_op jit(solution)/shard_map/dot_general | solution.py:74
  62.8 0.0 copy-done.2
  62.8 0.0 copy-start.4
  62.8 1.0 fusion.12
  63.8 0.4 copy-done.4
  64.1 1.0 convolution_add_fusion
  65.1 1.1 convolution_convert_fusion
  66.2 0.9 multiply_convert_fusion.2
  67.2 0.0 copy-start.8
  67.2 0.0 copy-start.9
  67.2 0.0 copy-start.3
  67.2 0.2 dynamic_update_slice.9
  67.4 1.6 %copy-done.3 = bf16[512,1408]{1,0:T(8,128)(2,1)S(1)} copy-done((bf16[512,1408]{1,0:T(8,128)(2,1)S(1)}, bf16[512,1408]{1,0:T(8,128)(2,1)}, u32[]{:S(2)}) %copy-start.3) | copy-done | bytes 1441816
  69.1 1.0 fusion.5
  70.1 0.0 copy-done.8
  70.1 0.0 copy-done.9
  70.1 1.0 fusion.6
  71.2 0.0 copy-start.1
  71.2 1.3 %copy-done.1 = bf16[512,2048]{1,0:T(8,128)(2,1)} copy-done((bf16[512,2048]{1,0:T(8,128)(2,1)}, bf16[512,2048]{1,0:T(8,128)(2,1)S(1)}, u32[]{:S(2)}) %copy-start.1) | copy-done | bytes 2097176
  72.5 4.9 %all-to-all-start.1 = ((bf16[16,32,2048]{2,1,0:T(8,128)(2,1)}), bf16[16,32,2048]{2,1,0:T(8,128)(2,1)S(1)}, u32[]{:S(2)}, u32[]{:S(2)}) async-start(bf16[16,32,2048]{2,1,0:T(8,128)(2,1)} %bitcast.33), calls=%async_computation.1 | async-start | bytes 4194304 | tf_op jit(solution)/shard_map/all_to_all | solution.py:105
  77.4 3.5 %fusion.14 = bf16[1024,1408]{1,0:T(8,128)(2,1)S(1)} fusion(bf16[512,704]{0,1:T(8,128)(2,1)} %copy-done.9, bf16[512,704]{0,1:T(8,128)(2,1)} %copy-done.8, bf16[512,2048]{1,0:T(8,128)(2,1)} %bitcast.6), kind=kOutput, calls=%fused_computation.33 | convolution fusion | flops 1479278592 | bytes 5373952 | tf_op jit(solution)/shard_map/dot_general | solution.py:125
  80.9 0.0 copy-start.5
  80.9 0.0 copy-start.10
  80.9 1.3 %dynamic-slice_convert_fusion = bf16[512,1408]{1,0:T(8,128)(2,1)} fusion(bf16[1024,1408]{1,0:T(8,128)(2,1)S(1)} %fusion.14, s32[]{:T(128)S(6)} %select_n.76), kind=kLoop, calls=%fused_computation.3 | loop fusion | bytes 2883588 | tf_op jit(solution)/shard_map/convert_element_type | solution.py:135
  82.2 0.7 copy-done.5
  82.9 1.2 collective-permute-start.1
  84.2 1.6 %convert_element_type.61 = f32[64,1024]{1,0:T(8,128)} convert(bf16[64,1024]{1,0:T(8,128)(2,1)} %param.7) | non-fusion elementwise | flops 65536 | bytes 393216 | tf_op jit(solution)/shard_map/convert_element_type | solution.py:124
  85.8 0.0 copy-done.10
  85.8 30.2 %collective-permute-done.1 = bf16[512,1408]{1,0:T(8,128)(2,1)} collective-permute-done((bf16[512,1408]{1,0:T(8,128)(2,1)}, bf16[512,1408]{1,0:T(8,128)(2,1)}, u32[]{:S(2)}, u32[]{:S(2)}) %collective-permute-start.1) | collective-permute-done | bytes 1441824 | tf_op jit(solution)/shard_map/ppermute | solution.py:134
  116.1 3.2 %fusion = bf16[1,512,1408]{2,1,0:T(8,128)(2,1)} fusion(bf16[512,1408]{1,0:T(8,128)(2,1)} %collective-permute-done.1, bf16[1024,1408]{1,0:T(8,128)(2,1)} %copy-done.5, s32[]{:T(128)S(6)} %select_n.74), kind=kLoop, calls=%fused_computation.9 | loop fusion | flops 2883584 | bytes 4325380 | tf_op jit(solution)/shard_map/broadcast_in_dim | solution.py:140
  119.3 5.5 %all-to-all-done.1 = bf16[16,32,2048]{2,1,0:T(8,128)(2,1)S(1)} async-done(((bf16[16,32,2048]{2,1,0:T(8,128)(2,1)}), bf16[16,32,2048]{2,1,0:T(8,128)(2,1)S(1)}, u32[]{:S(2)}, u32[]{:S(2)}) %all-to-all-start.1) | async-done | bytes 2097184 | tf_op jit(solution)/shard_map/all_to_all | solution.py:105
  124.8 0.0 copy-start.7
  124.8 0.0 copy-start.11
  124.8 1.0 fusion.9
  125.9 0.0 copy-done.7
  125.9 0.0 copy-done.11
  125.9 1.0 multiply_reduce_fusion
  (5 shorter events, 0.0 us)
Async XLA Ops:
  0.6 60.0 %copy-start = (bf16[1,704,1024]{2,1,0:T(8,128)(2,1)S(1)}, bf16[1,704,1024]{2,1,0:T(8,128)(2,1)}, u32[]{:S(2)}) copy-start(bf16[1,704,1024]{2,1,0:T(8,128)(2,1)} %param.11) | copy-start | bytes 4325380
  5.1 6.7 %copy-start.6 = (bf16[1,512,1408]{2,1,0:T(8,128)(2,1)S(1)}, bf16[1,512,1408]{2,1,0:T(8,128)(2,1)}, u32[]{:S(2)}) copy-start(bf16[1,512,1408]{2,1,0:T(8,128)(2,1)} %param.10) | copy-start | bytes 4325380
  5.1 54.2 %all-to-all-start = ((bf16[16,32,2048]{2,1,0:T(8,128)(2,1)}), bf16[16,32,2048]{2,1,0:T(8,128)(2,1)}, u32[]{:S(2)}, u32[]{:S(2)}) async-start(bf16[16,32,2048]{2,1,0:T(8,128)(2,1)} %bitcast.5), calls=%async_computation | async-start | bytes 4194304 | tf_op jit(solution)/shard_map/all_to_all | solution.py:59
  11.8 33.0 %collective-permute-start = (bf16[512,1408]{1,0:T(8,128)(2,1)S(1)}, bf16[512,1408]{1,0:T(8,128)(2,1)}, u32[]{:S(2)}, u32[]{:S(2)}) collective-permute-start(bf16[512,1408]{1,0:T(8,128)(2,1)S(1)} %bitcast.35), channel_id=1, source_target_pairs={{0,16},{16,0},{1,17},{17,1},{2,18},{18,2},{3,19},{19,3},{4,20},{20... | collective-permute-start | bytes 4325384 | tf_op jit(solution)/shard_map/ppermute | solution.py:11
  47.9 14.9 %copy-start.2 = (bf16[512,1408]{1,0:T(8,128)(2,1)}, bf16[512,1408]{1,0:T(8,128)(2,1)S(1)}, u32[]{:S(2)}) copy-start(bf16[512,1408]{1,0:T(8,128)(2,1)S(1)} %get-tuple-element.15) | copy-start | bytes 4325380
  62.8 1.4 %copy-start.4 = (bf16[512,1408]{1,0:T(8,128)(2,1)S(1)}, bf16[512,1408]{1,0:T(8,128)(2,1)}, u32[]{:S(2)}) copy-start(bf16[512,1408]{1,0:T(8,128)(2,1)} %get-tuple-element.16) | copy-start | bytes 4325380
  67.2 2.9 %copy-start.8 = (bf16[512,704]{0,1:T(8,128)(2,1)}, bf16[512,704]{0,1:T(8,128)(2,1)S(1)}, u32[]{:S(2)}) copy-start(bf16[512,704]{0,1:T(8,128)(2,1)S(1)} %get-tuple-element.21) | copy-start | bytes 2162692
  67.2 2.9 %copy-start.9 = (bf16[512,704]{0,1:T(8,128)(2,1)}, bf16[512,704]{0,1:T(8,128)(2,1)S(1)}, u32[]{:S(2)}) copy-start(bf16[512,704]{0,1:T(8,128)(2,1)S(1)} %get-tuple-element.22) | copy-start | bytes 2162692
  67.2 1.9 %copy-start.3 = (bf16[512,1408]{1,0:T(8,128)(2,1)S(1)}, bf16[512,1408]{1,0:T(8,128)(2,1)}, u32[]{:S(2)}) copy-start(bf16[512,1408]{1,0:T(8,128)(2,1)} %copy-done.2) | copy-start | bytes 4325380
  71.2 1.3 %copy-start.1 = (bf16[512,2048]{1,0:T(8,128)(2,1)}, bf16[512,2048]{1,0:T(8,128)(2,1)S(1)}, u32[]{:S(2)}) copy-start(bf16[512,2048]{1,0:T(8,128)(2,1)S(1)} %fusion.6) | copy-start | bytes 6291460
  72.5 52.3 %all-to-all-start.1 = ((bf16[16,32,2048]{2,1,0:T(8,128)(2,1)}), bf16[16,32,2048]{2,1,0:T(8,128)(2,1)S(1)}, u32[]{:S(2)}, u32[]{:S(2)}) async-start(bf16[16,32,2048]{2,1,0:T(8,128)(2,1)} %bitcast.33), calls=%async_computation.1 | async-start | bytes 4194304 | tf_op jit(solution)/shard_map/all_to_all | solution.py:105
  80.9 2.0 %copy-start.5 = (bf16[1024,1408]{1,0:T(8,128)(2,1)}, bf16[1024,1408]{1,0:T(8,128)(2,1)S(1)}, u32[]{:S(2)}) copy-start(bf16[1024,1408]{1,0:T(8,128)(2,1)S(1)} %fusion.14) | copy-start | bytes 8650756
  80.9 4.9 %copy-start.10 = (s32[64,6]{0,1:T(8,128)S(1)}, s32[64,6]{0,1:T(8,128)}, u32[]{:S(2)}) copy-start(s32[64,6]{0,1:T(8,128)} %param.8) | copy-start | bytes 4612
  82.9 33.1 %collective-permute-start.1 = (bf16[512,1408]{1,0:T(8,128)(2,1)}, bf16[512,1408]{1,0:T(8,128)(2,1)}, u32[]{:S(2)}, u32[]{:S(2)}) collective-permute-start(bf16[512,1408]{1,0:T(8,128)(2,1)} %dynamic-slice_convert_fusion), channel_id=1, source_target_pairs={{0,16},{16,0},{1,17},{17,1},{2,18},{18,2},{3,19},{19,3},{4,20},{20... | collective-permute-start | bytes 4325384 | tf_op jit(solution)/shard_map/ppermute | solution.py:134
  124.8 1.0 copy-start.7
  124.8 1.0 copy-start.11
